TPU v7x, 32 devices: a whole 2x2x4 slice. The times are simulated.
32 devices in a mesh: tm: 4 (over y, x), height: 2 (over core), chan: 4 (over z).
Axes of the slice: x: 2, y: 2, z: 4, core: 2. Of those that a mesh axis runs over, the one named last changes fastest.
Arguments:
- features: bfloat16 [384, 8, 8, 160], P('chan', 'tm', 'height'), may hold values from -400 to 400, as said below
- cotangent: bfloat16 [384, 8, 8, 160], P('chan', 'tm', 'height'), may hold values from -6 to 6
- conv_weight: bfloat16 [384, 27, 384], P('chan'), may hold values from -0.0625 to 0.0625
- norm_gain: float32 [384], replicated, may hold values from 0.5 to 1.5
- norm_bias: float32 [384], replicated, may hold values from -3 to 3
Outputs:
- input_grad: bfloat16 [384, 8, 8, 160], P('chan', 'tm', 'height')
- weight_grad: float32 [384, 27, 384], P('chan')
Inputs may be any that keep to these rules, and one draw needn't show every extreme that they name: `features`: bounded activations.
All inputs are finite; a program needn't handle non-finite values.
Results may differ from a plain program's by a relative error of at most 0.003.
Values may be sent and summed in bfloat16 or wider, within the bound.
No kernel may reach another device: no remote copies, remote signals or barrier semaphores. Data moves between devices by JAX's collectives and lax.ppermute only.
A program may use at most 64 MiB of HBM per device.

v0:
```python
import math

import jax
import jax.numpy as jnp
from jax import lax
from jax.sharding import PartitionSpec as P


def from_behind(block, axis, distance):
    devices = range(lax.axis_size(axis))
    route = [(i - distance, i) for i in devices if i - distance in devices]
    return lax.ppermute(block, axis, route)


def with_halo(array, sides, width):
    for axis, dim in sides:
        size, length = (lax.axis_size(axis), array.shape[dim])
        up = [(i, (i + 1) % size) for i in range(size - 1)]
        down = [(j, i) for i, j in up]
        last = lax.slice_in_dim(array, length - width, length, axis=dim)
        first = lax.slice_in_dim(array, 0, width, axis=dim)
        before = lax.ppermute(last, axis, up)
        after = lax.ppermute(first, axis, down)
        array = jnp.concatenate([before, array, after], axis=dim)
    return array


def gather_blocks(block, axis):
    size = lax.axis_size(axis)
    me = lax.axis_index(axis)
    got = [block] + [
        lax.ppermute(block, axis, [(j, (j + d) % size) for j in range(size)])
        for d in range(1, size)
    ]
    return jnp.concatenate(
        [lax.select_n((me - j) % size, *got) for j in range(size)], axis=0
    )


def on_device(features, cotangent, conv_weight, norm_gain, norm_bias):
    chans, frames, rows, cols = features.shape
    n_chan = lax.axis_size("chan")
    whole_x = gather_blocks(features, "chan")
    total = whole_x.shape[0]
    cells = frames * rows * cols
    flat_x = whole_x.reshape(total, cells).astype(jnp.float32)
    inv_rms = lax.rsqrt(jnp.mean(flat_x * flat_x, axis=0, keepdims=True) + 1e-06)
    normed = flat_x * inv_rms * norm_gain[:, None] + norm_bias[:, None]
    active = jax.nn.silu(normed).astype(jnp.bfloat16).reshape(total, frames, rows, cols)

    ahead = from_behind(lax.slice_in_dim(cotangent, 0, 2, axis=1), "tm", -1)
    longer = jnp.concatenate([cotangent, ahead], axis=1)
    bordered = with_halo(longer, (("height", 2),), 1)
    padded = jnp.pad(bordered, ((0, 0), (0, 0), (0, 0), (1, 1)))

    positions = frames * lax.axis_size("tm") * rows * lax.axis_size("height") * cols
    cells_major = jnp.transpose(padded, (1, 2, 3, 0))
    taps = []
    for kt in range(3):
        for kh in range(3):
            for kw in range(3):
                taps.append(
                    cells_major[
                        2 - kt : 2 - kt + frames, 2 - kh : 2 - kh + rows, 2 - kw : 2 - kw + cols
                    ].reshape(cells, chans)
                )
    stacked = jnp.stack(taps, axis=0)
    active_t = jnp.transpose(active.reshape(total, cells))
    local_sums = lax.dot_general(
        stacked, active_t, (((1,), (0,)), ((), ())), preferred_element_type=jnp.float32
    )
    summed = lax.psum(local_sums, ("tm", "height"))
    weight_grad = jnp.transpose(summed / math.sqrt(positions), (1, 0, 2))

    kernel = conv_weight.reshape(chans, 3, 3, 3, total)
    kernel = lax.rev(kernel, (1, 2, 3))
    adn = lax.ConvDimensionNumbers(
        lhs_spec=(0, 1, 2, 3, 4), rhs_spec=(4, 0, 1, 2, 3), out_spec=(0, 1, 2, 3, 4)
    )
    partial = lax.conv_general_dilated(
        padded[None],
        kernel,
        window_strides=(1, 1, 1),
        padding="VALID",
        dimension_numbers=adn,
        preferred_element_type=jnp.float32,
    )[0].reshape(total, cells)

    sig = jax.nn.sigmoid(normed)
    slope = sig * (1.0 + normed * (1.0 - sig)) * norm_gain[:, None]
    part_dots = jnp.sum(partial * slope * flat_x, axis=0, keepdims=True)
    packed = jnp.concatenate(
        [
            partial.reshape(n_chan, chans, cells),
            jnp.broadcast_to(part_dots[None], (n_chan, 1, cells)),
        ],
        axis=1,
    )
    mine = lax.psum_scatter(packed, "chan", scatter_dimension=0, tiled=True)[0]
    act_grad = mine[:chans]
    dots = mine[chans:]

    offset = lax.axis_index("chan") * chans
    own_x = features.reshape(chans, -1).astype(jnp.float32)
    own_slope = lax.dynamic_slice_in_dim(slope, offset, chans, 0)
    upstream = act_grad * own_slope
    own_back = inv_rms * upstream - own_x * inv_rms**3 * dots / total
    result = cotangent.reshape(chans, -1).astype(jnp.float32) + own_back
    return (result.astype(jnp.bfloat16).reshape(features.shape), weight_grad)


def solution(mesh):
    return jax.shard_map(
        on_device,
        mesh=mesh,
        in_specs=(
            P("chan", "tm", "height", None),
            P("chan", "tm", "height", None),
            P("chan", None, None),
            P(),
            P(),
        ),
        out_specs=(P("chan", "tm", "height", None), P("chan", None, None)),
        check_vma=False,
    )
```

profile of v0, /device:TPU:9, one launch (start us, length us, event | category | flops | bytes accessed | tf_op | source)
XLA Modules:
  0.0 239.8 jit_solution(15556411908181220196)
XLA Ops:
  14.3 2.6 %collective-permute-done = bf16[96,2,4,160]{0,3,2,1:T(8,128)(2,1)S(1)} collective-permute-done((bf16[96,2,4,160]{0,3,2,1:T(8,128)(2,1)}, bf16[96,2,4,160]{0,3,2,1:T(8,128)(2,1)S(1)}, u32[]{:S(2)}, u32[]{:S(2)}) %collective-permute-start) | collective-permute-done | bytes 245792 | tf_op jit(solution)/shard_map/ppermute | solution.py:32
  16.9 20.3 %collective-permute-done.1 = bf16[96,2,4,160]{0,3,2,1:T(8,128)(2,1)S(1)} collective-permute-done((bf16[96,2,4,160]{0,3,2,1:T(8,128)(2,1)}, bf16[96,2,4,160]{0,3,2,1:T(8,128)(2,1)S(1)}, u32[]{:S(2)}, u32[]{:S(2)}) %collective-permute-start.1) | collective-permute-done | bytes 245792 | tf_op jit(solution)/shard_map/ppermute | solution.py:32
  37.9 2.1 collective-permute-done.2
  42.5 1.8 maximum_convert_fusion
  48.3 3.7 %collective-permute-start.5 = (bf16[96,4,1,160]{0,3,2,1:T(8,128)(2,1)}, bf16[96,4,1,160]{0,3,2,1:T(8,128)(2,1)}, u32[]{:S(2)}, u32[]{:S(2)}) collective-permute-start(bf16[96,4,1,160]{0,3,2,1:T(8,128)(2,1)} %get-tuple-element.38), channel_id=1, source_target_pairs={{4,0},{5,1},{6,2},{7,3},{12,8},{13,9},{14,10},{15,11},{20,16},{21,... | collective-permute-start | bytes 368648 | tf_op jit(solution)/shard_map/ppermute | solution.py:23
  52.1 4.0 %add_divide_fusion = (f32[384,1280]{0,1:T(8,128)}, f32[384,1280]{0,1:T(8,128)}) fusion(f32[384]{0:T(512)S(1)} %copy-done.30, f32[384]{0:T(512)S(1)} %copy-done.32, f32[1280]{0:T(1024)S(1)} %rsqrt.16, f32[384,2,4,160]{0,3,2,1:T(8,128)} %maximum_convert_fusion), kind=kLoop, calls=%fused_computation.25 | loop fusion | flops 2949120 | bytes 5906432 | tf_op jit(solution)/shard_map/div | solution.py:89
  56.2 2.2 fusion.45
  60.0 2.8 %fusion.47 = (bf16[2,4,160,96]{3,2,1,0:T(8,128)(2,1)}, bf16[2,4,160,96]{3,2,1,0:T(8,128)(2,1)}, bf16[2,4,160,96]{3,2,1,0:T(8,128)(2,1)}, bf16[2,4,160,96]{3,2,1,...) fusion(bf16[4,6,162,96]{3,2,1,0:T(8,128)(2,1)S(1)} %get-tuple-e, ...), kind=kLoop, calls=%fused_computation.96 | loop fusion | bytes 9338880 | tf_op jit(solution)/shard_map/slice | solution.py:63
  66.4 1.8 copy.223
  70.1 1.8 copy.225
  73.7 1.8 copy.227
  81.1 1.8 copy.231
  82.9 1.8 copy.232
  84.7 1.8 copy.233
  88.4 1.9 copy.235
  90.3 1.8 copy.236
  92.1 1.8 copy.237
  93.9 1.8 copy.238
  95.8 1.8 copy.239
  97.6 1.8 copy.240
  106.8 1.8 copy.245
  109.8 1.9 copy.247
  135.4 8.5 %fusion.28 = f32[27,96,384]{2,1,0:T(8,128)} fusion(bf16[27,1280,96]{1,2,0:T(8,128)(2,1)} %constant_dynamic-update-slice_fusion.2, f32[384,1280]{0,1:T(8,128)S(1)} %copy-done.2), kind=kOutput, calls=%fused_computation.40 | convolution fusion | flops 2550497280 | bytes 12582912 | tf_op jit(solution)/shard_map/dot_general | solution.py:69
  146.5 4.2 %convolution_select_fusion = f32[2,4,8,21,384]{4,2,3,1,0:T(8,128)S(1)} fusion(bf16[96,3,3,3,384]{4,0,3,2,1:T(8,128)(2,1)S(1)} %bitcast.73, bf16[96,4,6,1,7,2]{0,4,5,2,1,3:T(8,128)(2,1)S(1)} %slice.133, bf16[96,4,6,1,8,21]{0,4,5,2,1,3:T(8,128)(2,1)S(1)} %copy.214, pred[8,21]{0,1:T(8,128)(4,1)S(1)} %copy-done.34), kind=kOutput, calls=%fused_computation.28 | convolution fusion | flops 2678501376 | bytes 4893864 | tf_op jit(solution)/shard_map/conv_general_dilated | solution.py:80
  153.2 2.1 fusion.15
  155.4 3.0 %reshape_reshape_squeeze.3 = f32[4,96,1280]{1,0,2:T(4,128)S(1)} reshape(f32[1,384,2,4,160]{1,4,3,2,0:T(8,128)} %bitcast.75) | data formatting | bytes 3932160 | tf_op jit(solution)/shard_map/reshape;reshape;squeeze | solution.py:94
  158.5 3.6 %broadcast_in_dim.16 = f32[4,1,1280]{1,0,2:T(4,128)S(1)} broadcast(f32[1280]{0:T(1024)S(1)} %broadcast_in_dim.7), dimensions={2} | broadcast | bytes 25600 | tf_op jit(solution)/shard_map/broadcast_in_dim | solution.py:95
  162.1 2.6 %pad_maximum_fusion = f32[4,97,1280]{1,0,2:T(4,128)} fusion(f32[4,1,1280]{1,0,2:T(4,128)S(1)} %broadcast_in_dim.16, f32[4,96,1280]{1,0,2:T(4,128)S(1)} %reshape_reshape_squeeze.3), kind=kLoop, calls=%fused_computation.3 | loop fusion | flops 496640 | bytes 3973120 | tf_op jit(solution)/shard_map/concatenate | solution.py:92
  164.7 4.2 %copy.219 = f32[4,97,1280]{2,1,0:T(8,128)} copy(f32[4,97,1280]{1,0,2:T(4,128)} %pad_maximum_fusion) | data formatting | bytes 3973120 | tf_op jit(solution)/shard_map/concatenate | solution.py:92
  169.0 53.6 %all-reduce.3.cloned.1.call-done = f32[27,96,384]{2,1,0:T(8,128)} async-done(((f32[27,96,384]{2,1,0:T(8,128)}), f32[27,96,384]{2,1,0:T(8,128)}) %all-reduce.3.cloned.1.call-update) | async-done | bytes 3981328 | tf_op jit(solution)/shard_map/psum | solution.py:72
  222.6 4.4 %multiply_bitcast_fusion = f32[96,27,384]{2,0,1:T(8,128)} fusion(f32[27,96,384]{2,1,0:T(8,128)} %all-reduce.3.cloned.1.call-done), kind=kLoop, calls=%fused_computation | loop fusion | flops 995328 | bytes 7962624 | tf_op jit(solution)/shard_map/transpose | solution.py:73
  229.3 3.1 %fusion.37 = bf16[96,1280]{0,1:T(8,128)(2,1)} fusion(f32[384,1280]{0,1:T(8,128)} %get-tuple-element.3, s32[]{:T(128)S(6)} %select_n.170, f32[1,96,1280]{1,2,0:T(8,128)S(1)} %copy.254, f32[384,1280]{0,1:T(8,128)} %get-tuple-element.2, f32[96]{0:T(128)S(1)} %dynamic-slice, bf16[96,2,4,160]{0,3,2,1:T(8,128)(2,1)S(1)} %copy-done.5, ...), kind=kLoop, calls=%fused_computation.50 | loop fusion | flops 1843200 | bytes 2227588 | tf_op jit(solution)/shard_map/convert_element_type | solution.py:109
  (144 shorter events, 69.0 us)
Async XLA Ops:
  8.0 138.5 %copy-start = (bf16[96,27,384]{2,0,1:T(8,128)(2,1)S(1)}, bf16[96,27,384]{2,0,1:T(8,128)(2,1)}, u32[]{:S(2)}) copy-start(bf16[96,27,384]{2,0,1:T(8,128)(2,1)} %param.7) | copy-start | bytes 5971972
  8.0 214.6 %all-reduce.3.cloned.1.call-start = ((), (), s32[]{:S(2)}) async-start(), calls=%async_computation.2 | async-start | bytes 7962624 | tf_op jit(solution)/shard_map/psum | solution.py:72
  8.1 8.8 %collective-permute-start = (bf16[96,2,4,160]{0,3,2,1:T(8,128)(2,1)}, bf16[96,2,4,160]{0,3,2,1:T(8,128)(2,1)S(1)}, u32[]{:S(2)}, u32[]{:S(2)}) collective-permute-start(bf16[96,2,4,160]{0,3,2,1:T(8,128)(2,1)} %param.5), channel_id=1, source_target_pairs={{0,1},{1,2},{2,3},{3,0},{4,5},{5,6},{6,7},{7,4},{8,9},{9,10},{10,1... | collective-permute-start | bytes 737288 | tf_op jit(solution)/shard_map/ppermute | solution.py:32
  9.4 27.8 %collective-permute-start.1 = (bf16[96,2,4,160]{0,3,2,1:T(8,128)(2,1)}, bf16[96,2,4,160]{0,3,2,1:T(8,128)(2,1)S(1)}, u32[]{:S(2)}, u32[]{:S(2)}) collective-permute-start(bf16[96,2,4,160]{0,3,2,1:T(8,128)(2,1)} %param.5), channel_id=1, source_target_pairs={{0,2},{1,3},{2,0},{3,1},{4,6},{5,7},{6,4},{7,5},{8,10},{9,11},{10,... | collective-permute-start | bytes 737288 | tf_op jit(solution)/shard_map/ppermute | solution.py:32
  10.5 29.5 %collective-permute-start.2 = (bf16[96,2,4,160]{0,3,2,1:T(8,128)(2,1)}, bf16[96,2,4,160]{0,3,2,1:T(8,128)(2,1)}, u32[]{:S(2)}, u32[]{:S(2)}) collective-permute-start(bf16[96,2,4,160]{0,3,2,1:T(8,128)(2,1)} %param.5), channel_id=1, source_target_pairs={{0,3},{1,0},{2,1},{3,2},{4,7},{5,4},{6,5},{7,6},{8,11},{9,8},{10,9... | collective-permute-start | bytes 737288 | tf_op jit(solution)/shard_map/ppermute | solution.py:32
  11.9 32.5 %collective-permute-start.3 = (bf16[96,2,4,160]{0,3,2,1:T(8,128)(2,1)}, bf16[96,2,4,160]{0,3,2,1:T(8,128)(2,1)}, u32[]{:S(2)}, u32[]{:S(2)}) collective-permute-start(bf16[96,2,4,160]{0,3,2,1:T(8,128)(2,1)} %param.6), channel_id=1, source_target_pairs={{8,0},{16,8},{24,16},{9,1},{17,9},{25,17},{10,2},{18,10},{26,18},{... | collective-permute-start | bytes 737288 | tf_op jit(solution)/shard_map/ppermute | solution.py:12
  16.9 20.3 %copy-start.26 = (bf16[96,2,4,160]{0,3,2,1:T(8,128)(2,1)}, bf16[96,2,4,160]{0,3,2,1:T(8,128)(2,1)S(1)}, u32[]{:S(2)}) copy-start(bf16[96,2,4,160]{0,3,2,1:T(8,128)(2,1)S(1)} %collective-permute-done) | copy-start | bytes 737284
  42.5 9.6 %copy-start.30 = (f32[384]{0:T(512)S(1)}, f32[384]{0:T(512)}, u32[]{:S(2)}) copy-start(f32[384]{0:T(512)} %param.9) | copy-start | bytes 4612
  42.5 9.6 %copy-start.32 = (f32[384]{0:T(512)S(1)}, f32[384]{0:T(512)}, u32[]{:S(2)}) copy-start(f32[384]{0:T(512)} %param.8) | copy-start | bytes 4612
  47.0 9.2 %collective-permute-start.4 = (bf16[96,4,1,160]{0,3,2,1:T(8,128)(2,1)}, bf16[96,4,1,160]{0,3,2,1:T(8,128)(2,1)S(1)}, u32[]{:S(2)}, u32[]{:S(2)}) collective-permute-start(bf16[96,4,1,160]{0,3,2,1:T(8,128)(2,1)} %get-tuple-element.37), channel_id=1, source_target_pairs={{0,4},{1,5},{2,6},{3,7},{8,12},{9,13},{10,14},{11,15},{16,20},{17,... | collective-permute-start | bytes 368648 | tf_op jit(solution)/shard_map/ppermute | solution.py:22
  48.3 7.9 %collective-permute-start.5 = (bf16[96,4,1,160]{0,3,2,1:T(8,128)(2,1)}, bf16[96,4,1,160]{0,3,2,1:T(8,128)(2,1)}, u32[]{:S(2)}, u32[]{:S(2)}) collective-permute-start(bf16[96,4,1,160]{0,3,2,1:T(8,128)(2,1)} %get-tuple-element.38), channel_id=1, source_target_pairs={{4,0},{5,1},{6,2},{7,3},{12,8},{13,9},{14,10},{15,11},{20,16},{21,... | collective-permute-start | bytes 368648 | tf_op jit(solution)/shard_map/ppermute | solution.py:23
  111.6 8.6 %copy-start.24 = (bf16[1,1280,96]{1,2,0:T(8,128)(2,1)S(1)}, bf16[1,1280,96]{1,2,0:T(8,128)(2,1)}, u32[]{:S(2)}) copy-start(bf16[1,1280,96]{1,2,0:T(8,128)(2,1)} %copy.227) | copy-start | bytes 737284
  111.6 9.3 %copy-start.25 = (bf16[1,1280,96]{1,2,0:T(8,128)(2,1)S(1)}, bf16[1,1280,96]{1,2,0:T(8,128)(2,1)}, u32[]{:S(2)}) copy-start(bf16[1,1280,96]{1,2,0:T(8,128)(2,1)} %copy.228) | copy-start | bytes 737284
  111.6 10.0 %copy-start.23 = (bf16[1,1280,96]{1,2,0:T(8,128)(2,1)S(1)}, bf16[1,1280,96]{1,2,0:T(8,128)(2,1)}, u32[]{:S(2)}) copy-start(bf16[1,1280,96]{1,2,0:T(8,128)(2,1)} %copy.229) | copy-start | bytes 737284
  111.6 10.8 %copy-start.22 = (bf16[1,1280,96]{1,2,0:T(8,128)(2,1)S(1)}, bf16[1,1280,96]{1,2,0:T(8,128)(2,1)}, u32[]{:S(2)}) copy-start(bf16[1,1280,96]{1,2,0:T(8,128)(2,1)} %copy.230) | copy-start | bytes 737284
  111.6 11.5 %copy-start.21 = (bf16[1,1280,96]{1,2,0:T(8,128)(2,1)S(1)}, bf16[1,1280,96]{1,2,0:T(8,128)(2,1)}, u32[]{:S(2)}) copy-start(bf16[1,1280,96]{1,2,0:T(8,128)(2,1)} %copy.231) | copy-start | bytes 737284
  113.4 10.4 %copy-start.20 = (bf16[1,1280,96]{1,2,0:T(8,128)(2,1)S(1)}, bf16[1,1280,96]{1,2,0:T(8,128)(2,1)}, u32[]{:S(2)}) copy-start(bf16[1,1280,96]{1,2,0:T(8,128)(2,1)} %copy.232) | copy-start | bytes 737284
  115.1 9.5 %copy-start.19 = (bf16[1,1280,96]{1,2,0:T(8,128)(2,1)S(1)}, bf16[1,1280,96]{1,2,0:T(8,128)(2,1)}, u32[]{:S(2)}) copy-start(bf16[1,1280,96]{1,2,0:T(8,128)(2,1)} %copy.233) | copy-start | bytes 737284
  116.8 8.5 %copy-start.18 = (bf16[1,1280,96]{1,2,0:T(8,128)(2,1)S(1)}, bf16[1,1280,96]{1,2,0:T(8,128)(2,1)}, u32[]{:S(2)}) copy-start(bf16[1,1280,96]{1,2,0:T(8,128)(2,1)} %copy.234) | copy-start | bytes 737284
  118.5 7.5 %copy-start.17 = (bf16[1,1280,96]{1,2,0:T(8,128)(2,1)S(1)}, bf16[1,1280,96]{1,2,0:T(8,128)(2,1)}, u32[]{:S(2)}) copy-start(bf16[1,1280,96]{1,2,0:T(8,128)(2,1)} %copy.235) | copy-start | bytes 737284
  120.2 6.5 %copy-start.16 = (bf16[1,1280,96]{1,2,0:T(8,128)(2,1)S(1)}, bf16[1,1280,96]{1,2,0:T(8,128)(2,1)}, u32[]{:S(2)}) copy-start(bf16[1,1280,96]{1,2,0:T(8,128)(2,1)} %copy.236) | copy-start | bytes 737284
  121.7 6.5 %copy-start.14 = (bf16[1,1280,96]{1,2,0:T(8,128)(2,1)S(1)}, bf16[1,1280,96]{1,2,0:T(8,128)(2,1)}, u32[]{:S(2)}) copy-start(bf16[1,1280,96]{1,2,0:T(8,128)(2,1)} %copy.238) | copy-start | bytes 737284
  122.4 6.5 %copy-start.13 = (bf16[1,1280,96]{1,2,0:T(8,128)(2,1)S(1)}, bf16[1,1280,96]{1,2,0:T(8,128)(2,1)}, u32[]{:S(2)}) copy-start(bf16[1,1280,96]{1,2,0:T(8,128)(2,1)} %copy.239) | copy-start | bytes 737284
  123.1 6.5 %copy-start.12 = (bf16[1,1280,96]{1,2,0:T(8,128)(2,1)S(1)}, bf16[1,1280,96]{1,2,0:T(8,128)(2,1)}, u32[]{:S(2)}) copy-start(bf16[1,1280,96]{1,2,0:T(8,128)(2,1)} %copy.240) | copy-start | bytes 737284
  123.8 6.5 %copy-start.11 = (bf16[1,1280,96]{1,2,0:T(8,128)(2,1)S(1)}, bf16[1,1280,96]{1,2,0:T(8,128)(2,1)}, u32[]{:S(2)}) copy-start(bf16[1,1280,96]{1,2,0:T(8,128)(2,1)} %copy.241) | copy-start | bytes 737284
  124.5 6.5 %copy-start.10 = (bf16[1,1280,96]{1,2,0:T(8,128)(2,1)S(1)}, bf16[1,1280,96]{1,2,0:T(8,128)(2,1)}, u32[]{:S(2)}) copy-start(bf16[1,1280,96]{1,2,0:T(8,128)(2,1)} %copy.242) | copy-start | bytes 737284
  125.2 6.5 %copy-start.9 = (bf16[1,1280,96]{1,2,0:T(8,128)(2,1)S(1)}, bf16[1,1280,96]{1,2,0:T(8,128)(2,1)}, u32[]{:S(2)}) copy-start(bf16[1,1280,96]{1,2,0:T(8,128)(2,1)} %copy.243) | copy-start | bytes 737284
  126.0 6.5 %copy-start.8 = (bf16[1,1280,96]{1,2,0:T(8,128)(2,1)S(1)}, bf16[1,1280,96]{1,2,0:T(8,128)(2,1)}, u32[]{:S(2)}) copy-start(bf16[1,1280,96]{1,2,0:T(8,128)(2,1)} %copy.244) | copy-start | bytes 737284
  126.7 6.6 %copy-start.7 = (bf16[1,1280,96]{1,2,0:T(8,128)(2,1)S(1)}, bf16[1,1280,96]{1,2,0:T(8,128)(2,1)}, u32[]{:S(2)}) copy-start(bf16[1,1280,96]{1,2,0:T(8,128)(2,1)} %copy.245) | copy-start | bytes 737284
  128.1 6.5 %copy-start.6 = (bf16[1,1280,96]{1,2,0:T(8,128)(2,1)S(1)}, bf16[1,1280,96]{1,2,0:T(8,128)(2,1)}, u32[]{:S(2)}) copy-start(bf16[1,1280,96]{1,2,0:T(8,128)(2,1)} %copy.247) | copy-start | bytes 737284
  128.9 6.5 %copy-start.2 = (f32[384,1280]{0,1:T(8,128)S(1)}, f32[384,1280]{0,1:T(8,128)}, u32[]{:S(2)}) copy-start(f32[384,1280]{0,1:T(8,128)} %get-tuple-element.3) | copy-start | bytes 5898244
  143.9 83.1 %reduce-scatter.2.cloned.1.call-start = ((), (), s32[]{:S(2)}) async-start(), calls=%async_computation.1 | async-start | bytes 2662400 | tf_op jit(solution)/shard_map/reduce_scatter | solution.py:99
  (11 other events, 29.0 us)
Sparse Core Ops, SparseCore 0:
  144.0 78.4 all-reduce.2
Sparse Core Ops, SparseCore 1:
  169.0 42.6 reduce-scatter.1
where the time goes:
time: 243 us; the launch traced here: 240 us
  local copies, waits for them, and re-layouts  99.2 us (41%)
  waiting for transfers between devices  78.7 us (32%)
  other arithmetic  22.8 us (9%)
  between operations  15.9 us (7%)
  matrix products  12.8 us (5%)
  starting transfers between devices  10.4 us (4%)
    psum x1, waiting for transfers between devices, on_device(): summed = lax.psum(local_sums, ('tm', 'height'))  53.6 us
    another operation x28, local copies, waits for them, and re-layouts, on_device(): stacked = jnp.stack(taps, axis=0)  48.8 us
    unnamed x100, local copies, waits for them, and re-layouts  29.6 us
    ppermute x3, waiting for transfers between devices, gather_blocks(): lax.ppermute(block, axis, [(j, (j + d) % size) for j in range(size)])  25 us
    dot_general x1, matrix products, on_device(): lax.dot_general(stacked, active_t, (((1,), (0,)), ((), ())), preferred_el...  8.54 us
  transfers between devices with their start and end apart: 8, of which 4 were waited for; matrix products, arithmetic and copies ran while one was open for 16% of the time, Pallas kernels for 0%

commit v1 on v0

--- a/solution.py
+++ b/solution.py
@@ -3,6 +3,8 @@
 import jax
 import jax.numpy as jnp
 from jax import lax
+from jax.experimental import pallas as pl
+from jax.experimental.pallas import tpu as pltpu
 from jax.sharding import PartitionSpec as P
 
 
@@ -37,6 +39,80 @@
     )
 
 
+def weight_taps(shifted, active_t, frames, rows):
+    _, _, _, cols, outs = shifted.shape
+    cells, ins = active_t.shape
+
+    def body(cot_ref, act_ref, out_ref):
+        act = act_ref[...]
+        for kt in range(3):
+            for kh in range(3):
+                for kw in range(3):
+                    piece = cot_ref[kw, 2 - kt : 2 - kt + frames, 2 - kh : 2 - kh + rows]
+                    out_ref[9 * kt + 3 * kh + kw] = lax.dot_general(
+                        piece.reshape(cells, outs),
+                        act,
+                        (((0,), (0,)), ((), ())),
+                        preferred_element_type=jnp.float32,
+                    )
+
+    return pl.pallas_call(
+        body,
+        out_shape=jax.ShapeDtypeStruct((27, outs, ins), jnp.float32),
+        in_specs=[pl.BlockSpec(memory_space=pltpu.VMEM)] * 2,
+        out_specs=pl.BlockSpec(memory_space=pltpu.VMEM),
+        cost_estimate=pl.CostEstimate(
+            flops=2 * 27 * ins * cells * outs,
+            bytes_accessed=shifted.size * 2 + active_t.size * 2 + 27 * ins * outs * 4,
+            transcendentals=0,
+        ),
+    )(shifted, active_t)
+
+
+def halving_steps(axes):
+    steps = []
+    for axis in axes:
+        size = lax.axis_size(axis)
+        idx = lax.axis_index(axis)
+        level = 1
+        while level < size:
+            steps.append((axis, level, (idx // level) % 2))
+            level *= 2
+    return steps
+
+
+def exchange(block, axis, level):
+    size = lax.axis_size(axis)
+    return lax.ppermute(block, axis, [(i, i ^ level) for i in range(size)])
+
+
+def halving_sum(x, steps):
+    for axis, level, bit in steps:
+        m = x.shape[0] // 2
+        keep = lax.dynamic_slice_in_dim(x, bit * m, m, 0)
+        send = lax.dynamic_slice_in_dim(x, (1 - bit) * m, m, 0)
+        x = keep + exchange(send, axis, level)
+    for axis, level, bit in reversed(steps):
+        got = exchange(x, axis, level)
+        m = x.shape[0]
+        full = jnp.zeros((2 * m,) + x.shape[1:], x.dtype)
+        full = lax.dynamic_update_slice_in_dim(full, x, bit * m, 0)
+        x = lax.dynamic_update_slice_in_dim(full, got, (1 - bit) * m, 0)
+    return x
+
+
+def group_sum(x, near, far):
+    near_steps, far_steps = halving_steps(near), halving_steps(far)
+    unit = 2 ** (len(near_steps) + len(far_steps) + 1)
+    rows = x.shape[0]
+    padded_rows = -(-rows // unit) * unit
+    x = jnp.pad(x, ((0, padded_rows - rows), (0, 0)))
+    half = padded_rows // 2
+    first = halving_sum(x[:half], near_steps + far_steps)
+    second = halving_sum(x[half:], near_steps + far_steps[::-1])
+    return jnp.concatenate([first, second], axis=0)[:rows]
+
+
 def on_device(features, cotangent, conv_weight, norm_gain, norm_bias):
     chans, frames, rows, cols = features.shape
     n_chan = lax.axis_size("chan")
@@ -55,22 +131,15 @@
 
     positions = frames * lax.axis_size("tm") * rows * lax.axis_size("height") * cols
     cells_major = jnp.transpose(padded, (1, 2, 3, 0))
-    taps = []
-    for kt in range(3):
-        for kh in range(3):
-            for kw in range(3):
-                taps.append(
-                    cells_major[
-                        2 - kt : 2 - kt + frames, 2 - kh : 2 - kh + rows, 2 - kw : 2 - kw + cols
-                    ].reshape(cells, chans)
-                )
-    stacked = jnp.stack(taps, axis=0)
+    shifted = jnp.stack(
+        [cells_major[:, :, 2 - kw : 2 - kw + cols] for kw in range(3)], axis=0
+    )
     active_t = jnp.transpose(active.reshape(total, cells))
-    local_sums = lax.dot_general(
-        stacked, active_t, (((1,), (0,)), ((), ())), preferred_element_type=jnp.float32
+    local_sums = weight_taps(shifted, active_t, frames, rows)
+    summed = group_sum(local_sums.reshape(27 * chans, total), ("height",), ("tm",))
+    weight_grad = jnp.transpose(
+        (summed / math.sqrt(positions)).reshape(27, chans, total), (1, 0, 2)
     )
-    summed = lax.psum(local_sums, ("tm", "height"))
-    weight_grad = jnp.transpose(summed / math.sqrt(positions), (1, 0, 2))
 
     kernel = conv_weight.reshape(chans, 3, 3, 3, total)
     kernel = lax.rev(kernel, (1, 2, 3))

time: 243 us -> 160 us (0.66)
  local copies, waits for them, and re-layouts: 99.2 us -> 41.8 us
  waiting for transfers between devices: 78.7 us -> 41.9 us
  starting transfers between devices: 10.4 us -> 22.5 us
  matrix products: 12.8 us -> 4.26 us
  Pallas kernels: 0 us -> 8.52 us
    psum x1 -> x0, waiting for transfers between devices: 53.6 us -> none  [on_device(): summed = lax.psum(local_sums, ('tm', 'height'))]
    another operation x28 -> x7, local copies, waits for them, and re-layouts: 48.8 us -> 2.85 us  [on_device(): stacked = jnp.stack(taps, axis=0)]
    unnamed x100 -> x37, local copies, waits for them, and re-layouts: 29.6 us -> 6.78 us
    ppermute x0 -> x12, waiting for transfers between devices: none -> 18.5 us  [exchange(): return lax.ppermute(block, axis, [(i, i ^ level) for i in range(size)])]
    dynamic_update_slice x0 -> x12, local copies, waits for them, and re-layouts: none -> 16.2 us  [the longest x6 8.36 us: halving_sum(): x = lax.dynamic_update_slice_in_dim(full, got, (1 - bit) * m, 0)]
    ppermute x0 -> x12, starting transfers between devices: none -> 12.9 us  [exchange(): return lax.ppermute(block, axis, [(i, i ^ level) for i in range(size)])]
    dot_general x1 -> x0, matrix products: 8.54 us -> none  [on_device(): lax.dot_general(stacked, active_t, (((1,), (0,)), ((), ())), preferred_el...]
    pallas_call x0 -> x1, Pallas kernels: none -> 8.52 us  [weight_taps(): pl.pallas_call(body, out_shape=jax.ShapeDtypeStruct((27, outs, ins), jnp....]
  transfers between devices with their start and end apart: 8 -> 19, of which waited for: 4 -> 9; matrix products, arithmetic and copies ran while one was open for 16% -> 31% of each run, Pallas kernels for 0% -> 0%
where the time goes in v1:
time: 160 us; the launch traced here: 159 us
  waiting for transfers between devices  41.9 us (26%)
  local copies, waits for them, and re-layouts  41.8 us (26%)
  other arithmetic  25.1 us (16%)
  starting transfers between devices  22.5 us (14%)
  between operations  14.6 us (9%)
  Pallas kernels  8.52 us (5%)
  matrix products  4.26 us (3%)
    ppermute x3, waiting for transfers between devices, gather_blocks(): lax.ppermute(block, axis, [(j, (j + d) % size) for j in range(size)])  23.4 us
    ppermute x12, waiting for transfers between devices, exchange(): return lax.ppermute(block, axis, [(i, i ^ level) for i in range(size)])  18.5 us
    ppermute x12, starting transfers between devices, exchange(): return lax.ppermute(block, axis, [(i, i ^ level) for i in range(size)])  12.9 us
    pallas_call x1, Pallas kernels, weight_taps(): pl.pallas_call(body, out_shape=jax.ShapeDtypeStruct((27, outs, ins), jnp....  8.52 us
    dynamic_update_slice x6, local copies, waits for them, and re-layouts, halving_sum(): x = lax.dynamic_update_slice_in_dim(full, got, (1 - bit) * m, 0)  8.36 us
    dynamic_update_slice x6, local copies, waits for them, and re-layouts, halving_sum(): full = lax.dynamic_update_slice_in_dim(full, x, bit * m, 0)  7.85 us
    unnamed x37, local copies, waits for them, and re-layouts  6.78 us
    another operation x2, local copies, waits for them, and re-layouts, on_device(): partial.reshape(n_chan, chans, cells)  5.78 us
  transfers between devices with their start and end apart: 19, of which 9 were waited for; matrix products, arithmetic and copies ran while one was open for 31% of the time, Pallas kernels for 0%

profile of v1, /device:TPU:9, one launch (start us, length us, event | category | flops | bytes accessed | tf_op | source)
XLA Modules:
  0.0 158.6 jit_solution(6322561209855124781)
XLA Ops:
  7.2 2.4 %collective-permute-start.1 = (bf16[96,2,4,160]{0,3,2,1:T(8,128)(2,1)}, bf16[96,2,4,160]{0,3,2,1:T(8,128)(2,1)S(1)}, u32[]{:S(2)}, u32[]{:S(2)}) collective-permute-start(bf16[96,2,4,160]{0,3,2,1:T(8,128)(2,1)} %param.5), channel_id=1, source_target_pairs={{0,2},{1,3},{2,0},{3,1},{4,6},{5,7},{6,4},{7,5},{8,10},{9,11},{10,... | collective-permute-start | bytes 737288 | tf_op jit(solution)/shard_map/ppermute | solution.py:34
  12.5 1.7 %constant_dynamic-update-slice_fusion.1 = bf16[96,4,4,160]{0,3,2,1:T(8,128)(2,1)} fusion(bf16[96,2,4,160]{0,3,2,1:T(8,128)(2,1)} %param.6), kind=kLoop, calls=%fused_computation.73 | loop fusion | bytes 573440
  14.2 17.1 %collective-permute-done.1 = bf16[96,2,4,160]{0,3,2,1:T(8,128)(2,1)S(1)} collective-permute-done((bf16[96,2,4,160]{0,3,2,1:T(8,128)(2,1)}, bf16[96,2,4,160]{0,3,2,1:T(8,128)(2,1)S(1)}, u32[]{:S(2)}, u32[]{:S(2)}) %collective-permute-start.1) | collective-permute-done | bytes 245792 | tf_op jit(solution)/shard_map/ppermute | solution.py:34
  31.3 6.0 %collective-permute-done.2 = bf16[96,2,4,160]{0,3,2,1:T(8,128)(2,1)S(1)} collective-permute-done((bf16[96,2,4,160]{0,3,2,1:T(8,128)(2,1)}, bf16[96,2,4,160]{0,3,2,1:T(8,128)(2,1)S(1)}, u32[]{:S(2)}, u32[]{:S(2)}) %collective-permute-start.2) | collective-permute-done | bytes 245792 | tf_op jit(solution)/shard_map/ppermute | solution.py:34
  43.1 2.9 %collective-permute-start.5 = (bf16[96,4,1,160]{0,3,2,1:T(8,128)(2,1)S(1)}, bf16[96,4,1,160]{0,3,2,1:T(8,128)(2,1)S(1)}, u32[]{:S(2)}, u32[]{:S(2)}) collective-permute-start(bf16[96,4,1,160]{0,3,2,1:T(8,128)(2,1)S(1)} %get-tuple-element.16), channel_id=1, source_target_pairs={{4,0},{5,1},{6,2},{7,3},{12,8},{13,9},{14,10},{15,11},{20,16},{21,... | collective-permute-start | bytes 368648 | tf_op jit(solution)/shard_map/ppermute | solution.py:25
  47.5 2.2 %fusion.27 = (bf16[1280,384]{1,0:T(8,128)(2,1)}, f32[384,1280]{0,1:T(8,128)}) fusion(f32[384]{0:T(512)S(1)} %copy-done.14, f32[384]{0:T(512)S(1)} %copy-done.15, f32[1280]{0:T(1024)S(1)} %rsqrt.16, f32[384,2,4,160]{0,3,2,1:T(8,128)S(1)} %maximum_convert_fusion), kind=kLoop, calls=%fused_computation.42 | loop fusion | flops 3932160 | bytes 4923392 | tf_op jit(solution)/shard_map/transpose | solution.py:137
  51.2 4.3 %convolution_select_fusion = f32[2,4,8,21,384]{4,2,3,1,0:T(8,128)S(1)} fusion(bf16[96,3,3,3,384]{4,0,3,2,1:T(8,128)(2,1)S(1)} %bitcast.54, bf16[96,4,6,1,7,2]{0,4,5,2,1,3:T(8,128)(2,1)S(1)} %slice.45, bf16[96,4,6,1,8,21]{0,4,5,2,1,3:T(8,128)(2,1)S(1)} %copy.73, pred[8,21]{0,1:T(8,128)(4,1)S(1)} %copy-done.16), kind=kOutput, calls=%fused_computation.29 | convolution fusion | flops 2678501376 | bytes 4893864 | tf_op jit(solution)/shard_map/conv_general_dilated | solution.py:149
  57.0 2.3 %pad_maximum_fusion.cot_ref = bf16[3,4,6,160,96]{4,3,2,1,0:T(8,128)(2,1)} fusion(bf16[1,4,6,160,96]{4,3,2,1,0:T(8,128)(2,1)S(1)} %get-tuple-element.11, bf16[1,4,6,160,96]{4,3,2,1,0:T(8,128)(2,1)S(1)} %get-tuple-element.12, bf16[1,4,6,160,96]{4,3,2,1,0:T(8,128)(2,1)S(1)} %get-tuple-element.10), kind=kLoop, calls=%fused_computation.3 | loop fusion | flops 2211840 | bytes 4423680 | tf_op jit(solution)/shard_map/stack | solution.py:134
  59.4 8.5 %shard_map.68 = f32[27,96,384]{2,1,0:T(8,128)} custom-call(bf16[3,4,6,160,96]{4,3,2,1,0:T(8,128)(2,1)} %pad_maximum_fusion.cot_ref, bf16[1280,384]{1,0:T(8,128)(2,1)} %get-tuple-element.2.act_ref), custom_call_target="tpu_custom_call" | custom-call | flops 2548039680 | bytes 7176192 | tf_op jit(solution)/shard_map/pallas_call | solution.py:59
  67.9 2.4 %fusion.45 = (f32[1296,384]{1,0:T(8,128)S(1)}, f32[1296,384]{1,0:T(8,128)S(1)}) fusion(f32[2592,384]{1,0:T(8,128)} %bitcast.63), kind=kLoop, calls=%fused_computation.89 | loop fusion | bytes 7962624 | tf_op jit(solution)/shard_map/slice | solution.py:111
  74.0 2.1 %fusion.15 = f32[2,4,160]{2,1,0:T(4,128)S(1)} fusion(bf16[1,96,2,4,160]{1,4,3,2,0:T(8,128)(2,1)S(1)} %bitcast.58, bf16[1,96,2,4,160]{1,4,3,2,0:T(8,128)(2,1)S(1)} %bitcast.59, bf16[1,96,2,4,160]{1,4,3,2,0:T(8,128)(2,1)S(1)} %bitcast.60, bf16[1,96,2,4,160]{1,4,3,2,0:T(8,128)(2,1)S(1)} %bitcast.57, f32[384]{0:T(512)S(1)} %copy-done.14, f32[384]{0:T(512)S(1)} %copy-done.15, ...), kind=kLoop, calls=%fused_computation.28 | loop fusion | flops 10812160 | bytes 2962432 | tf_op jit(solution)/shard_map/reduce_sum | solution.py:160
  77.6 3.9 %reshape_reshape_squeeze.3 = f32[4,96,1280]{1,0,2:T(4,128)} reshape(f32[1,384,2,4,160]{1,4,3,2,0:T(8,128)} %bitcast.56) | data formatting | bytes 3932160 | tf_op jit(solution)/shard_map/reshape;reshape;squeeze | solution.py:163
  81.5 1.9 %copy.78 = f32[4,96,1280]{1,2,0:T(8,128)S(1)} copy(f32[4,96,1280]{1,0,2:T(4,128)} %reshape_reshape_squeeze.3) | data formatting | bytes 3932160 | tf_op jit(solution)/shard_map/reshape;reshape;squeeze | solution.py:163
  83.7 2.3 %pad_maximum_fusion.1 = f32[4,97,1280]{1,2,0:T(8,128)} fusion(f32[4,1,1280]{1,2,0:T(8,128)S(1)} %broadcast_in_dim.16, f32[4,96,1280]{1,2,0:T(8,128)S(1)} %copy.78), kind=kLoop, calls=%fused_computation.4 | loop fusion | flops 496640 | bytes 3973120 | tf_op jit(solution)/shard_map/concatenate | solution.py:161
  86.0 1.7 %dynamic-slice_add_fusion = f32[648,384]{1,0:T(8,128)S(1)} fusion(f32[648,384]{1,0:T(8,128)} %collective-permute-done.12, f32[1296,384]{1,0:T(8,128)} %copy-done.5, s32[]{:T(128)S(6)} %select_n.234), kind=kLoop, calls=%fused_computation.40 | loop fusion | flops 248832 | bytes 2985988 | tf_op jit(solution)/shard_map/add | solution.py:94
  93.5 7.4 %collective-permute-done.13 = f32[324,384]{1,0:T(8,128)} collective-permute-done((f32[324,384]{1,0:T(8,128)S(1)}, f32[324,384]{1,0:T(8,128)}, u32[]{:S(2)}, u32[]{:S(2)}) %collective-permute-start.13) | collective-permute-done | bytes 497696 | tf_op jit(solution)/shard_map/ppermute | solution.py:86
  103.4 1.9 %collective-permute-done.7 = f32[324,384]{1,0:T(8,128)} collective-permute-done((f32[324,384]{1,0:T(8,128)}, f32[324,384]{1,0:T(8,128)}, u32[]{:S(2)}, u32[]{:S(2)}) %collective-permute-start.7) | collective-permute-done | bytes 497696 | tf_op jit(solution)/shard_map/ppermute | solution.py:86
  106.8 4.0 %collective-permute-done.14 = f32[162,384]{1,0:T(8,128)S(1)} collective-permute-done((f32[162,384]{1,0:T(8,128)S(1)}, f32[162,384]{1,0:T(8,128)S(1)}, u32[]{:S(2)}, u32[]{:S(2)}) %collective-permute-start.14) | collective-permute-done | bytes 248864 | tf_op jit(solution)/shard_map/ppermute | solution.py:86
  113.3 1.8 %dynamic_update_slice.42 = f32[324,384]{1,0:T(8,128)S(1)} dynamic-update-slice(f32[324,384]{1,0:T(8,128)S(1)} %broadcast.132.clone, f32[162,384]{1,0:T(8,128)S(1)} %dynamic-slice_add_fusion.4, s32[]{:T(128)S(6)} %select_n.245, s32[]{:T(128)} %constant.100.clone.1) | dynamic-update-slice | bytes 497668 | tf_op jit(solution)/shard_map/dynamic_update_slice | solution.py:99
  115.2 2.5 %collective-permute-done.15 = f32[162,384]{1,0:T(8,128)S(1)} collective-permute-done((f32[162,384]{1,0:T(8,128)S(1)}, f32[162,384]{1,0:T(8,128)S(1)}, u32[]{:S(2)}, u32[]{:S(2)}) %collective-permute-start.15) | collective-permute-done | bytes 248864 | tf_op jit(solution)/shard_map/ppermute | solution.py:86
  119.6 1.9 %dynamic_update_slice.36 = f32[324,384]{1,0:T(8,128)} dynamic-update-slice(f32[324,384]{1,0:T(8,128)} %broadcast.132.clone.1, f32[162,384]{1,0:T(8,128)S(1)} %dynamic-slice_add_fusion.5, s32[]{:T(128)S(6)} %select_n.241, s32[]{:T(128)} %constant.100.clone.1) | dynamic-update-slice | bytes 497668 | tf_op jit(solution)/shard_map/dynamic_update_slice | solution.py:99
  121.5 1.7 %dynamic_update_slice.37 = f32[324,384]{1,0:T(8,128)} dynamic-update-slice(f32[324,384]{1,0:T(8,128)} %dynamic_update_slice.36, f32[162,384]{1,0:T(8,128)S(1)} %collective-permute-done.9, s32[]{:T(128)S(6)} %select_n.242, s32[]{:T(128)} %constant.100.clone.1) | dynamic-update-slice | bytes 497668 | tf_op jit(solution)/shard_map/dynamic_update_slice | solution.py:100
  123.2 2.0 %collective-permute-start.10 = (f32[324,384]{1,0:T(8,128)}, f32[324,384]{1,0:T(8,128)}, u32[]{:S(2)}, u32[]{:S(2)}) collective-permute-start(f32[324,384]{1,0:T(8,128)} %dynamic_update_slice.37), channel_id=1, source_target_pairs={{0,8},{8,0},{16,24},{24,16},{1,9},{9,1},{17,25},{25,17},{2,10},{10... | collective-permute-start | bytes 1493000 | tf_op jit(solution)/shard_map/ppermute | solution.py:86
  125.3 2.0 %dynamic_update_slice.44 = f32[648,384]{1,0:T(8,128)S(1)} dynamic-update-slice(f32[648,384]{1,0:T(8,128)S(1)} %broadcast.131.clone, f32[324,384]{1,0:T(8,128)S(1)} %dynamic_update_slice.43, s32[]{:T(128)S(6)} %select_n.243, s32[]{:T(128)} %constant.100.clone.1) | dynamic-update-slice | bytes 995332 | tf_op jit(solution)/shard_map/dynamic_update_slice | solution.py:99
  127.4 2.5 %collective-permute-done.16 = f32[324,384]{1,0:T(8,128)} collective-permute-done((f32[324,384]{1,0:T(8,128)S(1)}, f32[324,384]{1,0:T(8,128)}, u32[]{:S(2)}, u32[]{:S(2)}) %collective-permute-start.16) | collective-permute-done | bytes 497696 | tf_op jit(solution)/shard_map/ppermute | solution.py:86
  129.9 2.3 %dynamic_update_slice.45 = f32[648,384]{1,0:T(8,128)S(1)} dynamic-update-slice(f32[648,384]{1,0:T(8,128)S(1)} %dynamic_update_slice.44, f32[324,384]{1,0:T(8,128)} %collective-permute-done.16, s32[]{:T(128)S(6)} %select_n.244, s32[]{:T(128)} %constant.100.clone.1) | dynamic-update-slice | bytes 995332 | tf_op jit(solution)/shard_map/dynamic_update_slice | solution.py:100
  132.2 2.9 %collective-permute-start.17 = (f32[648,384]{1,0:T(8,128)S(1)}, f32[648,384]{1,0:T(8,128)}, u32[]{:S(2)}, u32[]{:S(2)}) collective-permute-start(f32[648,384]{1,0:T(8,128)S(1)} %dynamic_update_slice.45), channel_id=1, source_target_pairs={{0,4},{4,0},{1,5},{5,1},{2,6},{6,2},{3,7},{7,3},{8,12},{12,8},{9,1... | collective-permute-start | bytes 2985992 | tf_op jit(solution)/shard_map/ppermute | solution.py:86
  136.2 2.0 %dynamic_update_slice.38 = f32[648,384]{1,0:T(8,128)} dynamic-update-slice(f32[648,384]{1,0:T(8,128)} %broadcast.131.clone.1, f32[324,384]{1,0:T(8,128)} %dynamic_update_slice.37, s32[]{:T(128)S(6)} %select_n.237, s32[]{:T(128)} %constant.100.clone.1) | dynamic-update-slice | bytes 995332 | tf_op jit(solution)/shard_map/dynamic_update_slice | solution.py:99
  138.1 2.0 %dynamic_update_slice.39 = f32[648,384]{1,0:T(8,128)} dynamic-update-slice(f32[648,384]{1,0:T(8,128)} %dynamic_update_slice.38, f32[324,384]{1,0:T(8,128)} %collective-permute-done.10, s32[]{:T(128)S(6)} %select_n.238, s32[]{:T(128)} %constant.100.clone.1) | dynamic-update-slice | bytes 995332 | tf_op jit(solution)/shard_map/dynamic_update_slice | solution.py:100
  140.1 1.8 %add_divide_fusion = f32[384,1280]{0,1:T(8,128)} fusion(f32[384,1280]{0,1:T(8,128)S(1)} %copy-done.2), kind=kLoop, calls=%fused_computation.26 | loop fusion | flops 1474560 | bytes 3932160 | tf_op jit(solution)/shard_map/div | solution.py:158
  144.7 2.3 %maximum_multiply_fusion = f32[2592,384]{1,0:T(8,128)} fusion(f32[1296,384]{1,0:T(8,128)S(1)} %constant_dynamic-update-slice_fusion.2, f32[1296,384]{1,0:T(8,128)S(1)} %constant_dynamic-update-slice_fusion.4), kind=kLoop, calls=%fused_computation | loop fusion | flops 1990656 | bytes 7962624 | tf_op jit(solution)/shard_map/div | solution.py:141
  148.6 3.1 %fusion.35 = bf16[96,1280]{0,1:T(8,128)(2,1)} fusion(f32[384,1280]{0,1:T(8,128)} %get-tuple-element.3, s32[]{:T(128)S(6)} %select_n.232, f32[1,97,1280]{1,2,0:T(8,128)} %reduce-scatter.2.cloned.1.call-done, f32[384,1280]{0,1:T(8,128)} %add_divide_fusion, f32[96]{0:T(128)S(1)} %dynamic-slice, bf16[96,2,4,160]{0,3,2,1:T(8,128)(2,1)S(1)} %copy-done.10, ...), kind=kLoop, calls=%fused_computation.56 | loop fusion | flops 1843200 | bytes 2227588 | tf_op jit(solution)/shard_map/convert_element_type | solution.py:178
  (105 shorter events, 38.0 us)
Async XLA Ops:
  7.2 44.0 %copy-start = (bf16[96,27,384]{2,0,1:T(8,128)(2,1)S(1)}, bf16[96,27,384]{2,0,1:T(8,128)(2,1)}, u32[]{:S(2)}) copy-start(bf16[96,27,384]{2,0,1:T(8,128)(2,1)} %param.7) | copy-start | bytes 5971972
  7.2 139.8 %reduce-scatter.2.cloned.1.call-start = ((), (), s32[]{:S(2)}) async-start(), calls=%async_computation.1 | async-start | bytes 3276800 | tf_op jit(solution)/shard_map/reduce_scatter | solution.py:168
  7.2 24.1 %collective-permute-start.1 = (bf16[96,2,4,160]{0,3,2,1:T(8,128)(2,1)}, bf16[96,2,4,160]{0,3,2,1:T(8,128)(2,1)S(1)}, u32[]{:S(2)}, u32[]{:S(2)}) collective-permute-start(bf16[96,2,4,160]{0,3,2,1:T(8,128)(2,1)} %param.5), channel_id=1, source_target_pairs={{0,2},{1,3},{2,0},{3,1},{4,6},{5,7},{6,4},{7,5},{8,10},{9,11},{10,... | collective-permute-start | bytes 737288 | tf_op jit(solution)/shard_map/ppermute | solution.py:34
  9.6 27.8 %collective-permute-start.2 = (bf16[96,2,4,160]{0,3,2,1:T(8,128)(2,1)}, bf16[96,2,4,160]{0,3,2,1:T(8,128)(2,1)S(1)}, u32[]{:S(2)}, u32[]{:S(2)}) collective-permute-start(bf16[96,2,4,160]{0,3,2,1:T(8,128)(2,1)} %param.5), channel_id=1, source_target_pairs={{0,3},{1,0},{2,1},{3,2},{4,7},{5,4},{6,5},{7,6},{8,11},{9,8},{10,9... | collective-permute-start | bytes 737288 | tf_op jit(solution)/shard_map/ppermute | solution.py:34
  9.8 28.6 %collective-permute-start = (bf16[96,2,4,160]{0,3,2,1:T(8,128)(2,1)}, bf16[96,2,4,160]{0,3,2,1:T(8,128)(2,1)}, u32[]{:S(2)}, u32[]{:S(2)}) collective-permute-start(bf16[96,2,4,160]{0,3,2,1:T(8,128)(2,1)} %param.5), channel_id=1, source_target_pairs={{0,1},{1,2},{2,3},{3,0},{4,5},{5,6},{6,7},{7,4},{8,9},{9,10},{10,1... | collective-permute-start | bytes 737288 | tf_op jit(solution)/shard_map/ppermute | solution.py:34
  11.1 30.5 %collective-permute-start.3 = (bf16[96,2,4,160]{0,3,2,1:T(8,128)(2,1)}, bf16[96,2,4,160]{0,3,2,1:T(8,128)(2,1)}, u32[]{:S(2)}, u32[]{:S(2)}) collective-permute-start(bf16[96,2,4,160]{0,3,2,1:T(8,128)(2,1)} %param.6), channel_id=1, source_target_pairs={{8,0},{16,8},{24,16},{9,1},{17,9},{25,17},{10,2},{18,10},{26,18},{... | collective-permute-start | bytes 737288 | tf_op jit(solution)/shard_map/ppermute | solution.py:14
  31.3 6.0 %copy-start.12 = (bf16[96,2,4,160]{0,3,2,1:T(8,128)(2,1)}, bf16[96,2,4,160]{0,3,2,1:T(8,128)(2,1)S(1)}, u32[]{:S(2)}) copy-start(bf16[96,2,4,160]{0,3,2,1:T(8,128)(2,1)S(1)} %collective-permute-done.1) | copy-start | bytes 737284
  40.9 6.5 %copy-start.14 = (f32[384]{0:T(512)S(1)}, f32[384]{0:T(512)}, u32[]{:S(2)}) copy-start(f32[384]{0:T(512)} %param.9) | copy-start | bytes 4612
  40.9 6.5 %copy-start.15 = (f32[384]{0:T(512)S(1)}, f32[384]{0:T(512)}, u32[]{:S(2)}) copy-start(f32[384]{0:T(512)} %param.8) | copy-start | bytes 4612
  43.1 6.6 %collective-permute-start.5 = (bf16[96,4,1,160]{0,3,2,1:T(8,128)(2,1)S(1)}, bf16[96,4,1,160]{0,3,2,1:T(8,128)(2,1)S(1)}, u32[]{:S(2)}, u32[]{:S(2)}) collective-permute-start(bf16[96,4,1,160]{0,3,2,1:T(8,128)(2,1)S(1)} %get-tuple-element.16), channel_id=1, source_target_pairs={{4,0},{5,1},{6,2},{7,3},{12,8},{13,9},{14,10},{15,11},{20,16},{21,... | collective-permute-start | bytes 368648 | tf_op jit(solution)/shard_map/ppermute | solution.py:25
  46.0 3.7 %collective-permute-start.4 = (bf16[96,4,1,160]{0,3,2,1:T(8,128)(2,1)S(1)}, bf16[96,4,1,160]{0,3,2,1:T(8,128)(2,1)S(1)}, u32[]{:S(2)}, u32[]{:S(2)}) collective-permute-start(bf16[96,4,1,160]{0,3,2,1:T(8,128)(2,1)S(1)} %get-tuple-element.15), channel_id=1, source_target_pairs={{0,4},{1,5},{2,6},{3,7},{8,12},{9,13},{10,14},{11,15},{16,20},{17,... | collective-permute-start | bytes 368648 | tf_op jit(solution)/shard_map/ppermute | solution.py:24
  70.3 3.4 %copy-start.3 = (f32[1296,384]{1,0:T(8,128)}, f32[1296,384]{1,0:T(8,128)S(1)}, u32[]{:S(2)}) copy-start(f32[1296,384]{1,0:T(8,128)S(1)} %get-tuple-element.4) | copy-start | bytes 5971972
  70.3 3.3 %copy-start.5 = (f32[1296,384]{1,0:T(8,128)}, f32[1296,384]{1,0:T(8,128)S(1)}, u32[]{:S(2)}) copy-start(f32[1296,384]{1,0:T(8,128)S(1)} %get-tuple-element.5) | copy-start | bytes 5971972
  71.5 14.5 %collective-permute-start.12 = (f32[648,384]{1,0:T(8,128)}, f32[648,384]{1,0:T(8,128)}, u32[]{:S(2)}, u32[]{:S(2)}) collective-permute-start(f32[648,384]{1,0:T(8,128)} %constant_dynamic-slice_fusion.2), channel_id=1, source_target_pairs={{0,4},{4,0},{1,5},{5,1},{2,6},{6,2},{3,7},{7,3},{8,12},{12,8},{9,1... | collective-permute-start | bytes 2985992 | tf_op jit(solution)/shard_map/ppermute | solution.py:86
  73.7 15.5 %collective-permute-start.6 = (f32[648,384]{1,0:T(8,128)}, f32[648,384]{1,0:T(8,128)}, u32[]{:S(2)}, u32[]{:S(2)}) collective-permute-start(f32[648,384]{1,0:T(8,128)} %constant_dynamic-slice_fusion.5), channel_id=1, source_target_pairs={{0,4},{4,0},{1,5},{5,1},{2,6},{6,2},{3,7},{7,3},{8,12},{12,8},{9,1... | collective-permute-start | bytes 2985992 | tf_op jit(solution)/shard_map/ppermute | solution.py:86
  86.0 3.2 %copy-start.4 = (f32[1296,384]{1,0:T(8,128)S(1)}, f32[1296,384]{1,0:T(8,128)}, u32[]{:S(2)}) copy-start(f32[1296,384]{1,0:T(8,128)} %copy-done.3) | copy-start | bytes 5971972
  87.8 13.1 %collective-permute-start.13 = (f32[324,384]{1,0:T(8,128)S(1)}, f32[324,384]{1,0:T(8,128)}, u32[]{:S(2)}, u32[]{:S(2)}) collective-permute-start(f32[324,384]{1,0:T(8,128)S(1)} %constant_dynamic-slice_fusion.1), channel_id=1, source_target_pairs={{0,16},{8,24},{16,0},{24,8},{1,17},{9,25},{17,1},{25,9},{2,18},{10... | collective-permute-start | bytes 1493000 | tf_op jit(solution)/shard_map/ppermute | solution.py:86
  92.3 13.0 %copy-start.7 = (f32[648,384]{1,0:T(8,128)S(1)}, f32[648,384]{1,0:T(8,128)}, u32[]{:S(2)}) copy-start(f32[648,384]{1,0:T(8,128)} %copy-done.6) | copy-start | bytes 2985988
  92.3 13.0 %collective-permute-start.7 = (f32[324,384]{1,0:T(8,128)}, f32[324,384]{1,0:T(8,128)}, u32[]{:S(2)}, u32[]{:S(2)}) collective-permute-start(f32[324,384]{1,0:T(8,128)} %constant_dynamic-slice_fusion.4), channel_id=1, source_target_pairs={{0,8},{8,0},{16,24},{24,16},{1,9},{9,1},{17,25},{25,17},{2,10},{10... | collective-permute-start | bytes 1493000 | tf_op jit(solution)/shard_map/ppermute | solution.py:86
  102.1 8.8 %collective-permute-start.14 = (f32[162,384]{1,0:T(8,128)S(1)}, f32[162,384]{1,0:T(8,128)S(1)}, u32[]{:S(2)}, u32[]{:S(2)}) collective-permute-start(f32[162,384]{1,0:T(8,128)S(1)} %constant_dynamic-slice_fusion), channel_id=1, source_target_pairs={{0,8},{8,0},{16,24},{24,16},{1,9},{9,1},{17,25},{25,17},{2,10},{10... | collective-permute-start | bytes 746504 | tf_op jit(solution)/shard_map/ppermute | solution.py:86
  106.5 5.8 %collective-permute-start.8 = (f32[162,384]{1,0:T(8,128)S(1)}, f32[162,384]{1,0:T(8,128)S(1)}, u32[]{:S(2)}, u32[]{:S(2)}) collective-permute-start(f32[162,384]{1,0:T(8,128)S(1)} %constant_dynamic-slice_fusion.3), channel_id=1, source_target_pairs={{0,16},{8,24},{16,0},{24,8},{1,17},{9,25},{17,1},{25,9},{2,18},{10... | collective-permute-start | bytes 746504 | tf_op jit(solution)/shard_map/ppermute | solution.py:86
  110.9 6.8 %collective-permute-start.15 = (f32[162,384]{1,0:T(8,128)S(1)}, f32[162,384]{1,0:T(8,128)S(1)}, u32[]{:S(2)}, u32[]{:S(2)}) collective-permute-start(f32[162,384]{1,0:T(8,128)S(1)} %dynamic-slice_add_fusion.4), channel_id=1, source_target_pairs={{0,8},{8,0},{16,24},{24,16},{1,9},{9,1},{17,25},{25,17},{2,10},{10... | collective-permute-start | bytes 746504 | tf_op jit(solution)/shard_map/ppermute | solution.py:86
  112.4 9.1 %collective-permute-start.9 = (f32[162,384]{1,0:T(8,128)S(1)}, f32[162,384]{1,0:T(8,128)S(1)}, u32[]{:S(2)}, u32[]{:S(2)}) collective-permute-start(f32[162,384]{1,0:T(8,128)S(1)} %dynamic-slice_add_fusion.5), channel_id=1, source_target_pairs={{0,16},{8,24},{16,0},{24,8},{1,17},{9,25},{17,1},{25,9},{2,18},{10... | collective-permute-start | bytes 746504 | tf_op jit(solution)/shard_map/ppermute | solution.py:86
  118.7 11.2 %collective-permute-start.16 = (f32[324,384]{1,0:T(8,128)S(1)}, f32[324,384]{1,0:T(8,128)}, u32[]{:S(2)}, u32[]{:S(2)}) collective-permute-start(f32[324,384]{1,0:T(8,128)S(1)} %dynamic_update_slice.43), channel_id=1, source_target_pairs={{0,16},{8,24},{16,0},{24,8},{1,17},{9,25},{17,1},{25,9},{2,18},{10... | collective-permute-start | bytes 1493000 | tf_op jit(solution)/shard_map/ppermute | solution.py:86
  123.2 14.9 %collective-permute-start.10 = (f32[324,384]{1,0:T(8,128)}, f32[324,384]{1,0:T(8,128)}, u32[]{:S(2)}, u32[]{:S(2)}) collective-permute-start(f32[324,384]{1,0:T(8,128)} %dynamic_update_slice.37), channel_id=1, source_target_pairs={{0,8},{8,0},{16,24},{24,16},{1,9},{9,1},{17,25},{25,17},{2,10},{10... | collective-permute-start | bytes 1493000 | tf_op jit(solution)/shard_map/ppermute | solution.py:86
  127.3 12.8 %copy-start.2 = (f32[384,1280]{0,1:T(8,128)S(1)}, f32[384,1280]{0,1:T(8,128)}, u32[]{:S(2)}) copy-start(f32[384,1280]{0,1:T(8,128)} %get-tuple-element.3) | copy-start | bytes 5898244
  132.2 11.1 %collective-permute-start.17 = (f32[648,384]{1,0:T(8,128)S(1)}, f32[648,384]{1,0:T(8,128)}, u32[]{:S(2)}, u32[]{:S(2)}) collective-permute-start(f32[648,384]{1,0:T(8,128)S(1)} %dynamic_update_slice.45), channel_id=1, source_target_pairs={{0,4},{4,0},{1,5},{5,1},{2,6},{6,2},{3,7},{7,3},{8,12},{12,8},{9,1... | collective-permute-start | bytes 2985992 | tf_op jit(solution)/shard_map/ppermute | solution.py:86
  140.1 4.5 %collective-permute-start.11 = (f32[648,384]{1,0:T(8,128)}, f32[648,384]{1,0:T(8,128)S(1)}, u32[]{:S(2)}, u32[]{:S(2)}) collective-permute-start(f32[648,384]{1,0:T(8,128)} %dynamic_update_slice.39), channel_id=1, source_target_pairs={{0,4},{4,0},{1,5},{5,1},{2,6},{6,2},{3,7},{7,3},{8,12},{12,8},{9,1... | collective-permute-start | bytes 2985992 | tf_op jit(solution)/shard_map/ppermute | solution.py:86
  142.0 1.2 copy-start.8
  144.7 3.8 %copy-start.10 = (bf16[96,2,4,160]{0,3,2,1:T(8,128)(2,1)S(1)}, bf16[96,2,4,160]{0,3,2,1:T(8,128)(2,1)}, u32[]{:S(2)}) copy-start(bf16[96,2,4,160]{0,3,2,1:T(8,128)(2,1)} %param.5) | copy-start | bytes 737284
  144.7 3.8 %copy-start.11 = (bf16[96,2,4,160]{0,3,2,1:T(8,128)(2,1)S(1)}, bf16[96,2,4,160]{0,3,2,1:T(8,128)(2,1)}, u32[]{:S(2)}) copy-start(bf16[96,2,4,160]{0,3,2,1:T(8,128)(2,1)} %param.6) | copy-start | bytes 737284
  144.7 7.0 %copy-start.1 = (bf16[96,27,384]{2,0,1:T(8,128)(2,1)S(1)}, bf16[96,27,384]{2,0,1:T(8,128)(2,1)}, u32[]{:S(2)}) copy-start(bf16[96,27,384]{2,0,1:T(8,128)(2,1)} %param.7) | copy-start | bytes 5971972
  (4 other events, 3.5 us)
Sparse Core Ops, SparseCore 0:
  86.1 51.2 reduce-scatter.1

commit v2 on v1

--- a/solution.py
+++ b/solution.py
@@ -94,10 +94,9 @@
         x = keep + exchange(send, axis, level)
     for axis, level, bit in reversed(steps):
         got = exchange(x, axis, level)
-        m = x.shape[0]
-        full = jnp.zeros((2 * m,) + x.shape[1:], x.dtype)
-        full = lax.dynamic_update_slice_in_dim(full, x, bit * m, 0)
-        x = lax.dynamic_update_slice_in_dim(full, got, (1 - bit) * m, 0)
+        x = lax.select_n(
+            bit, jnp.concatenate([x, got], axis=0), jnp.concatenate([got, x], axis=0)
+        )
     return x
 
 
@@ -129,18 +128,6 @@
     bordered = with_halo(longer, (("height", 2),), 1)
     padded = jnp.pad(bordered, ((0, 0), (0, 0), (0, 0), (1, 1)))
 
-    positions = frames * lax.axis_size("tm") * rows * lax.axis_size("height") * cols
-    cells_major = jnp.transpose(padded, (1, 2, 3, 0))
-    shifted = jnp.stack(
-        [cells_major[:, :, 2 - kw : 2 - kw + cols] for kw in range(3)], axis=0
-    )
-    active_t = jnp.transpose(active.reshape(total, cells))
-    local_sums = weight_taps(shifted, active_t, frames, rows)
-    summed = group_sum(local_sums.reshape(27 * chans, total), ("height",), ("tm",))
-    weight_grad = jnp.transpose(
-        (summed / math.sqrt(positions)).reshape(27, chans, total), (1, 0, 2)
-    )
-
     kernel = conv_weight.reshape(chans, 3, 3, 3, total)
     kernel = lax.rev(kernel, (1, 2, 3))
     adn = lax.ConvDimensionNumbers(
@@ -165,6 +152,19 @@
         ],
         axis=1,
     )
+    packed, padded, active = lax.optimization_barrier((packed, padded, active))
+    positions = frames * lax.axis_size("tm") * rows * lax.axis_size("height") * cols
+    cells_major = jnp.transpose(padded, (1, 2, 3, 0))
+    shifted = jnp.stack(
+        [cells_major[:, :, 2 - kw : 2 - kw + cols] for kw in range(3)], axis=0
+    )
+    active_t = jnp.transpose(active.reshape(total, cells))
+    local_sums = weight_taps(shifted, active_t, frames, rows)
+    summed = group_sum(local_sums.reshape(27 * chans, total), ("height",), ("tm",))
+    weight_grad = jnp.transpose(
+        (summed / math.sqrt(positions)).reshape(27, chans, total), (1, 0, 2)
+    )
+
     mine = lax.psum_scatter(packed, "chan", scatter_dimension=0, tiled=True)[0]
     act_grad = mine[:chans]
     dots = mine[chans:]

time: 160 us -> 177 us (1.11)
  matrix products: 4.26 us -> 30 us
  local copies, waits for them, and re-layouts: 41.8 us -> 23.6 us
  waiting for transfers between devices: 41.9 us -> 52.4 us
  starting transfers between devices: 22.5 us -> 20 us
    conv_general_dilated x1, matrix products: 4.26 us -> 30 us  [on_device(): lax.conv_general_dilated(padded[None], kernel, window_strides=(1, 1, 1),...]
    dynamic_update_slice x12 -> x0, local copies, waits for them, and re-layouts: 16.2 us -> none  [the longest x6 8.36 us: halving_sum(): x = lax.dynamic_update_slice_in_dim(full, got, (1 - bit) * m, 0)]
    ppermute x12, waiting for transfers between devices: 18.5 us -> 27.3 us  [exchange(): return lax.ppermute(block, axis, [(i, i ^ level) for i in range(size)])]
    broadcast_in_dim x2, local copies, waits for them, and re-layouts: 0.31 us -> 3.65 us  [on_device(): jnp.broadcast_to(part_dots[None], (n_chan, 1, cells))]
    another operation x2 -> x1, local copies, waits for them, and re-layouts: 5.78 us -> 2.57 us  [on_device(): partial.reshape(n_chan, chans, cells)]
    optimization_barrier x0 -> x1, local copies, waits for them, and re-layouts: none -> 2.97 us  [on_device(): packed, padded, active = lax.optimization_barrier((packed, padded, active))]
    transpose x2 -> x0, other arithmetic: 2.56 us -> none  [the longest x1 2.21 us: on_device(): active_t = jnp.transpose(active.reshape(total, cells))]
    unnamed x37 -> x50, local copies, waits for them, and re-layouts: 6.78 us -> 4.29 us
  transfers between devices with their start and end apart: 19 -> 19, of which waited for: 9 -> 10; matrix products, arithmetic and copies ran while one was open for 31% -> 13% of each run, Pallas kernels for 0% -> 0%
where the time goes in v2:
time: 177 us; the launch traced here: 174 us
  waiting for transfers between devices  52.4 us (30%)
  matrix products  30 us (17%)
  other arithmetic  25.5 us (14%)
  local copies, waits for them, and re-layouts  23.6 us (13%)
  starting transfers between devices  20 us (11%)
  between operations  14.5 us (8%)
  Pallas kernels  8.27 us (5%)
    conv_general_dilated x1, matrix products, on_device(): lax.conv_general_dilated(padded[None], kernel, window_strides=(1, 1, 1),...  30 us
    ppermute x12, waiting for transfers between devices, exchange(): return lax.ppermute(block, axis, [(i, i ^ level) for i in range(size)])  27.3 us
    ppermute x3, waiting for transfers between devices, gather_blocks(): lax.ppermute(block, axis, [(j, (j + d) % size) for j in range(size)])  25 us
    ppermute x12, starting transfers between devices, exchange(): return lax.ppermute(block, axis, [(i, i ^ level) for i in range(size)])  10.5 us
    pallas_call x1, Pallas kernels, weight_taps(): pl.pallas_call(body, out_shape=jax.ShapeDtypeStruct((27, outs, ins), jnp....  8.27 us
    add x6, other arithmetic, halving_sum(): x = keep + exchange(send, axis, level)  5.3 us
    unnamed x50, local copies, waits for them, and re-layouts  4.29 us
    dynamic_slice x6, local copies, waits for them, and re-layouts, halving_sum(): send = lax.dynamic_slice_in_dim(x, (1 - bit) * m, m, 0)  3.84 us
  transfers between devices with their start and end apart: 19, of which 10 were waited for; matrix products, arithmetic and copies ran while one was open for 13% of the time, Pallas kernels for 0%

profile of v2, /device:TPU:9, one launch (start us, length us, event | category | flops | bytes accessed | tf_op | source)
XLA Modules:
  0.0 174.2 jit_solution(13621285095029394688)
XLA Ops:
  7.2 1.3 collective-permute-start
  9.7 1.4 collective-permute-start.2
  13.4 2.6 %collective-permute-done = bf16[96,2,4,160]{0,3,2,1:T(8,128)(2,1)S(1)} collective-permute-done((bf16[96,2,4,160]{0,3,2,1:T(8,128)(2,1)}, bf16[96,2,4,160]{0,3,2,1:T(8,128)(2,1)S(1)}, u32[]{:S(2)}, u32[]{:S(2)}) %collective-permute-start) | collective-permute-done | bytes 245792 | tf_op jit(solution)/shard_map/ppermute | solution.py:34
  16.1 20.3 %collective-permute-done.1 = bf16[96,2,4,160]{0,3,2,1:T(8,128)(2,1)S(1)} collective-permute-done((bf16[96,2,4,160]{0,3,2,1:T(8,128)(2,1)}, bf16[96,2,4,160]{0,3,2,1:T(8,128)(2,1)S(1)}, u32[]{:S(2)}, u32[]{:S(2)}) %collective-permute-start.1) | collective-permute-done | bytes 245792 | tf_op jit(solution)/shard_map/ppermute | solution.py:34
  37.1 2.1 %collective-permute-done.2 = bf16[96,2,4,160]{0,3,2,1:T(8,128)(2,1)} collective-permute-done((bf16[96,2,4,160]{0,3,2,1:T(8,128)(2,1)}, bf16[96,2,4,160]{0,3,2,1:T(8,128)(2,1)}, u32[]{:S(2)}, u32[]{:S(2)}) %collective-permute-start.2) | collective-permute-done | bytes 245792 | tf_op jit(solution)/shard_map/ppermute | solution.py:34
  39.2 1.4 select_select_fusion.3
  44.1 3.0 %collective-permute-start.5 = (bf16[96,4,1,160]{0,3,2,1:T(8,128)(2,1)S(1)}, bf16[96,4,1,160]{0,3,2,1:T(8,128)(2,1)S(1)}, u32[]{:S(2)}, u32[]{:S(2)}) collective-permute-start(bf16[96,4,1,160]{0,3,2,1:T(8,128)(2,1)S(1)} %get-tuple-element.22), channel_id=1, source_target_pairs={{4,0},{5,1},{6,2},{7,3},{12,8},{13,9},{14,10},{15,11},{20,16},{21,... | collective-permute-start | bytes 368648 | tf_op jit(solution)/shard_map/ppermute | solution.py:25
  47.2 2.1 %multiply_convert_fusion = bf16[384,2,4,160]{0,3,2,1:T(8,128)(2,1)} fusion(f32[384]{0:T(512)S(1)} %copy-done.22, f32[384]{0:T(512)S(1)} %copy-done.23, f32[2,4,160]{2,1,0:T(4,128)S(1)} %add_rsqrt_fusion, bf16[96,2,4,160]{0,3,2,1:T(8,128)(2,1)S(1)} %get-tuple-element.15, bf16[96,2,4,160]{0,3,2,1:T(8,128)(2,1)S(1)} %get-tuple-element.16, ...), kind=kLoop, calls=%fused_computation.27 | loop fusion | flops 7864320 | bytes 1974272 | tf_op jit(solution)/shard_map/convert_element_type | solution.py:124
  49.7 30.0 %fusion.35 = (f32[384,2,4,160]{0,3,2,1:T(8,128)}, f32[1,384,2,4,160]{1,0,4,3,2:T(1,128)S(1)}) fusion(bf16[96,3,3,3,384]{4,0,3,2,1:T(8,128)(2,1)S(1)} %bitcast.42, bf16[1,96,4,6,162]{1,4,3,2,0:T(8,128)(2,1)S(1)} %fusion.37), kind=kOutput, calls=%fused_computation.79 | convolution fusion | flops 2548039680 | bytes 6669312 | tf_op jit(solution)/shard_map/conv_general_dilated | solution.py:136
  79.7 2.2 %fusion.16 = f32[2,4,160]{2,1,0:T(4,128)S(1)} fusion(f32[1,384,2,4,160]{1,0,4,3,2:T(1,128)S(1)} %get-tuple-element.24, bf16[1,96,2,4,160]{1,4,3,2,0:T(8,128)(2,1)S(1)} %bitcast.45, bf16[1,96,2,4,160]{1,4,3,2,0:T(8,128)(2,1)S(1)} %bitcast.46, bf16[1,96,2,4,160]{1,4,3,2,0:T(8,128)(2,1)S(1)} %bitcast.47, bf16[1,96,2,4,160]{1,4,3,2,0:T(8,128)(2,1)S(1)} %bitcast.44, ...), kind=kLoop, calls=%fused_computation.29 | loop fusion | flops 10812160 | bytes 2962432 | tf_op jit(solution)/shard_map/reduce_sum | solution.py:147
  81.9 2.6 %reshape_reshape_squeeze.3 = f32[4,96,1280]{1,0,2:T(4,128)} reshape(f32[384,2,4,160]{0,3,2,1:T(8,128)S(1)} %copy-done.16) | data formatting | bytes 3932160 | tf_op jit(solution)/shard_map/reshape;reshape;squeeze | solution.py:150
  84.5 3.6 %broadcast_in_dim.16 = f32[4,1,1280]{1,0,2:T(4,128)S(1)} broadcast(f32[1280]{0:T(1024)S(1)} %broadcast_in_dim.7), dimensions={2} | broadcast | bytes 25600 | tf_op jit(solution)/shard_map/broadcast_in_dim | solution.py:151
  88.1 1.5 pad_maximum_fusion.1
  90.7 2.3 %pad_maximum_fusion.cot_ref = bf16[3,4,6,160,96]{4,3,2,1,0:T(8,128)(2,1)} fusion(bf16[1,4,6,160,96]{4,3,2,1,0:T(8,128)(2,1)S(1)} %get-tuple-element.19, bf16[1,4,6,160,96]{4,3,2,1,0:T(8,128)(2,1)S(1)} %get-tuple-element.20, bf16[1,4,6,160,96]{4,3,2,1,0:T(8,128)(2,1)S(1)} %get-tuple-element.18), kind=kLoop, calls=%fused_computation.3 | loop fusion | flops 2211840 | bytes 4423680 | tf_op jit(solution)/shard_map/stack | solution.py:158
  93.0 8.3 %shard_map.68 = f32[27,96,384]{2,1,0:T(8,128)} custom-call(bf16[3,4,6,160,96]{4,3,2,1,0:T(8,128)(2,1)} %pad_maximum_fusion.cot_ref, bf16[1280,384]{1,0:T(8,128)(2,1)} %bitcast.50), custom_call_target="tpu_custom_call" | custom-call | flops 2548039680 | bytes 7176192 | tf_op jit(solution)/shard_map/pallas_call | solution.py:59
  101.3 2.4 %fusion.33 = (f32[1296,384]{1,0:T(8,128)S(1)}, f32[1296,384]{1,0:T(8,128)S(1)}) fusion(f32[2592,384]{1,0:T(8,128)} %bitcast.49), kind=kLoop, calls=%fused_computation.77 | loop fusion | bytes 7962624 | tf_op jit(solution)/shard_map/slice | solution.py:110
  103.7 1.3 copy-done.9
  107.6 1.4 collective-permute-done.6
  108.9 1.6 dynamic-slice_add_fusion.1
  112.7 1.3 dynamic-slice_add_fusion
  117.0 3.0 %copy.48 = f32[4,97,1280]{2,1,0:T(8,128)} copy(f32[4,97,1280]{1,0,2:T(4,128)S(1)} %pad_maximum_fusion.1) | data formatting | bytes 3973120 | tf_op jit(solution)/shard_map/optimization_barrier | solution.py:155
  120.0 4.7 %collective-permute-done.7 = f32[324,384]{1,0:T(8,128)} collective-permute-done((f32[324,384]{1,0:T(8,128)}, f32[324,384]{1,0:T(8,128)}, u32[]{:S(2)}, u32[]{:S(2)}) %collective-permute-start.7) | collective-permute-done | bytes 497696 | tf_op jit(solution)/shard_map/ppermute | solution.py:86
  126.0 1.3 collective-permute-start.8
  127.3 1.4 collective-permute-done.13
  130.2 4.3 %collective-permute-done.8 = f32[162,384]{1,0:T(8,128)S(1)} collective-permute-done((f32[162,384]{1,0:T(8,128)S(1)}, f32[162,384]{1,0:T(8,128)S(1)}, u32[]{:S(2)}, u32[]{:S(2)}) %collective-permute-start.8) | collective-permute-done | bytes 248864 | tf_op jit(solution)/shard_map/ppermute | solution.py:86
  134.5 1.3 collective-permute-start.9
  136.7 4.7 %collective-permute-done.9 = f32[162,384]{1,0:T(8,128)S(1)} collective-permute-done((f32[162,384]{1,0:T(8,128)S(1)}, f32[162,384]{1,0:T(8,128)S(1)}, u32[]{:S(2)}, u32[]{:S(2)}) %collective-permute-start.9) | collective-permute-done | bytes 248864 | tf_op jit(solution)/shard_map/ppermute | solution.py:86
  143.1 10.4 %collective-permute-done.10 = f32[324,384]{1,0:T(8,128)S(1)} collective-permute-done((f32[324,384]{1,0:T(8,128)S(1)}, f32[324,384]{1,0:T(8,128)S(1)}, u32[]{:S(2)}, u32[]{:S(2)}) %collective-permute-start.10) | collective-permute-done | bytes 497696 | tf_op jit(solution)/shard_map/ppermute | solution.py:86
  153.7 2.3 %collective-permute-start.11 = (f32[648,384]{1,0:T(8,128)S(1)}, f32[648,384]{1,0:T(8,128)S(1)}, u32[]{:S(2)}, u32[]{:S(2)}) collective-permute-start(f32[648,384]{1,0:T(8,128)S(1)} %maximum_select_fusion.2), channel_id=1, source_target_pairs={{0,4},{4,0},{1,5},{5,1},{2,6},{6,2},{3,7},{7,3},{8,12},{12,8},{9,1... | collective-permute-start | bytes 2985992 | tf_op jit(solution)/shard_map/ppermute | solution.py:86
  156.8 2.4 %exponential_add_fusion = (f32[384,1280]{0,1:T(8,128)}, f32[384,1280]{0,1:T(8,128)}) fusion(f32[384]{0:T(512)S(1)} %copy-done.22, f32[384]{0:T(512)S(1)} %copy-done.23, f32[1280]{0:T(1024)S(1)} %rsqrt.16, f32[384,2,4,160]{0,3,2,1:T(8,128)S(1)} %maximum_convert_fusion), kind=kLoop, calls=%fused_computation.26 | loop fusion | flops 2457600 | bytes 5906432 | tf_op jit(solution)/shard_map/add | solution.py:145
  159.8 2.3 %maximum_multiply_fusion = f32[2592,384]{1,0:T(8,128)} fusion(f32[1296,384]{1,0:T(8,128)S(1)} %maximum_select_fusion.1, f32[1296,384]{1,0:T(8,128)S(1)} %maximum_select_fusion), kind=kLoop, calls=%fused_computation | loop fusion | flops 1990656 | bytes 7962624 | tf_op jit(solution)/shard_map/div | solution.py:165
  164.3 3.1 %fusion.29 = bf16[96,1280]{0,1:T(8,128)(2,1)} fusion(f32[384,1280]{0,1:T(8,128)} %get-tuple-element.11, s32[]{:T(128)S(6)} %select_n.266, f32[1,96,1280]{1,2,0:T(8,128)S(1)} %copy.50, f32[384,1280]{0,1:T(8,128)} %get-tuple-element.10, f32[96]{0:T(128)S(1)} %dynamic-slice, bf16[96,2,4,160]{0,3,2,1:T(8,128)(2,1)S(1)} %copy-done.17, ...), kind=kLoop, calls=%fused_computation.51 | loop fusion | flops 1966080 | bytes 2227588 | tf_op jit(solution)/shard_map/convert_element_type | solution.py:178
  (103 shorter events, 25.8 us)
Async XLA Ops:
  7.2 42.5 %copy-start = (bf16[96,27,384]{2,0,1:T(8,128)(2,1)S(1)}, bf16[96,27,384]{2,0,1:T(8,128)(2,1)}, u32[]{:S(2)}) copy-start(bf16[96,27,384]{2,0,1:T(8,128)(2,1)} %param.7) | copy-start | bytes 5971972
  7.2 154.9 %reduce-scatter.2.cloned.1.call-start = ((), (), s32[]{:S(2)}) async-start(), calls=%async_computation.1 | async-start | bytes 2662400 | tf_op jit(solution)/shard_map/reduce_scatter | solution.py:168
  7.2 8.8 %collective-permute-start = (bf16[96,2,4,160]{0,3,2,1:T(8,128)(2,1)}, bf16[96,2,4,160]{0,3,2,1:T(8,128)(2,1)S(1)}, u32[]{:S(2)}, u32[]{:S(2)}) collective-permute-start(bf16[96,2,4,160]{0,3,2,1:T(8,128)(2,1)} %param.5), channel_id=1, source_target_pairs={{0,1},{1,2},{2,3},{3,0},{4,5},{5,6},{6,7},{7,4},{8,9},{9,10},{10,1... | collective-permute-start | bytes 737288 | tf_op jit(solution)/shard_map/ppermute | solution.py:34
  8.6 27.8 %collective-permute-start.1 = (bf16[96,2,4,160]{0,3,2,1:T(8,128)(2,1)}, bf16[96,2,4,160]{0,3,2,1:T(8,128)(2,1)S(1)}, u32[]{:S(2)}, u32[]{:S(2)}) collective-permute-start(bf16[96,2,4,160]{0,3,2,1:T(8,128)(2,1)} %param.5), channel_id=1, source_target_pairs={{0,2},{1,3},{2,0},{3,1},{4,6},{5,7},{6,4},{7,5},{8,10},{9,11},{10,... | collective-permute-start | bytes 737288 | tf_op jit(solution)/shard_map/ppermute | solution.py:34
  9.7 29.5 %collective-permute-start.2 = (bf16[96,2,4,160]{0,3,2,1:T(8,128)(2,1)}, bf16[96,2,4,160]{0,3,2,1:T(8,128)(2,1)}, u32[]{:S(2)}, u32[]{:S(2)}) collective-permute-start(bf16[96,2,4,160]{0,3,2,1:T(8,128)(2,1)} %param.5), channel_id=1, source_target_pairs={{0,3},{1,0},{2,1},{3,2},{4,7},{5,4},{6,5},{7,6},{8,11},{9,8},{10,9... | collective-permute-start | bytes 737288 | tf_op jit(solution)/shard_map/ppermute | solution.py:34
  11.1 30.7 %collective-permute-start.3 = (bf16[96,2,4,160]{0,3,2,1:T(8,128)(2,1)}, bf16[96,2,4,160]{0,3,2,1:T(8,128)(2,1)}, u32[]{:S(2)}, u32[]{:S(2)}) collective-permute-start(bf16[96,2,4,160]{0,3,2,1:T(8,128)(2,1)} %param.6), channel_id=1, source_target_pairs={{8,0},{16,8},{24,16},{9,1},{17,9},{25,17},{10,2},{18,10},{26,18},{... | collective-permute-start | bytes 737288 | tf_op jit(solution)/shard_map/ppermute | solution.py:14
  16.1 20.3 %copy-start.20 = (bf16[96,2,4,160]{0,3,2,1:T(8,128)(2,1)}, bf16[96,2,4,160]{0,3,2,1:T(8,128)(2,1)S(1)}, u32[]{:S(2)}) copy-start(bf16[96,2,4,160]{0,3,2,1:T(8,128)(2,1)S(1)} %collective-permute-done) | copy-start | bytes 737284
  40.6 39.1 %copy-start.3 = (bf16[96,2,4,160]{0,3,2,1:T(8,128)(2,1)}, bf16[96,2,4,160]{0,3,2,1:T(8,128)(2,1)S(1)}, u32[]{:S(2)}) copy-start(bf16[96,2,4,160]{0,3,2,1:T(8,128)(2,1)S(1)} %get-tuple-element.16) | copy-start | bytes 737284
  40.6 39.1 %copy-start.5 = (bf16[96,2,4,160]{0,3,2,1:T(8,128)(2,1)}, bf16[96,2,4,160]{0,3,2,1:T(8,128)(2,1)S(1)}, u32[]{:S(2)}) copy-start(bf16[96,2,4,160]{0,3,2,1:T(8,128)(2,1)S(1)} %get-tuple-element.17) | copy-start | bytes 737284
  40.6 6.5 %copy-start.22 = (f32[384]{0:T(512)S(1)}, f32[384]{0:T(512)}, u32[]{:S(2)}) copy-start(f32[384]{0:T(512)} %param.9) | copy-start | bytes 4612
  40.6 6.5 %copy-start.23 = (f32[384]{0:T(512)S(1)}, f32[384]{0:T(512)}, u32[]{:S(2)}) copy-start(f32[384]{0:T(512)} %param.8) | copy-start | bytes 4612
  42.8 6.9 %copy-start.10 = (bf16[96,4,4,160]{0,3,2,1:T(8,128)(2,1)}, bf16[96,4,4,160]{0,3,2,1:T(8,128)(2,1)S(1)}, u32[]{:S(2)}) copy-start(bf16[96,4,4,160]{0,3,2,1:T(8,128)(2,1)S(1)} %constant_dynamic-update-slice_fusion) | copy-start | bytes 1474564
  42.8 6.5 %collective-permute-start.4 = (bf16[96,4,1,160]{0,3,2,1:T(8,128)(2,1)S(1)}, bf16[96,4,1,160]{0,3,2,1:T(8,128)(2,1)S(1)}, u32[]{:S(2)}, u32[]{:S(2)}) collective-permute-start(bf16[96,4,1,160]{0,3,2,1:T(8,128)(2,1)S(1)} %get-tuple-element.21), channel_id=1, source_target_pairs={{0,4},{1,5},{2,6},{3,7},{8,12},{9,13},{10,14},{11,15},{16,20},{17,... | collective-permute-start | bytes 368648 | tf_op jit(solution)/shard_map/ppermute | solution.py:24
  44.1 5.2 %collective-permute-start.5 = (bf16[96,4,1,160]{0,3,2,1:T(8,128)(2,1)S(1)}, bf16[96,4,1,160]{0,3,2,1:T(8,128)(2,1)S(1)}, u32[]{:S(2)}, u32[]{:S(2)}) collective-permute-start(bf16[96,4,1,160]{0,3,2,1:T(8,128)(2,1)S(1)} %get-tuple-element.22), channel_id=1, source_target_pairs={{4,0},{5,1},{6,2},{7,3},{12,8},{13,9},{14,10},{15,11},{20,16},{21,... | collective-permute-start | bytes 368648 | tf_op jit(solution)/shard_map/ppermute | solution.py:25
  49.3 30.4 %copy-start.18 = (bf16[96,4,1,160]{0,3,2,1:T(8,128)(2,1)}, bf16[96,4,1,160]{0,3,2,1:T(8,128)(2,1)S(1)}, u32[]{:S(2)}) copy-start(bf16[96,4,1,160]{0,3,2,1:T(8,128)(2,1)S(1)} %collective-permute-done.5) | copy-start | bytes 368644
  106.0 2.9 %collective-permute-start.6 = (f32[648,384]{1,0:T(8,128)}, f32[648,384]{1,0:T(8,128)}, u32[]{:S(2)}, u32[]{:S(2)}) collective-permute-start(f32[648,384]{1,0:T(8,128)} %constant_dynamic-slice_fusion.5), channel_id=1, source_target_pairs={{0,4},{4,0},{1,5},{5,1},{2,6},{6,2},{3,7},{7,3},{8,12},{12,8},{9,1... | collective-permute-start | bytes 2985992 | tf_op jit(solution)/shard_map/ppermute | solution.py:86
  107.1 5.6 %collective-permute-start.12 = (f32[648,384]{1,0:T(8,128)}, f32[648,384]{1,0:T(8,128)}, u32[]{:S(2)}, u32[]{:S(2)}) collective-permute-start(f32[648,384]{1,0:T(8,128)} %constant_dynamic-slice_fusion.2), channel_id=1, source_target_pairs={{0,4},{4,0},{1,5},{5,1},{2,6},{6,2},{3,7},{7,3},{8,12},{12,8},{9,1... | collective-permute-start | bytes 2985992 | tf_op jit(solution)/shard_map/ppermute | solution.py:86
  107.6 5.1 %copy-start.8 = (f32[1296,384]{1,0:T(8,128)S(1)}, f32[1296,384]{1,0:T(8,128)}, u32[]{:S(2)}) copy-start(f32[1296,384]{1,0:T(8,128)} %copy-done.7) | copy-start | bytes 5971972
  111.5 13.3 %collective-permute-start.7 = (f32[324,384]{1,0:T(8,128)}, f32[324,384]{1,0:T(8,128)}, u32[]{:S(2)}, u32[]{:S(2)}) collective-permute-start(f32[324,384]{1,0:T(8,128)} %constant_dynamic-slice_fusion.4), channel_id=1, source_target_pairs={{0,8},{8,0},{16,24},{24,16},{1,9},{9,1},{17,25},{25,17},{2,10},{10... | collective-permute-start | bytes 1493000 | tf_op jit(solution)/shard_map/ppermute | solution.py:86
  115.8 12.9 %collective-permute-start.13 = (f32[324,384]{1,0:T(8,128)}, f32[324,384]{1,0:T(8,128)}, u32[]{:S(2)}, u32[]{:S(2)}) collective-permute-start(f32[324,384]{1,0:T(8,128)} %constant_dynamic-slice_fusion.1), channel_id=1, source_target_pairs={{0,16},{8,24},{16,0},{24,8},{1,17},{9,25},{17,1},{25,9},{2,18},{10... | collective-permute-start | bytes 1493000 | tf_op jit(solution)/shard_map/ppermute | solution.py:86
  120.0 8.7 %copy-start.13 = (f32[648,384]{1,0:T(8,128)S(1)}, f32[648,384]{1,0:T(8,128)}, u32[]{:S(2)}) copy-start(f32[648,384]{1,0:T(8,128)} %copy-done.12) | copy-start | bytes 2985988
  126.0 8.5 %collective-permute-start.8 = (f32[162,384]{1,0:T(8,128)S(1)}, f32[162,384]{1,0:T(8,128)S(1)}, u32[]{:S(2)}, u32[]{:S(2)}) collective-permute-start(f32[162,384]{1,0:T(8,128)S(1)} %constant_dynamic-slice_fusion.3), channel_id=1, source_target_pairs={{0,16},{8,24},{16,0},{24,8},{1,17},{9,25},{17,1},{25,9},{2,18},{10... | collective-permute-start | bytes 746504 | tf_op jit(solution)/shard_map/ppermute | solution.py:86
  129.9 5.9 %collective-permute-start.14 = (f32[162,384]{1,0:T(8,128)S(1)}, f32[162,384]{1,0:T(8,128)S(1)}, u32[]{:S(2)}, u32[]{:S(2)}) collective-permute-start(f32[162,384]{1,0:T(8,128)S(1)} %constant_dynamic-slice_fusion), channel_id=1, source_target_pairs={{0,8},{8,0},{16,24},{24,16},{1,9},{9,1},{17,25},{25,17},{2,10},{10... | collective-permute-start | bytes 746504 | tf_op jit(solution)/shard_map/ppermute | solution.py:86
  134.5 6.9 %collective-permute-start.9 = (f32[162,384]{1,0:T(8,128)S(1)}, f32[162,384]{1,0:T(8,128)S(1)}, u32[]{:S(2)}, u32[]{:S(2)}) collective-permute-start(f32[162,384]{1,0:T(8,128)S(1)} %dynamic-slice_add_fusion.5), channel_id=1, source_target_pairs={{0,16},{8,24},{16,0},{24,8},{1,17},{9,25},{17,1},{25,9},{2,18},{10... | collective-permute-start | bytes 746504 | tf_op jit(solution)/shard_map/ppermute | solution.py:86
  135.8 5.7 %collective-permute-start.15 = (f32[162,384]{1,0:T(8,128)S(1)}, f32[162,384]{1,0:T(8,128)S(1)}, u32[]{:S(2)}, u32[]{:S(2)}) collective-permute-start(f32[162,384]{1,0:T(8,128)S(1)} %dynamic-slice_add_fusion.4), channel_id=1, source_target_pairs={{0,8},{8,0},{16,24},{24,16},{1,9},{9,1},{17,25},{25,17},{2,10},{10... | collective-permute-start | bytes 746504 | tf_op jit(solution)/shard_map/ppermute | solution.py:86
  141.5 12.0 %collective-permute-start.10 = (f32[324,384]{1,0:T(8,128)S(1)}, f32[324,384]{1,0:T(8,128)S(1)}, u32[]{:S(2)}, u32[]{:S(2)}) collective-permute-start(f32[324,384]{1,0:T(8,128)S(1)} %maximum_select_fusion.4), channel_id=1, source_target_pairs={{0,8},{8,0},{16,24},{24,16},{1,9},{9,1},{17,25},{25,17},{2,10},{10... | collective-permute-start | bytes 1493000 | tf_op jit(solution)/shard_map/ppermute | solution.py:86
  141.6 14.3 %collective-permute-start.16 = (f32[324,384]{1,0:T(8,128)S(1)}, f32[324,384]{1,0:T(8,128)S(1)}, u32[]{:S(2)}, u32[]{:S(2)}) collective-permute-start(f32[324,384]{1,0:T(8,128)S(1)} %maximum_select_fusion.5), channel_id=1, source_target_pairs={{0,16},{8,24},{16,0},{24,8},{1,17},{9,25},{17,1},{25,9},{2,18},{10... | collective-permute-start | bytes 1493000 | tf_op jit(solution)/shard_map/ppermute | solution.py:86
  143.1 13.2 %copy-start.4 = (bf16[96,2,4,160]{0,3,2,1:T(8,128)(2,1)S(1)}, bf16[96,2,4,160]{0,3,2,1:T(8,128)(2,1)}, u32[]{:S(2)}) copy-start(bf16[96,2,4,160]{0,3,2,1:T(8,128)(2,1)} %copy-done.3) | copy-start | bytes 737284
  143.1 13.2 %copy-start.6 = (bf16[96,2,4,160]{0,3,2,1:T(8,128)(2,1)S(1)}, bf16[96,2,4,160]{0,3,2,1:T(8,128)(2,1)}, u32[]{:S(2)}) copy-start(bf16[96,2,4,160]{0,3,2,1:T(8,128)(2,1)} %copy-done.5) | copy-start | bytes 737284
  153.7 5.5 %collective-permute-start.11 = (f32[648,384]{1,0:T(8,128)S(1)}, f32[648,384]{1,0:T(8,128)S(1)}, u32[]{:S(2)}, u32[]{:S(2)}) collective-permute-start(f32[648,384]{1,0:T(8,128)S(1)} %maximum_select_fusion.2), channel_id=1, source_target_pairs={{0,4},{4,0},{1,5},{5,1},{2,6},{6,2},{3,7},{7,3},{8,12},{12,8},{9,1... | collective-permute-start | bytes 2985992 | tf_op jit(solution)/shard_map/ppermute | solution.py:86
  156.1 3.5 %collective-permute-start.17 = (f32[648,384]{1,0:T(8,128)S(1)}, f32[648,384]{1,0:T(8,128)S(1)}, u32[]{:S(2)}, u32[]{:S(2)}) collective-permute-start(f32[648,384]{1,0:T(8,128)S(1)} %maximum_select_fusion.3), channel_id=1, source_target_pairs={{0,4},{4,0},{1,5},{5,1},{2,6},{6,2},{3,7},{7,3},{8,12},{12,8},{9,1... | collective-permute-start | bytes 2985992 | tf_op jit(solution)/shard_map/ppermute | solution.py:86
  162.0 5.3 %copy-start.1 = (bf16[96,27,384]{2,0,1:T(8,128)(2,1)S(1)}, bf16[96,27,384]{2,0,1:T(8,128)(2,1)}, u32[]{:S(2)}) copy-start(bf16[96,27,384]{2,0,1:T(8,128)(2,1)} %param.7) | copy-start | bytes 5971972
  (11 other events, 24.4 us)
Sparse Core Ops, SparseCore 0:
  120.1 40.2 reduce-scatter.1

commit v3 on v2

--- a/solution.py
+++ b/solution.py
@@ -39,11 +39,11 @@
     )
 
 
-def weight_taps(shifted, active_t, frames, rows):
+def weight_taps(shifted, active_t, anchor, frames, rows):
     _, _, _, cols, outs = shifted.shape
     cells, ins = active_t.shape
 
-    def body(cot_ref, act_ref, out_ref):
+    def body(cot_ref, act_ref, anchor_ref, out_ref):
         act = act_ref[...]
         for kt in range(3):
             for kh in range(3):
@@ -59,14 +59,14 @@
     return pl.pallas_call(
         body,
         out_shape=jax.ShapeDtypeStruct((27, outs, ins), jnp.float32),
-        in_specs=[pl.BlockSpec(memory_space=pltpu.VMEM)] * 2,
+        in_specs=[pl.BlockSpec(memory_space=pltpu.VMEM)] * 3,
         out_specs=pl.BlockSpec(memory_space=pltpu.VMEM),
         cost_estimate=pl.CostEstimate(
             flops=2 * 27 * ins * cells * outs,
             bytes_accessed=shifted.size * 2 + active_t.size * 2 + 27 * ins * outs * 4,
             transcendentals=0,
         ),
-    )(shifted, active_t)
+    )(shifted, active_t, anchor)
 
 
 def halving_steps(axes):
@@ -97,6 +97,15 @@
         x = lax.select_n(
             bit, jnp.concatenate([x, got], axis=0), jnp.concatenate([got, x], axis=0)
         )
+    return x
+
+
+def xor_sum(x, axis):
+    size = lax.axis_size(axis)
+    level = 1
+    while level < size:
+        x = x + exchange(x, axis, level)
+        level *= 2
     return x
 
 
@@ -142,37 +151,29 @@
         preferred_element_type=jnp.float32,
     )[0].reshape(total, cells)
 
-    sig = jax.nn.sigmoid(normed)
-    slope = sig * (1.0 + normed * (1.0 - sig)) * norm_gain[:, None]
-    part_dots = jnp.sum(partial * slope * flat_x, axis=0, keepdims=True)
-    packed = jnp.concatenate(
-        [
-            partial.reshape(n_chan, chans, cells),
-            jnp.broadcast_to(part_dots[None], (n_chan, 1, cells)),
-        ],
-        axis=1,
-    )
-    packed, padded, active = lax.optimization_barrier((packed, padded, active))
+    mine = lax.psum_scatter(
+        partial.reshape(n_chan, chans, cells), "chan", scatter_dimension=0, tiled=True
+    )[0]
+
     positions = frames * lax.axis_size("tm") * rows * lax.axis_size("height") * cols
     cells_major = jnp.transpose(padded, (1, 2, 3, 0))
     shifted = jnp.stack(
         [cells_major[:, :, 2 - kw : 2 - kw + cols] for kw in range(3)], axis=0
     )
     active_t = jnp.transpose(active.reshape(total, cells))
-    local_sums = weight_taps(shifted, active_t, frames, rows)
+    local_sums = weight_taps(shifted, active_t, partial[:8, :128], frames, rows)
     summed = group_sum(local_sums.reshape(27 * chans, total), ("height",), ("tm",))
     weight_grad = jnp.transpose(
         (summed / math.sqrt(positions)).reshape(27, chans, total), (1, 0, 2)
     )
 
-    mine = lax.psum_scatter(packed, "chan", scatter_dimension=0, tiled=True)[0]
-    act_grad = mine[:chans]
-    dots = mine[chans:]
-
     offset = lax.axis_index("chan") * chans
     own_x = features.reshape(chans, -1).astype(jnp.float32)
-    own_slope = lax.dynamic_slice_in_dim(slope, offset, chans, 0)
-    upstream = act_grad * own_slope
+    own_normed = lax.dynamic_slice_in_dim(normed, offset, chans, 0)
+    own_gain = lax.dynamic_slice_in_dim(norm_gain, offset, chans, 0)
+    sig = jax.nn.sigmoid(own_normed)
+    upstream = mine * (sig * (1.0 + own_normed * (1.0 - sig))) * own_gain[:, None]
+    dots = xor_sum(jnp.sum(upstream * own_x, axis=0, keepdims=True), "chan")
     own_back = inv_rms * upstream - own_x * inv_rms**3 * dots / total
     result = cotangent.reshape(chans, -1).astype(jnp.float32) + own_back
     return (result.astype(jnp.bfloat16).reshape(features.shape), weight_grad)

time: 177 us -> 198 us (1.12)
  waiting for transfers between devices: 52.4 us -> 62.7 us
  other arithmetic: 25.5 us -> 33.3 us
  starting transfers between devices: 20 us -> 27.3 us
  local copies, waits for them, and re-layouts: 23.6 us -> 18.8 us
    ppermute x12 -> x14, waiting for transfers between devices: 27.3 us -> 39.3 us  [exchange(): return lax.ppermute(block, axis, [(i, i ^ level) for i in range(size)])]
    select_n x6, other arithmetic: 0.65 us -> 9.27 us  [halving_sum(): lax.select_n(bit, jnp.concatenate([x, got], axis=0), jnp.concatenate([got...]
    ppermute x12 -> x14, starting transfers between devices: 10.5 us -> 18 us  [exchange(): return lax.ppermute(block, axis, [(i, i ^ level) for i in range(size)])]
    another operation x1 -> x2, local copies, waits for them, and re-layouts: 2.57 us -> 7.32 us  [on_device(): partial.reshape(n_chan, chans, cells)]
    broadcast_in_dim x2 -> x1, local copies, waits for them, and re-layouts: 3.65 us -> 0.01 us  [on_device(): dots = xor_sum(jnp.sum(upstream * own_x, axis=0, keepdims=True), 'chan')]
    optimization_barrier x1 -> x0, local copies, waits for them, and re-layouts: 2.97 us -> none  [on_device(): packed, padded, active = lax.optimization_barrier((packed, padded, active))]
    transpose x0 -> x2, other arithmetic: none -> 2.61 us  [the longest x1 2.26 us: on_device(): active_t = jnp.transpose(active.reshape(total, cells))]
    add x1 -> x2, other arithmetic: 2.35 us -> 0.03 us  [xor_sum(): x = x + exchange(x, axis, level)]
  transfers between devices with their start and end apart: 19 -> 21, of which waited for: 10 -> 11; matrix products, arithmetic and copies ran while one was open for 13% -> 19% of each run, Pallas kernels for 0% -> 0%
where the time goes in v3:
time: 198 us; the launch traced here: 195 us
  waiting for transfers between devices  62.7 us (32%)
  other arithmetic  33.3 us (17%)
  matrix products  29.9 us (15%)
  starting transfers between devices  27.3 us (14%)
  local copies, waits for them, and re-layouts  18.8 us (9%)
  between operations  14.5 us (7%)
  Pallas kernels  8.32 us (4%)
    ppermute x14, waiting for transfers between devices, exchange(): return lax.ppermute(block, axis, [(i, i ^ level) for i in range(size)])  39.3 us
    conv_general_dilated x1, matrix products, on_device(): lax.conv_general_dilated(padded[None], kernel, window_strides=(1, 1, 1),...  29.9 us
    ppermute x3, waiting for transfers between devices, gather_blocks(): lax.ppermute(block, axis, [(j, (j + d) % size) for j in range(size)])  23.4 us
    ppermute x14, starting transfers between devices, exchange(): return lax.ppermute(block, axis, [(i, i ^ level) for i in range(size)])  18 us
    select_n x6, other arithmetic, halving_sum(): lax.select_n(bit, jnp.concatenate([x, got], axis=0), jnp.concatenate([got...  9.27 us
    pallas_call x1, Pallas kernels, weight_taps(): pl.pallas_call(body, out_shape=jax.ShapeDtypeStruct((27, outs, ins), jnp....  8.32 us
    add x6, other arithmetic, halving_sum(): x = keep + exchange(send, axis, level)  7.56 us
    another operation x2, local copies, waits for them, and re-layouts, on_device(): partial.reshape(n_chan, chans, cells)  7.32 us
  transfers between devices with their start and end apart: 21, of which 11 were waited for; matrix products, arithmetic and copies ran while one was open for 19% of the time, Pallas kernels for 0%

profile of v3, /device:TPU:9, one launch (start us, length us, event | category | flops | bytes accessed | tf_op | source)
XLA Modules:
  0.0 194.9 jit_solution(5994216217421528431)
XLA Ops:
  7.2 2.4 %collective-permute-start.1 = (bf16[96,2,4,160]{0,3,2,1:T(8,128)(2,1)}, bf16[96,2,4,160]{0,3,2,1:T(8,128)(2,1)S(1)}, u32[]{:S(2)}, u32[]{:S(2)}) collective-permute-start(bf16[96,2,4,160]{0,3,2,1:T(8,128)(2,1)} %param.5), channel_id=1, source_target_pairs={{0,2},{1,3},{2,0},{3,1},{4,6},{5,7},{6,4},{7,5},{8,10},{9,11},{10,... | collective-permute-start | bytes 737288 | tf_op jit(solution)/shard_map/ppermute | solution.py:34
  9.8 1.3 collective-permute-start
  12.5 1.7 constant_dynamic-update-slice_fusion.1
  14.2 17.2 %collective-permute-done.1 = bf16[96,2,4,160]{0,3,2,1:T(8,128)(2,1)S(1)} collective-permute-done((bf16[96,2,4,160]{0,3,2,1:T(8,128)(2,1)}, bf16[96,2,4,160]{0,3,2,1:T(8,128)(2,1)S(1)}, u32[]{:S(2)}, u32[]{:S(2)}) %collective-permute-start.1) | collective-permute-done | bytes 245792 | tf_op jit(solution)/shard_map/ppermute | solution.py:34
  31.3 6.0 %collective-permute-done.2 = bf16[96,2,4,160]{0,3,2,1:T(8,128)(2,1)S(1)} collective-permute-done((bf16[96,2,4,160]{0,3,2,1:T(8,128)(2,1)}, bf16[96,2,4,160]{0,3,2,1:T(8,128)(2,1)S(1)}, u32[]{:S(2)}, u32[]{:S(2)}) %collective-permute-start.2) | collective-permute-done | bytes 245792 | tf_op jit(solution)/shard_map/ppermute | solution.py:34
  38.3 1.4 select_select_fusion.3
  43.1 2.9 %collective-permute-start.5 = (bf16[96,4,1,160]{0,3,2,1:T(8,128)(2,1)S(1)}, bf16[96,4,1,160]{0,3,2,1:T(8,128)(2,1)S(1)}, u32[]{:S(2)}, u32[]{:S(2)}) collective-permute-start(bf16[96,4,1,160]{0,3,2,1:T(8,128)(2,1)S(1)} %get-tuple-element.16), channel_id=1, source_target_pairs={{4,0},{5,1},{6,2},{7,3},{12,8},{13,9},{14,10},{15,11},{20,16},{21,... | collective-permute-start | bytes 368648 | tf_op jit(solution)/shard_map/ppermute | solution.py:25
  47.3 2.3 %fusion.10 = (bf16[1280,384]{1,0:T(8,128)(2,1)}, f32[384,1280]{0,1:T(8,128)}) fusion(f32[384]{0:T(512)S(1)} %copy-done.12, f32[384]{0:T(512)S(1)} %copy-done.13, f32[1280]{0:T(1024)S(1)} %rsqrt.15, f32[384,2,4,160]{0,3,2,1:T(8,128)S(1)} %maximum_convert_fusion), kind=kLoop, calls=%fused_computation.27 | loop fusion | flops 3932160 | bytes 4923392 | tf_op jit(solution)/shard_map/transpose | solution.py:163
  49.9 1.9 slice_bitcast_fusion.2
  51.8 29.9 %fusion.23 = (f32[384,2,4,160]{0,3,2,1:T(8,128)}, f32[1,384,2,4,160]{1,0,4,3,2:T(1,128)S(1)}) fusion(bf16[96,3,3,3,384]{4,0,3,2,1:T(8,128)(2,1)S(1)} %bitcast.46, bf16[1,96,4,6,162]{1,4,3,2,0:T(8,128)(2,1)S(1)} %get-tuple-element.14), kind=kOutput, calls=%fused_computation.63 | convolution fusion | flops 2548039680 | bytes 6669312 | tf_op jit(solution)/shard_map/conv_general_dilated | solution.py:145
  82.6 3.8 %pad_maximum_fusion.cot_ref = bf16[3,4,6,160,96]{4,3,2,1,0:T(8,128)(2,1)} fusion(bf16[1,4,6,160,96]{4,3,2,1,0:T(8,128)(2,1)} %get-tuple-element.11, bf16[1,4,6,160,96]{4,3,2,1,0:T(8,128)(2,1)} %get-tuple-element.12, bf16[1,4,6,160,96]{4,3,2,1,0:T(8,128)(2,1)S(1)} %get-tuple-element.10), kind=kLoop, calls=%fused_computation.3 | loop fusion | flops 2211840 | bytes 4423680 | tf_op jit(solution)/shard_map/stack | solution.py:160
  86.4 8.3 %shard_map.68 = f32[27,96,384]{2,1,0:T(8,128)} custom-call(bf16[3,4,6,160,96]{4,3,2,1,0:T(8,128)(2,1)} %pad_maximum_fusion.cot_ref, bf16[1280,384]{1,0:T(8,128)(2,1)} %get-tuple-element.2.act_ref, f32[8,128]{1,0:T(8,128)} %copy.13.anchor_ref), custom_call_target="tpu_custom_call" | custom-call | flops 2548039680 | bytes 7176192 | tf_op jit(solution)/shard_map/pallas_call | solution.py:59
  94.7 2.4 %fusion.21 = (f32[1296,384]{1,0:T(8,128)S(1)}, f32[1296,384]{1,0:T(8,128)S(1)}) fusion(f32[2592,384]{1,0:T(8,128)} %bitcast.48), kind=kLoop, calls=%fused_computation.61 | loop fusion | bytes 7962624 | tf_op jit(solution)/shard_map/slice | solution.py:119
  100.8 1.6 dynamic-slice_add_fusion
  102.5 1.3 collective-permute-start.15
  103.8 3.9 %reshape_reshape_squeeze.3 = f32[4,96,1280]{1,0,2:T(4,128)} reshape(f32[384,2,4,160]{0,3,2,1:T(8,128)} %get-tuple-element.17) | data formatting | bytes 3932160 | tf_op jit(solution)/shard_map/reshape;reshape;squeeze | solution.py:155
  107.7 3.5 %copy.10 = f32[4,96,1280]{1,2,0:T(8,128)} copy(f32[4,96,1280]{1,0,2:T(4,128)} %reshape_reshape_squeeze.3) | data formatting | bytes 3932160 | tf_op jit(solution)/shard_map/reshape;reshape;squeeze | solution.py:155
  111.2 1.6 dynamic-slice_add_fusion.1
  116.5 1.3 collective-permute-start.16
  117.8 14.2 %collective-permute-done.16 = f32[162,384]{1,0:T(8,128)} collective-permute-done((f32[162,384]{1,0:T(8,128)S(1)}, f32[162,384]{1,0:T(8,128)}, u32[]{:S(2)}, u32[]{:S(2)}) %collective-permute-start.16) | collective-permute-done | bytes 248864 | tf_op jit(solution)/shard_map/ppermute | solution.py:86
  135.9 3.5 %collective-permute-done.17 = f32[162,384]{1,0:T(8,128)S(1)} collective-permute-done((f32[162,384]{1,0:T(8,128)S(1)}, f32[162,384]{1,0:T(8,128)S(1)}, u32[]{:S(2)}, u32[]{:S(2)}) %collective-permute-start.17) | collective-permute-done | bytes 248864 | tf_op jit(solution)/shard_map/ppermute | solution.py:86
  143.1 14.9 %collective-permute-done.11 = f32[162,384]{1,0:T(8,128)S(1)} collective-permute-done((f32[162,384]{1,0:T(8,128)S(1)}, f32[162,384]{1,0:T(8,128)S(1)}, u32[]{:S(2)}, u32[]{:S(2)}) %collective-permute-start.11) | collective-permute-done | bytes 248864 | tf_op jit(solution)/shard_map/ppermute | solution.py:86
  158.2 2.3 %maximum_select_fusion.3 = f32[648,384]{1,0:T(8,128)} fusion(f32[324,384]{1,0:T(8,128)} %collective-permute-done.18, f32[324,384]{1,0:T(8,128)S(1)} %maximum_select_fusion.5, pred[]{:T(512)S(6)} %select_n.276), kind=kLoop, calls=%fused_computation.20 | loop fusion | flops 746496 | bytes 1990657 | tf_op jit(solution)/shard_map/select_n | solution.py:97
  160.5 3.4 %collective-permute-start.19 = (f32[648,384]{1,0:T(8,128)}, f32[648,384]{1,0:T(8,128)}, u32[]{:S(2)}, u32[]{:S(2)}) collective-permute-start(f32[648,384]{1,0:T(8,128)} %maximum_select_fusion.3), channel_id=1, source_target_pairs={{0,4},{4,0},{1,5},{5,1},{2,6},{6,2},{3,7},{7,3},{8,12},{12,8},{9,1... | collective-permute-start | bytes 2985992 | tf_op jit(solution)/shard_map/ppermute | solution.py:86
  163.9 4.6 %collective-permute-done.12 = f32[324,384]{1,0:T(8,128)S(1)} collective-permute-done((f32[324,384]{1,0:T(8,128)S(1)}, f32[324,384]{1,0:T(8,128)S(1)}, u32[]{:S(2)}, u32[]{:S(2)}) %collective-permute-start.12) | collective-permute-done | bytes 497696 | tf_op jit(solution)/shard_map/ppermute | solution.py:86
  168.7 3.6 %collective-permute-start.13 = (f32[648,384]{1,0:T(8,128)S(1)}, f32[648,384]{1,0:T(8,128)}, u32[]{:S(2)}, u32[]{:S(2)}) collective-permute-start(f32[648,384]{1,0:T(8,128)S(1)} %maximum_select_fusion.2), channel_id=1, source_target_pairs={{0,4},{4,0},{1,5},{5,1},{2,6},{6,2},{3,7},{7,3},{8,12},{12,8},{9,1... | collective-permute-start | bytes 2985992 | tf_op jit(solution)/shard_map/ppermute | solution.py:86
  172.3 3.7 %maximum_select_fusion.1 = f32[1296,384]{1,0:T(8,128)} fusion(f32[648,384]{1,0:T(8,128)} %collective-permute-done.19, f32[648,384]{1,0:T(8,128)} %maximum_select_fusion.3, pred[]{:T(512)S(6)} %select_n.269), kind=kLoop, calls=%fused_computation.6 | loop fusion | flops 1492992 | bytes 3981313 | tf_op jit(solution)/shard_map/select_n | solution.py:97
  176.1 2.0 %fusion.16 = f32[1280]{0:T(1024)S(1)} fusion(bf16[96,2,4,160]{0,3,2,1:T(8,128)(2,1)S(1)} %copy-done.5, f32[96]{0:T(128)S(1)} %dynamic_slice.43, f32[384,1280]{0,1:T(8,128)} %get-tuple-element.3, s32[]{:T(128)S(6)} %select_n.267, f32[1,96,1280]{1,2,0:T(8,128)} %reduce-scatter.2.cloned.1.call-done), kind=kLoop, calls=%fused_computation.35 | loop fusion | flops 1473280 | bytes 1234308 | tf_op jit(solution)/shard_map/reduce_sum | solution.py:176
  178.2 1.8 maximum_select_fusion
  180.7 2.3 %collective-permute-start.7 = (f32[1,1280]{1,0:T(1,128)S(1)}, f32[1,1280]{1,0:T(1,128)S(1)}, u32[]{:S(2)}, u32[]{:S(2)}) collective-permute-start(f32[1,1280]{1,0:T(1,128)S(1)} %reshape_add_fusion), channel_id=1, source_target_pairs={{0,2},{1,3},{2,0},{3,1},{4,6},{5,7},{6,4},{7,5},{8,10},{9,11},{10,... | collective-permute-start | bytes 15368 | tf_op jit(solution)/shard_map/ppermute | solution.py:86
  183.0 2.3 %maximum_multiply_fusion = f32[2592,384]{1,0:T(8,128)} fusion(f32[1296,384]{1,0:T(8,128)S(1)} %copy-done.3, f32[1296,384]{1,0:T(8,128)S(1)} %maximum_select_fusion), kind=kLoop, calls=%fused_computation | loop fusion | flops 1990656 | bytes 7962624 | tf_op jit(solution)/shard_map/div | solution.py:167
  185.3 2.7 %fusion.15 = bf16[96,1280]{0,1:T(8,128)(2,1)} fusion(bf16[96,2,4,160]{0,3,2,1:T(8,128)(2,1)S(1)} %copy-done.8, bf16[96,2,4,160]{0,3,2,1:T(8,128)(2,1)S(1)} %copy-done.5, f32[1280]{0:T(1024)S(1)} %add_reduce_fusion, f32[1280]{0:T(1024)S(1)} %multiply_multiply_fusion, f32[1280]{0:T(1024)S(1)} %rsqrt.15, f32[96]{0:T(128)S(1)} %dynamic_slice.43, ...), kind=kLoop, calls=%fused_computation.34 | loop fusion | flops 2211840 | bytes 1736068 | tf_op jit(solution)/shard_map/convert_element_type | solution.py:179
  (85 shorter events, 24.3 us)
Async XLA Ops:
  7.2 44.7 %copy-start = (bf16[96,27,384]{2,0,1:T(8,128)(2,1)S(1)}, bf16[96,27,384]{2,0,1:T(8,128)(2,1)}, u32[]{:S(2)}) copy-start(bf16[96,27,384]{2,0,1:T(8,128)(2,1)} %param.7) | copy-start | bytes 5971972
  7.2 168.9 %reduce-scatter.2.cloned.1.call-start = ((), (), s32[]{:S(2)}) async-start(), calls=%async_computation.1 | async-start | bytes 3276800 | tf_op jit(solution)/shard_map/reduce_scatter | solution.py:154
  7.2 24.1 %collective-permute-start.1 = (bf16[96,2,4,160]{0,3,2,1:T(8,128)(2,1)}, bf16[96,2,4,160]{0,3,2,1:T(8,128)(2,1)S(1)}, u32[]{:S(2)}, u32[]{:S(2)}) collective-permute-start(bf16[96,2,4,160]{0,3,2,1:T(8,128)(2,1)} %param.5), channel_id=1, source_target_pairs={{0,2},{1,3},{2,0},{3,1},{4,6},{5,7},{6,4},{7,5},{8,10},{9,11},{10,... | collective-permute-start | bytes 737288 | tf_op jit(solution)/shard_map/ppermute | solution.py:34
  9.6 27.8 %collective-permute-start.2 = (bf16[96,2,4,160]{0,3,2,1:T(8,128)(2,1)}, bf16[96,2,4,160]{0,3,2,1:T(8,128)(2,1)S(1)}, u32[]{:S(2)}, u32[]{:S(2)}) collective-permute-start(bf16[96,2,4,160]{0,3,2,1:T(8,128)(2,1)} %param.5), channel_id=1, source_target_pairs={{0,3},{1,0},{2,1},{3,2},{4,7},{5,4},{6,5},{7,6},{8,11},{9,8},{10,9... | collective-permute-start | bytes 737288 | tf_op jit(solution)/shard_map/ppermute | solution.py:34
  9.8 28.6 %collective-permute-start = (bf16[96,2,4,160]{0,3,2,1:T(8,128)(2,1)}, bf16[96,2,4,160]{0,3,2,1:T(8,128)(2,1)}, u32[]{:S(2)}, u32[]{:S(2)}) collective-permute-start(bf16[96,2,4,160]{0,3,2,1:T(8,128)(2,1)} %param.5), channel_id=1, source_target_pairs={{0,1},{1,2},{2,3},{3,0},{4,5},{5,6},{6,7},{7,4},{8,9},{9,10},{10,1... | collective-permute-start | bytes 737288 | tf_op jit(solution)/shard_map/ppermute | solution.py:34
  11.1 30.5 %collective-permute-start.3 = (bf16[96,2,4,160]{0,3,2,1:T(8,128)(2,1)}, bf16[96,2,4,160]{0,3,2,1:T(8,128)(2,1)}, u32[]{:S(2)}, u32[]{:S(2)}) collective-permute-start(bf16[96,2,4,160]{0,3,2,1:T(8,128)(2,1)} %param.6), channel_id=1, source_target_pairs={{8,0},{16,8},{24,16},{9,1},{17,9},{25,17},{10,2},{18,10},{26,18},{... | collective-permute-start | bytes 737288 | tf_op jit(solution)/shard_map/ppermute | solution.py:14
  31.3 6.0 %copy-start.10 = (bf16[96,2,4,160]{0,3,2,1:T(8,128)(2,1)}, bf16[96,2,4,160]{0,3,2,1:T(8,128)(2,1)S(1)}, u32[]{:S(2)}) copy-start(bf16[96,2,4,160]{0,3,2,1:T(8,128)(2,1)S(1)} %collective-permute-done.1) | copy-start | bytes 737284
  40.9 6.3 %copy-start.12 = (f32[384]{0:T(512)S(1)}, f32[384]{0:T(512)}, u32[]{:S(2)}) copy-start(f32[384]{0:T(512)} %param.9) | copy-start | bytes 4612
  40.9 6.3 %copy-start.13 = (f32[384]{0:T(512)S(1)}, f32[384]{0:T(512)}, u32[]{:S(2)}) copy-start(f32[384]{0:T(512)} %param.8) | copy-start | bytes 4612
  43.1 6.5 %collective-permute-start.5 = (bf16[96,4,1,160]{0,3,2,1:T(8,128)(2,1)S(1)}, bf16[96,4,1,160]{0,3,2,1:T(8,128)(2,1)S(1)}, u32[]{:S(2)}, u32[]{:S(2)}) collective-permute-start(bf16[96,4,1,160]{0,3,2,1:T(8,128)(2,1)S(1)} %get-tuple-element.16), channel_id=1, source_target_pairs={{4,0},{5,1},{6,2},{7,3},{12,8},{13,9},{14,10},{15,11},{20,16},{21,... | collective-permute-start | bytes 368648 | tf_op jit(solution)/shard_map/ppermute | solution.py:25
  46.0 3.6 %collective-permute-start.4 = (bf16[96,4,1,160]{0,3,2,1:T(8,128)(2,1)S(1)}, bf16[96,4,1,160]{0,3,2,1:T(8,128)(2,1)S(1)}, u32[]{:S(2)}, u32[]{:S(2)}) collective-permute-start(bf16[96,4,1,160]{0,3,2,1:T(8,128)(2,1)S(1)} %get-tuple-element.15), channel_id=1, source_target_pairs={{0,4},{1,5},{2,6},{3,7},{8,12},{9,13},{10,14},{11,15},{16,20},{17,... | collective-permute-start | bytes 368648 | tf_op jit(solution)/shard_map/ppermute | solution.py:24
  97.1 2.3 %copy-start.1 = (f32[1296,384]{1,0:T(8,128)}, f32[1296,384]{1,0:T(8,128)S(1)}, u32[]{:S(2)}) copy-start(f32[1296,384]{1,0:T(8,128)S(1)} %get-tuple-element.4) | copy-start | bytes 5971972
  97.2 3.5 %collective-permute-start.14 = (f32[648,384]{1,0:T(8,128)S(1)}, f32[648,384]{1,0:T(8,128)}, u32[]{:S(2)}, u32[]{:S(2)}) collective-permute-start(f32[648,384]{1,0:T(8,128)S(1)} %constant_dynamic-slice_fusion.2), channel_id=1, source_target_pairs={{0,4},{4,0},{1,5},{5,1},{2,6},{6,2},{3,7},{7,3},{8,12},{12,8},{9,1... | collective-permute-start | bytes 2985992 | tf_op jit(solution)/shard_map/ppermute | solution.py:86
  99.5 11.7 %collective-permute-start.8 = (f32[648,384]{1,0:T(8,128)}, f32[648,384]{1,0:T(8,128)}, u32[]{:S(2)}, u32[]{:S(2)}) collective-permute-start(f32[648,384]{1,0:T(8,128)} %constant_dynamic-slice_fusion.5), channel_id=1, source_target_pairs={{0,4},{4,0},{1,5},{5,1},{2,6},{6,2},{3,7},{7,3},{8,12},{12,8},{9,1... | collective-permute-start | bytes 2985992 | tf_op jit(solution)/shard_map/ppermute | solution.py:86
  102.5 12.9 %collective-permute-start.15 = (f32[324,384]{1,0:T(8,128)S(1)}, f32[324,384]{1,0:T(8,128)}, u32[]{:S(2)}, u32[]{:S(2)}) collective-permute-start(f32[324,384]{1,0:T(8,128)S(1)} %constant_dynamic-slice_fusion.1), channel_id=1, source_target_pairs={{0,16},{8,24},{16,0},{24,8},{1,17},{9,25},{17,1},{25,9},{2,18},{10... | collective-permute-start | bytes 1493000 | tf_op jit(solution)/shard_map/ppermute | solution.py:86
  112.8 3.6 %copy-start.4 = (f32[648,384]{1,0:T(8,128)}, f32[648,384]{1,0:T(8,128)S(1)}, u32[]{:S(2)}) copy-start(f32[648,384]{1,0:T(8,128)S(1)} %dynamic-slice_add_fusion.1) | copy-start | bytes 2985988
  113.8 20.5 %collective-permute-start.9 = (f32[324,384]{1,0:T(8,128)}, f32[324,384]{1,0:T(8,128)}, u32[]{:S(2)}, u32[]{:S(2)}) collective-permute-start(f32[324,384]{1,0:T(8,128)} %constant_dynamic-slice_fusion.4), channel_id=1, source_target_pairs={{0,8},{8,0},{16,24},{24,16},{1,9},{9,1},{17,25},{25,17},{2,10},{10... | collective-permute-start | bytes 1493000 | tf_op jit(solution)/shard_map/ppermute | solution.py:86
  116.5 15.5 %collective-permute-start.16 = (f32[162,384]{1,0:T(8,128)S(1)}, f32[162,384]{1,0:T(8,128)}, u32[]{:S(2)}, u32[]{:S(2)}) collective-permute-start(f32[162,384]{1,0:T(8,128)S(1)} %constant_dynamic-slice_fusion), channel_id=1, source_target_pairs={{0,8},{8,0},{16,24},{24,16},{1,9},{9,1},{17,25},{25,17},{2,10},{10... | collective-permute-start | bytes 746504 | tf_op jit(solution)/shard_map/ppermute | solution.py:86
  133.0 2.9 %copy-start.9 = (f32[162,384]{1,0:T(8,128)}, f32[162,384]{1,0:T(8,128)S(1)}, u32[]{:S(2)}) copy-start(f32[162,384]{1,0:T(8,128)S(1)} %dynamic-slice_add_fusion.4) | copy-start | bytes 746500
  133.0 6.4 %collective-permute-start.17 = (f32[162,384]{1,0:T(8,128)S(1)}, f32[162,384]{1,0:T(8,128)S(1)}, u32[]{:S(2)}, u32[]{:S(2)}) collective-permute-start(f32[162,384]{1,0:T(8,128)S(1)} %dynamic-slice_add_fusion.4), channel_id=1, source_target_pairs={{0,8},{8,0},{16,24},{24,16},{1,9},{9,1},{17,25},{25,17},{2,10},{10... | collective-permute-start | bytes 746504 | tf_op jit(solution)/shard_map/ppermute | solution.py:86
  135.5 6.1 %collective-permute-start.10 = (f32[162,384]{1,0:T(8,128)S(1)}, f32[162,384]{1,0:T(8,128)}, u32[]{:S(2)}, u32[]{:S(2)}) collective-permute-start(f32[162,384]{1,0:T(8,128)S(1)} %constant_dynamic-slice_fusion.3), channel_id=1, source_target_pairs={{0,16},{8,24},{16,0},{24,8},{1,17},{9,25},{17,1},{25,9},{2,18},{10... | collective-permute-start | bytes 746504 | tf_op jit(solution)/shard_map/ppermute | solution.py:86
  140.5 17.7 %collective-permute-start.18 = (f32[324,384]{1,0:T(8,128)S(1)}, f32[324,384]{1,0:T(8,128)}, u32[]{:S(2)}, u32[]{:S(2)}) collective-permute-start(f32[324,384]{1,0:T(8,128)S(1)} %maximum_select_fusion.5), channel_id=1, source_target_pairs={{0,16},{8,24},{16,0},{24,8},{1,17},{9,25},{17,1},{25,9},{2,18},{10... | collective-permute-start | bytes 1493000 | tf_op jit(solution)/shard_map/ppermute | solution.py:86
  142.6 15.4 %collective-permute-start.11 = (f32[162,384]{1,0:T(8,128)S(1)}, f32[162,384]{1,0:T(8,128)S(1)}, u32[]{:S(2)}, u32[]{:S(2)}) collective-permute-start(f32[162,384]{1,0:T(8,128)S(1)} %dynamic-slice_add_fusion.5), channel_id=1, source_target_pairs={{0,16},{8,24},{16,0},{24,8},{1,17},{9,25},{17,1},{25,9},{2,18},{10... | collective-permute-start | bytes 746504 | tf_op jit(solution)/shard_map/ppermute | solution.py:86
  158.1 10.5 %collective-permute-start.12 = (f32[324,384]{1,0:T(8,128)S(1)}, f32[324,384]{1,0:T(8,128)S(1)}, u32[]{:S(2)}, u32[]{:S(2)}) collective-permute-start(f32[324,384]{1,0:T(8,128)S(1)} %maximum_select_fusion.4), channel_id=1, source_target_pairs={{0,8},{8,0},{16,24},{24,16},{1,9},{9,1},{17,25},{25,17},{2,10},{10... | collective-permute-start | bytes 1493000 | tf_op jit(solution)/shard_map/ppermute | solution.py:86
  160.5 11.8 %collective-permute-start.19 = (f32[648,384]{1,0:T(8,128)}, f32[648,384]{1,0:T(8,128)}, u32[]{:S(2)}, u32[]{:S(2)}) collective-permute-start(f32[648,384]{1,0:T(8,128)} %maximum_select_fusion.3), channel_id=1, source_target_pairs={{0,4},{4,0},{1,5},{5,1},{2,6},{6,2},{3,7},{7,3},{8,12},{12,8},{9,1... | collective-permute-start | bytes 2985992 | tf_op jit(solution)/shard_map/ppermute | solution.py:86
  168.7 9.5 %collective-permute-start.13 = (f32[648,384]{1,0:T(8,128)S(1)}, f32[648,384]{1,0:T(8,128)}, u32[]{:S(2)}, u32[]{:S(2)}) collective-permute-start(f32[648,384]{1,0:T(8,128)S(1)} %maximum_select_fusion.2), channel_id=1, source_target_pairs={{0,4},{4,0},{1,5},{5,1},{2,6},{6,2},{3,7},{7,3},{8,12},{12,8},{9,1... | collective-permute-start | bytes 2985992 | tf_op jit(solution)/shard_map/ppermute | solution.py:86
  172.3 3.7 %copy-start.5 = (bf16[96,2,4,160]{0,3,2,1:T(8,128)(2,1)S(1)}, bf16[96,2,4,160]{0,3,2,1:T(8,128)(2,1)}, u32[]{:S(2)}) copy-start(bf16[96,2,4,160]{0,3,2,1:T(8,128)(2,1)} %param.5) | copy-start | bytes 737284
  178.1 4.9 %copy-start.3 = (f32[1296,384]{1,0:T(8,128)S(1)}, f32[1296,384]{1,0:T(8,128)}, u32[]{:S(2)}) copy-start(f32[1296,384]{1,0:T(8,128)} %maximum_select_fusion.1) | copy-start | bytes 5971972
  178.1 2.5 %collective-permute-start.6 = (f32[1,1280]{1,0:T(1,128)S(1)}, f32[1,1280]{1,0:T(1,128)S(1)}, u32[]{:S(2)}, u32[]{:S(2)}) collective-permute-start(f32[1,1280]{1,0:T(1,128)S(1)} %broadcast_in_dim.5), channel_id=1, source_target_pairs={{0,1},{1,0},{2,3},{3,2},{4,5},{5,4},{6,7},{7,6},{8,9},{9,8},{10,11... | collective-permute-start | bytes 15368 | tf_op jit(solution)/shard_map/ppermute | solution.py:86
  180.6 4.7 %copy-start.6 = (f32[1,96,1280]{1,2,0:T(8,128)S(1)}, f32[1,96,1280]{1,2,0:T(8,128)}, u32[]{:S(2)}) copy-start(f32[1,96,1280]{1,2,0:T(8,128)} %reduce-scatter.2.cloned.1.call-done) | copy-start | bytes 1474564
  180.6 4.7 %copy-start.8 = (bf16[96,2,4,160]{0,3,2,1:T(8,128)(2,1)S(1)}, bf16[96,2,4,160]{0,3,2,1:T(8,128)(2,1)}, u32[]{:S(2)}) copy-start(bf16[96,2,4,160]{0,3,2,1:T(8,128)(2,1)} %param.6) | copy-start | bytes 737284
  180.7 4.6 %collective-permute-start.7 = (f32[1,1280]{1,0:T(1,128)S(1)}, f32[1,1280]{1,0:T(1,128)S(1)}, u32[]{:S(2)}, u32[]{:S(2)}) collective-permute-start(f32[1,1280]{1,0:T(1,128)S(1)} %reshape_add_fusion), channel_id=1, source_target_pairs={{0,2},{1,3},{2,0},{3,1},{4,6},{5,7},{6,4},{7,5},{8,10},{9,11},{10,... | collective-permute-start | bytes 15368 | tf_op jit(solution)/shard_map/ppermute | solution.py:86
  (3 other events, 4.2 us)
Sparse Core Ops, SparseCore 0:
  111.3 50.7 reduce-scatter.1

commit v4 on v1

--- a/solution.py
+++ b/solution.py
@@ -94,10 +94,9 @@
         x = keep + exchange(send, axis, level)
     for axis, level, bit in reversed(steps):
         got = exchange(x, axis, level)
-        m = x.shape[0]
-        full = jnp.zeros((2 * m,) + x.shape[1:], x.dtype)
-        full = lax.dynamic_update_slice_in_dim(full, x, bit * m, 0)
-        x = lax.dynamic_update_slice_in_dim(full, got, (1 - bit) * m, 0)
+        x = lax.select_n(
+            bit, jnp.concatenate([x, got], axis=0), jnp.concatenate([got, x], axis=0)
+        )
     return x
 
 

time: 160 us -> 157 us (0.981)
  local copies, waits for them, and re-layouts: 41.8 us -> 21.9 us
  waiting for transfers between devices: 41.9 us -> 55 us
  other arithmetic: 25.1 us -> 28.7 us
    dynamic_update_slice x12 -> x0, local copies, waits for them, and re-layouts: 16.2 us -> none  [the longest x6 8.36 us: halving_sum(): x = lax.dynamic_update_slice_in_dim(full, got, (1 - bit) * m, 0)]
    ppermute x12, waiting for transfers between devices: 18.5 us -> 27.5 us  [exchange(): return lax.ppermute(block, axis, [(i, i ^ level) for i in range(size)])]
    select_n x0 -> x6, other arithmetic: none -> 5.03 us  [halving_sum(): lax.select_n(bit, jnp.concatenate([x, got], axis=0), jnp.concatenate([got...]
    reduce_scatter x1, waiting for transfers between devices: 0.01 us -> 4.14 us  [on_device(): mine = lax.psum_scatter(packed, 'chan', scatter_dimension=0, tiled=True)[0]]
    another operation x6 -> x0, local copies, waits for them, and re-layouts: 2.2 us -> none
    unnamed x37 -> x43, local copies, waits for them, and re-layouts: 6.78 us -> 6.11 us
  transfers between devices with their start and end apart: 19 -> 19, of which waited for: 9 -> 11; matrix products, arithmetic and copies ran while one was open for 31% -> 25% of each run, Pallas kernels for 0% -> 0%
where the time goes in v4:
time: 157 us; the launch traced here: 154 us
  waiting for transfers between devices  55 us (35%)
  other arithmetic  28.7 us (18%)
  local copies, waits for them, and re-layouts  21.9 us (14%)
  starting transfers between devices  21.4 us (14%)
  between operations  14.6 us (9%)
  Pallas kernels  8.27 us (5%)
  matrix products  4.32 us (3%)
    ppermute x12, waiting for transfers between devices, exchange(): return lax.ppermute(block, axis, [(i, i ^ level) for i in range(size)])  27.5 us
    ppermute x3, waiting for transfers between devices, gather_blocks(): lax.ppermute(block, axis, [(j, (j + d) % size) for j in range(size)])  23.4 us
    ppermute x12, starting transfers between devices, exchange(): return lax.ppermute(block, axis, [(i, i ^ level) for i in range(size)])  11.9 us
    pallas_call x1, Pallas kernels, weight_taps(): pl.pallas_call(body, out_shape=jax.ShapeDtypeStruct((27, outs, ins), jnp....  8.27 us
    unnamed x43, local copies, waits for them, and re-layouts  6.11 us
    another operation x2, local copies, waits for them, and re-layouts, on_device(): partial.reshape(n_chan, chans, cells)  5.92 us
    select_n x6, other arithmetic, halving_sum(): lax.select_n(bit, jnp.concatenate([x, got], axis=0), jnp.concatenate([got...  5.03 us
    conv_general_dilated x1, matrix products, on_device(): lax.conv_general_dilated(padded[None], kernel, window_strides=(1, 1, 1),...  4.32 us
  transfers between devices with their start and end apart: 19, of which 11 were waited for; matrix products, arithmetic and copies ran while one was open for 25% of the time, Pallas kernels for 0%

profile of v4, /device:TPU:9, one launch (start us, length us, event | category | flops | bytes accessed | tf_op | source)
XLA Modules:
  0.0 154.2 jit_solution(811894203268918575)
XLA Ops:
  7.2 2.4 %collective-permute-start.1 = (bf16[96,2,4,160]{0,3,2,1:T(8,128)(2,1)}, bf16[96,2,4,160]{0,3,2,1:T(8,128)(2,1)S(1)}, u32[]{:S(2)}, u32[]{:S(2)}) collective-permute-start(bf16[96,2,4,160]{0,3,2,1:T(8,128)(2,1)} %param.5), channel_id=1, source_target_pairs={{0,2},{1,3},{2,0},{3,1},{4,6},{5,7},{6,4},{7,5},{8,10},{9,11},{10,... | collective-permute-start | bytes 737288 | tf_op jit(solution)/shard_map/ppermute | solution.py:34
  12.5 1.7 %constant_dynamic-update-slice_fusion.1 = bf16[96,4,4,160]{0,3,2,1:T(8,128)(2,1)} fusion(bf16[96,2,4,160]{0,3,2,1:T(8,128)(2,1)} %param.6), kind=kLoop, calls=%fused_computation.79 | loop fusion | bytes 573440
  14.2 17.1 %collective-permute-done.1 = bf16[96,2,4,160]{0,3,2,1:T(8,128)(2,1)S(1)} collective-permute-done((bf16[96,2,4,160]{0,3,2,1:T(8,128)(2,1)}, bf16[96,2,4,160]{0,3,2,1:T(8,128)(2,1)S(1)}, u32[]{:S(2)}, u32[]{:S(2)}) %collective-permute-start.1) | collective-permute-done | bytes 245792 | tf_op jit(solution)/shard_map/ppermute | solution.py:34
  31.3 6.0 %collective-permute-done.2 = bf16[96,2,4,160]{0,3,2,1:T(8,128)(2,1)S(1)} collective-permute-done((bf16[96,2,4,160]{0,3,2,1:T(8,128)(2,1)}, bf16[96,2,4,160]{0,3,2,1:T(8,128)(2,1)S(1)}, u32[]{:S(2)}, u32[]{:S(2)}) %collective-permute-start.2) | collective-permute-done | bytes 245792 | tf_op jit(solution)/shard_map/ppermute | solution.py:34
  38.3 1.4 select_select_fusion.3
  43.1 2.9 %collective-permute-start.5 = (bf16[96,4,1,160]{0,3,2,1:T(8,128)(2,1)S(1)}, bf16[96,4,1,160]{0,3,2,1:T(8,128)(2,1)S(1)}, u32[]{:S(2)}, u32[]{:S(2)}) collective-permute-start(bf16[96,4,1,160]{0,3,2,1:T(8,128)(2,1)S(1)} %get-tuple-element.16), channel_id=1, source_target_pairs={{4,0},{5,1},{6,2},{7,3},{12,8},{13,9},{14,10},{15,11},{20,16},{21,... | collective-permute-start | bytes 368648 | tf_op jit(solution)/shard_map/ppermute | solution.py:25
  46.0 1.5 collective-permute-start.4
  47.5 2.2 %fusion.27 = (bf16[1280,384]{1,0:T(8,128)(2,1)}, f32[384,1280]{0,1:T(8,128)}) fusion(f32[384]{0:T(512)S(1)} %copy-done.17, f32[384]{0:T(512)S(1)} %copy-done.18, f32[1280]{0:T(1024)S(1)} %rsqrt.16, f32[384,2,4,160]{0,3,2,1:T(8,128)S(1)} %maximum_convert_fusion), kind=kLoop, calls=%fused_computation.46 | loop fusion | flops 3932160 | bytes 4923392 | tf_op jit(solution)/shard_map/transpose | solution.py:136
  52.8 2.3 %pad_maximum_fusion.cot_ref = bf16[3,4,6,160,96]{4,3,2,1,0:T(8,128)(2,1)} fusion(bf16[1,4,6,160,96]{4,3,2,1,0:T(8,128)(2,1)S(1)} %get-tuple-element.11, bf16[1,4,6,160,96]{4,3,2,1,0:T(8,128)(2,1)S(1)} %get-tuple-element.12, bf16[1,4,6,160,96]{4,3,2,1,0:T(8,128)(2,1)S(1)} %get-tuple-element.10), kind=kLoop, calls=%fused_computation.3 | loop fusion | flops 2211840 | bytes 4423680 | tf_op jit(solution)/shard_map/stack | solution.py:133
  55.1 8.3 %shard_map.68 = f32[27,96,384]{2,1,0:T(8,128)} custom-call(bf16[3,4,6,160,96]{4,3,2,1,0:T(8,128)(2,1)} %pad_maximum_fusion.cot_ref, bf16[1280,384]{1,0:T(8,128)(2,1)} %get-tuple-element.2.act_ref), custom_call_target="tpu_custom_call" | custom-call | flops 2548039680 | bytes 7176192 | tf_op jit(solution)/shard_map/pallas_call | solution.py:59
  63.4 2.4 %fusion.45 = (f32[1296,384]{1,0:T(8,128)S(1)}, f32[1296,384]{1,0:T(8,128)S(1)}) fusion(f32[2592,384]{1,0:T(8,128)} %bitcast.63), kind=kLoop, calls=%fused_computation.91 | loop fusion | bytes 7962624 | tf_op jit(solution)/shard_map/slice | solution.py:110
  69.5 4.3 %convolution_select_fusion = f32[2,4,8,21,384]{4,2,3,1,0:T(8,128)S(1)} fusion(bf16[96,3,3,3,384]{4,0,3,2,1:T(8,128)(2,1)S(1)} %bitcast.54, bf16[96,4,6,1,7,2]{0,4,5,2,1,3:T(8,128)(2,1)S(1)} %slice.45, bf16[96,4,6,1,8,21]{0,4,5,2,1,3:T(8,128)(2,1)S(1)} %copy-done.14, pred[8,21]{0,1:T(8,128)(4,1)S(1)} %copy-done.19), kind=kOutput, calls=%fused_computation.31 | convolution fusion | flops 2678501376 | bytes 4893864 | tf_op jit(solution)/shard_map/conv_general_dilated | solution.py:148
  74.7 1.5 copy.86
  76.2 2.1 %fusion.15 = f32[2,4,160]{2,1,0:T(4,128)S(1)} fusion(bf16[1,96,2,4,160]{1,4,3,2,0:T(8,128)(2,1)S(1)} %bitcast.58, bf16[1,96,2,4,160]{1,4,3,2,0:T(8,128)(2,1)S(1)} %bitcast.59, bf16[1,96,2,4,160]{1,4,3,2,0:T(8,128)(2,1)S(1)} %bitcast.60, bf16[1,96,2,4,160]{1,4,3,2,0:T(8,128)(2,1)S(1)} %bitcast.57, f32[384]{0:T(512)S(1)} %copy-done.17, f32[384]{0:T(512)S(1)} %copy-done.18, ...), kind=kLoop, calls=%fused_computation.30 | loop fusion | flops 10812160 | bytes 2962432 | tf_op jit(solution)/shard_map/reduce_sum | solution.py:159
  78.4 3.9 %reshape_reshape_squeeze.3 = f32[4,96,1280]{1,0,2:T(4,128)} reshape(f32[1,384,2,4,160]{1,4,3,2,0:T(8,128)} %bitcast.56) | data formatting | bytes 3932160 | tf_op jit(solution)/shard_map/reshape;reshape;squeeze | solution.py:162
  82.3 2.1 %copy.78 = f32[4,96,1280]{1,2,0:T(8,128)S(1)} copy(f32[4,96,1280]{1,0,2:T(4,128)} %reshape_reshape_squeeze.3) | data formatting | bytes 3932160 | tf_op jit(solution)/shard_map/reshape;reshape;squeeze | solution.py:162
  84.6 1.5 dynamic-slice_add_fusion
  86.2 1.4 collective-permute-start.13
  90.4 2.2 %pad_maximum_fusion.1 = f32[4,97,1280]{1,2,0:T(8,128)} fusion(f32[4,1,1280]{1,2,0:T(8,128)S(1)} %broadcast_in_dim.16, f32[4,96,1280]{1,2,0:T(8,128)S(1)} %copy.78), kind=kLoop, calls=%fused_computation.4 | loop fusion | flops 496640 | bytes 3973120 | tf_op jit(solution)/shard_map/concatenate | solution.py:160
  92.7 6.8 %collective-permute-done.13 = f32[324,384]{1,0:T(8,128)S(1)} collective-permute-done((f32[324,384]{1,0:T(8,128)S(1)}, f32[324,384]{1,0:T(8,128)S(1)}, u32[]{:S(2)}, u32[]{:S(2)}) %collective-permute-start.13) | collective-permute-done | bytes 497696 | tf_op jit(solution)/shard_map/ppermute | solution.py:86
  103.3 3.8 %collective-permute-done.14 = f32[162,384]{1,0:T(8,128)S(1)} collective-permute-done((f32[162,384]{1,0:T(8,128)S(1)}, f32[162,384]{1,0:T(8,128)S(1)}, u32[]{:S(2)}, u32[]{:S(2)}) %collective-permute-start.14) | collective-permute-done | bytes 248864 | tf_op jit(solution)/shard_map/ppermute | solution.py:86
  110.2 3.5 %collective-permute-done.15 = f32[162,384]{1,0:T(8,128)S(1)} collective-permute-done((f32[162,384]{1,0:T(8,128)S(1)}, f32[162,384]{1,0:T(8,128)S(1)}, u32[]{:S(2)}, u32[]{:S(2)}) %collective-permute-start.15) | collective-permute-done | bytes 248864 | tf_op jit(solution)/shard_map/ppermute | solution.py:86
  115.5 1.3 collective-permute-start.10
  116.8 10.7 %collective-permute-done.16 = f32[324,384]{1,0:T(8,128)} collective-permute-done((f32[324,384]{1,0:T(8,128)S(1)}, f32[324,384]{1,0:T(8,128)}, u32[]{:S(2)}, u32[]{:S(2)}) %collective-permute-start.16) | collective-permute-done | bytes 497696 | tf_op jit(solution)/shard_map/ppermute | solution.py:86
  127.5 1.6 %maximum_select_fusion.3 = f32[648,384]{1,0:T(8,128)S(1)} fusion(f32[324,384]{1,0:T(8,128)} %collective-permute-done.16, f32[324,384]{1,0:T(8,128)} %copy-done.10, pred[]{:T(512)S(6)} %select_n.275), kind=kLoop, calls=%fused_computation.43 | loop fusion | flops 746496 | bytes 1990657 | tf_op jit(solution)/shard_map/select_n | solution.py:97
  129.1 1.8 %collective-permute-start.17 = (f32[648,384]{1,0:T(8,128)S(1)}, f32[648,384]{1,0:T(8,128)}, u32[]{:S(2)}, u32[]{:S(2)}) collective-permute-start(f32[648,384]{1,0:T(8,128)S(1)} %maximum_select_fusion.3), channel_id=1, source_target_pairs={{0,4},{4,0},{1,5},{5,1},{2,6},{6,2},{3,7},{7,3},{8,12},{12,8},{9,1... | collective-permute-start | bytes 2985992 | tf_op jit(solution)/shard_map/ppermute | solution.py:86
  132.4 1.8 %add_divide_fusion = f32[384,1280]{0,1:T(8,128)} fusion(f32[384,1280]{0,1:T(8,128)S(1)} %copy-done.2), kind=kLoop, calls=%fused_computation.28 | loop fusion | flops 1474560 | bytes 3932160 | tf_op jit(solution)/shard_map/div | solution.py:157
  134.2 1.7 %maximum_select_fusion.1 = f32[1296,384]{1,0:T(8,128)S(1)} fusion(f32[648,384]{1,0:T(8,128)} %collective-permute-done.17, f32[648,384]{1,0:T(8,128)S(1)} %maximum_select_fusion.3, pred[]{:T(512)S(6)} %select_n.268), kind=kLoop, calls=%fused_computation.11 | loop fusion | flops 1492992 | bytes 3981313 | tf_op jit(solution)/shard_map/select_n | solution.py:97
  136.2 2.3 %maximum_multiply_fusion = f32[2592,384]{1,0:T(8,128)} fusion(f32[1296,384]{1,0:T(8,128)S(1)} %maximum_select_fusion.1, f32[1296,384]{1,0:T(8,128)S(1)} %maximum_select_fusion), kind=kLoop, calls=%fused_computation | loop fusion | flops 1990656 | bytes 7962624 | tf_op jit(solution)/shard_map/div | solution.py:140
  138.5 4.1 %reduce-scatter.2.cloned.1.call-done = f32[1,97,1280]{1,2,0:T(8,128)} async-done(((f32[4,97,1280]{1,2,0:T(8,128)}), f32[1,97,1280]{1,2,0:T(8,128)}) %reduce-scatter.2.cloned.1.call-update) | async-done | bytes 496656 | tf_op jit(solution)/shard_map/reduce_scatter | solution.py:167
  142.7 1.5 slice_reduce_fusion
  144.2 3.1 %fusion.35 = bf16[96,1280]{0,1:T(8,128)(2,1)} fusion(f32[384,1280]{0,1:T(8,128)} %get-tuple-element.3, s32[]{:T(128)S(6)} %select_n.266, f32[1,97,1280]{1,2,0:T(8,128)} %reduce-scatter.2.cloned.1.call-done, f32[384,1280]{0,1:T(8,128)} %add_divide_fusion, f32[96]{0:T(128)S(1)} %dynamic-slice, bf16[96,2,4,160]{0,3,2,1:T(8,128)(2,1)S(1)} %copy-done.11, ...), kind=kLoop, calls=%fused_computation.60 | loop fusion | flops 1843200 | bytes 2227588 | tf_op jit(solution)/shard_map/convert_element_type | solution.py:177
  (99 shorter events, 28.4 us)
Async XLA Ops:
  7.2 62.3 %copy-start = (bf16[96,27,384]{2,0,1:T(8,128)(2,1)S(1)}, bf16[96,27,384]{2,0,1:T(8,128)(2,1)}, u32[]{:S(2)}) copy-start(bf16[96,27,384]{2,0,1:T(8,128)(2,1)} %param.7) | copy-start | bytes 5971972
  7.2 135.5 %reduce-scatter.2.cloned.1.call-start = ((), (), s32[]{:S(2)}) async-start(), calls=%async_computation.1 | async-start | bytes 3276800 | tf_op jit(solution)/shard_map/reduce_scatter | solution.py:167
  7.2 24.1 %collective-permute-start.1 = (bf16[96,2,4,160]{0,3,2,1:T(8,128)(2,1)}, bf16[96,2,4,160]{0,3,2,1:T(8,128)(2,1)S(1)}, u32[]{:S(2)}, u32[]{:S(2)}) collective-permute-start(bf16[96,2,4,160]{0,3,2,1:T(8,128)(2,1)} %param.5), channel_id=1, source_target_pairs={{0,2},{1,3},{2,0},{3,1},{4,6},{5,7},{6,4},{7,5},{8,10},{9,11},{10,... | collective-permute-start | bytes 737288 | tf_op jit(solution)/shard_map/ppermute | solution.py:34
  9.6 27.8 %collective-permute-start.2 = (bf16[96,2,4,160]{0,3,2,1:T(8,128)(2,1)}, bf16[96,2,4,160]{0,3,2,1:T(8,128)(2,1)S(1)}, u32[]{:S(2)}, u32[]{:S(2)}) collective-permute-start(bf16[96,2,4,160]{0,3,2,1:T(8,128)(2,1)} %param.5), channel_id=1, source_target_pairs={{0,3},{1,0},{2,1},{3,2},{4,7},{5,4},{6,5},{7,6},{8,11},{9,8},{10,9... | collective-permute-start | bytes 737288 | tf_op jit(solution)/shard_map/ppermute | solution.py:34
  9.8 28.6 %collective-permute-start = (bf16[96,2,4,160]{0,3,2,1:T(8,128)(2,1)}, bf16[96,2,4,160]{0,3,2,1:T(8,128)(2,1)}, u32[]{:S(2)}, u32[]{:S(2)}) collective-permute-start(bf16[96,2,4,160]{0,3,2,1:T(8,128)(2,1)} %param.5), channel_id=1, source_target_pairs={{0,1},{1,2},{2,3},{3,0},{4,5},{5,6},{6,7},{7,4},{8,9},{9,10},{10,1... | collective-permute-start | bytes 737288 | tf_op jit(solution)/shard_map/ppermute | solution.py:34
  11.1 30.5 %collective-permute-start.3 = (bf16[96,2,4,160]{0,3,2,1:T(8,128)(2,1)}, bf16[96,2,4,160]{0,3,2,1:T(8,128)(2,1)}, u32[]{:S(2)}, u32[]{:S(2)}) collective-permute-start(bf16[96,2,4,160]{0,3,2,1:T(8,128)(2,1)} %param.6), channel_id=1, source_target_pairs={{8,0},{16,8},{24,16},{9,1},{17,9},{25,17},{10,2},{18,10},{26,18},{... | collective-permute-start | bytes 737288 | tf_op jit(solution)/shard_map/ppermute | solution.py:14
  31.3 6.0 %copy-start.15 = (bf16[96,2,4,160]{0,3,2,1:T(8,128)(2,1)}, bf16[96,2,4,160]{0,3,2,1:T(8,128)(2,1)S(1)}, u32[]{:S(2)}) copy-start(bf16[96,2,4,160]{0,3,2,1:T(8,128)(2,1)S(1)} %collective-permute-done.1) | copy-start | bytes 737284
  40.9 6.5 %copy-start.17 = (f32[384]{0:T(512)S(1)}, f32[384]{0:T(512)}, u32[]{:S(2)}) copy-start(f32[384]{0:T(512)} %param.9) | copy-start | bytes 4612
  40.9 6.5 %copy-start.18 = (f32[384]{0:T(512)S(1)}, f32[384]{0:T(512)}, u32[]{:S(2)}) copy-start(f32[384]{0:T(512)} %param.8) | copy-start | bytes 4612
  43.1 6.7 %collective-permute-start.5 = (bf16[96,4,1,160]{0,3,2,1:T(8,128)(2,1)S(1)}, bf16[96,4,1,160]{0,3,2,1:T(8,128)(2,1)S(1)}, u32[]{:S(2)}, u32[]{:S(2)}) collective-permute-start(bf16[96,4,1,160]{0,3,2,1:T(8,128)(2,1)S(1)} %get-tuple-element.16), channel_id=1, source_target_pairs={{4,0},{5,1},{6,2},{7,3},{12,8},{13,9},{14,10},{15,11},{20,16},{21,... | collective-permute-start | bytes 368648 | tf_op jit(solution)/shard_map/ppermute | solution.py:25
  46.0 3.8 %collective-permute-start.4 = (bf16[96,4,1,160]{0,3,2,1:T(8,128)(2,1)S(1)}, bf16[96,4,1,160]{0,3,2,1:T(8,128)(2,1)S(1)}, u32[]{:S(2)}, u32[]{:S(2)}) collective-permute-start(bf16[96,4,1,160]{0,3,2,1:T(8,128)(2,1)S(1)} %get-tuple-element.15), channel_id=1, source_target_pairs={{0,4},{1,5},{2,6},{3,7},{8,12},{9,13},{10,14},{11,15},{16,20},{17,... | collective-permute-start | bytes 368648 | tf_op jit(solution)/shard_map/ppermute | solution.py:24
  65.8 3.2 %copy-start.3 = (f32[1296,384]{1,0:T(8,128)}, f32[1296,384]{1,0:T(8,128)S(1)}, u32[]{:S(2)}) copy-start(f32[1296,384]{1,0:T(8,128)S(1)} %get-tuple-element.4) | copy-start | bytes 5971972
  65.8 3.2 %copy-start.5 = (f32[1296,384]{1,0:T(8,128)}, f32[1296,384]{1,0:T(8,128)S(1)}, u32[]{:S(2)}) copy-start(f32[1296,384]{1,0:T(8,128)S(1)} %get-tuple-element.5) | copy-start | bytes 5971972
  65.8 3.7 %copy-start.14 = (bf16[96,4,6,1,8,21]{0,4,5,2,1,3:T(8,128)(2,1)S(1)}, bf16[96,4,6,1,8,21]{0,4,5,2,1,3:T(8,128)(2,1)}, u32[]{:S(2)}) copy-start(bf16[96,4,6,1,8,21]{0,4,5,2,1,3:T(8,128)(2,1)} %copy-done.13) | copy-start | bytes 2322436
  65.8 3.7 %copy-start.19 = (pred[8,21]{0,1:T(8,128)(4,1)S(1)}, pred[8,21]{0,1:T(8,128)(4,1)}, u32[]{:S(2)}) copy-start(pred[8,21]{0,1:T(8,128)(4,1)} %constant.127) | copy-start | bytes 508
  66.9 17.5 %collective-permute-start.12 = (f32[648,384]{1,0:T(8,128)}, f32[648,384]{1,0:T(8,128)}, u32[]{:S(2)}, u32[]{:S(2)}) collective-permute-start(f32[648,384]{1,0:T(8,128)} %constant_dynamic-slice_fusion.2), channel_id=1, source_target_pairs={{0,4},{4,0},{1,5},{5,1},{2,6},{6,2},{3,7},{7,3},{8,12},{12,8},{9,1... | collective-permute-start | bytes 2985992 | tf_op jit(solution)/shard_map/ppermute | solution.py:86
  69.1 18.5 %collective-permute-start.6 = (f32[648,384]{1,0:T(8,128)}, f32[648,384]{1,0:T(8,128)}, u32[]{:S(2)}, u32[]{:S(2)}) collective-permute-start(f32[648,384]{1,0:T(8,128)} %constant_dynamic-slice_fusion.5), channel_id=1, source_target_pairs={{0,4},{4,0},{1,5},{5,1},{2,6},{6,2},{3,7},{7,3},{8,12},{12,8},{9,1... | collective-permute-start | bytes 2985992 | tf_op jit(solution)/shard_map/ppermute | solution.py:86
  86.2 13.3 %collective-permute-start.13 = (f32[324,384]{1,0:T(8,128)S(1)}, f32[324,384]{1,0:T(8,128)S(1)}, u32[]{:S(2)}, u32[]{:S(2)}) collective-permute-start(f32[324,384]{1,0:T(8,128)S(1)} %constant_dynamic-slice_fusion.1), channel_id=1, source_target_pairs={{0,16},{8,24},{16,0},{24,8},{1,17},{9,25},{17,1},{25,9},{2,18},{10... | collective-permute-start | bytes 1493000 | tf_op jit(solution)/shard_map/ppermute | solution.py:86
  88.9 12.9 %collective-permute-start.7 = (f32[324,384]{1,0:T(8,128)S(1)}, f32[324,384]{1,0:T(8,128)}, u32[]{:S(2)}, u32[]{:S(2)}) collective-permute-start(f32[324,384]{1,0:T(8,128)S(1)} %constant_dynamic-slice_fusion.4), channel_id=1, source_target_pairs={{0,8},{8,0},{16,24},{24,16},{1,9},{9,1},{17,25},{25,17},{2,10},{10... | collective-permute-start | bytes 1493000 | tf_op jit(solution)/shard_map/ppermute | solution.py:86
  92.7 6.8 %copy-start.8 = (f32[648,384]{1,0:T(8,128)S(1)}, f32[648,384]{1,0:T(8,128)}, u32[]{:S(2)}) copy-start(f32[648,384]{1,0:T(8,128)} %copy-done.7) | copy-start | bytes 2985988
  99.6 7.5 %collective-permute-start.14 = (f32[162,384]{1,0:T(8,128)S(1)}, f32[162,384]{1,0:T(8,128)S(1)}, u32[]{:S(2)}, u32[]{:S(2)}) collective-permute-start(f32[162,384]{1,0:T(8,128)S(1)} %constant_dynamic-slice_fusion), channel_id=1, source_target_pairs={{0,8},{8,0},{16,24},{24,16},{1,9},{9,1},{17,25},{25,17},{2,10},{10... | collective-permute-start | bytes 746504 | tf_op jit(solution)/shard_map/ppermute | solution.py:86
  102.9 6.6 %collective-permute-start.8 = (f32[162,384]{1,0:T(8,128)S(1)}, f32[162,384]{1,0:T(8,128)S(1)}, u32[]{:S(2)}, u32[]{:S(2)}) collective-permute-start(f32[162,384]{1,0:T(8,128)S(1)} %constant_dynamic-slice_fusion.3), channel_id=1, source_target_pairs={{0,16},{8,24},{16,0},{24,8},{1,17},{9,25},{17,1},{25,9},{2,18},{10... | collective-permute-start | bytes 746504 | tf_op jit(solution)/shard_map/ppermute | solution.py:86
  107.1 6.6 %collective-permute-start.15 = (f32[162,384]{1,0:T(8,128)S(1)}, f32[162,384]{1,0:T(8,128)S(1)}, u32[]{:S(2)}, u32[]{:S(2)}) collective-permute-start(f32[162,384]{1,0:T(8,128)S(1)} %dynamic-slice_add_fusion.4), channel_id=1, source_target_pairs={{0,8},{8,0},{16,24},{24,16},{1,9},{9,1},{17,25},{25,17},{2,10},{10... | collective-permute-start | bytes 746504 | tf_op jit(solution)/shard_map/ppermute | solution.py:86
  109.6 5.8 %collective-permute-start.9 = (f32[162,384]{1,0:T(8,128)S(1)}, f32[162,384]{1,0:T(8,128)S(1)}, u32[]{:S(2)}, u32[]{:S(2)}) collective-permute-start(f32[162,384]{1,0:T(8,128)S(1)} %dynamic-slice_add_fusion.5), channel_id=1, source_target_pairs={{0,16},{8,24},{16,0},{24,8},{1,17},{9,25},{17,1},{25,9},{2,18},{10... | collective-permute-start | bytes 746504 | tf_op jit(solution)/shard_map/ppermute | solution.py:86
  113.8 13.7 %collective-permute-start.16 = (f32[324,384]{1,0:T(8,128)S(1)}, f32[324,384]{1,0:T(8,128)}, u32[]{:S(2)}, u32[]{:S(2)}) collective-permute-start(f32[324,384]{1,0:T(8,128)S(1)} %maximum_select_fusion.5), channel_id=1, source_target_pairs={{0,16},{8,24},{16,0},{24,8},{1,17},{9,25},{17,1},{25,9},{2,18},{10... | collective-permute-start | bytes 1493000 | tf_op jit(solution)/shard_map/ppermute | solution.py:86
  115.5 16.9 %copy-start.2 = (f32[384,1280]{0,1:T(8,128)S(1)}, f32[384,1280]{0,1:T(8,128)}, u32[]{:S(2)}) copy-start(f32[384,1280]{0,1:T(8,128)} %get-tuple-element.3) | copy-start | bytes 5898244
  115.5 15.5 %collective-permute-start.10 = (f32[324,384]{1,0:T(8,128)S(1)}, f32[324,384]{1,0:T(8,128)}, u32[]{:S(2)}, u32[]{:S(2)}) collective-permute-start(f32[324,384]{1,0:T(8,128)S(1)} %maximum_select_fusion.4), channel_id=1, source_target_pairs={{0,8},{8,0},{16,24},{24,16},{1,9},{9,1},{17,25},{25,17},{2,10},{10... | collective-permute-start | bytes 1493000 | tf_op jit(solution)/shard_map/ppermute | solution.py:86
  129.1 5.1 %collective-permute-start.17 = (f32[648,384]{1,0:T(8,128)S(1)}, f32[648,384]{1,0:T(8,128)}, u32[]{:S(2)}, u32[]{:S(2)}) collective-permute-start(f32[648,384]{1,0:T(8,128)S(1)} %maximum_select_fusion.3), channel_id=1, source_target_pairs={{0,4},{4,0},{1,5},{5,1},{2,6},{6,2},{3,7},{7,3},{8,12},{12,8},{9,1... | collective-permute-start | bytes 2985992 | tf_op jit(solution)/shard_map/ppermute | solution.py:86
  132.3 3.7 %collective-permute-start.11 = (f32[648,384]{1,0:T(8,128)S(1)}, f32[648,384]{1,0:T(8,128)S(1)}, u32[]{:S(2)}, u32[]{:S(2)}) collective-permute-start(f32[648,384]{1,0:T(8,128)S(1)} %maximum_select_fusion.2), channel_id=1, source_target_pairs={{0,4},{4,0},{1,5},{5,1},{2,6},{6,2},{3,7},{7,3},{8,12},{12,8},{9,1... | collective-permute-start | bytes 2985992 | tf_op jit(solution)/shard_map/ppermute | solution.py:86
  136.2 8.0 %copy-start.11 = (bf16[96,2,4,160]{0,3,2,1:T(8,128)(2,1)S(1)}, bf16[96,2,4,160]{0,3,2,1:T(8,128)(2,1)}, u32[]{:S(2)}) copy-start(bf16[96,2,4,160]{0,3,2,1:T(8,128)(2,1)} %param.5) | copy-start | bytes 737284
  136.2 8.0 %copy-start.12 = (bf16[96,2,4,160]{0,3,2,1:T(8,128)(2,1)S(1)}, bf16[96,2,4,160]{0,3,2,1:T(8,128)(2,1)}, u32[]{:S(2)}) copy-start(bf16[96,2,4,160]{0,3,2,1:T(8,128)(2,1)} %param.6) | copy-start | bytes 737284
  136.2 11.1 %copy-start.1 = (bf16[96,27,384]{2,0,1:T(8,128)(2,1)S(1)}, bf16[96,27,384]{2,0,1:T(8,128)(2,1)}, u32[]{:S(2)}) copy-start(bf16[96,27,384]{2,0,1:T(8,128)(2,1)} %param.7) | copy-start | bytes 5971972
  (7 other events, 14.2 us)
Sparse Core Ops, SparseCore 0:
  92.8 49.8 reduce-scatter.1

commit v5 on v4

--- a/solution.py
+++ b/solution.py
@@ -39,34 +39,46 @@
     )
 
 
-def weight_taps(shifted, active_t, frames, rows):
+def tap_kernel(shifted, active_t, weight_t, frames, rows):
     _, _, _, cols, outs = shifted.shape
     cells, ins = active_t.shape
 
-    def body(cot_ref, act_ref, out_ref):
+    def body(cot_ref, act_ref, w_ref, wg_ref, ag_ref):
         act = act_ref[...]
         for kt in range(3):
             for kh in range(3):
                 for kw in range(3):
+                    k = 9 * kt + 3 * kh + kw
                     piece = cot_ref[kw, 2 - kt : 2 - kt + frames, 2 - kh : 2 - kh + rows]
-                    out_ref[9 * kt + 3 * kh + kw] = lax.dot_general(
-                        piece.reshape(cells, outs),
-                        act,
-                        (((0,), (0,)), ((), ())),
+                    piece = piece.reshape(cells, outs)
+                    wg_ref[k] = lax.dot_general(
+                        piece, act, (((0,), (0,)), ((), ())),
                         preferred_element_type=jnp.float32,
                     )
+                    term = jnp.dot(piece, w_ref[k], preferred_element_type=jnp.float32)
+                    if k == 0:
+                        ag_ref[...] = term
+                    else:
+                        ag_ref[...] += term
 
     return pl.pallas_call(
         body,
-        out_shape=jax.ShapeDtypeStruct((27, outs, ins), jnp.float32),
-        in_specs=[pl.BlockSpec(memory_space=pltpu.VMEM)] * 2,
-        out_specs=pl.BlockSpec(memory_space=pltpu.VMEM),
+        out_shape=(
+            jax.ShapeDtypeStruct((27, outs, ins), jnp.float32),
+            jax.ShapeDtypeStruct((cells, ins), jnp.float32),
+        ),
+        in_specs=[pl.BlockSpec(memory_space=pltpu.VMEM)] * 3,
+        out_specs=(
+            pl.BlockSpec(memory_space=pltpu.VMEM),
+            pl.BlockSpec(memory_space=pltpu.VMEM),
+        ),
         cost_estimate=pl.CostEstimate(
-            flops=2 * 27 * ins * cells * outs,
-            bytes_accessed=shifted.size * 2 + active_t.size * 2 + 27 * ins * outs * 4,
+            flops=4 * 27 * ins * cells * outs,
+            bytes_accessed=shifted.size * 2 + active_t.size * 2 + weight_t.size * 2
+            + 27 * ins * outs * 4 + cells * ins * 4,
             transcendentals=0,
         ),
-    )(shifted, active_t)
+    )(shifted, active_t, weight_t)
 
 
 def halving_steps(axes):
@@ -134,25 +146,13 @@
         [cells_major[:, :, 2 - kw : 2 - kw + cols] for kw in range(3)], axis=0
     )
     active_t = jnp.transpose(active.reshape(total, cells))
-    local_sums = weight_taps(shifted, active_t, frames, rows)
+    weight_t = jnp.transpose(conv_weight, (1, 0, 2))
+    local_sums, act_part = tap_kernel(shifted, active_t, weight_t, frames, rows)
+    partial = jnp.transpose(act_part)
     summed = group_sum(local_sums.reshape(27 * chans, total), ("height",), ("tm",))
     weight_grad = jnp.transpose(
         (summed / math.sqrt(positions)).reshape(27, chans, total), (1, 0, 2)
     )
-
-    kernel = conv_weight.reshape(chans, 3, 3, 3, total)
-    kernel = lax.rev(kernel, (1, 2, 3))
-    adn = lax.ConvDimensionNumbers(
-        lhs_spec=(0, 1, 2, 3, 4), rhs_spec=(4, 0, 1, 2, 3), out_spec=(0, 1, 2, 3, 4)
-    )
-    partial = lax.conv_general_dilated(
-        padded[None],
-        kernel,
-        window_strides=(1, 1, 1),
-        padding="VALID",
-        dimension_numbers=adn,
-        preferred_element_type=jnp.float32,
-    )[0].reshape(total, cells)
 
     sig = jax.nn.sigmoid(normed)
     slope = sig * (1.0 + normed * (1.0 - sig)) * norm_gain[:, None]

time: 157 us -> 155 us (0.987)
  Pallas kernels: 8.27 us -> 16.6 us
  local copies, waits for them, and re-layouts: 21.9 us -> 14.9 us
  matrix products: 4.32 us -> 0 us
  waiting for transfers between devices: 55 us -> 58.6 us
  other arithmetic: 28.7 us -> 26.4 us
    pallas_call x1, Pallas kernels: 8.27 us -> 16.6 us  [tap_kernel(): pl.pallas_call(body, out_shape=(jax.ShapeDtypeStruct((27, outs, ins), jnp...]
    another operation x2 -> x0, local copies, waits for them, and re-layouts: 5.92 us -> none  [on_device(): partial.reshape(n_chan, chans, cells)]
    conv_general_dilated x1 -> x0, matrix products: 4.32 us -> none  [on_device(): lax.conv_general_dilated(padded[None], kernel, window_strides=(1, 1, 1),...]
    unnamed x43 -> x31, local copies, waits for them, and re-layouts: 6.11 us -> 1.99 us
    select_n x6, other arithmetic: 5.03 us -> 2.33 us  [halving_sum(): lax.select_n(bit, jnp.concatenate([x, got], axis=0), jnp.concatenate([got...]
    ppermute x3, waiting for transfers between devices: 23.4 us -> 25.6 us  [gather_blocks(): lax.ppermute(block, axis, [(j, (j + d) % size) for j in range(size)])]
    reduce_sum x1, other arithmetic: 2.13 us -> 4.41 us  [on_device(): part_dots = jnp.sum(partial * slope * flat_x, axis=0, keepdims=True)]
    transpose x1 -> x0, other arithmetic: 2.25 us -> none  [on_device(): active_t = jnp.transpose(active.reshape(total, cells))]
  transfers between devices with their start and end apart: 19 -> 19, of which waited for: 11 -> 13; matrix products, arithmetic and copies ran while one was open for 25% -> 19% of each run, Pallas kernels for 0% -> 0%
where the time goes in v5:
time: 155 us; the launch traced here: 152 us
  waiting for transfers between devices  58.6 us (38%)
  other arithmetic  26.4 us (17%)
  starting transfers between devices  21 us (14%)
  Pallas kernels  16.6 us (11%)
  local copies, waits for them, and re-layouts  14.9 us (10%)
  between operations  14.4 us (9%)
    ppermute x12, waiting for transfers between devices, exchange(): return lax.ppermute(block, axis, [(i, i ^ level) for i in range(size)])  28.4 us
    ppermute x3, waiting for transfers between devices, gather_blocks(): lax.ppermute(block, axis, [(j, (j + d) % size) for j in range(size)])  25.6 us
    pallas_call x1, Pallas kernels, tap_kernel(): pl.pallas_call(body, out_shape=(jax.ShapeDtypeStruct((27, outs, ins), jnp...  16.6 us
    ppermute x12, starting transfers between devices, exchange(): return lax.ppermute(block, axis, [(i, i ^ level) for i in range(size)])  11.5 us
    add x6, other arithmetic, halving_sum(): x = keep + exchange(send, axis, level)  5.09 us
    reduce_scatter x1, waiting for transfers between devices, on_device(): mine = lax.psum_scatter(packed, 'chan', scatter_dimension=0, tiled=True)[0]  4.53 us
    reduce_sum x1, other arithmetic, on_device(): part_dots = jnp.sum(partial * slope * flat_x, axis=0, keepdims=True)  4.41 us
    dynamic_slice x6, local copies, waits for them, and re-layouts, halving_sum(): send = lax.dynamic_slice_in_dim(x, (1 - bit) * m, m, 0)  4.08 us
  transfers between devices with their start and end apart: 19, of which 13 were waited for; matrix products, arithmetic and copies ran while one was open for 19% of the time, Pallas kernels for 0%

profile of v5, /device:TPU:9, one launch (start us, length us, event | category | flops | bytes accessed | tf_op | source)
XLA Modules:
  0.0 151.9 jit_solution(16051677401040831373)
XLA Ops:
  7.2 1.3 collective-permute-start
  9.7 1.4 collective-permute-start.2
  13.4 2.6 %collective-permute-done = bf16[96,2,4,160]{0,3,2,1:T(8,128)(2,1)S(1)} collective-permute-done((bf16[96,2,4,160]{0,3,2,1:T(8,128)(2,1)}, bf16[96,2,4,160]{0,3,2,1:T(8,128)(2,1)S(1)}, u32[]{:S(2)}, u32[]{:S(2)}) %collective-permute-start) | collective-permute-done | bytes 245792 | tf_op jit(solution)/shard_map/ppermute | solution.py:34
  16.1 20.3 %collective-permute-done.1 = bf16[96,2,4,160]{0,3,2,1:T(8,128)(2,1)S(1)} collective-permute-done((bf16[96,2,4,160]{0,3,2,1:T(8,128)(2,1)}, bf16[96,2,4,160]{0,3,2,1:T(8,128)(2,1)S(1)}, u32[]{:S(2)}, u32[]{:S(2)}) %collective-permute-start.1) | collective-permute-done | bytes 245792 | tf_op jit(solution)/shard_map/ppermute | solution.py:34
  36.3 2.7 %collective-permute-done.2 = bf16[96,2,4,160]{0,3,2,1:T(8,128)(2,1)S(1)} collective-permute-done((bf16[96,2,4,160]{0,3,2,1:T(8,128)(2,1)}, bf16[96,2,4,160]{0,3,2,1:T(8,128)(2,1)S(1)}, u32[]{:S(2)}, u32[]{:S(2)}) %collective-permute-start.2) | collective-permute-done | bytes 245792 | tf_op jit(solution)/shard_map/ppermute | solution.py:34
  41.5 1.3 collective-permute-start.4
  42.8 3.0 %collective-permute-start.5 = (bf16[96,4,1,160]{0,3,2,1:T(8,128)(2,1)S(1)}, bf16[96,4,1,160]{0,3,2,1:T(8,128)(2,1)S(1)}, u32[]{:S(2)}, u32[]{:S(2)}) collective-permute-start(bf16[96,4,1,160]{0,3,2,1:T(8,128)(2,1)S(1)} %get-tuple-element.18), channel_id=1, source_target_pairs={{4,0},{5,1},{6,2},{7,3},{12,8},{13,9},{14,10},{15,11},{20,16},{21,... | collective-permute-start | bytes 368648 | tf_op jit(solution)/shard_map/ppermute | solution.py:25
  45.8 2.1 %fusion.10 = bf16[384,1280]{0,1:T(8,128)(2,1)} fusion(f32[384]{0:T(512)S(1)} %copy-done.13, f32[384]{0:T(512)S(1)} %copy-done.14, f32[1280]{0:T(1024)S(1)} %rsqrt.15, bf16[96,2,4,160]{0,3,2,1:T(8,128)(2,1)S(1)} %get-tuple-element.11, bf16[96,2,4,160]{0,3,2,1:T(8,128)(2,1)S(1)} %get-tuple-element.12, bf16[96,2,4,160]{0,3,2,1:T(8,128)(2,1)S(1)} %get-tuple-element.13, ...), kind=kLoop, calls=%fused_computation.20 | loop fusion | flops 7864320 | bytes 1974272 | tf_op jit(solution)/shard_map/convert_element_type | solution.py:136
  49.0 2.4 %pad_maximum_fusion.cot_ref = bf16[3,4,6,160,96]{4,3,2,1,0:T(8,128)(2,1)} fusion(bf16[1,4,6,160,96]{4,3,2,1,0:T(8,128)(2,1)S(1)} %get-tuple-element.15, bf16[1,4,6,160,96]{4,3,2,1,0:T(8,128)(2,1)S(1)} %get-tuple-element.16, bf16[1,4,6,160,96]{4,3,2,1,0:T(8,128)(2,1)S(1)} %get-tuple-element.14), kind=kLoop, calls=%fused_computation.3 | loop fusion | flops 2211840 | bytes 4423680 | tf_op jit(solution)/shard_map/stack | solution.py:145
  51.4 16.6 %shard_map.68 = (f32[27,96,384]{2,1,0:T(8,128)}, f32[1280,384]{1,0:T(8,128)}) custom-call(bf16[3,4,6,160,96]{4,3,2,1,0:T(8,128)(2,1)} %pad_maximum_fusion.cot_ref, bf16[1280,384]{1,0:T(8,128)(2,1)} %bitcast.74, bf16[27,96,384]{2,1,0:T(8,128)(2,1)} %bitcast.76), custom_call_target="tpu_custom_call" | custom-call | flops 5096079360 | bytes 11132928 | tf_op jit(solution)/shard_map/pallas_call | solution.py:64
  68.0 2.4 %fusion.29 = (f32[1296,384]{1,0:T(8,128)S(1)}, f32[1296,384]{1,0:T(8,128)S(1)}) fusion(f32[2592,384]{1,0:T(8,128)} %bitcast.73), kind=kLoop, calls=%fused_computation.69 | loop fusion | bytes 7962624 | tf_op jit(solution)/shard_map/slice | solution.py:122
  73.4 1.8 %copy.7 = f32[384,1280]{1,0:T(8,128)} copy(f32[384,1280]{0,1:T(8,128)S(1)} %bitcast.70) | data formatting | bytes 3932160 | tf_op jit(solution)/shard_map/transpose | solution.py:151
  75.2 2.0 %copy.8 = f32[4,96,1280]{1,2,0:T(8,128)S(1)} copy(f32[4,96,1280]{2,1,0:T(8,128)} %bitcast.71) | data formatting | bytes 3932160 | tf_op jit(solution)/shard_map/reshape | solution.py:162
  77.3 4.4 %fusion.14 = (f32[1280]{0:T(1024)S(1)}, f32[384,1280]{0,1:T(8,128)}) fusion(f32[1280,384]{1,0:T(8,128)} %get-tuple-element.4, bf16[96,2,4,160]{0,3,2,1:T(8,128)(2,1)S(1)} %get-tuple-element.11, bf16[96,2,4,160]{0,3,2,1:T(8,128)(2,1)} %copy-done.5, bf16[96,2,4,160]{0,3,2,1:T(8,128)(2,1)} %copy-done.6, bf16[96,2,4,160]{0,3,2,1:T(8,128)(2,1)S(1)} %get-tuple-element.10, ...), kind=kLoop, calls=%fused_computation.24 | loop fusion | flops 10812160 | bytes 4928512 | tf_op jit(solution)/shard_map/reduce_sum | solution.py:159
  81.7 1.5 dynamic-slice_add_fusion.1
  85.4 1.3 dynamic-slice_add_fusion
  89.1 2.2 %pad_maximum_fusion.1 = f32[4,97,1280]{1,2,0:T(8,128)} fusion(f32[4,1,1280]{1,2,0:T(8,128)S(1)} %broadcast_in_dim.2, f32[4,96,1280]{1,2,0:T(8,128)S(1)} %copy.8), kind=kLoop, calls=%fused_computation.4 | loop fusion | flops 496640 | bytes 3973120 | tf_op jit(solution)/shard_map/concatenate | solution.py:160
  91.4 6.1 %collective-permute-done.7 = f32[324,384]{1,0:T(8,128)} collective-permute-done((f32[324,384]{1,0:T(8,128)}, f32[324,384]{1,0:T(8,128)}, u32[]{:S(2)}, u32[]{:S(2)}) %collective-permute-start.7) | collective-permute-done | bytes 497696 | tf_op jit(solution)/shard_map/ppermute | solution.py:98
  98.6 1.3 collective-permute-start.8
  102.3 3.2 %collective-permute-done.8 = f32[162,384]{1,0:T(8,128)S(1)} collective-permute-done((f32[162,384]{1,0:T(8,128)S(1)}, f32[162,384]{1,0:T(8,128)S(1)}, u32[]{:S(2)}, u32[]{:S(2)}) %collective-permute-start.8) | collective-permute-done | bytes 248864 | tf_op jit(solution)/shard_map/ppermute | solution.py:98
  105.6 1.3 collective-permute-start.9
  106.9 1.4 collective-permute-done.14
  109.0 2.7 %collective-permute-done.9 = f32[162,384]{1,0:T(8,128)S(1)} collective-permute-done((f32[162,384]{1,0:T(8,128)S(1)}, f32[162,384]{1,0:T(8,128)S(1)}, u32[]{:S(2)}, u32[]{:S(2)}) %collective-permute-start.9) | collective-permute-done | bytes 248864 | tf_op jit(solution)/shard_map/ppermute | solution.py:98
  115.5 9.9 %collective-permute-done.10 = f32[324,384]{1,0:T(8,128)S(1)} collective-permute-done((f32[324,384]{1,0:T(8,128)S(1)}, f32[324,384]{1,0:T(8,128)S(1)}, u32[]{:S(2)}, u32[]{:S(2)}) %collective-permute-start.10) | collective-permute-done | bytes 497696 | tf_op jit(solution)/shard_map/ppermute | solution.py:98
  125.6 2.5 %collective-permute-start.11 = (f32[648,384]{1,0:T(8,128)S(1)}, f32[648,384]{1,0:T(8,128)S(1)}, u32[]{:S(2)}, u32[]{:S(2)}) collective-permute-start(f32[648,384]{1,0:T(8,128)S(1)} %maximum_select_fusion.2), channel_id=1, source_target_pairs={{0,4},{4,0},{1,5},{5,1},{2,6},{6,2},{3,7},{7,3},{8,12},{12,8},{9,1... | collective-permute-start | bytes 2985992 | tf_op jit(solution)/shard_map/ppermute | solution.py:98
  128.6 1.8 %collective-permute-done.11 = f32[648,384]{1,0:T(8,128)S(1)} collective-permute-done((f32[648,384]{1,0:T(8,128)S(1)}, f32[648,384]{1,0:T(8,128)S(1)}, u32[]{:S(2)}, u32[]{:S(2)}) %collective-permute-start.11) | collective-permute-done | bytes 995360 | tf_op jit(solution)/shard_map/ppermute | solution.py:98
  130.4 1.4 collective-permute-done.17
  131.9 1.8 %maximum_select_fusion.1 = f32[1296,384]{1,0:T(8,128)S(1)} fusion(f32[648,384]{1,0:T(8,128)} %collective-permute-done.17, f32[648,384]{1,0:T(8,128)S(1)} %maximum_select_fusion.3, pred[]{:T(512)S(6)} %select_n.268), kind=kLoop, calls=%fused_computation.7 | loop fusion | flops 1492992 | bytes 3981313 | tf_op jit(solution)/shard_map/select_n | solution.py:109
  133.7 2.3 %maximum_multiply_fusion = f32[2592,384]{1,0:T(8,128)} fusion(f32[1296,384]{1,0:T(8,128)S(1)} %maximum_select_fusion.1, f32[1296,384]{1,0:T(8,128)S(1)} %maximum_select_fusion), kind=kLoop, calls=%fused_computation | loop fusion | flops 1990656 | bytes 7962624 | tf_op jit(solution)/shard_map/div | solution.py:154
  135.9 4.5 %reduce-scatter.2.cloned.1.call-done = f32[1,97,1280]{1,2,0:T(8,128)} async-done(((f32[4,97,1280]{1,2,0:T(8,128)}), f32[1,97,1280]{1,2,0:T(8,128)}) %reduce-scatter.2.cloned.1.call-update) | async-done | bytes 496656 | tf_op jit(solution)/shard_map/reduce_scatter | solution.py:167
  140.5 1.5 slice_reduce_fusion
  142.0 3.0 %fusion.25 = bf16[96,1280]{0,1:T(8,128)(2,1)} fusion(f32[1,97,1280]{1,2,0:T(8,128)} %reduce-scatter.2.cloned.1.call-done, f32[384,1280]{0,1:T(8,128)} %get-tuple-element.7, s32[]{:T(128)S(6)} %select_n.266, bf16[96,2,4,160]{0,3,2,1:T(8,128)(2,1)S(1)} %copy-done.11, bf16[96,2,4,160]{0,3,2,1:T(8,128)(2,1)S(1)} %copy-done.12, f32[1280]{0:T(1024)S(1)} %slice_reduce_fusion, ...), kind=kLoop, calls=%fused_computation.45 | loop fusion | flops 1228800 | bytes 1735684 | tf_op jit(solution)/shard_map/convert_element_type | solution.py:177
  (77 shorter events, 23.1 us)
Async XLA Ops:
  7.2 133.3 %reduce-scatter.2.cloned.1.call-start = ((), (), s32[]{:S(2)}) async-start(), calls=%async_computation.1 | async-start | bytes 3276800 | tf_op jit(solution)/shard_map/reduce_scatter | solution.py:167
  7.2 8.8 %collective-permute-start = (bf16[96,2,4,160]{0,3,2,1:T(8,128)(2,1)}, bf16[96,2,4,160]{0,3,2,1:T(8,128)(2,1)S(1)}, u32[]{:S(2)}, u32[]{:S(2)}) collective-permute-start(bf16[96,2,4,160]{0,3,2,1:T(8,128)(2,1)} %param.5), channel_id=1, source_target_pairs={{0,1},{1,2},{2,3},{3,0},{4,5},{5,6},{6,7},{7,4},{8,9},{9,10},{10,1... | collective-permute-start | bytes 737288 | tf_op jit(solution)/shard_map/ppermute | solution.py:34
  8.6 27.8 %collective-permute-start.1 = (bf16[96,2,4,160]{0,3,2,1:T(8,128)(2,1)}, bf16[96,2,4,160]{0,3,2,1:T(8,128)(2,1)S(1)}, u32[]{:S(2)}, u32[]{:S(2)}) collective-permute-start(bf16[96,2,4,160]{0,3,2,1:T(8,128)(2,1)} %param.5), channel_id=1, source_target_pairs={{0,2},{1,3},{2,0},{3,1},{4,6},{5,7},{6,4},{7,5},{8,10},{9,11},{10,... | collective-permute-start | bytes 737288 | tf_op jit(solution)/shard_map/ppermute | solution.py:34
  9.7 29.4 %collective-permute-start.2 = (bf16[96,2,4,160]{0,3,2,1:T(8,128)(2,1)}, bf16[96,2,4,160]{0,3,2,1:T(8,128)(2,1)S(1)}, u32[]{:S(2)}, u32[]{:S(2)}) collective-permute-start(bf16[96,2,4,160]{0,3,2,1:T(8,128)(2,1)} %param.5), channel_id=1, source_target_pairs={{0,3},{1,0},{2,1},{3,2},{4,7},{5,4},{6,5},{7,6},{8,11},{9,8},{10,9... | collective-permute-start | bytes 737288 | tf_op jit(solution)/shard_map/ppermute | solution.py:34
  11.0 30.4 %collective-permute-start.3 = (bf16[96,2,4,160]{0,3,2,1:T(8,128)(2,1)}, bf16[96,2,4,160]{0,3,2,1:T(8,128)(2,1)S(1)}, u32[]{:S(2)}, u32[]{:S(2)}) collective-permute-start(bf16[96,2,4,160]{0,3,2,1:T(8,128)(2,1)} %param.6), channel_id=1, source_target_pairs={{8,0},{16,8},{24,16},{9,1},{17,9},{25,17},{10,2},{18,10},{26,18},{... | collective-permute-start | bytes 737288 | tf_op jit(solution)/shard_map/ppermute | solution.py:14
  40.2 7.8 %copy-start.5 = (bf16[96,2,4,160]{0,3,2,1:T(8,128)(2,1)}, bf16[96,2,4,160]{0,3,2,1:T(8,128)(2,1)S(1)}, u32[]{:S(2)}) copy-start(bf16[96,2,4,160]{0,3,2,1:T(8,128)(2,1)S(1)} %get-tuple-element.12) | copy-start | bytes 737284
  40.2 7.8 %copy-start.6 = (bf16[96,2,4,160]{0,3,2,1:T(8,128)(2,1)}, bf16[96,2,4,160]{0,3,2,1:T(8,128)(2,1)S(1)}, u32[]{:S(2)}) copy-start(bf16[96,2,4,160]{0,3,2,1:T(8,128)(2,1)S(1)} %get-tuple-element.13) | copy-start | bytes 737284
  40.2 5.6 %copy-start.13 = (f32[384]{0:T(512)S(1)}, f32[384]{0:T(512)}, u32[]{:S(2)}) copy-start(f32[384]{0:T(512)} %param.9) | copy-start | bytes 4612
  40.2 5.6 %copy-start.14 = (f32[384]{0:T(512)S(1)}, f32[384]{0:T(512)}, u32[]{:S(2)}) copy-start(f32[384]{0:T(512)} %param.8) | copy-start | bytes 4612
  41.5 6.5 %collective-permute-start.4 = (bf16[96,4,1,160]{0,3,2,1:T(8,128)(2,1)S(1)}, bf16[96,4,1,160]{0,3,2,1:T(8,128)(2,1)S(1)}, u32[]{:S(2)}, u32[]{:S(2)}) collective-permute-start(bf16[96,4,1,160]{0,3,2,1:T(8,128)(2,1)S(1)} %get-tuple-element.17), channel_id=1, source_target_pairs={{0,4},{1,5},{2,6},{3,7},{8,12},{9,13},{10,14},{11,15},{16,20},{17,... | collective-permute-start | bytes 368648 | tf_op jit(solution)/shard_map/ppermute | solution.py:24
  42.8 5.2 %collective-permute-start.5 = (bf16[96,4,1,160]{0,3,2,1:T(8,128)(2,1)S(1)}, bf16[96,4,1,160]{0,3,2,1:T(8,128)(2,1)S(1)}, u32[]{:S(2)}, u32[]{:S(2)}) collective-permute-start(bf16[96,4,1,160]{0,3,2,1:T(8,128)(2,1)S(1)} %get-tuple-element.18), channel_id=1, source_target_pairs={{4,0},{5,1},{6,2},{7,3},{12,8},{13,9},{14,10},{15,11},{20,16},{21,... | collective-permute-start | bytes 368648 | tf_op jit(solution)/shard_map/ppermute | solution.py:25
  70.4 2.7 %copy-start.2 = (f32[1296,384]{1,0:T(8,128)}, f32[1296,384]{1,0:T(8,128)S(1)}, u32[]{:S(2)}) copy-start(f32[1296,384]{1,0:T(8,128)S(1)} %get-tuple-element.8) | copy-start | bytes 5971972
  70.4 3.0 %copy-start.4 = (f32[1280,384]{1,0:T(8,128)S(1)}, f32[1280,384]{1,0:T(8,128)}, u32[]{:S(2)}) copy-start(f32[1280,384]{1,0:T(8,128)} %get-tuple-element.4) | copy-start | bytes 5898244
  71.4 10.2 %collective-permute-start.6 = (f32[648,384]{1,0:T(8,128)}, f32[648,384]{1,0:T(8,128)}, u32[]{:S(2)}, u32[]{:S(2)}) collective-permute-start(f32[648,384]{1,0:T(8,128)} %constant_dynamic-slice_fusion.5), channel_id=1, source_target_pairs={{0,4},{4,0},{1,5},{5,1},{2,6},{6,2},{3,7},{7,3},{8,12},{12,8},{9,1... | collective-permute-start | bytes 2985992 | tf_op jit(solution)/shard_map/ppermute | solution.py:98
  73.1 12.4 %collective-permute-start.12 = (f32[648,384]{1,0:T(8,128)}, f32[648,384]{1,0:T(8,128)}, u32[]{:S(2)}, u32[]{:S(2)}) collective-permute-start(f32[648,384]{1,0:T(8,128)} %constant_dynamic-slice_fusion.2), channel_id=1, source_target_pairs={{0,4},{4,0},{1,5},{5,1},{2,6},{6,2},{3,7},{7,3},{8,12},{12,8},{9,1... | collective-permute-start | bytes 2985992 | tf_op jit(solution)/shard_map/ppermute | solution.py:98
  77.3 4.4 %copy-start.3 = (f32[1296,384]{1,0:T(8,128)S(1)}, f32[1296,384]{1,0:T(8,128)}, u32[]{:S(2)}) copy-start(f32[1296,384]{1,0:T(8,128)} %copy-done.2) | copy-start | bytes 5971972
  81.7 3.7 %copy-start.1 = (f32[1296,384]{1,0:T(8,128)S(1)}, f32[1296,384]{1,0:T(8,128)}, u32[]{:S(2)}) copy-start(f32[1296,384]{1,0:T(8,128)} %copy-done) | copy-start | bytes 5971972
  83.2 3.6 %copy-start.9 = (f32[648,384]{1,0:T(8,128)}, f32[648,384]{1,0:T(8,128)S(1)}, u32[]{:S(2)}) copy-start(f32[648,384]{1,0:T(8,128)S(1)} %dynamic-slice_add_fusion.1) | copy-start | bytes 2985988
  84.2 13.3 %collective-permute-start.7 = (f32[324,384]{1,0:T(8,128)}, f32[324,384]{1,0:T(8,128)}, u32[]{:S(2)}, u32[]{:S(2)}) collective-permute-start(f32[324,384]{1,0:T(8,128)} %constant_dynamic-slice_fusion.4), channel_id=1, source_target_pairs={{0,8},{8,0},{16,24},{24,16},{1,9},{9,1},{17,25},{25,17},{2,10},{10... | collective-permute-start | bytes 1493000 | tf_op jit(solution)/shard_map/ppermute | solution.py:98
  87.7 12.9 %collective-permute-start.13 = (f32[324,384]{1,0:T(8,128)}, f32[324,384]{1,0:T(8,128)}, u32[]{:S(2)}, u32[]{:S(2)}) collective-permute-start(f32[324,384]{1,0:T(8,128)} %constant_dynamic-slice_fusion.1), channel_id=1, source_target_pairs={{0,16},{8,24},{16,0},{24,8},{1,17},{9,25},{17,1},{25,9},{2,18},{10... | collective-permute-start | bytes 1493000 | tf_op jit(solution)/shard_map/ppermute | solution.py:98
  91.4 6.1 %copy-start.10 = (f32[648,384]{1,0:T(8,128)S(1)}, f32[648,384]{1,0:T(8,128)}, u32[]{:S(2)}) copy-start(f32[648,384]{1,0:T(8,128)} %copy-done.9) | copy-start | bytes 2985988
  91.4 9.2 %copy-start.8 = (f32[648,384]{1,0:T(8,128)S(1)}, f32[648,384]{1,0:T(8,128)}, u32[]{:S(2)}) copy-start(f32[648,384]{1,0:T(8,128)} %copy-done.7) | copy-start | bytes 2985988
  98.6 6.9 %collective-permute-start.8 = (f32[162,384]{1,0:T(8,128)S(1)}, f32[162,384]{1,0:T(8,128)S(1)}, u32[]{:S(2)}, u32[]{:S(2)}) collective-permute-start(f32[162,384]{1,0:T(8,128)S(1)} %constant_dynamic-slice_fusion.3), channel_id=1, source_target_pairs={{0,16},{8,24},{16,0},{24,8},{1,17},{9,25},{17,1},{25,9},{2,18},{10... | collective-permute-start | bytes 746504 | tf_op jit(solution)/shard_map/ppermute | solution.py:98
  101.7 6.6 %collective-permute-start.14 = (f32[162,384]{1,0:T(8,128)S(1)}, f32[162,384]{1,0:T(8,128)S(1)}, u32[]{:S(2)}, u32[]{:S(2)}) collective-permute-start(f32[162,384]{1,0:T(8,128)S(1)} %constant_dynamic-slice_fusion), channel_id=1, source_target_pairs={{0,8},{8,0},{16,24},{24,16},{1,9},{9,1},{17,25},{25,17},{2,10},{10... | collective-permute-start | bytes 746504 | tf_op jit(solution)/shard_map/ppermute | solution.py:98
  105.6 6.1 %collective-permute-start.9 = (f32[162,384]{1,0:T(8,128)S(1)}, f32[162,384]{1,0:T(8,128)S(1)}, u32[]{:S(2)}, u32[]{:S(2)}) collective-permute-start(f32[162,384]{1,0:T(8,128)S(1)} %dynamic-slice_add_fusion.5), channel_id=1, source_target_pairs={{0,16},{8,24},{16,0},{24,8},{1,17},{9,25},{17,1},{25,9},{2,18},{10... | collective-permute-start | bytes 746504 | tf_op jit(solution)/shard_map/ppermute | solution.py:98
  108.4 5.8 %collective-permute-start.15 = (f32[162,384]{1,0:T(8,128)S(1)}, f32[162,384]{1,0:T(8,128)S(1)}, u32[]{:S(2)}, u32[]{:S(2)}) collective-permute-start(f32[162,384]{1,0:T(8,128)S(1)} %dynamic-slice_add_fusion.4), channel_id=1, source_target_pairs={{0,8},{8,0},{16,24},{24,16},{1,9},{9,1},{17,25},{25,17},{2,10},{10... | collective-permute-start | bytes 746504 | tf_op jit(solution)/shard_map/ppermute | solution.py:98
  111.8 13.6 %collective-permute-start.10 = (f32[324,384]{1,0:T(8,128)S(1)}, f32[324,384]{1,0:T(8,128)S(1)}, u32[]{:S(2)}, u32[]{:S(2)}) collective-permute-start(f32[324,384]{1,0:T(8,128)S(1)} %maximum_select_fusion.4), channel_id=1, source_target_pairs={{0,8},{8,0},{16,24},{24,16},{1,9},{9,1},{17,25},{25,17},{2,10},{10... | collective-permute-start | bytes 1493000 | tf_op jit(solution)/shard_map/ppermute | solution.py:98
  114.2 13.9 %collective-permute-start.16 = (f32[324,384]{1,0:T(8,128)S(1)}, f32[324,384]{1,0:T(8,128)S(1)}, u32[]{:S(2)}, u32[]{:S(2)}) collective-permute-start(f32[324,384]{1,0:T(8,128)S(1)} %maximum_select_fusion.5), channel_id=1, source_target_pairs={{0,16},{8,24},{16,0},{24,8},{1,17},{9,25},{17,1},{25,9},{2,18},{10... | collective-permute-start | bytes 1493000 | tf_op jit(solution)/shard_map/ppermute | solution.py:98
  125.6 4.7 %collective-permute-start.11 = (f32[648,384]{1,0:T(8,128)S(1)}, f32[648,384]{1,0:T(8,128)S(1)}, u32[]{:S(2)}, u32[]{:S(2)}) collective-permute-start(f32[648,384]{1,0:T(8,128)S(1)} %maximum_select_fusion.2), channel_id=1, source_target_pairs={{0,4},{4,0},{1,5},{5,1},{2,6},{6,2},{3,7},{7,3},{8,12},{12,8},{9,1... | collective-permute-start | bytes 2985992 | tf_op jit(solution)/shard_map/ppermute | solution.py:98
  128.3 3.6 %collective-permute-start.17 = (f32[648,384]{1,0:T(8,128)S(1)}, f32[648,384]{1,0:T(8,128)}, u32[]{:S(2)}, u32[]{:S(2)}) collective-permute-start(f32[648,384]{1,0:T(8,128)S(1)} %maximum_select_fusion.3), channel_id=1, source_target_pairs={{0,4},{4,0},{1,5},{5,1},{2,6},{6,2},{3,7},{7,3},{8,12},{12,8},{9,1... | collective-permute-start | bytes 2985992 | tf_op jit(solution)/shard_map/ppermute | solution.py:98
  133.6 8.4 %copy-start.11 = (bf16[96,2,4,160]{0,3,2,1:T(8,128)(2,1)S(1)}, bf16[96,2,4,160]{0,3,2,1:T(8,128)(2,1)}, u32[]{:S(2)}) copy-start(bf16[96,2,4,160]{0,3,2,1:T(8,128)(2,1)} %param.5) | copy-start | bytes 737284
  133.7 8.4 %copy-start.12 = (bf16[96,2,4,160]{0,3,2,1:T(8,128)(2,1)S(1)}, bf16[96,2,4,160]{0,3,2,1:T(8,128)(2,1)}, u32[]{:S(2)}) copy-start(bf16[96,2,4,160]{0,3,2,1:T(8,128)(2,1)} %param.6) | copy-start | bytes 737284
  (2 other events, 4.2 us)
Sparse Core Ops, SparseCore 0:
  91.5 48.9 reduce-scatter.1

commit v6 on v5

--- a/solution.py
+++ b/solution.py
@@ -39,11 +39,12 @@
     )
 
 
-def tap_kernel(shifted, active_t, weight_t, frames, rows):
+def tap_kernel(shifted, active_t, weight_t, slope_x, n_chan, frames, rows):
     _, _, _, cols, outs = shifted.shape
     cells, ins = active_t.shape
+    block = ins // n_chan
 
-    def body(cot_ref, act_ref, w_ref, wg_ref, ag_ref):
+    def body(cot_ref, act_ref, w_ref, sx_ref, wg_ref, pk_ref, ag_ref):
         act = act_ref[...]
         for kt in range(3):
             for kh in range(3):
@@ -55,30 +56,39 @@
                         piece, act, (((0,), (0,)), ((), ())),
                         preferred_element_type=jnp.float32,
                     )
-                    term = jnp.dot(piece, w_ref[k], preferred_element_type=jnp.float32)
+                    term = lax.dot_general(
+                        w_ref[k], piece, (((1,), (1,)), ((), ())),
+                        preferred_element_type=jnp.float32,
+                    )
                     if k == 0:
                         ag_ref[...] = term
                     else:
                         ag_ref[...] += term
+        ag = ag_ref[...]
+        dots = jnp.sum(ag * sx_ref[...], axis=0, keepdims=True)
+        for j in range(n_chan):
+            pk_ref[j, 0:block, :] = ag[j * block : (j + 1) * block]
+            pk_ref[j, block : block + 1, :] = dots
 
     return pl.pallas_call(
         body,
         out_shape=(
             jax.ShapeDtypeStruct((27, outs, ins), jnp.float32),
-            jax.ShapeDtypeStruct((cells, ins), jnp.float32),
+            jax.ShapeDtypeStruct((n_chan, block + 1, cells), jnp.float32),
         ),
-        in_specs=[pl.BlockSpec(memory_space=pltpu.VMEM)] * 3,
+        in_specs=[pl.BlockSpec(memory_space=pltpu.VMEM)] * 4,
         out_specs=(
             pl.BlockSpec(memory_space=pltpu.VMEM),
             pl.BlockSpec(memory_space=pltpu.VMEM),
         ),
+        scratch_shapes=[pltpu.VMEM((ins, cells), jnp.float32)],
         cost_estimate=pl.CostEstimate(
             flops=4 * 27 * ins * cells * outs,
             bytes_accessed=shifted.size * 2 + active_t.size * 2 + weight_t.size * 2
-            + 27 * ins * outs * 4 + cells * ins * 4,
+            + slope_x.size * 4 + 27 * ins * outs * 4 + (ins + n_chan) * cells * 4,
             transcendentals=0,
         ),
-    )(shifted, active_t, weight_t)
+    )(shifted, active_t, weight_t, slope_x)
 
 
 def halving_steps(axes):
@@ -146,24 +156,17 @@
         [cells_major[:, :, 2 - kw : 2 - kw + cols] for kw in range(3)], axis=0
     )
     active_t = jnp.transpose(active.reshape(total, cells))
-    weight_t = jnp.transpose(conv_weight, (1, 0, 2))
-    local_sums, act_part = tap_kernel(shifted, active_t, weight_t, frames, rows)
-    partial = jnp.transpose(act_part)
+    sig = jax.nn.sigmoid(normed)
+    slope = sig * (1.0 + normed * (1.0 - sig)) * norm_gain[:, None]
+    weight_t = jnp.transpose(conv_weight, (1, 2, 0))
+    local_sums, packed = tap_kernel(
+        shifted, active_t, weight_t, slope * flat_x, n_chan, frames, rows
+    )
     summed = group_sum(local_sums.reshape(27 * chans, total), ("height",), ("tm",))
     weight_grad = jnp.transpose(
         (summed / math.sqrt(positions)).reshape(27, chans, total), (1, 0, 2)
     )
 
-    sig = jax.nn.sigmoid(normed)
-    slope = sig * (1.0 + normed * (1.0 - sig)) * norm_gain[:, None]
-    part_dots = jnp.sum(partial * slope * flat_x, axis=0, keepdims=True)
-    packed = jnp.concatenate(
-        [
-            partial.reshape(n_chan, chans, cells),
-            jnp.broadcast_to(part_dots[None], (n_chan, 1, cells)),
-        ],
-        axis=1,
-    )
     mine = lax.psum_scatter(packed, "chan", scatter_dimension=0, tiled=True)[0]
     act_grad = mine[:chans]
     dots = mine[chans:]

time: 155 us -> 148 us (0.955); the launches traced: 152 us -> 148 us
  waiting for transfers between devices: 58.6 us -> 53.2 us
    reduce_scatter x1, waiting for transfers between devices: 4.53 us -> 0.01 us  [on_device(): mine = lax.psum_scatter(packed, 'chan', scatter_dimension=0, tiled=True)[0]]
    reduce_sum x1 -> x0, other arithmetic: 4.41 us -> none  [on_device(): part_dots = jnp.sum(partial * slope * flat_x, axis=0, keepdims=True)]
    ppermute x3, waiting for transfers between devices: 25.6 us -> 21.5 us  [gather_blocks(): lax.ppermute(block, axis, [(j, (j + d) % size) for j in range(size)])]
    convert_element_type x0 -> x4, local copies, waits for them, and re-layouts: none -> 4.05 us  [the longest x1 1.91 us: on_device(): flat_x = whole_x.reshape(total, cells).astype(jnp.float32)]
    ppermute x12, waiting for transfers between devices: 28.4 us -> 31.8 us  [exchange(): return lax.ppermute(block, axis, [(i, i ^ level) for i in range(size)])]
    mul x0 -> x1, other arithmetic: none -> 2.97 us  [on_device(): slope = sig * (1.0 + normed * (1.0 - sig)) * norm_gain[:, None]]
    unnamed x31 -> x25, local copies, waits for them, and re-layouts: 1.99 us -> 4.75 us
    concatenate x1 -> x0, other arithmetic: 2.24 us -> none  [on_device(): jnp.concatenate([partial.reshape(n_chan, chans, cells), jnp.broadcast_to(...]
  transfers between devices with their start and end apart: 19 -> 19, of which waited for: 13 -> 11; matrix products, arithmetic and copies ran while one was open for 19% -> 20% of each run, Pallas kernels for 0% -> 0%
where the time goes in v6:
time: 148 us
  waiting for transfers between devices  53.2 us (36%)
  other arithmetic  25.3 us (17%)
  starting transfers between devices  20.7 us (14%)
  Pallas kernels  17.7 us (12%)
  local copies, waits for them, and re-layouts  16.3 us (11%)
  between operations  14.4 us (10%)
    ppermute x12, waiting for transfers between devices, exchange(): return lax.ppermute(block, axis, [(i, i ^ level) for i in range(size)])  31.8 us
    ppermute x3, waiting for transfers between devices, gather_blocks(): lax.ppermute(block, axis, [(j, (j + d) % size) for j in range(size)])  21.5 us
    pallas_call x1, Pallas kernels, tap_kernel(): pl.pallas_call(body, out_shape=(jax.ShapeDtypeStruct((27, outs, ins), jnp...  17.7 us
    ppermute x12, starting transfers between devices, exchange(): return lax.ppermute(block, axis, [(i, i ^ level) for i in range(size)])  10.6 us
    add x6, other arithmetic, halving_sum(): x = keep + exchange(send, axis, level)  5.19 us
    unnamed x25, local copies, waits for them, and re-layouts  4.75 us
    select_n x6, other arithmetic, halving_sum(): lax.select_n(bit, jnp.concatenate([x, got], axis=0), jnp.concatenate([got...  3.94 us
    ppermute x3, starting transfers between devices, gather_blocks(): lax.ppermute(block, axis, [(j, (j + d) % size) for j in range(size)])  3.83 us
  transfers between devices with their start and end apart: 19, of which 11 were waited for; matrix products, arithmetic and copies ran while one was open for 20% of the time, Pallas kernels for 0%

profile of v6, /device:TPU:9, one launch (start us, length us, event | category | flops | bytes accessed | tf_op | source)
XLA Modules:
  0.0 147.6 jit_solution(4816244093871871337)
XLA Ops:
  7.2 1.3 collective-permute-start
  9.6 1.4 collective-permute-start.2
  11.0 1.3 collective-permute-start.3
  12.4 4.3 %copy.14 = bf16[96,27,384]{0,2,1:T(8,128)(2,1)} copy(bf16[96,27,384]{2,0,1:T(8,128)(2,1)} %param.7) | data formatting | bytes 3981312 | tf_op args[2]
  17.7 18.6 %collective-permute-done.1 = bf16[96,2,4,160]{0,3,2,1:T(8,128)(2,1)} collective-permute-done((bf16[96,2,4,160]{0,3,2,1:T(8,128)(2,1)}, bf16[96,2,4,160]{0,3,2,1:T(8,128)(2,1)}, u32[]{:S(2)}, u32[]{:S(2)}) %collective-permute-start.1) | collective-permute-done | bytes 245792 | tf_op jit(solution)/shard_map/ppermute | solution.py:34
  36.3 2.8 %collective-permute-done.2 = bf16[96,2,4,160]{0,3,2,1:T(8,128)(2,1)} collective-permute-done((bf16[96,2,4,160]{0,3,2,1:T(8,128)(2,1)}, bf16[96,2,4,160]{0,3,2,1:T(8,128)(2,1)}, u32[]{:S(2)}, u32[]{:S(2)}) %collective-permute-start.2) | collective-permute-done | bytes 245792 | tf_op jit(solution)/shard_map/ppermute | solution.py:34
  39.2 2.1 %select_select_fusion.3 = (bf16[96,2,4,160]{0,3,2,1:T(8,128)(2,1)S(1)}, bf16[96,2,4,160]{0,3,2,1:T(8,128)(2,1)S(1)}, bf16[96,2,4,160]{0,3,2,1:T(8,128)(2,1)S(1)}...) fusion(bf16[96,2,4,160]{0,3,2,1:T(8,128)(2,1)} %collective-permute-done.1, ...), kind=kLoop, calls=%fused_computation.42 | loop fusion | flops 1597440 | bytes 2457612 | tf_op jit(solution)/shard_map/select_n | solution.py:38
  42.4 1.8 %maximum_convert_fusion = f32[384,2,4,160]{0,3,2,1:T(8,128)} fusion(bf16[96,2,4,160]{0,3,2,1:T(8,128)(2,1)S(1)} %get-tuple-element.14, bf16[96,2,4,160]{0,3,2,1:T(8,128)(2,1)S(1)} %get-tuple-element.15, bf16[96,2,4,160]{0,3,2,1:T(8,128)(2,1)S(1)} %get-tuple-element.16, bf16[96,2,4,160]{0,3,2,1:T(8,128)(2,1)S(1)} %get-tuple-element.13), kind=kLoop, calls=%fused_computation.25 | loop fusion | flops 3932160 | bytes 2949120 | tf_op jit(solution)/shard_map/convert_element_type | solution.py:143
  44.3 1.9 %copy.13 = f32[384,1280]{1,0:T(8,128)S(1)} copy(f32[384,1280]{0,1:T(8,128)} %bitcast.35) | data formatting | bytes 3932160 | tf_op jit(solution)/shard_map/convert_element_type | solution.py:143
  46.3 1.3 collective-permute-start.4
  47.6 3.7 %collective-permute-start.5 = (bf16[96,4,1,160]{0,3,2,1:T(8,128)(2,1)S(1)}, bf16[96,4,1,160]{0,3,2,1:T(8,128)(2,1)}, u32[]{:S(2)}, u32[]{:S(2)}) collective-permute-start(bf16[96,4,1,160]{0,3,2,1:T(8,128)(2,1)S(1)} %get-tuple-element.21), channel_id=1, source_target_pairs={{4,0},{5,1},{6,2},{7,3},{12,8},{13,9},{14,10},{15,11},{20,16},{21,... | collective-permute-start | bytes 368648 | tf_op jit(solution)/shard_map/ppermute | solution.py:25
  51.3 3.0 %multiply_multiply_fusion = (f32[384,1280]{1,0:T(8,128)}, bf16[1280,384]{0,1:T(8,128)(2,1)S(1)}, f32[384,1280]{1,0:T(8,128)}) fusion(f32[384,1280]{1,0:T(8,128)S(1)} %copy.13, f32[384]{0:T(512)S(1)} %copy-done.10, f32[384]{0:T(512)S(1)} %copy-done.11, f32[1280]{0:T(1024)S(1)} %rsqrt.15), kind=kLoop, calls=%fused_computation.7 | loop fusion | flops 6881280 | bytes 6889472 | tf_op jit(solution)/shard_map/mul | solution.py:160
  54.3 1.3 copy.16.act_ref
  57.6 2.3 %pad_maximum_fusion.cot_ref = bf16[3,4,6,160,96]{4,3,2,1,0:T(8,128)(2,1)} fusion(bf16[1,4,6,160,96]{4,3,2,1,0:T(8,128)(2,1)S(1)} %get-tuple-element.18, bf16[1,4,6,160,96]{4,3,2,1,0:T(8,128)(2,1)S(1)} %get-tuple-element.19, bf16[1,4,6,160,96]{4,3,2,1,0:T(8,128)(2,1)S(1)} %get-tuple-element.17), kind=kLoop, calls=%fused_computation.3 | loop fusion | flops 2211840 | bytes 4423680 | tf_op jit(solution)/shard_map/stack | solution.py:155
  59.9 17.7 %shard_map.68 = (f32[27,96,384]{2,1,0:T(8,128)}, f32[4,97,1280]{2,1,0:T(8,128)}) custom-call(bf16[3,4,6,160,96]{4,3,2,1,0:T(8,128)(2,1)} %pad_maximum_fusion.cot_ref, bf16[1280,384]{1,0:T(8,128)(2,1)} %copy.16.act_ref, bf16[27,384,96]{2,1,0:T(8,128)(2,1)} %bitcast.38, f32[384,1280]{1,0:T(8,128)} %get-tuple-element.12.sx_ref), custom_call_target="tpu_custom_call" | custom-call | flops 5096079360 | bytes 13119488 | tf_op jit(solution)/shard_map/pallas_call | solution.py:73
  77.5 2.4 %fusion.14 = (f32[1296,384]{1,0:T(8,128)S(1)}, f32[1296,384]{1,0:T(8,128)S(1)}) fusion(f32[2592,384]{1,0:T(8,128)} %bitcast.37), kind=kLoop, calls=%fused_computation.57 | loop fusion | bytes 7962624 | tf_op jit(solution)/shard_map/slice | solution.py:132
  81.7 2.3 %collective-permute-done.12 = f32[648,384]{1,0:T(8,128)} collective-permute-done((f32[648,384]{1,0:T(8,128)}, f32[648,384]{1,0:T(8,128)}, u32[]{:S(2)}, u32[]{:S(2)}) %collective-permute-start.12) | collective-permute-done | bytes 995360 | tf_op jit(solution)/shard_map/ppermute | solution.py:108
  84.0 1.6 %dynamic-slice_add_fusion = f32[648,384]{1,0:T(8,128)S(1)} fusion(f32[648,384]{1,0:T(8,128)} %collective-permute-done.12, f32[1296,384]{1,0:T(8,128)} %copy-done, s32[]{:T(128)S(6)} %select_n.277), kind=kLoop, calls=%fused_computation.20 | loop fusion | flops 248832 | bytes 2985988 | tf_op jit(solution)/shard_map/add | solution.py:116
  85.7 1.3 collective-permute-start.13
  87.0 1.3 dynamic-slice_add_fusion.1
  90.4 8.4 %collective-permute-done.13 = f32[324,384]{1,0:T(8,128)} collective-permute-done((f32[324,384]{1,0:T(8,128)S(1)}, f32[324,384]{1,0:T(8,128)}, u32[]{:S(2)}, u32[]{:S(2)}) %collective-permute-start.13) | collective-permute-done | bytes 497696 | tf_op jit(solution)/shard_map/ppermute | solution.py:108
  100.0 1.3 collective-permute-start.14
  103.7 3.5 %collective-permute-done.14 = f32[162,384]{1,0:T(8,128)S(1)} collective-permute-done((f32[162,384]{1,0:T(8,128)S(1)}, f32[162,384]{1,0:T(8,128)S(1)}, u32[]{:S(2)}, u32[]{:S(2)}) %collective-permute-start.14) | collective-permute-done | bytes 248864 | tf_op jit(solution)/shard_map/ppermute | solution.py:108
  107.2 1.3 collective-permute-start.15
  110.4 3.1 %collective-permute-done.15 = f32[162,384]{1,0:T(8,128)S(1)} collective-permute-done((f32[162,384]{1,0:T(8,128)S(1)}, f32[162,384]{1,0:T(8,128)S(1)}, u32[]{:S(2)}, u32[]{:S(2)}) %collective-permute-start.15) | collective-permute-done | bytes 248864 | tf_op jit(solution)/shard_map/ppermute | solution.py:108
  115.6 1.3 collective-permute-start.10
  116.9 10.4 %collective-permute-done.16 = f32[324,384]{1,0:T(8,128)S(1)} collective-permute-done((f32[324,384]{1,0:T(8,128)S(1)}, f32[324,384]{1,0:T(8,128)S(1)}, u32[]{:S(2)}, u32[]{:S(2)}) %collective-permute-start.16) | collective-permute-done | bytes 497696 | tf_op jit(solution)/shard_map/ppermute | solution.py:108
  127.4 2.1 %collective-permute-start.17 = (f32[648,384]{1,0:T(8,128)S(1)}, f32[648,384]{1,0:T(8,128)}, u32[]{:S(2)}, u32[]{:S(2)}) collective-permute-start(f32[648,384]{1,0:T(8,128)S(1)} %maximum_select_fusion.3), channel_id=1, source_target_pairs={{0,4},{4,0},{1,5},{5,1},{2,6},{6,2},{3,7},{7,3},{8,12},{12,8},{9,1... | collective-permute-start | bytes 2985992 | tf_op jit(solution)/shard_map/ppermute | solution.py:108
  131.9 1.7 %maximum_select_fusion.1 = f32[1296,384]{1,0:T(8,128)S(1)} fusion(f32[648,384]{1,0:T(8,128)} %collective-permute-done.17, f32[648,384]{1,0:T(8,128)S(1)} %maximum_select_fusion.3, pred[]{:T(512)S(6)} %select_n.268), kind=kLoop, calls=%fused_computation.6 | loop fusion | flops 1492992 | bytes 3981313 | tf_op jit(solution)/shard_map/select_n | solution.py:119
  133.6 1.8 %maximum_select_fusion = f32[1296,384]{1,0:T(8,128)S(1)} fusion(f32[648,384]{1,0:T(8,128)} %collective-permute-done.11, f32[648,384]{1,0:T(8,128)S(1)} %maximum_select_fusion.2, pred[]{:T(512)S(6)} %select_n.268), kind=kLoop, calls=%fused_computation.5 | loop fusion | flops 1492992 | bytes 3981313 | tf_op jit(solution)/shard_map/select_n | solution.py:119
  135.4 2.3 %maximum_multiply_fusion = f32[2592,384]{1,0:T(8,128)} fusion(f32[1296,384]{1,0:T(8,128)S(1)} %maximum_select_fusion.1, f32[1296,384]{1,0:T(8,128)S(1)} %maximum_select_fusion), kind=kLoop, calls=%fused_computation | loop fusion | flops 1990656 | bytes 7962624 | tf_op jit(solution)/shard_map/div | solution.py:167
  138.5 1.4 fusion.12
  (73 shorter events, 20.9 us)
Async XLA Ops:
  7.2 130.5 %reduce-scatter.2.cloned.1.call-start = ((), (), s32[]{:S(2)}) async-start(), calls=%async_computation.1 | async-start | bytes 2662400 | tf_op jit(solution)/shard_map/reduce_scatter | solution.py:170
  7.2 10.5 %collective-permute-start = (bf16[96,2,4,160]{0,3,2,1:T(8,128)(2,1)}, bf16[96,2,4,160]{0,3,2,1:T(8,128)(2,1)S(1)}, u32[]{:S(2)}, u32[]{:S(2)}) collective-permute-start(bf16[96,2,4,160]{0,3,2,1:T(8,128)(2,1)} %param.5), channel_id=1, source_target_pairs={{0,1},{1,2},{2,3},{3,0},{4,5},{5,6},{6,7},{7,4},{8,9},{9,10},{10,1... | collective-permute-start | bytes 737288 | tf_op jit(solution)/shard_map/ppermute | solution.py:34
  8.6 27.8 %collective-permute-start.1 = (bf16[96,2,4,160]{0,3,2,1:T(8,128)(2,1)}, bf16[96,2,4,160]{0,3,2,1:T(8,128)(2,1)}, u32[]{:S(2)}, u32[]{:S(2)}) collective-permute-start(bf16[96,2,4,160]{0,3,2,1:T(8,128)(2,1)} %param.5), channel_id=1, source_target_pairs={{0,2},{1,3},{2,0},{3,1},{4,6},{5,7},{6,4},{7,5},{8,10},{9,11},{10,... | collective-permute-start | bytes 737288 | tf_op jit(solution)/shard_map/ppermute | solution.py:34
  9.6 29.5 %collective-permute-start.2 = (bf16[96,2,4,160]{0,3,2,1:T(8,128)(2,1)}, bf16[96,2,4,160]{0,3,2,1:T(8,128)(2,1)}, u32[]{:S(2)}, u32[]{:S(2)}) collective-permute-start(bf16[96,2,4,160]{0,3,2,1:T(8,128)(2,1)} %param.5), channel_id=1, source_target_pairs={{0,3},{1,0},{2,1},{3,2},{4,7},{5,4},{6,5},{7,6},{8,11},{9,8},{10,9... | collective-permute-start | bytes 737288 | tf_op jit(solution)/shard_map/ppermute | solution.py:34
  11.0 35.2 %collective-permute-start.3 = (bf16[96,2,4,160]{0,3,2,1:T(8,128)(2,1)}, bf16[96,2,4,160]{0,3,2,1:T(8,128)(2,1)S(1)}, u32[]{:S(2)}, u32[]{:S(2)}) collective-permute-start(bf16[96,2,4,160]{0,3,2,1:T(8,128)(2,1)} %param.6), channel_id=1, source_target_pairs={{8,0},{16,8},{24,16},{9,1},{17,9},{25,17},{10,2},{18,10},{26,18},{... | collective-permute-start | bytes 737288 | tf_op jit(solution)/shard_map/ppermute | solution.py:14
  12.4 4.3 %copy-start.8 = (bf16[96,2,4,160]{0,3,2,1:T(8,128)(2,1)S(1)}, bf16[96,2,4,160]{0,3,2,1:T(8,128)(2,1)}, u32[]{:S(2)}) copy-start(bf16[96,2,4,160]{0,3,2,1:T(8,128)(2,1)} %param.6) | copy-start | bytes 737284
  12.4 26.7 %copy-start.9 = (bf16[96,2,4,160]{0,3,2,1:T(8,128)(2,1)S(1)}, bf16[96,2,4,160]{0,3,2,1:T(8,128)(2,1)}, u32[]{:S(2)}) copy-start(bf16[96,2,4,160]{0,3,2,1:T(8,128)(2,1)} %param.5) | copy-start | bytes 737284
  44.3 7.1 %copy-start.10 = (f32[384]{0:T(512)S(1)}, f32[384]{0:T(512)}, u32[]{:S(2)}) copy-start(f32[384]{0:T(512)} %param.9) | copy-start | bytes 4612
  44.3 7.1 %copy-start.11 = (f32[384]{0:T(512)S(1)}, f32[384]{0:T(512)}, u32[]{:S(2)}) copy-start(f32[384]{0:T(512)} %param.8) | copy-start | bytes 4612
  46.3 1.3 copy-start.4
  46.3 9.3 %collective-permute-start.4 = (bf16[96,4,1,160]{0,3,2,1:T(8,128)(2,1)S(1)}, bf16[96,4,1,160]{0,3,2,1:T(8,128)(2,1)S(1)}, u32[]{:S(2)}, u32[]{:S(2)}) collective-permute-start(bf16[96,4,1,160]{0,3,2,1:T(8,128)(2,1)S(1)} %get-tuple-element.20), channel_id=1, source_target_pairs={{0,4},{1,5},{2,6},{3,7},{8,12},{9,13},{10,14},{11,15},{16,20},{17,... | collective-permute-start | bytes 368648 | tf_op jit(solution)/shard_map/ppermute | solution.py:24
  47.6 8.0 %collective-permute-start.5 = (bf16[96,4,1,160]{0,3,2,1:T(8,128)(2,1)S(1)}, bf16[96,4,1,160]{0,3,2,1:T(8,128)(2,1)}, u32[]{:S(2)}, u32[]{:S(2)}) collective-permute-start(bf16[96,4,1,160]{0,3,2,1:T(8,128)(2,1)S(1)} %get-tuple-element.21), channel_id=1, source_target_pairs={{4,0},{5,1},{6,2},{7,3},{12,8},{13,9},{14,10},{15,11},{20,16},{21,... | collective-permute-start | bytes 368648 | tf_op jit(solution)/shard_map/ppermute | solution.py:25
  54.3 1.3 copy-start.5
  80.0 1.6 %copy-start = (f32[1296,384]{1,0:T(8,128)}, f32[1296,384]{1,0:T(8,128)S(1)}, u32[]{:S(2)}) copy-start(f32[1296,384]{1,0:T(8,128)S(1)} %get-tuple-element.9) | copy-start | bytes 5971972
  81.1 2.9 %collective-permute-start.12 = (f32[648,384]{1,0:T(8,128)}, f32[648,384]{1,0:T(8,128)}, u32[]{:S(2)}, u32[]{:S(2)}) collective-permute-start(f32[648,384]{1,0:T(8,128)} %constant_dynamic-slice_fusion.2), channel_id=1, source_target_pairs={{0,4},{4,0},{1,5},{5,1},{2,6},{6,2},{3,7},{7,3},{8,12},{12,8},{9,1... | collective-permute-start | bytes 2985992 | tf_op jit(solution)/shard_map/ppermute | solution.py:108
  81.6 5.4 %collective-permute-start.6 = (f32[648,384]{1,0:T(8,128)S(1)}, f32[648,384]{1,0:T(8,128)}, u32[]{:S(2)}, u32[]{:S(2)}) collective-permute-start(f32[648,384]{1,0:T(8,128)S(1)} %constant_dynamic-slice_fusion.5), channel_id=1, source_target_pairs={{0,4},{4,0},{1,5},{5,1},{2,6},{6,2},{3,7},{7,3},{8,12},{12,8},{9,1... | collective-permute-start | bytes 2985992 | tf_op jit(solution)/shard_map/ppermute | solution.py:108
  85.6 2.7 %copy-start.1 = (f32[648,384]{1,0:T(8,128)}, f32[648,384]{1,0:T(8,128)S(1)}, u32[]{:S(2)}) copy-start(f32[648,384]{1,0:T(8,128)S(1)} %dynamic-slice_add_fusion) | copy-start | bytes 2985988
  85.7 13.1 %collective-permute-start.13 = (f32[324,384]{1,0:T(8,128)S(1)}, f32[324,384]{1,0:T(8,128)}, u32[]{:S(2)}, u32[]{:S(2)}) collective-permute-start(f32[324,384]{1,0:T(8,128)S(1)} %constant_dynamic-slice_fusion.1), channel_id=1, source_target_pairs={{0,16},{8,24},{16,0},{24,8},{1,17},{9,25},{17,1},{25,9},{2,18},{10... | collective-permute-start | bytes 1493000 | tf_op jit(solution)/shard_map/ppermute | solution.py:108
  89.2 9.7 %copy-start.2 = (f32[648,384]{1,0:T(8,128)S(1)}, f32[648,384]{1,0:T(8,128)}, u32[]{:S(2)}) copy-start(f32[648,384]{1,0:T(8,128)} %copy-done.1) | copy-start | bytes 2985988
  89.2 12.9 %collective-permute-start.7 = (f32[324,384]{1,0:T(8,128)}, f32[324,384]{1,0:T(8,128)}, u32[]{:S(2)}, u32[]{:S(2)}) collective-permute-start(f32[324,384]{1,0:T(8,128)} %constant_dynamic-slice_fusion.4), channel_id=1, source_target_pairs={{0,8},{8,0},{16,24},{24,16},{1,9},{9,1},{17,25},{25,17},{2,10},{10... | collective-permute-start | bytes 1493000 | tf_op jit(solution)/shard_map/ppermute | solution.py:108
  100.0 7.2 %collective-permute-start.14 = (f32[162,384]{1,0:T(8,128)S(1)}, f32[162,384]{1,0:T(8,128)S(1)}, u32[]{:S(2)}, u32[]{:S(2)}) collective-permute-start(f32[162,384]{1,0:T(8,128)S(1)} %constant_dynamic-slice_fusion), channel_id=1, source_target_pairs={{0,8},{8,0},{16,24},{24,16},{1,9},{9,1},{17,25},{25,17},{2,10},{10... | collective-permute-start | bytes 746504 | tf_op jit(solution)/shard_map/ppermute | solution.py:108
  103.3 6.5 %collective-permute-start.8 = (f32[162,384]{1,0:T(8,128)S(1)}, f32[162,384]{1,0:T(8,128)S(1)}, u32[]{:S(2)}, u32[]{:S(2)}) collective-permute-start(f32[162,384]{1,0:T(8,128)S(1)} %constant_dynamic-slice_fusion.3), channel_id=1, source_target_pairs={{0,16},{8,24},{16,0},{24,8},{1,17},{9,25},{17,1},{25,9},{2,18},{10... | collective-permute-start | bytes 746504 | tf_op jit(solution)/shard_map/ppermute | solution.py:108
  107.2 6.3 %collective-permute-start.15 = (f32[162,384]{1,0:T(8,128)S(1)}, f32[162,384]{1,0:T(8,128)S(1)}, u32[]{:S(2)}, u32[]{:S(2)}) collective-permute-start(f32[162,384]{1,0:T(8,128)S(1)} %dynamic-slice_add_fusion.4), channel_id=1, source_target_pairs={{0,8},{8,0},{16,24},{24,16},{1,9},{9,1},{17,25},{25,17},{2,10},{10... | collective-permute-start | bytes 746504 | tf_op jit(solution)/shard_map/ppermute | solution.py:108
  109.8 5.7 %collective-permute-start.9 = (f32[162,384]{1,0:T(8,128)S(1)}, f32[162,384]{1,0:T(8,128)S(1)}, u32[]{:S(2)}, u32[]{:S(2)}) collective-permute-start(f32[162,384]{1,0:T(8,128)S(1)} %dynamic-slice_add_fusion.5), channel_id=1, source_target_pairs={{0,16},{8,24},{16,0},{24,8},{1,17},{9,25},{17,1},{25,9},{2,18},{10... | collective-permute-start | bytes 746504 | tf_op jit(solution)/shard_map/ppermute | solution.py:108
  113.6 13.7 %collective-permute-start.16 = (f32[324,384]{1,0:T(8,128)S(1)}, f32[324,384]{1,0:T(8,128)S(1)}, u32[]{:S(2)}, u32[]{:S(2)}) collective-permute-start(f32[324,384]{1,0:T(8,128)S(1)} %maximum_select_fusion.5), channel_id=1, source_target_pairs={{0,16},{8,24},{16,0},{24,8},{1,17},{9,25},{17,1},{25,9},{2,18},{10... | collective-permute-start | bytes 1493000 | tf_op jit(solution)/shard_map/ppermute | solution.py:108
  115.6 14.2 %copy-start.3 = (f32[96,1280]{0,1:T(8,128)S(1)}, f32[96,1280]{0,1:T(8,128)}, u32[]{:S(2)}) copy-start(f32[96,1280]{0,1:T(8,128)} %get-tuple-element.24) | copy-start | bytes 1474564
  115.6 14.0 %collective-permute-start.10 = (f32[324,384]{1,0:T(8,128)S(1)}, f32[324,384]{1,0:T(8,128)S(1)}, u32[]{:S(2)}, u32[]{:S(2)}) collective-permute-start(f32[324,384]{1,0:T(8,128)S(1)} %maximum_select_fusion.4), channel_id=1, source_target_pairs={{0,8},{8,0},{16,24},{24,16},{1,9},{9,1},{17,25},{25,17},{2,10},{10... | collective-permute-start | bytes 1493000 | tf_op jit(solution)/shard_map/ppermute | solution.py:108
  127.4 3.4 %copy-start.6 = (f32[96,1280]{0,1:T(8,128)S(1)}, f32[96,1280]{0,1:T(8,128)}, u32[]{:S(2)}) copy-start(f32[96,1280]{0,1:T(8,128)} %get-tuple-element.22) | copy-start | bytes 1474564
  127.4 4.4 %collective-permute-start.17 = (f32[648,384]{1,0:T(8,128)S(1)}, f32[648,384]{1,0:T(8,128)}, u32[]{:S(2)}, u32[]{:S(2)}) collective-permute-start(f32[648,384]{1,0:T(8,128)S(1)} %maximum_select_fusion.3), channel_id=1, source_target_pairs={{0,4},{4,0},{1,5},{5,1},{2,6},{6,2},{3,7},{7,3},{8,12},{12,8},{9,1... | collective-permute-start | bytes 2985992 | tf_op jit(solution)/shard_map/ppermute | solution.py:108
  129.7 3.9 %collective-permute-start.11 = (f32[648,384]{1,0:T(8,128)S(1)}, f32[648,384]{1,0:T(8,128)}, u32[]{:S(2)}, u32[]{:S(2)}) collective-permute-start(f32[648,384]{1,0:T(8,128)S(1)} %maximum_select_fusion.2), channel_id=1, source_target_pairs={{0,4},{4,0},{1,5},{5,1},{2,6},{6,2},{3,7},{7,3},{8,12},{12,8},{9,1... | collective-permute-start | bytes 2985992 | tf_op jit(solution)/shard_map/ppermute | solution.py:108
  135.4 3.1 %copy-start.7 = (f32[96,1280]{1,0:T(8,128)S(1)}, f32[96,1280]{1,0:T(8,128)}, u32[]{:S(2)}) copy-start(f32[96,1280]{1,0:T(8,128)} %copy.18) | copy-start | bytes 1474564
Sparse Core Ops, SparseCore 0:
  90.5 39.6 reduce-scatter.1

commit v7 on v6

--- a/solution.py
+++ b/solution.py
@@ -39,7 +39,7 @@
     )
 
 
-def tap_kernel(shifted, active_t, weight_t, slope_x, n_chan, frames, rows):
+def tap_kernel(shifted, active_t, weight_t, slope_x, n_chan, frames, rows, scale):
     _, _, _, cols, outs = shifted.shape
     cells, ins = active_t.shape
     block = ins // n_chan
@@ -52,7 +52,7 @@
                     k = 9 * kt + 3 * kh + kw
                     piece = cot_ref[kw, 2 - kt : 2 - kt + frames, 2 - kh : 2 - kh + rows]
                     piece = piece.reshape(cells, outs)
-                    wg_ref[k] = lax.dot_general(
+                    wg_ref[:, k, :] = scale * lax.dot_general(
                         piece, act, (((0,), (0,)), ((), ())),
                         preferred_element_type=jnp.float32,
                     )
@@ -73,7 +73,7 @@
     return pl.pallas_call(
         body,
         out_shape=(
-            jax.ShapeDtypeStruct((27, outs, ins), jnp.float32),
+            jax.ShapeDtypeStruct((outs, 27, ins), jnp.float32),
             jax.ShapeDtypeStruct((n_chan, block + 1, cells), jnp.float32),
         ),
         in_specs=[pl.BlockSpec(memory_space=pltpu.VMEM)] * 4,
@@ -125,13 +125,16 @@
 def group_sum(x, near, far):
     near_steps, far_steps = halving_steps(near), halving_steps(far)
     unit = 2 ** (len(near_steps) + len(far_steps) + 1)
+    shape = x.shape
+    if shape[0] % unit:
+        x = x.reshape(shape[0] * shape[1], shape[2])
     rows = x.shape[0]
     padded_rows = -(-rows // unit) * unit
-    x = jnp.pad(x, ((0, padded_rows - rows), (0, 0)))
+    x = jnp.pad(x, ((0, padded_rows - rows),) + ((0, 0),) * (x.ndim - 1))
     half = padded_rows // 2
     first = halving_sum(x[:half], near_steps + far_steps)
     second = halving_sum(x[half:], near_steps + far_steps[::-1])
-    return jnp.concatenate([first, second], axis=0)[:rows]
+    return jnp.concatenate([first, second], axis=0)[:rows].reshape(shape)
 
 
 def on_device(features, cotangent, conv_weight, norm_gain, norm_bias):
@@ -160,12 +163,10 @@
     slope = sig * (1.0 + normed * (1.0 - sig)) * norm_gain[:, None]
     weight_t = jnp.transpose(conv_weight, (1, 2, 0))
     local_sums, packed = tap_kernel(
-        shifted, active_t, weight_t, slope * flat_x, n_chan, frames, rows
+        shifted, active_t, weight_t, slope * flat_x, n_chan, frames, rows,
+        1.0 / math.sqrt(positions),
     )
-    summed = group_sum(local_sums.reshape(27 * chans, total), ("height",), ("tm",))
-    weight_grad = jnp.transpose(
-        (summed / math.sqrt(positions)).reshape(27, chans, total), (1, 0, 2)
-    )
+    weight_grad = group_sum(local_sums, ("height",), ("tm",))
 
     mine = lax.psum_scatter(packed, "chan", scatter_dimension=0, tiled=True)[0]
     act_grad = mine[:chans]

time: 148 us -> 160 us (1.081)
  local copies, waits for them, and re-layouts: 16.3 us -> 28.5 us
  other arithmetic: 25.3 us -> 20 us
  starting transfers between devices: 20.7 us -> 23.8 us
    unnamed x25 -> x22, local copies, waits for them, and re-layouts: 4.75 us -> 9.27 us
    select_n x6, other arithmetic: 3.94 us -> 0.75 us  [halving_sum(): lax.select_n(bit, jnp.concatenate([x, got], axis=0), jnp.concatenate([got...]
    ppermute x12, starting transfers between devices: 10.6 us -> 13.7 us  [exchange(): return lax.ppermute(block, axis, [(i, i ^ level) for i in range(size)])]
    select_n x0 -> x2, local copies, waits for them, and re-layouts: none -> 3.06 us  [halving_sum(): lax.select_n(bit, jnp.concatenate([x, got], axis=0), jnp.concatenate([got...]
    ppermute x0 -> x2, local copies, waits for them, and re-layouts: none -> 2.83 us  [exchange(): return lax.ppermute(block, axis, [(i, i ^ level) for i in range(size)])]
    div x1 -> x0, other arithmetic: 2.28 us -> none  [on_device(): summed / math.sqrt(positions)]
    dynamic_slice x6 -> x8, local copies, waits for them, and re-layouts: 2.14 us -> 3.4 us  [halving_sum(): send = lax.dynamic_slice_in_dim(x, (1 - bit) * m, m, 0)]
  transfers between devices with their start and end apart: 19 -> 19, of which waited for: 11 -> 7; matrix products, arithmetic and copies ran while one was open for 20% -> 23% of each run, Pallas kernels for 0% -> 0%
where the time goes in v7:
time: 160 us; the launch traced here: 159 us
  waiting for transfers between devices  53.7 us (34%)
  local copies, waits for them, and re-layouts  28.5 us (18%)
  starting transfers between devices  23.8 us (15%)
  other arithmetic  20 us (12%)
  Pallas kernels  18.7 us (12%)
  between operations  14.5 us (9%)
    ppermute x12, waiting for transfers between devices, exchange(): return lax.ppermute(block, axis, [(i, i ^ level) for i in range(size)])  32.9 us
    ppermute x3, waiting for transfers between devices, gather_blocks(): lax.ppermute(block, axis, [(j, (j + d) % size) for j in range(size)])  20.8 us
    pallas_call x1, Pallas kernels, tap_kernel(): pl.pallas_call(body, out_shape=(jax.ShapeDtypeStruct((outs, 27, ins), jnp...  18.7 us
    ppermute x12, starting transfers between devices, exchange(): return lax.ppermute(block, axis, [(i, i ^ level) for i in range(size)])  13.7 us
    unnamed x22, local copies, waits for them, and re-layouts  9.27 us
    add x6, other arithmetic, halving_sum(): x = keep + exchange(send, axis, level)  4.96 us
    ppermute x3, starting transfers between devices, gather_blocks(): lax.ppermute(block, axis, [(j, (j + d) % size) for j in range(size)])  3.83 us
    ppermute x1, starting transfers between devices, with_halo(): after = lax.ppermute(first, axis, down)  3.7 us
  transfers between devices with their start and end apart: 19, of which 7 were waited for; matrix products, arithmetic and copies ran while one was open for 23% of the time, Pallas kernels for 0%

profile of v7, /device:TPU:9, one launch (start us, length us, event | category | flops | bytes accessed | tf_op | source)
XLA Modules:
  0.0 159.1 jit_solution(8497955848139543128)
XLA Ops:
  7.2 1.3 collective-permute-start
  9.6 1.4 collective-permute-start.2
  12.4 4.3 %copy.23 = bf16[96,27,384]{0,2,1:T(8,128)(2,1)} copy(bf16[96,27,384]{2,0,1:T(8,128)(2,1)} %param.7) | data formatting | bytes 3981312 | tf_op args[2]
  17.7 18.7 %collective-permute-done.1 = bf16[96,2,4,160]{0,3,2,1:T(8,128)(2,1)S(1)} collective-permute-done((bf16[96,2,4,160]{0,3,2,1:T(8,128)(2,1)}, bf16[96,2,4,160]{0,3,2,1:T(8,128)(2,1)S(1)}, u32[]{:S(2)}, u32[]{:S(2)}) %collective-permute-start.1) | collective-permute-done | bytes 245792 | tf_op jit(solution)/shard_map/ppermute | solution.py:34
  37.0 2.1 %collective-permute-done.2 = bf16[96,2,4,160]{0,3,2,1:T(8,128)(2,1)} collective-permute-done((bf16[96,2,4,160]{0,3,2,1:T(8,128)(2,1)}, bf16[96,2,4,160]{0,3,2,1:T(8,128)(2,1)}, u32[]{:S(2)}, u32[]{:S(2)}) %collective-permute-start.2) | collective-permute-done | bytes 245792 | tf_op jit(solution)/shard_map/ppermute | solution.py:34
  39.2 2.1 %select_select_fusion.3 = (bf16[96,2,4,160]{0,3,2,1:T(8,128)(2,1)S(1)}, bf16[96,2,4,160]{0,3,2,1:T(8,128)(2,1)S(1)}, bf16[96,2,4,160]{0,3,2,1:T(8,128)(2,1)S(1)}...) fusion(bf16[96,2,4,160]{0,3,2,1:T(8,128)(2,1)} %copy-done.7, bf16[96,2,4,160]{0,3,2,1:T(8,128)(2,1)} %collective-permute-done.2, ...), kind=kLoop, calls=%fused_computation.42 | loop fusion | flops 1597440 | bytes 2457612 | tf_op jit(solution)/shard_map/select_n | solution.py:38
  42.4 1.8 %maximum_convert_fusion = f32[384,2,4,160]{0,3,2,1:T(8,128)} fusion(bf16[96,2,4,160]{0,3,2,1:T(8,128)(2,1)S(1)} %get-tuple-element.18, bf16[96,2,4,160]{0,3,2,1:T(8,128)(2,1)S(1)} %get-tuple-element.19, bf16[96,2,4,160]{0,3,2,1:T(8,128)(2,1)S(1)} %get-tuple-element.20, bf16[96,2,4,160]{0,3,2,1:T(8,128)(2,1)S(1)} %get-tuple-element.17), kind=kLoop, calls=%fused_computation.25 | loop fusion | flops 3932160 | bytes 2949120 | tf_op jit(solution)/shard_map/convert_element_type | solution.py:146
  44.2 1.9 %copy.22 = f32[384,1280]{1,0:T(8,128)S(1)} copy(f32[384,1280]{0,1:T(8,128)} %bitcast.31) | data formatting | bytes 3932160 | tf_op jit(solution)/shard_map/convert_element_type | solution.py:146
  47.6 3.7 %collective-permute-start.5 = (bf16[96,4,1,160]{0,3,2,1:T(8,128)(2,1)S(1)}, bf16[96,4,1,160]{0,3,2,1:T(8,128)(2,1)}, u32[]{:S(2)}, u32[]{:S(2)}) collective-permute-start(bf16[96,4,1,160]{0,3,2,1:T(8,128)(2,1)S(1)} %get-tuple-element.25), channel_id=1, source_target_pairs={{4,0},{5,1},{6,2},{7,3},{12,8},{13,9},{14,10},{15,11},{20,16},{21,... | collective-permute-start | bytes 368648 | tf_op jit(solution)/shard_map/ppermute | solution.py:25
  51.3 3.0 %multiply_multiply_fusion = (f32[384,1280]{1,0:T(8,128)}, bf16[1280,384]{0,1:T(8,128)(2,1)S(1)}, f32[384,1280]{1,0:T(8,128)}) fusion(f32[384,1280]{1,0:T(8,128)S(1)} %copy.22, f32[384]{0:T(512)S(1)} %copy-done.8, f32[384]{0:T(512)S(1)} %copy-done.9, f32[1280]{0:T(1024)S(1)} %rsqrt.15), kind=kLoop, calls=%fused_computation.7 | loop fusion | flops 6881280 | bytes 6889472 | tf_op jit(solution)/shard_map/mul | solution.py:163
  57.6 2.3 %pad_maximum_fusion.1.cot_ref = bf16[3,4,6,160,96]{4,3,2,1,0:T(8,128)(2,1)} fusion(bf16[1,4,6,160,96]{4,3,2,1,0:T(8,128)(2,1)S(1)} %get-tuple-element.22, bf16[1,4,6,160,96]{4,3,2,1,0:T(8,128)(2,1)S(1)} %get-tuple-element.23, bf16[1,4,6,160,96]{4,3,2,1,0:T(8,128)(2,1)S(1)} %get-tuple-element.21), kind=kLoop, calls=%fused_computation.3 | loop fusion | flops 2211840 | bytes 4423680 | tf_op jit(solution)/shard_map/stack | solution.py:158
  59.9 18.7 %shard_map.68 = (f32[96,27,384]{2,1,0:T(8,128)}, f32[4,97,1280]{2,1,0:T(8,128)}) custom-call(bf16[3,4,6,160,96]{4,3,2,1,0:T(8,128)(2,1)} %pad_maximum_fusion.1.cot_ref, bf16[1280,384]{1,0:T(8,128)(2,1)} %copy.25.act_ref, bf16[27,384,96]{2,1,0:T(8,128)(2,1)} %bitcast.32, f32[384,1280]{1,0:T(8,128)} %get-tuple-element.16.sx_ref), custom_call_target="tpu_custom_call" | custom-call | flops 5096079360 | bytes 13119488 | tf_op jit(solution)/shard_map/pallas_call | solution.py:73
  78.6 2.7 %fusion.14 = (f32[48,27,384]{2,1,0:T(8,128)S(1)}, f32[48,27,384]{2,1,0:T(8,128)S(1)}) fusion(f32[96,27,384]{2,1,0:T(8,128)} %get-tuple-element.5), kind=kLoop, calls=%fused_computation.57 | loop fusion | bytes 7962624 | tf_op jit(solution)/shard_map/slice | solution.py:135
  81.4 1.6 %copy.29 = f32[24,27,384]{2,0,1:T(8,128)} copy(f32[24,27,384]{2,1,0:T(8,128)S(1)} %constant_dynamic-slice_fusion.5) | data formatting | bytes 1990656 | tf_op jit(solution)/shard_map/dynamic_slice | solution.py:115
  84.3 1.7 %collective-permute-done.6 = f32[24,27,384]{2,0,1:T(8,128)} collective-permute-done((f32[24,27,384]{2,0,1:T(8,128)}, f32[24,27,384]{2,0,1:T(8,128)}, u32[]{:S(2)}, u32[]{:S(2)}) %collective-permute-start.6) | collective-permute-done | bytes 995360 | tf_op jit(solution)/shard_map/ppermute | solution.py:108
  85.9 1.8 %copy_add_fusion.1 = f32[24,27,384]{2,1,0:T(8,128)S(1)} fusion(f32[24,27,384]{2,0,1:T(8,128)} %collective-permute-done.6, f32[48,27,384]{2,1,0:T(8,128)} %copy-done, s32[]{:T(128)S(6)} %select_n.277), kind=kLoop, calls=%fused_computation.18 | loop fusion | flops 248832 | bytes 2985988 | tf_op jit(solution)/shard_map/add | solution.py:116
  89.9 1.7 %copy_add_fusion = f32[24,27,384]{2,1,0:T(8,128)S(1)} fusion(f32[24,27,384]{2,0,1:T(8,128)} %collective-permute-done.12, f32[48,27,384]{2,1,0:T(8,128)S(1)} %get-tuple-element.13, s32[]{:T(128)S(6)} %select_n.277), kind=kLoop, calls=%fused_computation.17 | loop fusion | flops 248832 | bytes 2985988 | tf_op jit(solution)/shard_map/add | solution.py:116
  91.7 1.3 collective-permute-start.13
  93.0 10.8 %collective-permute-done.7 = f32[12,27,384]{2,1,0:T(8,128)} collective-permute-done((f32[12,27,384]{2,1,0:T(8,128)}, f32[12,27,384]{2,1,0:T(8,128)}, u32[]{:S(2)}, u32[]{:S(2)}) %collective-permute-start.7) | collective-permute-done | bytes 497696 | tf_op jit(solution)/shard_map/ppermute | solution.py:108
  103.8 1.3 dynamic-slice_add_fusion.1
  105.2 1.3 collective-permute-start.8
  107.9 5.0 %collective-permute-done.8 = f32[6,27,384]{2,1,0:T(8,128)S(1)} collective-permute-done((f32[6,27,384]{2,1,0:T(8,128)S(1)}, f32[6,27,384]{2,1,0:T(8,128)S(1)}, u32[]{:S(2)}, u32[]{:S(2)}) %collective-permute-start.8) | collective-permute-done | bytes 248864 | tf_op jit(solution)/shard_map/ppermute | solution.py:108
  115.6 4.3 %collective-permute-done.9 = f32[6,27,384]{2,1,0:T(8,128)S(1)} collective-permute-done((f32[6,27,384]{2,1,0:T(8,128)S(1)}, f32[6,27,384]{2,1,0:T(8,128)S(1)}, u32[]{:S(2)}, u32[]{:S(2)}) %collective-permute-start.9) | collective-permute-done | bytes 248864 | tf_op jit(solution)/shard_map/ppermute | solution.py:108
  122.6 11.1 %collective-permute-done.10 = f32[12,27,384]{2,1,0:T(8,128)S(1)} collective-permute-done((f32[12,27,384]{2,1,0:T(8,128)S(1)}, f32[12,27,384]{2,1,0:T(8,128)S(1)}, u32[]{:S(2)}, u32[]{:S(2)}) %collective-permute-start.10) | collective-permute-done | bytes 497696 | tf_op jit(solution)/shard_map/ppermute | solution.py:108
  133.7 1.5 copy.31
  135.3 2.8 %collective-permute-start.11 = (f32[24,27,384]{2,0,1:T(8,128)}, f32[24,27,384]{2,0,1:T(8,128)}, u32[]{:S(2)}, u32[]{:S(2)}) collective-permute-start(f32[24,27,384]{2,0,1:T(8,128)} %copy.31), channel_id=1, source_target_pairs={{0,4},{4,0},{1,5},{5,1},{2,6},{6,2},{3,7},{7,3},{8,12},{12,8},{9,1... | collective-permute-start | bytes 2985992 | tf_op jit(solution)/shard_map/ppermute | solution.py:108
  138.2 1.5 copy.36
  140.0 1.3 copy.26
  141.3 1.4 copy.32
  142.7 1.4 copy.37
  145.0 4.2 %copy.39 = f32[96,27,384]{2,0,1:T(8,128)} copy(f32[96,27,384]{2,1,0:T(8,128)S(1)} %pad_maximum_fusion) | data formatting | bytes 7962624
  150.1 1.3 fusion.12
  (76 shorter events, 23.1 us)
Async XLA Ops:
  7.2 142.1 %reduce-scatter.2.cloned.1.call-start = ((), (), s32[]{:S(2)}) async-start(), calls=%async_computation.1 | async-start | bytes 2662400 | tf_op jit(solution)/shard_map/reduce_scatter | solution.py:171
  7.2 10.4 %collective-permute-start = (bf16[96,2,4,160]{0,3,2,1:T(8,128)(2,1)}, bf16[96,2,4,160]{0,3,2,1:T(8,128)(2,1)S(1)}, u32[]{:S(2)}, u32[]{:S(2)}) collective-permute-start(bf16[96,2,4,160]{0,3,2,1:T(8,128)(2,1)} %param.5), channel_id=1, source_target_pairs={{0,1},{1,2},{2,3},{3,0},{4,5},{5,6},{6,7},{7,4},{8,9},{9,10},{10,1... | collective-permute-start | bytes 737288 | tf_op jit(solution)/shard_map/ppermute | solution.py:34
  8.6 27.8 %collective-permute-start.1 = (bf16[96,2,4,160]{0,3,2,1:T(8,128)(2,1)}, bf16[96,2,4,160]{0,3,2,1:T(8,128)(2,1)S(1)}, u32[]{:S(2)}, u32[]{:S(2)}) collective-permute-start(bf16[96,2,4,160]{0,3,2,1:T(8,128)(2,1)} %param.5), channel_id=1, source_target_pairs={{0,2},{1,3},{2,0},{3,1},{4,6},{5,7},{6,4},{7,5},{8,10},{9,11},{10,... | collective-permute-start | bytes 737288 | tf_op jit(solution)/shard_map/ppermute | solution.py:34
  9.6 29.5 %collective-permute-start.2 = (bf16[96,2,4,160]{0,3,2,1:T(8,128)(2,1)}, bf16[96,2,4,160]{0,3,2,1:T(8,128)(2,1)}, u32[]{:S(2)}, u32[]{:S(2)}) collective-permute-start(bf16[96,2,4,160]{0,3,2,1:T(8,128)(2,1)} %param.5), channel_id=1, source_target_pairs={{0,3},{1,0},{2,1},{3,2},{4,7},{5,4},{6,5},{7,6},{8,11},{9,8},{10,9... | collective-permute-start | bytes 737288 | tf_op jit(solution)/shard_map/ppermute | solution.py:34
  11.0 35.1 %collective-permute-start.3 = (bf16[96,2,4,160]{0,3,2,1:T(8,128)(2,1)}, bf16[96,2,4,160]{0,3,2,1:T(8,128)(2,1)S(1)}, u32[]{:S(2)}, u32[]{:S(2)}) collective-permute-start(bf16[96,2,4,160]{0,3,2,1:T(8,128)(2,1)} %param.6), channel_id=1, source_target_pairs={{8,0},{16,8},{24,16},{9,1},{17,9},{25,17},{10,2},{18,10},{26,18},{... | collective-permute-start | bytes 737288 | tf_op jit(solution)/shard_map/ppermute | solution.py:14
  12.4 4.3 %copy-start.5 = (bf16[96,2,4,160]{0,3,2,1:T(8,128)(2,1)S(1)}, bf16[96,2,4,160]{0,3,2,1:T(8,128)(2,1)}, u32[]{:S(2)}) copy-start(bf16[96,2,4,160]{0,3,2,1:T(8,128)(2,1)} %param.6) | copy-start | bytes 737284
  12.4 26.7 %copy-start.6 = (bf16[96,2,4,160]{0,3,2,1:T(8,128)(2,1)S(1)}, bf16[96,2,4,160]{0,3,2,1:T(8,128)(2,1)}, u32[]{:S(2)}) copy-start(bf16[96,2,4,160]{0,3,2,1:T(8,128)(2,1)} %param.5) | copy-start | bytes 737284
  36.3 0.7 copy-start.7
  44.2 7.0 %copy-start.8 = (f32[384]{0:T(512)S(1)}, f32[384]{0:T(512)}, u32[]{:S(2)}) copy-start(f32[384]{0:T(512)} %param.9) | copy-start | bytes 4612
  44.2 7.0 %copy-start.9 = (f32[384]{0:T(512)S(1)}, f32[384]{0:T(512)}, u32[]{:S(2)}) copy-start(f32[384]{0:T(512)} %param.8) | copy-start | bytes 4612
  46.2 1.3 copy-start.3
  46.3 9.4 %collective-permute-start.4 = (bf16[96,4,1,160]{0,3,2,1:T(8,128)(2,1)S(1)}, bf16[96,4,1,160]{0,3,2,1:T(8,128)(2,1)S(1)}, u32[]{:S(2)}, u32[]{:S(2)}) collective-permute-start(bf16[96,4,1,160]{0,3,2,1:T(8,128)(2,1)S(1)} %get-tuple-element.24), channel_id=1, source_target_pairs={{0,4},{1,5},{2,6},{3,7},{8,12},{9,13},{10,14},{11,15},{16,20},{17,... | collective-permute-start | bytes 368648 | tf_op jit(solution)/shard_map/ppermute | solution.py:24
  47.6 8.1 %collective-permute-start.5 = (bf16[96,4,1,160]{0,3,2,1:T(8,128)(2,1)S(1)}, bf16[96,4,1,160]{0,3,2,1:T(8,128)(2,1)}, u32[]{:S(2)}, u32[]{:S(2)}) collective-permute-start(bf16[96,4,1,160]{0,3,2,1:T(8,128)(2,1)S(1)} %get-tuple-element.25), channel_id=1, source_target_pairs={{4,0},{5,1},{6,2},{7,3},{12,8},{13,9},{14,10},{15,11},{20,16},{21,... | collective-permute-start | bytes 368648 | tf_op jit(solution)/shard_map/ppermute | solution.py:25
  54.3 1.3 copy-start.4
  81.3 1.7 %copy-start = (f32[48,27,384]{2,1,0:T(8,128)}, f32[48,27,384]{2,1,0:T(8,128)S(1)}, u32[]{:S(2)}) copy-start(f32[48,27,384]{2,1,0:T(8,128)S(1)} %get-tuple-element.12) | copy-start | bytes 5971972
  83.0 2.9 %collective-permute-start.6 = (f32[24,27,384]{2,0,1:T(8,128)}, f32[24,27,384]{2,0,1:T(8,128)}, u32[]{:S(2)}, u32[]{:S(2)}) collective-permute-start(f32[24,27,384]{2,0,1:T(8,128)} %copy.29), channel_id=1, source_target_pairs={{0,4},{4,0},{1,5},{5,1},{2,6},{6,2},{3,7},{7,3},{8,12},{12,8},{9,1... | collective-permute-start | bytes 2985992 | tf_op jit(solution)/shard_map/ppermute | solution.py:108
  83.7 6.2 %collective-permute-start.12 = (f32[24,27,384]{2,0,1:T(8,128)S(1)}, f32[24,27,384]{2,0,1:T(8,128)}, u32[]{:S(2)}, u32[]{:S(2)}) collective-permute-start(f32[24,27,384]{2,0,1:T(8,128)S(1)} %copy.34), channel_id=1, source_target_pairs={{0,4},{4,0},{1,5},{5,1},{2,6},{6,2},{3,7},{7,3},{8,12},{12,8},{9,1... | collective-permute-start | bytes 2985992 | tf_op jit(solution)/shard_map/ppermute | solution.py:108
  87.8 3.8 %copy-start.1 = (f32[24,27,384]{2,1,0:T(8,128)}, f32[24,27,384]{2,1,0:T(8,128)S(1)}, u32[]{:S(2)}) copy-start(f32[24,27,384]{2,1,0:T(8,128)S(1)} %copy_add_fusion.1) | copy-start | bytes 2985988
  88.7 15.1 %collective-permute-start.7 = (f32[12,27,384]{2,1,0:T(8,128)}, f32[12,27,384]{2,1,0:T(8,128)}, u32[]{:S(2)}, u32[]{:S(2)}) collective-permute-start(f32[12,27,384]{2,1,0:T(8,128)} %constant_dynamic-slice_fusion.4), channel_id=1, source_target_pairs={{0,8},{8,0},{16,24},{24,16},{1,9},{9,1},{17,25},{25,17},{2,10},{10... | collective-permute-start | bytes 1493000 | tf_op jit(solution)/shard_map/ppermute | solution.py:108
  91.7 14.8 %collective-permute-start.13 = (f32[12,27,384]{2,1,0:T(8,128)S(1)}, f32[12,27,384]{2,1,0:T(8,128)S(1)}, u32[]{:S(2)}, u32[]{:S(2)}) collective-permute-start(f32[12,27,384]{2,1,0:T(8,128)S(1)} %constant_dynamic-slice_fusion.1), channel_id=1, source_target_pairs={{0,16},{8,24},{16,0},{24,8},{1,17},{9,25},{17,1},{25,9},{2,18},{10... | collective-permute-start | bytes 1493000 | tf_op jit(solution)/shard_map/ppermute | solution.py:108
  105.2 7.7 %collective-permute-start.8 = (f32[6,27,384]{2,1,0:T(8,128)S(1)}, f32[6,27,384]{2,1,0:T(8,128)S(1)}, u32[]{:S(2)}, u32[]{:S(2)}) collective-permute-start(f32[6,27,384]{2,1,0:T(8,128)S(1)} %constant_dynamic-slice_fusion.3), channel_id=1, source_target_pairs={{0,16},{8,24},{16,0},{24,8},{1,17},{9,25},{17,1},{25,9},{2,18},{10... | collective-permute-start | bytes 746504 | tf_op jit(solution)/shard_map/ppermute | solution.py:108
  106.6 7.7 %collective-permute-start.14 = (f32[6,27,384]{2,1,0:T(8,128)S(1)}, f32[6,27,384]{2,1,0:T(8,128)S(1)}, u32[]{:S(2)}, u32[]{:S(2)}) collective-permute-start(f32[6,27,384]{2,1,0:T(8,128)S(1)} %constant_dynamic-slice_fusion), channel_id=1, source_target_pairs={{0,8},{8,0},{16,24},{24,16},{1,9},{9,1},{17,25},{25,17},{2,10},{10... | collective-permute-start | bytes 746504 | tf_op jit(solution)/shard_map/ppermute | solution.py:108
  113.0 6.9 %collective-permute-start.9 = (f32[6,27,384]{2,1,0:T(8,128)S(1)}, f32[6,27,384]{2,1,0:T(8,128)S(1)}, u32[]{:S(2)}, u32[]{:S(2)}) collective-permute-start(f32[6,27,384]{2,1,0:T(8,128)S(1)} %dynamic-slice_add_fusion.3), channel_id=1, source_target_pairs={{0,16},{8,24},{16,0},{24,8},{1,17},{9,25},{17,1},{25,9},{2,18},{10... | collective-permute-start | bytes 746504 | tf_op jit(solution)/shard_map/ppermute | solution.py:108
  114.3 6.9 %collective-permute-start.15 = (f32[6,27,384]{2,1,0:T(8,128)S(1)}, f32[6,27,384]{2,1,0:T(8,128)S(1)}, u32[]{:S(2)}, u32[]{:S(2)}) collective-permute-start(f32[6,27,384]{2,1,0:T(8,128)S(1)} %dynamic-slice_add_fusion.2), channel_id=1, source_target_pairs={{0,8},{8,0},{16,24},{24,16},{1,9},{9,1},{17,25},{25,17},{2,10},{10... | collective-permute-start | bytes 746504 | tf_op jit(solution)/shard_map/ppermute | solution.py:108
  119.9 13.7 %collective-permute-start.10 = (f32[12,27,384]{2,1,0:T(8,128)S(1)}, f32[12,27,384]{2,1,0:T(8,128)S(1)}, u32[]{:S(2)}, u32[]{:S(2)}) collective-permute-start(f32[12,27,384]{2,1,0:T(8,128)S(1)} %maximum_select_fusion.4), channel_id=1, source_target_pairs={{0,8},{8,0},{16,24},{24,16},{1,9},{9,1},{17,25},{25,17},{2,10},{10... | collective-permute-start | bytes 1493000 | tf_op jit(solution)/shard_map/ppermute | solution.py:108
  121.3 16.8 %collective-permute-start.16 = (f32[12,27,384]{2,1,0:T(8,128)S(1)}, f32[12,27,384]{2,1,0:T(8,128)S(1)}, u32[]{:S(2)}, u32[]{:S(2)}) collective-permute-start(f32[12,27,384]{2,1,0:T(8,128)S(1)} %maximum_select_fusion.5), channel_id=1, source_target_pairs={{0,16},{8,24},{16,0},{24,8},{1,17},{9,25},{17,1},{25,9},{2,18},{10... | collective-permute-start | bytes 1493000 | tf_op jit(solution)/shard_map/ppermute | solution.py:108
  135.3 4.4 %copy-start.2 = (f32[96,1280]{0,1:T(8,128)S(1)}, f32[96,1280]{0,1:T(8,128)}, u32[]{:S(2)}) copy-start(f32[96,1280]{0,1:T(8,128)} %get-tuple-element.28) | copy-start | bytes 1474564
  135.3 6.0 %collective-permute-start.11 = (f32[24,27,384]{2,0,1:T(8,128)}, f32[24,27,384]{2,0,1:T(8,128)}, u32[]{:S(2)}, u32[]{:S(2)}) collective-permute-start(f32[24,27,384]{2,0,1:T(8,128)} %copy.31), channel_id=1, source_target_pairs={{0,4},{4,0},{1,5},{5,1},{2,6},{6,2},{3,7},{7,3},{8,12},{12,8},{9,1... | collective-permute-start | bytes 2985992 | tf_op jit(solution)/shard_map/ppermute | solution.py:108
  139.7 3.0 %collective-permute-start.17 = (f32[24,27,384]{2,0,1:T(8,128)}, f32[24,27,384]{2,0,1:T(8,128)}, u32[]{:S(2)}, u32[]{:S(2)}) collective-permute-start(f32[24,27,384]{2,0,1:T(8,128)} %copy.36), channel_id=1, source_target_pairs={{0,4},{4,0},{1,5},{5,1},{2,6},{6,2},{3,7},{7,3},{8,12},{12,8},{9,1... | collective-permute-start | bytes 2985992 | tf_op jit(solution)/shard_map/ppermute | solution.py:108
Sparse Core Ops, SparseCore 0:
  84.4 41.5 reduce-scatter.1

commit v8 on v6

--- a/solution.py
+++ b/solution.py
@@ -39,25 +39,47 @@
     )
 
 
-def tap_kernel(shifted, active_t, weight_t, slope_x, n_chan, frames, rows):
+def weight_taps(shifted, active_t, frames, rows):
     _, _, _, cols, outs = shifted.shape
     cells, ins = active_t.shape
+
+    def body(cot_ref, act_ref, wg_ref):
+        act = act_ref[...]
+        for kt in range(3):
+            for kh in range(3):
+                for kw in range(3):
+                    piece = cot_ref[kw, 2 - kt : 2 - kt + frames, 2 - kh : 2 - kh + rows]
+                    wg_ref[9 * kt + 3 * kh + kw] = lax.dot_general(
+                        piece.reshape(cells, outs), act, (((0,), (0,)), ((), ())),
+                        preferred_element_type=jnp.float32,
+                    )
+
+    return pl.pallas_call(
+        body,
+        out_shape=jax.ShapeDtypeStruct((27, outs, ins), jnp.float32),
+        in_specs=[pl.BlockSpec(memory_space=pltpu.VMEM)] * 2,
+        out_specs=pl.BlockSpec(memory_space=pltpu.VMEM),
+        cost_estimate=pl.CostEstimate(
+            flops=2 * 27 * ins * cells * outs,
+            bytes_accessed=shifted.size * 2 + active_t.size * 2 + 27 * ins * outs * 4,
+            transcendentals=0,
+        ),
+    )(shifted, active_t)
+
+
+def act_taps(shifted, weight_t, slope_x, anchor, n_chan, frames, rows):
+    _, _, _, cols, outs = shifted.shape
+    ins, cells = slope_x.shape
     block = ins // n_chan
 
-    def body(cot_ref, act_ref, w_ref, sx_ref, wg_ref, pk_ref, ag_ref):
-        act = act_ref[...]
+    def body(cot_ref, w_ref, sx_ref, anchor_ref, pk_ref, ag_ref):
         for kt in range(3):
             for kh in range(3):
                 for kw in range(3):
                     k = 9 * kt + 3 * kh + kw
                     piece = cot_ref[kw, 2 - kt : 2 - kt + frames, 2 - kh : 2 - kh + rows]
-                    piece = piece.reshape(cells, outs)
-                    wg_ref[k] = lax.dot_general(
-                        piece, act, (((0,), (0,)), ((), ())),
-                        preferred_element_type=jnp.float32,
-                    )
                     term = lax.dot_general(
-                        w_ref[k], piece, (((1,), (1,)), ((), ())),
+                        w_ref[k], piece.reshape(cells, outs), (((1,), (1,)), ((), ())),
                         preferred_element_type=jnp.float32,
                     )
                     if k == 0:
@@ -72,23 +94,17 @@
 
     return pl.pallas_call(
         body,
-        out_shape=(
-            jax.ShapeDtypeStruct((27, outs, ins), jnp.float32),
-            jax.ShapeDtypeStruct((n_chan, block + 1, cells), jnp.float32),
-        ),
+        out_shape=jax.ShapeDtypeStruct((n_chan, block + 1, cells), jnp.float32),
         in_specs=[pl.BlockSpec(memory_space=pltpu.VMEM)] * 4,
-        out_specs=(
-            pl.BlockSpec(memory_space=pltpu.VMEM),
-            pl.BlockSpec(memory_space=pltpu.VMEM),
-        ),
+        out_specs=pl.BlockSpec(memory_space=pltpu.VMEM),
         scratch_shapes=[pltpu.VMEM((ins, cells), jnp.float32)],
         cost_estimate=pl.CostEstimate(
-            flops=4 * 27 * ins * cells * outs,
-            bytes_accessed=shifted.size * 2 + active_t.size * 2 + weight_t.size * 2
-            + slope_x.size * 4 + 27 * ins * outs * 4 + (ins + n_chan) * cells * 4,
+            flops=2 * 27 * ins * cells * outs,
+            bytes_accessed=shifted.size * 2 + weight_t.size * 2 + slope_x.size * 4
+            + (ins + n_chan) * cells * 4,
             transcendentals=0,
         ),
-    )(shifted, active_t, weight_t, slope_x)
+    )(shifted, weight_t, slope_x, anchor)
 
 
 def halving_steps(axes):
@@ -159,8 +175,9 @@
     sig = jax.nn.sigmoid(normed)
     slope = sig * (1.0 + normed * (1.0 - sig)) * norm_gain[:, None]
     weight_t = jnp.transpose(conv_weight, (1, 2, 0))
-    local_sums, packed = tap_kernel(
-        shifted, active_t, weight_t, slope * flat_x, n_chan, frames, rows
+    local_sums = weight_taps(shifted, active_t, frames, rows)
+    packed = act_taps(
+        shifted, weight_t, slope * flat_x, local_sums[0, :8, :128], n_chan, frames, rows
     )
     summed = group_sum(local_sums.reshape(27 * chans, total), ("height",), ("tm",))
     weight_grad = jnp.transpose(

time: 148 us -> 150 us (1.014)
  the two profiles are of different devices: /device:TPU:9 before, /device:TPU:0 now
where the time goes in v8:
time: 150 us
  waiting for transfers between devices  48.1 us (32%)
  other arithmetic  26.2 us (17%)
  starting transfers between devices  22.7 us (15%)
  Pallas kernels  19.9 us (13%)
  local copies, waits for them, and re-layouts  18.2 us (12%)
  between operations  14.4 us (10%)
    ppermute x12, waiting for transfers between devices, exchange(): return lax.ppermute(block, axis, [(i, i ^ level) for i in range(size)])  20.7 us
    ppermute x3, waiting for transfers between devices, gather_blocks(): lax.ppermute(block, axis, [(j, (j + d) % size) for j in range(size)])  16.9 us
    pallas_call x1, Pallas kernels, act_taps(): pl.pallas_call(body, out_shape=jax.ShapeDtypeStruct((n_chan, block + 1, c...  11.6 us
    ppermute x12, starting transfers between devices, exchange(): return lax.ppermute(block, axis, [(i, i ^ level) for i in range(size)])  11.3 us
    reduce_scatter x1, waiting for transfers between devices, on_device(): mine = lax.psum_scatter(packed, 'chan', scatter_dimension=0, tiled=True)[0]  10.5 us
    pallas_call x1, Pallas kernels, weight_taps(): pl.pallas_call(body, out_shape=jax.ShapeDtypeStruct((27, outs, ins), jnp....  8.27 us
    ppermute x3, starting transfers between devices, gather_blocks(): lax.ppermute(block, axis, [(j, (j + d) % size) for j in range(size)])  7.01 us
    unnamed x21, local copies, waits for them, and re-layouts  5.44 us
  transfers between devices with their start and end apart: 19, of which 10 were waited for; matrix products, arithmetic and copies ran while one was open for 22% of the time, Pallas kernels for 8%

profile of v8, /device:TPU:0, one launch (start us, length us, event | category | flops | bytes accessed | tf_op | source)
XLA Modules:
  0.0 149.5 jit_solution(5615352415734708084)
XLA Ops:
  7.2 3.1 %collective-permute-start = (bf16[96,2,4,160]{0,3,2,1:T(8,128)(2,1)}, bf16[96,2,4,160]{0,3,2,1:T(8,128)(2,1)S(1)}, u32[]{:S(2)}, u32[]{:S(2)}) collective-permute-start(bf16[96,2,4,160]{0,3,2,1:T(8,128)(2,1)} %param.5), channel_id=1, source_target_pairs={{0,1},{1,2},{2,3},{3,0},{4,5},{5,6},{6,7},{7,4},{8,9},{9,10},{10,1... | collective-permute-start | bytes 737288 | tf_op jit(solution)/shard_map/ppermute | solution.py:34
  10.3 2.6 %collective-permute-start.1 = (bf16[96,2,4,160]{0,3,2,1:T(8,128)(2,1)}, bf16[96,2,4,160]{0,3,2,1:T(8,128)(2,1)S(1)}, u32[]{:S(2)}, u32[]{:S(2)}) collective-permute-start(bf16[96,2,4,160]{0,3,2,1:T(8,128)(2,1)} %param.5), channel_id=1, source_target_pairs={{0,2},{1,3},{2,0},{3,1},{4,6},{5,7},{6,4},{7,5},{8,10},{9,11},{10,... | collective-permute-start | bytes 737288 | tf_op jit(solution)/shard_map/ppermute | solution.py:34
  12.9 1.3 collective-permute-start.2
  15.6 1.9 %constant_dynamic-update-slice_fusion.1 = (bf16[96,4,4,160]{0,3,2,1:T(8,128)(2,1)S(1)}, f32[96,1280]{0,1:T(8,128)}) fusion(bf16[96,2,4,160]{0,3,2,1:T(8,128)(2,1)} %param.6), kind=kLoop, calls=%fused_computation.48 | loop fusion | flops 122879 | bytes 1064960
  17.6 3.6 %collective-permute-done = bf16[96,2,4,160]{0,3,2,1:T(8,128)(2,1)S(1)} collective-permute-done((bf16[96,2,4,160]{0,3,2,1:T(8,128)(2,1)}, bf16[96,2,4,160]{0,3,2,1:T(8,128)(2,1)S(1)}, u32[]{:S(2)}, u32[]{:S(2)}) %collective-permute-start) | collective-permute-done | bytes 245792 | tf_op jit(solution)/shard_map/ppermute | solution.py:34
  21.2 13.2 %collective-permute-done.1 = bf16[96,2,4,160]{0,3,2,1:T(8,128)(2,1)S(1)} collective-permute-done((bf16[96,2,4,160]{0,3,2,1:T(8,128)(2,1)}, bf16[96,2,4,160]{0,3,2,1:T(8,128)(2,1)S(1)}, u32[]{:S(2)}, u32[]{:S(2)}) %collective-permute-start.1) | collective-permute-done | bytes 245792 | tf_op jit(solution)/shard_map/ppermute | solution.py:34
  34.4 2.0 %select_select_fusion.3 = (bf16[96,2,4,160]{0,3,2,1:T(8,128)(2,1)S(1)}, bf16[96,2,4,160]{0,3,2,1:T(8,128)(2,1)S(1)}, bf16[96,2,4,160]{0,3,2,1:T(8,128)(2,1)S(1)}...) fusion(bf16[96,2,4,160]{0,3,2,1:T(8,128)(2,1)S(1)} %collective-permute-done.1, ...), kind=kLoop, calls=%fused_computation.42 | loop fusion | flops 1597440 | bytes 2457612 | tf_op jit(solution)/shard_map/select_n | solution.py:38
  37.6 1.8 %maximum_convert_fusion = f32[384,2,4,160]{0,3,2,1:T(8,128)} fusion(bf16[96,2,4,160]{0,3,2,1:T(8,128)(2,1)S(1)} %get-tuple-element.10, bf16[96,2,4,160]{0,3,2,1:T(8,128)(2,1)S(1)} %get-tuple-element.11, bf16[96,2,4,160]{0,3,2,1:T(8,128)(2,1)S(1)} %get-tuple-element.12, bf16[96,2,4,160]{0,3,2,1:T(8,128)(2,1)S(1)} %get-tuple-element.9), kind=kLoop, calls=%fused_computation.25 | loop fusion | flops 3932160 | bytes 2949120 | tf_op jit(solution)/shard_map/convert_element_type | solution.py:159
  39.4 1.9 %copy.14 = f32[384,1280]{1,0:T(8,128)S(1)} copy(f32[384,1280]{0,1:T(8,128)} %bitcast.38) | data formatting | bytes 3932160 | tf_op jit(solution)/shard_map/convert_element_type | solution.py:159
  41.4 1.8 %collective-permute-start.4 = (bf16[96,4,1,160]{0,3,2,1:T(8,128)(2,1)S(1)}, bf16[96,4,1,160]{0,3,2,1:T(8,128)(2,1)S(1)}, u32[]{:S(2)}, u32[]{:S(2)}) collective-permute-start(bf16[96,4,1,160]{0,3,2,1:T(8,128)(2,1)S(1)} %get-tuple-element.16), channel_id=1, source_target_pairs={{0,4},{1,5},{2,6},{3,7},{8,12},{9,13},{10,14},{11,15},{16,20},{17,... | collective-permute-start | bytes 368648 | tf_op jit(solution)/shard_map/ppermute | solution.py:24
  43.3 1.3 collective-permute-start.5
  44.6 3.0 %multiply_multiply_fusion = (f32[384,1280]{1,0:T(8,128)}, f32[384,1280]{1,0:T(8,128)}, bf16[1280,384]{0,1:T(8,128)(2,1)S(1)}) fusion(f32[384,1280]{1,0:T(8,128)S(1)} %copy.14, f32[384]{0:T(512)S(1)} %copy-done.8, f32[384]{0:T(512)S(1)} %copy-done.9, f32[1280]{0:T(1024)S(1)} %rsqrt.15), kind=kLoop, calls=%fused_computation.8 | loop fusion | flops 6881280 | bytes 6889472 | tf_op jit(solution)/shard_map/mul | solution.py:176
  47.6 1.3 copy.16.act_ref
  50.8 2.3 %pad_maximum_fusion.cot_ref = bf16[3,4,6,160,96]{4,3,2,1,0:T(8,128)(2,1)} fusion(bf16[1,4,6,160,96]{4,3,2,1,0:T(8,128)(2,1)S(1)} %get-tuple-element.14, bf16[1,4,6,160,96]{4,3,2,1,0:T(8,128)(2,1)S(1)} %get-tuple-element.15, bf16[1,4,6,160,96]{4,3,2,1,0:T(8,128)(2,1)S(1)} %get-tuple-element.13), kind=kLoop, calls=%fused_computation.3 | loop fusion | flops 2211840 | bytes 4423680 | tf_op jit(solution)/shard_map/stack | solution.py:171
  53.1 8.3 %shard_map.68 = f32[27,96,384]{2,1,0:T(8,128)} custom-call(bf16[3,4,6,160,96]{4,3,2,1,0:T(8,128)(2,1)} %pad_maximum_fusion.cot_ref, bf16[1280,384]{1,0:T(8,128)(2,1)} %copy.16.act_ref), custom_call_target="tpu_custom_call" | custom-call | flops 2548039680 | bytes 7176192 | tf_op jit(solution)/shard_map/pallas_call | solution.py:57
  61.4 2.4 %fusion.14 = (f32[1296,384]{1,0:T(8,128)S(1)}, f32[1296,384]{1,0:T(8,128)S(1)}) fusion(f32[2592,384]{1,0:T(8,128)} %bitcast.39), kind=kLoop, calls=%fused_computation.58 | loop fusion | bytes 7962624 | tf_op jit(solution)/shard_map/slice | solution.py:148
  65.0 1.8 %collective-permute-start.12 = (f32[648,384]{1,0:T(8,128)}, f32[648,384]{1,0:T(8,128)}, u32[]{:S(2)}, u32[]{:S(2)}) collective-permute-start(f32[648,384]{1,0:T(8,128)} %constant_dynamic-slice_fusion.2), channel_id=1, source_target_pairs={{0,4},{4,0},{1,5},{5,1},{2,6},{6,2},{3,7},{7,3},{8,12},{12,8},{9,1... | collective-permute-start | bytes 2985992 | tf_op jit(solution)/shard_map/ppermute | solution.py:124
  67.2 4.2 %copy.13 = bf16[96,27,384]{0,2,1:T(8,128)(2,1)} copy(bf16[96,27,384]{2,0,1:T(8,128)(2,1)} %param.7) | data formatting | bytes 3981312 | tf_op args[2]
  72.7 1.6 %dynamic-slice_add_fusion = f32[648,384]{1,0:T(8,128)S(1)} fusion(f32[648,384]{1,0:T(8,128)} %collective-permute-done.12, f32[1296,384]{1,0:T(8,128)} %copy-done, s32[]{:T(128)S(6)} %select_n.277), kind=kLoop, calls=%fused_computation.20 | loop fusion | flops 248832 | bytes 2985988 | tf_op jit(solution)/shard_map/add | solution.py:132
  74.4 1.6 %collective-permute-start.13 = (f32[324,384]{1,0:T(8,128)S(1)}, f32[324,384]{1,0:T(8,128)}, u32[]{:S(2)}, u32[]{:S(2)}) collective-permute-start(f32[324,384]{1,0:T(8,128)S(1)} %constant_dynamic-slice_fusion.1), channel_id=1, source_target_pairs={{0,16},{8,24},{16,0},{24,8},{1,17},{9,25},{17,1},{25,9},{2,18},{10... | collective-permute-start | bytes 1493000 | tf_op jit(solution)/shard_map/ppermute | solution.py:124
  76.0 1.3 dynamic-slice_add_fusion.1
  78.1 1.5 collective-permute-start.7
  79.6 11.6 %shard_map.69 = f32[4,97,1280]{2,1,0:T(8,128)} custom-call(bf16[3,4,6,160,96]{4,3,2,1,0:T(8,128)(2,1)} %pad_maximum_fusion.cot_ref, bf16[27,384,96]{2,1,0:T(8,128)(2,1)} %bitcast.37, f32[384,1280]{1,0:T(8,128)} %get-tuple-element.7.sx_ref, f32[8,128]{1,0:T(8,128)} %slice_bitcast_fusion.4.anchor_ref), custom_call_target="tpu_custom_call" | custom-call | flops 2548039680 | bytes 8155136 | tf_op jit(solution)/shard_map/pallas_call | solution.py:95
  95.9 5.5 %collective-permute-done.14 = f32[162,384]{1,0:T(8,128)S(1)} collective-permute-done((f32[162,384]{1,0:T(8,128)S(1)}, f32[162,384]{1,0:T(8,128)S(1)}, u32[]{:S(2)}, u32[]{:S(2)}) %collective-permute-start.14) | collective-permute-done | bytes 248864 | tf_op jit(solution)/shard_map/ppermute | solution.py:124
  103.5 4.9 %collective-permute-done.15 = f32[162,384]{1,0:T(8,128)S(1)} collective-permute-done((f32[162,384]{1,0:T(8,128)S(1)}, f32[162,384]{1,0:T(8,128)S(1)}, u32[]{:S(2)}, u32[]{:S(2)}) %collective-permute-start.15) | collective-permute-done | bytes 248864 | tf_op jit(solution)/shard_map/ppermute | solution.py:124
  110.0 2.6 %collective-permute-start.10 = (f32[324,384]{1,0:T(8,128)S(1)}, f32[324,384]{1,0:T(8,128)S(1)}, u32[]{:S(2)}, u32[]{:S(2)}) collective-permute-start(f32[324,384]{1,0:T(8,128)S(1)} %maximum_select_fusion.4), channel_id=1, source_target_pairs={{0,8},{8,0},{16,24},{24,16},{1,9},{9,1},{17,25},{25,17},{2,10},{10... | collective-permute-start | bytes 1493000 | tf_op jit(solution)/shard_map/ppermute | solution.py:124
  112.6 7.7 %collective-permute-done.16 = f32[324,384]{1,0:T(8,128)S(1)} collective-permute-done((f32[324,384]{1,0:T(8,128)S(1)}, f32[324,384]{1,0:T(8,128)S(1)}, u32[]{:S(2)}, u32[]{:S(2)}) %collective-permute-start.16) | collective-permute-done | bytes 497696 | tf_op jit(solution)/shard_map/ppermute | solution.py:124
  123.3 1.7 %maximum_select_fusion.1 = f32[1296,384]{1,0:T(8,128)S(1)} fusion(f32[648,384]{1,0:T(8,128)} %collective-permute-done.17, f32[648,384]{1,0:T(8,128)S(1)} %maximum_select_fusion.3, pred[]{:T(512)S(6)} %select_n.268), kind=kLoop, calls=%fused_computation.6 | loop fusion | flops 1492992 | bytes 3981313 | tf_op jit(solution)/shard_map/select_n | solution.py:135
  125.0 1.8 %maximum_select_fusion = f32[1296,384]{1,0:T(8,128)S(1)} fusion(f32[648,384]{1,0:T(8,128)} %collective-permute-done.11, f32[648,384]{1,0:T(8,128)S(1)} %maximum_select_fusion.2, pred[]{:T(512)S(6)} %select_n.268), kind=kLoop, calls=%fused_computation.5 | loop fusion | flops 1492992 | bytes 3981313 | tf_op jit(solution)/shard_map/select_n | solution.py:135
  126.8 2.3 %maximum_multiply_fusion = f32[2592,384]{1,0:T(8,128)} fusion(f32[1296,384]{1,0:T(8,128)S(1)} %maximum_select_fusion.1, f32[1296,384]{1,0:T(8,128)S(1)} %maximum_select_fusion), kind=kLoop, calls=%fused_computation | loop fusion | flops 1990656 | bytes 7962624 | tf_op jit(solution)/shard_map/div | solution.py:184
  129.1 10.5 %reduce-scatter.2.cloned.1.call-done = f32[1,97,1280]{2,1,0:T(8,128)} async-done(((f32[4,97,1280]{2,1,0:T(8,128)}), f32[1,97,1280]{2,1,0:T(8,128)}) %reduce-scatter.2.cloned.1.call-update) | async-done | bytes 496656 | tf_op jit(solution)/shard_map/reduce_scatter | solution.py:187
  140.4 1.4 fusion.12
  (71 shorter events, 21.1 us)
Async XLA Ops:
  7.2 132.4 %reduce-scatter.2.cloned.1.call-start = ((), (), s32[]{:S(2)}) async-start(), calls=%async_computation.1 | async-start | bytes 2662400 | tf_op jit(solution)/shard_map/reduce_scatter | solution.py:187
  7.2 14.0 %collective-permute-start = (bf16[96,2,4,160]{0,3,2,1:T(8,128)(2,1)}, bf16[96,2,4,160]{0,3,2,1:T(8,128)(2,1)S(1)}, u32[]{:S(2)}, u32[]{:S(2)}) collective-permute-start(bf16[96,2,4,160]{0,3,2,1:T(8,128)(2,1)} %param.5), channel_id=1, source_target_pairs={{0,1},{1,2},{2,3},{3,0},{4,5},{5,6},{6,7},{7,4},{8,9},{9,10},{10,1... | collective-permute-start | bytes 737288 | tf_op jit(solution)/shard_map/ppermute | solution.py:34
  10.3 24.1 %collective-permute-start.1 = (bf16[96,2,4,160]{0,3,2,1:T(8,128)(2,1)}, bf16[96,2,4,160]{0,3,2,1:T(8,128)(2,1)S(1)}, u32[]{:S(2)}, u32[]{:S(2)}) collective-permute-start(bf16[96,2,4,160]{0,3,2,1:T(8,128)(2,1)} %param.5), channel_id=1, source_target_pairs={{0,2},{1,3},{2,0},{3,1},{4,6},{5,7},{6,4},{7,5},{8,10},{9,11},{10,... | collective-permute-start | bytes 737288 | tf_op jit(solution)/shard_map/ppermute | solution.py:34
  12.9 21.5 %collective-permute-start.2 = (bf16[96,2,4,160]{0,3,2,1:T(8,128)(2,1)}, bf16[96,2,4,160]{0,3,2,1:T(8,128)(2,1)S(1)}, u32[]{:S(2)}, u32[]{:S(2)}) collective-permute-start(bf16[96,2,4,160]{0,3,2,1:T(8,128)(2,1)} %param.5), channel_id=1, source_target_pairs={{0,3},{1,0},{2,1},{3,2},{4,7},{5,4},{6,5},{7,6},{8,11},{9,8},{10,9... | collective-permute-start | bytes 737288 | tf_op jit(solution)/shard_map/ppermute | solution.py:34
  14.2 27.1 %collective-permute-start.3 = (bf16[96,2,4,160]{0,3,2,1:T(8,128)(2,1)}, bf16[96,2,4,160]{0,3,2,1:T(8,128)(2,1)S(1)}, u32[]{:S(2)}, u32[]{:S(2)}) collective-permute-start(bf16[96,2,4,160]{0,3,2,1:T(8,128)(2,1)} %param.6), channel_id=1, source_target_pairs={{8,0},{16,8},{24,16},{9,1},{17,9},{25,17},{10,2},{18,10},{26,18},{... | collective-permute-start | bytes 737288 | tf_op jit(solution)/shard_map/ppermute | solution.py:14
  39.4 5.2 %copy-start.8 = (f32[384]{0:T(512)S(1)}, f32[384]{0:T(512)}, u32[]{:S(2)}) copy-start(f32[384]{0:T(512)} %param.9) | copy-start | bytes 4612
  39.4 5.2 %copy-start.9 = (f32[384]{0:T(512)S(1)}, f32[384]{0:T(512)}, u32[]{:S(2)}) copy-start(f32[384]{0:T(512)} %param.8) | copy-start | bytes 4612
  41.4 1.9 %copy-start.4 = (bf16[96,4,4,160]{0,3,2,1:T(8,128)(2,1)}, bf16[96,4,4,160]{0,3,2,1:T(8,128)(2,1)S(1)}, u32[]{:S(2)}) copy-start(bf16[96,4,4,160]{0,3,2,1:T(8,128)(2,1)S(1)} %constant_dynamic-update-slice_fusion) | copy-start | bytes 1474564
  41.4 7.5 %collective-permute-start.4 = (bf16[96,4,1,160]{0,3,2,1:T(8,128)(2,1)S(1)}, bf16[96,4,1,160]{0,3,2,1:T(8,128)(2,1)S(1)}, u32[]{:S(2)}, u32[]{:S(2)}) collective-permute-start(bf16[96,4,1,160]{0,3,2,1:T(8,128)(2,1)S(1)} %get-tuple-element.16), channel_id=1, source_target_pairs={{0,4},{1,5},{2,6},{3,7},{8,12},{9,13},{10,14},{11,15},{16,20},{17,... | collective-permute-start | bytes 368648 | tf_op jit(solution)/shard_map/ppermute | solution.py:24
  43.3 5.6 %collective-permute-start.5 = (bf16[96,4,1,160]{0,3,2,1:T(8,128)(2,1)S(1)}, bf16[96,4,1,160]{0,3,2,1:T(8,128)(2,1)}, u32[]{:S(2)}, u32[]{:S(2)}) collective-permute-start(bf16[96,4,1,160]{0,3,2,1:T(8,128)(2,1)S(1)} %get-tuple-element.17), channel_id=1, source_target_pairs={{4,0},{5,1},{6,2},{7,3},{12,8},{13,9},{14,10},{15,11},{20,16},{21,... | collective-permute-start | bytes 368648 | tf_op jit(solution)/shard_map/ppermute | solution.py:25
  47.6 1.3 copy-start.5
  63.8 3.0 %copy-start = (f32[1296,384]{1,0:T(8,128)}, f32[1296,384]{1,0:T(8,128)S(1)}, u32[]{:S(2)}) copy-start(f32[1296,384]{1,0:T(8,128)S(1)} %get-tuple-element.5) | copy-start | bytes 5971972
  65.0 7.7 %collective-permute-start.12 = (f32[648,384]{1,0:T(8,128)}, f32[648,384]{1,0:T(8,128)}, u32[]{:S(2)}, u32[]{:S(2)}) collective-permute-start(f32[648,384]{1,0:T(8,128)} %constant_dynamic-slice_fusion.2), channel_id=1, source_target_pairs={{0,4},{4,0},{1,5},{5,1},{2,6},{6,2},{3,7},{7,3},{8,12},{12,8},{9,1... | collective-permute-start | bytes 2985992 | tf_op jit(solution)/shard_map/ppermute | solution.py:124
  66.8 9.2 %collective-permute-start.6 = (f32[648,384]{1,0:T(8,128)S(1)}, f32[648,384]{1,0:T(8,128)}, u32[]{:S(2)}, u32[]{:S(2)}) collective-permute-start(f32[648,384]{1,0:T(8,128)S(1)} %constant_dynamic-slice_fusion.5), channel_id=1, source_target_pairs={{0,4},{4,0},{1,5},{5,1},{2,6},{6,2},{3,7},{7,3},{8,12},{12,8},{9,1... | collective-permute-start | bytes 2985992 | tf_op jit(solution)/shard_map/ppermute | solution.py:124
  74.3 3.0 %copy-start.1 = (f32[648,384]{1,0:T(8,128)}, f32[648,384]{1,0:T(8,128)S(1)}, u32[]{:S(2)}) copy-start(f32[648,384]{1,0:T(8,128)S(1)} %dynamic-slice_add_fusion) | copy-start | bytes 2985988
  74.4 16.9 %collective-permute-start.13 = (f32[324,384]{1,0:T(8,128)S(1)}, f32[324,384]{1,0:T(8,128)}, u32[]{:S(2)}, u32[]{:S(2)}) collective-permute-start(f32[324,384]{1,0:T(8,128)S(1)} %constant_dynamic-slice_fusion.1), channel_id=1, source_target_pairs={{0,16},{8,24},{16,0},{24,8},{1,17},{9,25},{17,1},{25,9},{2,18},{10... | collective-permute-start | bytes 1493000 | tf_op jit(solution)/shard_map/ppermute | solution.py:124
  78.1 16.0 %collective-permute-start.7 = (f32[324,384]{1,0:T(8,128)}, f32[324,384]{1,0:T(8,128)}, u32[]{:S(2)}, u32[]{:S(2)}) collective-permute-start(f32[324,384]{1,0:T(8,128)} %constant_dynamic-slice_fusion.4), channel_id=1, source_target_pairs={{0,8},{8,0},{16,24},{24,16},{1,9},{9,1},{17,25},{25,17},{2,10},{10... | collective-permute-start | bytes 1493000 | tf_op jit(solution)/shard_map/ppermute | solution.py:124
  91.2 1.2 copy-start.2
  93.6 7.8 %collective-permute-start.14 = (f32[162,384]{1,0:T(8,128)S(1)}, f32[162,384]{1,0:T(8,128)S(1)}, u32[]{:S(2)}, u32[]{:S(2)}) collective-permute-start(f32[162,384]{1,0:T(8,128)S(1)} %constant_dynamic-slice_fusion), channel_id=1, source_target_pairs={{0,8},{8,0},{16,24},{24,16},{1,9},{9,1},{17,25},{25,17},{2,10},{10... | collective-permute-start | bytes 746504 | tf_op jit(solution)/shard_map/ppermute | solution.py:124
  95.3 7.5 %collective-permute-start.8 = (f32[162,384]{1,0:T(8,128)S(1)}, f32[162,384]{1,0:T(8,128)S(1)}, u32[]{:S(2)}, u32[]{:S(2)}) collective-permute-start(f32[162,384]{1,0:T(8,128)S(1)} %constant_dynamic-slice_fusion.3), channel_id=1, source_target_pairs={{0,16},{8,24},{16,0},{24,8},{1,17},{9,25},{17,1},{25,9},{2,18},{10... | collective-permute-start | bytes 746504 | tf_op jit(solution)/shard_map/ppermute | solution.py:124
  101.5 7.0 %collective-permute-start.15 = (f32[162,384]{1,0:T(8,128)S(1)}, f32[162,384]{1,0:T(8,128)S(1)}, u32[]{:S(2)}, u32[]{:S(2)}) collective-permute-start(f32[162,384]{1,0:T(8,128)S(1)} %dynamic-slice_add_fusion.4), channel_id=1, source_target_pairs={{0,8},{8,0},{16,24},{24,16},{1,9},{9,1},{17,25},{25,17},{2,10},{10... | collective-permute-start | bytes 746504 | tf_op jit(solution)/shard_map/ppermute | solution.py:124
  102.9 7.0 %collective-permute-start.9 = (f32[162,384]{1,0:T(8,128)S(1)}, f32[162,384]{1,0:T(8,128)S(1)}, u32[]{:S(2)}, u32[]{:S(2)}) collective-permute-start(f32[162,384]{1,0:T(8,128)S(1)} %dynamic-slice_add_fusion.5), channel_id=1, source_target_pairs={{0,16},{8,24},{16,0},{24,8},{1,17},{9,25},{17,1},{25,9},{2,18},{10... | collective-permute-start | bytes 746504 | tf_op jit(solution)/shard_map/ppermute | solution.py:124
  108.5 11.8 %collective-permute-start.16 = (f32[324,384]{1,0:T(8,128)S(1)}, f32[324,384]{1,0:T(8,128)S(1)}, u32[]{:S(2)}, u32[]{:S(2)}) collective-permute-start(f32[324,384]{1,0:T(8,128)S(1)} %maximum_select_fusion.5), channel_id=1, source_target_pairs={{0,16},{8,24},{16,0},{24,8},{1,17},{9,25},{17,1},{25,9},{2,18},{10... | collective-permute-start | bytes 1493000 | tf_op jit(solution)/shard_map/ppermute | solution.py:124
  110.0 11.3 %copy-start.3 = (f32[96,1280]{0,1:T(8,128)S(1)}, f32[96,1280]{0,1:T(8,128)}, u32[]{:S(2)}) copy-start(f32[96,1280]{0,1:T(8,128)} %get-tuple-element.20) | copy-start | bytes 1474564
  110.0 10.7 %collective-permute-start.10 = (f32[324,384]{1,0:T(8,128)S(1)}, f32[324,384]{1,0:T(8,128)S(1)}, u32[]{:S(2)}, u32[]{:S(2)}) collective-permute-start(f32[324,384]{1,0:T(8,128)S(1)} %maximum_select_fusion.4), channel_id=1, source_target_pairs={{0,8},{8,0},{16,24},{24,16},{1,9},{9,1},{17,25},{25,17},{2,10},{10... | collective-permute-start | bytes 1493000 | tf_op jit(solution)/shard_map/ppermute | solution.py:124
  120.5 1.8 %copy-start.6 = (f32[96,1280]{0,1:T(8,128)S(1)}, f32[96,1280]{0,1:T(8,128)}, u32[]{:S(2)}) copy-start(f32[96,1280]{0,1:T(8,128)} %get-tuple-element.18) | copy-start | bytes 1474564
  120.5 2.8 %collective-permute-start.17 = (f32[648,384]{1,0:T(8,128)S(1)}, f32[648,384]{1,0:T(8,128)}, u32[]{:S(2)}, u32[]{:S(2)}) collective-permute-start(f32[648,384]{1,0:T(8,128)S(1)} %maximum_select_fusion.3), channel_id=1, source_target_pairs={{0,4},{4,0},{1,5},{5,1},{2,6},{6,2},{3,7},{7,3},{8,12},{12,8},{9,1... | collective-permute-start | bytes 2985992 | tf_op jit(solution)/shard_map/ppermute | solution.py:124
  120.8 4.2 %collective-permute-start.11 = (f32[648,384]{1,0:T(8,128)S(1)}, f32[648,384]{1,0:T(8,128)}, u32[]{:S(2)}, u32[]{:S(2)}) collective-permute-start(f32[648,384]{1,0:T(8,128)S(1)} %maximum_select_fusion.2), channel_id=1, source_target_pairs={{0,4},{4,0},{1,5},{5,1},{2,6},{6,2},{3,7},{7,3},{8,12},{12,8},{9,1... | collective-permute-start | bytes 2985992 | tf_op jit(solution)/shard_map/ppermute | solution.py:124
  126.8 13.6 %copy-start.7 = (f32[96,1280]{1,0:T(8,128)S(1)}, f32[96,1280]{1,0:T(8,128)}, u32[]{:S(2)}) copy-start(f32[96,1280]{1,0:T(8,128)} %copy.18) | copy-start | bytes 1474564
Sparse Core Ops, SparseCore 0:
  91.4 48.1 reduce-scatter.1

commit v9 on v8

--- a/solution.py
+++ b/solution.py
@@ -67,12 +67,12 @@
     )(shifted, active_t)
 
 
-def act_taps(shifted, weight_t, slope_x, anchor, n_chan, frames, rows):
+def act_taps(shifted, weight_t, frames, rows):
     _, _, _, cols, outs = shifted.shape
-    ins, cells = slope_x.shape
-    block = ins // n_chan
-
-    def body(cot_ref, w_ref, sx_ref, anchor_ref, pk_ref, ag_ref):
+    _, ins, _ = weight_t.shape
+    cells = frames * rows * cols
+
+    def body(cot_ref, w_ref, ag_ref):
         for kt in range(3):
             for kh in range(3):
                 for kw in range(3):
@@ -86,25 +86,18 @@
                         ag_ref[...] = term
                     else:
                         ag_ref[...] += term
-        ag = ag_ref[...]
-        dots = jnp.sum(ag * sx_ref[...], axis=0, keepdims=True)
-        for j in range(n_chan):
-            pk_ref[j, 0:block, :] = ag[j * block : (j + 1) * block]
-            pk_ref[j, block : block + 1, :] = dots
 
     return pl.pallas_call(
         body,
-        out_shape=jax.ShapeDtypeStruct((n_chan, block + 1, cells), jnp.float32),
-        in_specs=[pl.BlockSpec(memory_space=pltpu.VMEM)] * 4,
+        out_shape=jax.ShapeDtypeStruct((ins, cells), jnp.float32),
+        in_specs=[pl.BlockSpec(memory_space=pltpu.VMEM)] * 2,
         out_specs=pl.BlockSpec(memory_space=pltpu.VMEM),
-        scratch_shapes=[pltpu.VMEM((ins, cells), jnp.float32)],
         cost_estimate=pl.CostEstimate(
             flops=2 * 27 * ins * cells * outs,
-            bytes_accessed=shifted.size * 2 + weight_t.size * 2 + slope_x.size * 4
-            + (ins + n_chan) * cells * 4,
+            bytes_accessed=shifted.size * 2 + weight_t.size * 2 + ins * cells * 4,
             transcendentals=0,
         ),
-    )(shifted, weight_t, slope_x, anchor)
+    )(shifted, weight_t)
 
 
 def halving_steps(axes):
@@ -153,7 +146,20 @@
 def on_device(features, cotangent, conv_weight, norm_gain, norm_bias):
     chans, frames, rows, cols = features.shape
     n_chan = lax.axis_size("chan")
-    whole_x = gather_blocks(features, "chan")
+    ahead = from_behind(lax.slice_in_dim(cotangent, 0, 2, axis=1), "tm", -1)
+    longer = jnp.concatenate([cotangent, ahead], axis=1)
+    bordered = with_halo(longer, (("height", 2),), 1)
+    padded = jnp.pad(bordered, ((0, 0), (0, 0), (0, 0), (1, 1)))
+
+    cells_major = jnp.transpose(padded, (1, 2, 3, 0))
+    shifted = jnp.stack(
+        [cells_major[:, :, 2 - kw : 2 - kw + cols] for kw in range(3)], axis=0
+    )
+    weight_t = jnp.transpose(conv_weight, (1, 2, 0))
+    partial = act_taps(shifted, weight_t, frames, rows)
+
+    held, _ = lax.optimization_barrier((features, padded))
+    whole_x = gather_blocks(held, "chan")
     total = whole_x.shape[0]
     cells = frames * rows * cols
     flat_x = whole_x.reshape(total, cells).astype(jnp.float32)
@@ -161,24 +167,19 @@
     normed = flat_x * inv_rms * norm_gain[:, None] + norm_bias[:, None]
     active = jax.nn.silu(normed).astype(jnp.bfloat16).reshape(total, frames, rows, cols)
 
-    ahead = from_behind(lax.slice_in_dim(cotangent, 0, 2, axis=1), "tm", -1)
-    longer = jnp.concatenate([cotangent, ahead], axis=1)
-    bordered = with_halo(longer, (("height", 2),), 1)
-    padded = jnp.pad(bordered, ((0, 0), (0, 0), (0, 0), (1, 1)))
-
     positions = frames * lax.axis_size("tm") * rows * lax.axis_size("height") * cols
-    cells_major = jnp.transpose(padded, (1, 2, 3, 0))
-    shifted = jnp.stack(
-        [cells_major[:, :, 2 - kw : 2 - kw + cols] for kw in range(3)], axis=0
-    )
     active_t = jnp.transpose(active.reshape(total, cells))
     sig = jax.nn.sigmoid(normed)
     slope = sig * (1.0 + normed * (1.0 - sig)) * norm_gain[:, None]
-    weight_t = jnp.transpose(conv_weight, (1, 2, 0))
+    part_dots = jnp.sum(partial * slope * flat_x, axis=0, keepdims=True)
+    packed = jnp.concatenate(
+        [
+            partial.reshape(n_chan, chans, cells),
+            jnp.broadcast_to(part_dots[None], (n_chan, 1, cells)),
+        ],
+        axis=1,
+    )
     local_sums = weight_taps(shifted, active_t, frames, rows)
-    packed = act_taps(
-        shifted, weight_t, slope * flat_x, local_sums[0, :8, :128], n_chan, frames, rows
-    )
     summed = group_sum(local_sums.reshape(27 * chans, total), ("height",), ("tm",))
     weight_grad = jnp.transpose(
         (summed / math.sqrt(positions)).reshape(27, chans, total), (1, 0, 2)

time: 150 us -> 153 us (1.020)
  the two profiles are of different devices: /device:TPU:0 before, /device:TPU:9 now
where the time goes in v9:
time: 153 us; the launch traced here: 150 us
  waiting for transfers between devices  50.8 us (33%)
  other arithmetic  24.8 us (16%)
  starting transfers between devices  24.4 us (16%)
  Pallas kernels  19.2 us (13%)
  local copies, waits for them, and re-layouts  16.7 us (11%)
  between operations  14.4 us (9%)
    ppermute x12, waiting for transfers between devices, exchange(): return lax.ppermute(block, axis, [(i, i ^ level) for i in range(size)])  27.7 us
    ppermute x12, starting transfers between devices, exchange(): return lax.ppermute(block, axis, [(i, i ^ level) for i in range(size)])  14.3 us
    pallas_call x1, Pallas kernels, act_taps(): pl.pallas_call(body, out_shape=jax.ShapeDtypeStruct((ins, cells), jnp.flo...  11 us
    ppermute x3, waiting for transfers between devices, gather_blocks(): lax.ppermute(block, axis, [(j, (j + d) % size) for j in range(size)])  9.08 us
    ppermute x1, waiting for transfers between devices, from_behind(): return lax.ppermute(block, axis, route)  8.38 us
    pallas_call x1, Pallas kernels, weight_taps(): pl.pallas_call(body, out_shape=jax.ShapeDtypeStruct((27, outs, ins), jnp....  8.27 us
    reduce_scatter x1, waiting for transfers between devices, on_device(): mine = lax.psum_scatter(packed, 'chan', scatter_dimension=0, tiled=True)[0]  5.6 us
    add x6, other arithmetic, halving_sum(): x = keep + exchange(send, axis, level)  5.47 us
  transfers between devices with their start and end apart: 19, of which 14 were waited for; matrix products, arithmetic and copies ran while one was open for 18% of the time, Pallas kernels for 7%

profile of v9, /device:TPU:9, one launch (start us, length us, event | category | flops | bytes accessed | tf_op | source)
XLA Modules:
  0.0 150.3 jit_solution(1303080757306181488)
XLA Ops:
  7.2 1.4 collective-permute-start
  9.7 8.4 %collective-permute-done = bf16[96,2,4,160]{0,3,2,1:T(8,128)(2,1)S(1)} collective-permute-done((bf16[96,2,4,160]{0,3,2,1:T(8,128)(2,1)}, bf16[96,2,4,160]{0,3,2,1:T(8,128)(2,1)S(1)}, u32[]{:S(2)}, u32[]{:S(2)}) %collective-permute-start) | collective-permute-done | bytes 245792 | tf_op jit(solution)/shard_map/ppermute | solution.py:14
  18.1 3.5 %collective-permute-start.2 = (bf16[96,4,1,160]{0,3,2,1:T(8,128)(2,1)S(1)}, bf16[96,4,1,160]{0,3,2,1:T(8,128)(2,1)S(1)}, u32[]{:S(2)}, u32[]{:S(2)}) collective-permute-start(bf16[96,4,1,160]{0,3,2,1:T(8,128)(2,1)S(1)} %get-tuple-element.17), channel_id=1, source_target_pairs={{4,0},{5,1},{6,2},{7,3},{12,8},{13,9},{14,10},{15,11},{20,16},{21,... | collective-permute-start | bytes 368648 | tf_op jit(solution)/shard_map/ppermute | solution.py:25
  23.0 2.6 %copy.9 = bf16[96,27,384]{0,2,1:T(8,128)(2,1)} copy(bf16[96,27,384]{2,0,1:T(8,128)(2,1)S(1)} %copy-done.7) | data formatting | bytes 3981312 | tf_op args[2]
  25.6 2.4 %collective-permute-start.4 = (bf16[96,2,4,160]{0,3,2,1:T(8,128)(2,1)S(1)}, bf16[96,2,4,160]{0,3,2,1:T(8,128)(2,1)S(1)}, u32[]{:S(2)}, u32[]{:S(2)}) collective-permute-start(bf16[96,2,4,160]{0,3,2,1:T(8,128)(2,1)S(1)} %copy-done.8), channel_id=1, source_target_pairs={{0,2},{1,3},{2,0},{3,1},{4,6},{5,7},{6,4},{7,5},{8,10},{9,11},{10,... | collective-permute-start | bytes 737288 | tf_op jit(solution)/shard_map/ppermute | solution.py:34
  31.4 2.3 %pad_maximum_fusion.cot_ref = bf16[3,4,6,160,96]{4,3,2,1,0:T(8,128)(2,1)} fusion(bf16[1,4,6,160,96]{4,3,2,1,0:T(8,128)(2,1)S(1)} %get-tuple-element.14, bf16[1,4,6,160,96]{4,3,2,1,0:T(8,128)(2,1)S(1)} %get-tuple-element.15, bf16[1,4,6,160,96]{4,3,2,1,0:T(8,128)(2,1)S(1)} %get-tuple-element.13), kind=kLoop, calls=%fused_computation.3 | loop fusion | flops 2211840 | bytes 4423680 | tf_op jit(solution)/shard_map/stack | solution.py:155
  33.7 11.0 %shard_map.68 = f32[384,1280]{1,0:T(8,128)} custom-call(bf16[3,4,6,160,96]{4,3,2,1,0:T(8,128)(2,1)} %pad_maximum_fusion.cot_ref, bf16[27,384,96]{2,1,0:T(8,128)(2,1)} %bitcast.71), custom_call_target="tpu_custom_call" | custom-call | flops 2548039680 | bytes 6168576 | tf_op jit(solution)/shard_map/pallas_call | solution.py:90
  44.7 1.9 %copy.10 = f32[384,1280]{0,1:T(8,128)S(1)} copy(f32[384,1280]{1,0:T(8,128)} %shard_map.68) | data formatting | bytes 3932160 | tf_op jit(solution)/shard_map/pallas_call | solution.py:90
  46.6 2.8 %collective-permute-done.4 = bf16[96,2,4,160]{0,3,2,1:T(8,128)(2,1)S(1)} collective-permute-done((bf16[96,2,4,160]{0,3,2,1:T(8,128)(2,1)S(1)}, bf16[96,2,4,160]{0,3,2,1:T(8,128)(2,1)S(1)}, u32[]{:S(2)}, u32[]{:S(2)}) %collective-permute-start.4) | collective-permute-done | bytes 245792 | tf_op jit(solution)/shard_map/ppermute | solution.py:34
  49.4 5.7 %collective-permute-done.5 = bf16[96,2,4,160]{0,3,2,1:T(8,128)(2,1)S(1)} collective-permute-done((bf16[96,2,4,160]{0,3,2,1:T(8,128)(2,1)S(1)}, bf16[96,2,4,160]{0,3,2,1:T(8,128)(2,1)S(1)}, u32[]{:S(2)}, u32[]{:S(2)}) %collective-permute-start.5) | collective-permute-done | bytes 245792 | tf_op jit(solution)/shard_map/ppermute | solution.py:34
  59.0 3.3 %fusion.14 = (f32[1280]{0:T(1024)S(1)}, f32[384,1280]{0,1:T(8,128)}, bf16[384,1280]{0,1:T(8,128)(2,1)}) fusion(f32[384,1280]{0,1:T(8,128)S(1)} %copy.10, bf16[96,2,4,160]{0,3,2,1:T(8,128)(2,1)S(1)} %get-tuple-element.10, bf16[96,2,4,160]{0,3,2,1:T(8,128)(2,1)S(1)} %get-tuple-element.11, bf16[96,2,4,160]{0,3,2,1:T(8,128)(2,1)S(1)} %get-tuple-element.12, ...), kind=kLoop, calls=%fused_computation.24 | loop fusion | flops 11795200 | bytes 5911552 | tf_op jit(solution)/shard_map/reduce_sum | solution.py:174
  62.3 8.3 %shard_map.69 = f32[27,96,384]{2,1,0:T(8,128)} custom-call(bf16[3,4,6,160,96]{4,3,2,1,0:T(8,128)(2,1)} %pad_maximum_fusion.cot_ref, bf16[1280,384]{1,0:T(8,128)(2,1)} %bitcast.72), custom_call_target="tpu_custom_call" | custom-call | flops 2548039680 | bytes 7176192 | tf_op jit(solution)/shard_map/pallas_call | solution.py:57
  70.5 2.4 %fusion.28 = (f32[1296,384]{1,0:T(8,128)S(1)}, f32[1296,384]{1,0:T(8,128)S(1)}) fusion(f32[2592,384]{1,0:T(8,128)} %bitcast.70), kind=kLoop, calls=%fused_computation.68 | loop fusion | bytes 7962624 | tf_op jit(solution)/shard_map/slice | solution.py:141
  76.6 2.2 %copy.11 = f32[4,96,1280]{1,2,0:T(8,128)S(1)} copy(f32[4,96,1280]{2,1,0:T(8,128)} %bitcast.68) | data formatting | bytes 3932160 | tf_op jit(solution)/shard_map/reshape | solution.py:177
  78.9 1.7 %dynamic-slice_add_fusion = f32[648,384]{1,0:T(8,128)S(1)} fusion(f32[648,384]{1,0:T(8,128)} %collective-permute-done.12, f32[1296,384]{1,0:T(8,128)} %copy-done.2, s32[]{:T(128)S(6)} %select_n.277), kind=kLoop, calls=%fused_computation.32 | loop fusion | flops 248832 | bytes 2985988 | tf_op jit(solution)/shard_map/add | solution.py:125
  84.3 1.7 %collective-permute-start.7 = (f32[324,384]{1,0:T(8,128)}, f32[324,384]{1,0:T(8,128)}, u32[]{:S(2)}, u32[]{:S(2)}) collective-permute-start(f32[324,384]{1,0:T(8,128)} %constant_dynamic-slice_fusion.4), channel_id=1, source_target_pairs={{0,8},{8,0},{16,24},{24,16},{1,9},{9,1},{17,25},{25,17},{2,10},{10... | collective-permute-start | bytes 1493000 | tf_op jit(solution)/shard_map/ppermute | solution.py:117
  86.2 2.3 %pad_maximum_fusion.1 = f32[4,97,1280]{1,2,0:T(8,128)} fusion(f32[4,1,1280]{1,2,0:T(8,128)S(1)} %broadcast_in_dim.2, f32[4,96,1280]{1,2,0:T(8,128)S(1)} %copy.11), kind=kLoop, calls=%fused_computation.4 | loop fusion | flops 496640 | bytes 3973120 | tf_op jit(solution)/shard_map/concatenate | solution.py:175
  88.5 5.3 %collective-permute-done.13 = f32[324,384]{1,0:T(8,128)} collective-permute-done((f32[324,384]{1,0:T(8,128)S(1)}, f32[324,384]{1,0:T(8,128)}, u32[]{:S(2)}, u32[]{:S(2)}) %collective-permute-start.13) | collective-permute-done | bytes 497696 | tf_op jit(solution)/shard_map/ppermute | solution.py:117
  95.1 2.1 %collective-permute-start.14 = (f32[162,384]{1,0:T(8,128)S(1)}, f32[162,384]{1,0:T(8,128)S(1)}, u32[]{:S(2)}, u32[]{:S(2)}) collective-permute-start(f32[162,384]{1,0:T(8,128)S(1)} %constant_dynamic-slice_fusion), channel_id=1, source_target_pairs={{0,8},{8,0},{16,24},{24,16},{1,9},{9,1},{17,25},{25,17},{2,10},{10... | collective-permute-start | bytes 746504 | tf_op jit(solution)/shard_map/ppermute | solution.py:117
  99.6 3.3 %collective-permute-done.14 = f32[162,384]{1,0:T(8,128)S(1)} collective-permute-done((f32[162,384]{1,0:T(8,128)S(1)}, f32[162,384]{1,0:T(8,128)S(1)}, u32[]{:S(2)}, u32[]{:S(2)}) %collective-permute-start.14) | collective-permute-done | bytes 248864 | tf_op jit(solution)/shard_map/ppermute | solution.py:117
  104.2 1.5 collective-permute-done.8
  106.6 2.8 %collective-permute-done.15 = f32[162,384]{1,0:T(8,128)S(1)} collective-permute-done((f32[162,384]{1,0:T(8,128)S(1)}, f32[162,384]{1,0:T(8,128)S(1)}, u32[]{:S(2)}, u32[]{:S(2)}) %collective-permute-start.15) | collective-permute-done | bytes 248864 | tf_op jit(solution)/shard_map/ppermute | solution.py:117
  109.9 1.8 %collective-permute-done.9 = f32[162,384]{1,0:T(8,128)S(1)} collective-permute-done((f32[162,384]{1,0:T(8,128)S(1)}, f32[162,384]{1,0:T(8,128)S(1)}, u32[]{:S(2)}, u32[]{:S(2)}) %collective-permute-start.9) | collective-permute-done | bytes 248864 | tf_op jit(solution)/shard_map/ppermute | solution.py:117
  111.8 1.8 %collective-permute-start.10 = (f32[324,384]{1,0:T(8,128)S(1)}, f32[324,384]{1,0:T(8,128)S(1)}, u32[]{:S(2)}, u32[]{:S(2)}) collective-permute-start(f32[324,384]{1,0:T(8,128)S(1)} %maximum_select_fusion.4), channel_id=1, source_target_pairs={{0,8},{8,0},{16,24},{24,16},{1,9},{9,1},{17,25},{25,17},{2,10},{10... | collective-permute-start | bytes 1493000 | tf_op jit(solution)/shard_map/ppermute | solution.py:117
  113.6 9.6 %collective-permute-done.16 = f32[324,384]{1,0:T(8,128)S(1)} collective-permute-done((f32[324,384]{1,0:T(8,128)S(1)}, f32[324,384]{1,0:T(8,128)S(1)}, u32[]{:S(2)}, u32[]{:S(2)}) %collective-permute-start.16) | collective-permute-done | bytes 497696 | tf_op jit(solution)/shard_map/ppermute | solution.py:117
  123.4 2.1 %collective-permute-start.17 = (f32[648,384]{1,0:T(8,128)S(1)}, f32[648,384]{1,0:T(8,128)S(1)}, u32[]{:S(2)}, u32[]{:S(2)}) collective-permute-start(f32[648,384]{1,0:T(8,128)S(1)} %maximum_select_fusion.3), channel_id=1, source_target_pairs={{0,4},{4,0},{1,5},{5,1},{2,6},{6,2},{3,7},{7,3},{8,12},{12,8},{9,1... | collective-permute-start | bytes 2985992 | tf_op jit(solution)/shard_map/ppermute | solution.py:117
  127.8 1.4 collective-permute-done.11
  129.2 1.8 %maximum_select_fusion = f32[1296,384]{1,0:T(8,128)S(1)} fusion(f32[648,384]{1,0:T(8,128)} %collective-permute-done.11, f32[648,384]{1,0:T(8,128)S(1)} %maximum_select_fusion.2, pred[]{:T(512)S(6)} %select_n.268), kind=kLoop, calls=%fused_computation.6 | loop fusion | flops 1492992 | bytes 3981313 | tf_op jit(solution)/shard_map/select_n | solution.py:128
  131.1 2.3 %maximum_multiply_fusion = f32[2592,384]{1,0:T(8,128)} fusion(f32[1296,384]{1,0:T(8,128)S(1)} %maximum_select_fusion.1, f32[1296,384]{1,0:T(8,128)S(1)} %maximum_select_fusion), kind=kLoop, calls=%fused_computation | loop fusion | flops 1990656 | bytes 7962624 | tf_op jit(solution)/shard_map/div | solution.py:185
  133.3 5.6 %reduce-scatter.2.cloned.1.call-done = f32[1,97,1280]{1,2,0:T(8,128)} async-done(((f32[4,97,1280]{1,2,0:T(8,128)}), f32[1,97,1280]{1,2,0:T(8,128)}) %reduce-scatter.2.cloned.1.call-update) | async-done | bytes 496656 | tf_op jit(solution)/shard_map/reduce_scatter | solution.py:188
  138.9 1.5 %slice_reduce_fusion = f32[1280]{0:T(1024)S(1)} fusion(f32[1,97,1280]{1,2,0:T(8,128)} %reduce-scatter.2.cloned.1.call-done), kind=kLoop, calls=%fused_computation.38 | loop fusion | bytes 10240 | tf_op jit(solution)/shard_map/slice | solution.py:190
  140.5 3.0 %fusion.24 = bf16[96,1280]{0,1:T(8,128)(2,1)} fusion(f32[1,97,1280]{1,2,0:T(8,128)} %reduce-scatter.2.cloned.1.call-done, f32[384,1280]{0,1:T(8,128)} %get-tuple-element.5, s32[]{:T(128)S(6)} %select_n.266, bf16[96,2,4,160]{0,3,2,1:T(8,128)(2,1)S(1)} %copy-done.9, bf16[96,2,4,160]{0,3,2,1:T(8,128)(2,1)S(1)} %copy-done.10, f32[1280]{0:T(1024)S(1)} %slice_reduce_fusion, ...), kind=kLoop, calls=%fused_computation.44 | loop fusion | flops 1228800 | bytes 1735684 | tf_op jit(solution)/shard_map/convert_element_type | solution.py:198
  (78 shorter events, 26.1 us)
Async XLA Ops:
  7.2 15.8 %copy-start.7 = (bf16[96,27,384]{2,0,1:T(8,128)(2,1)S(1)}, bf16[96,27,384]{2,0,1:T(8,128)(2,1)}, u32[]{:S(2)}) copy-start(bf16[96,27,384]{2,0,1:T(8,128)(2,1)} %param.7) | copy-start | bytes 5971972
  7.2 131.8 %reduce-scatter.2.cloned.1.call-start = ((), (), s32[]{:S(2)}) async-start(), calls=%async_computation.1 | async-start | bytes 3276800 | tf_op jit(solution)/shard_map/reduce_scatter | solution.py:188
  7.2 10.8 %collective-permute-start = (bf16[96,2,4,160]{0,3,2,1:T(8,128)(2,1)}, bf16[96,2,4,160]{0,3,2,1:T(8,128)(2,1)S(1)}, u32[]{:S(2)}, u32[]{:S(2)}) collective-permute-start(bf16[96,2,4,160]{0,3,2,1:T(8,128)(2,1)} %param.6), channel_id=1, source_target_pairs={{8,0},{16,8},{24,16},{9,1},{17,9},{25,17},{10,2},{18,10},{26,18},{... | collective-permute-start | bytes 737288 | tf_op jit(solution)/shard_map/ppermute | solution.py:14
  18.1 7.5 %collective-permute-start.2 = (bf16[96,4,1,160]{0,3,2,1:T(8,128)(2,1)S(1)}, bf16[96,4,1,160]{0,3,2,1:T(8,128)(2,1)S(1)}, u32[]{:S(2)}, u32[]{:S(2)}) collective-permute-start(bf16[96,4,1,160]{0,3,2,1:T(8,128)(2,1)S(1)} %get-tuple-element.17), channel_id=1, source_target_pairs={{4,0},{5,1},{6,2},{7,3},{12,8},{13,9},{14,10},{15,11},{20,16},{21,... | collective-permute-start | bytes 368648 | tf_op jit(solution)/shard_map/ppermute | solution.py:25
  21.6 4.0 %collective-permute-start.1 = (bf16[96,4,1,160]{0,3,2,1:T(8,128)(2,1)S(1)}, bf16[96,4,1,160]{0,3,2,1:T(8,128)(2,1)}, u32[]{:S(2)}, u32[]{:S(2)}) collective-permute-start(bf16[96,4,1,160]{0,3,2,1:T(8,128)(2,1)S(1)} %get-tuple-element.16), channel_id=1, source_target_pairs={{0,4},{1,5},{2,6},{3,7},{8,12},{9,13},{10,14},{11,15},{16,20},{17,... | collective-permute-start | bytes 368648 | tf_op jit(solution)/shard_map/ppermute | solution.py:24
  23.0 2.6 %copy-start.8 = (bf16[96,2,4,160]{0,3,2,1:T(8,128)(2,1)S(1)}, bf16[96,2,4,160]{0,3,2,1:T(8,128)(2,1)}, u32[]{:S(2)}) copy-start(bf16[96,2,4,160]{0,3,2,1:T(8,128)(2,1)} %param.5) | copy-start | bytes 737284
  25.6 23.8 %collective-permute-start.4 = (bf16[96,2,4,160]{0,3,2,1:T(8,128)(2,1)S(1)}, bf16[96,2,4,160]{0,3,2,1:T(8,128)(2,1)S(1)}, u32[]{:S(2)}, u32[]{:S(2)}) collective-permute-start(bf16[96,2,4,160]{0,3,2,1:T(8,128)(2,1)S(1)} %copy-done.8), channel_id=1, source_target_pairs={{0,2},{1,3},{2,0},{3,1},{4,6},{5,7},{6,4},{7,5},{8,10},{9,11},{10,... | collective-permute-start | bytes 737288 | tf_op jit(solution)/shard_map/ppermute | solution.py:34
  28.0 27.1 %collective-permute-start.5 = (bf16[96,2,4,160]{0,3,2,1:T(8,128)(2,1)S(1)}, bf16[96,2,4,160]{0,3,2,1:T(8,128)(2,1)S(1)}, u32[]{:S(2)}, u32[]{:S(2)}) collective-permute-start(bf16[96,2,4,160]{0,3,2,1:T(8,128)(2,1)S(1)} %copy-done.8), channel_id=1, source_target_pairs={{0,3},{1,0},{2,1},{3,2},{4,7},{5,4},{6,5},{7,6},{8,11},{9,8},{10,9... | collective-permute-start | bytes 737288 | tf_op jit(solution)/shard_map/ppermute | solution.py:34
  28.2 28.3 %collective-permute-start.3 = (bf16[96,2,4,160]{0,3,2,1:T(8,128)(2,1)S(1)}, bf16[96,2,4,160]{0,3,2,1:T(8,128)(2,1)}, u32[]{:S(2)}, u32[]{:S(2)}) collective-permute-start(bf16[96,2,4,160]{0,3,2,1:T(8,128)(2,1)S(1)} %copy-done.8), channel_id=1, source_target_pairs={{0,1},{1,2},{2,3},{3,0},{4,5},{5,6},{6,7},{7,4},{8,9},{9,10},{10,1... | collective-permute-start | bytes 737288 | tf_op jit(solution)/shard_map/ppermute | solution.py:34
  46.6 12.4 %copy-start.13 = (f32[384]{0:T(512)S(1)}, f32[384]{0:T(512)}, u32[]{:S(2)}) copy-start(f32[384]{0:T(512)} %param.9) | copy-start | bytes 4612
  46.6 12.4 %copy-start.14 = (f32[384]{0:T(512)S(1)}, f32[384]{0:T(512)}, u32[]{:S(2)}) copy-start(f32[384]{0:T(512)} %param.8) | copy-start | bytes 4612
  49.4 5.7 %copy-start.11 = (bf16[96,2,4,160]{0,3,2,1:T(8,128)(2,1)}, bf16[96,2,4,160]{0,3,2,1:T(8,128)(2,1)S(1)}, u32[]{:S(2)}) copy-start(bf16[96,2,4,160]{0,3,2,1:T(8,128)(2,1)S(1)} %collective-permute-done.4) | copy-start | bytes 737284
  73.0 3.3 %copy-start = (f32[1296,384]{1,0:T(8,128)}, f32[1296,384]{1,0:T(8,128)S(1)}, u32[]{:S(2)}) copy-start(f32[1296,384]{1,0:T(8,128)S(1)} %get-tuple-element.6) | copy-start | bytes 5971972
  73.0 3.3 %copy-start.2 = (f32[1296,384]{1,0:T(8,128)}, f32[1296,384]{1,0:T(8,128)S(1)}, u32[]{:S(2)}) copy-start(f32[1296,384]{1,0:T(8,128)S(1)} %get-tuple-element.7) | copy-start | bytes 5971972
  74.2 4.7 %collective-permute-start.12 = (f32[648,384]{1,0:T(8,128)}, f32[648,384]{1,0:T(8,128)}, u32[]{:S(2)}, u32[]{:S(2)}) collective-permute-start(f32[648,384]{1,0:T(8,128)} %constant_dynamic-slice_fusion.2), channel_id=1, source_target_pairs={{0,4},{4,0},{1,5},{5,1},{2,6},{6,2},{3,7},{7,3},{8,12},{12,8},{9,1... | collective-permute-start | bytes 2985992 | tf_op jit(solution)/shard_map/ppermute | solution.py:117
  76.3 5.8 %collective-permute-start.6 = (f32[648,384]{1,0:T(8,128)}, f32[648,384]{1,0:T(8,128)}, u32[]{:S(2)}, u32[]{:S(2)}) collective-permute-start(f32[648,384]{1,0:T(8,128)} %constant_dynamic-slice_fusion.5), channel_id=1, source_target_pairs={{0,4},{4,0},{1,5},{5,1},{2,6},{6,2},{3,7},{7,3},{8,12},{12,8},{9,1... | collective-permute-start | bytes 2985992 | tf_op jit(solution)/shard_map/ppermute | solution.py:117
  78.9 3.2 %copy-start.1 = (f32[1296,384]{1,0:T(8,128)S(1)}, f32[1296,384]{1,0:T(8,128)}, u32[]{:S(2)}) copy-start(f32[1296,384]{1,0:T(8,128)} %copy-done) | copy-start | bytes 5971972
  80.7 13.1 %collective-permute-start.13 = (f32[324,384]{1,0:T(8,128)S(1)}, f32[324,384]{1,0:T(8,128)}, u32[]{:S(2)}, u32[]{:S(2)}) collective-permute-start(f32[324,384]{1,0:T(8,128)S(1)} %constant_dynamic-slice_fusion.1), channel_id=1, source_target_pairs={{0,16},{8,24},{16,0},{24,8},{1,17},{9,25},{17,1},{25,9},{2,18},{10... | collective-permute-start | bytes 1493000 | tf_op jit(solution)/shard_map/ppermute | solution.py:117
  83.4 2.6 %copy-start.3 = (f32[648,384]{1,0:T(8,128)}, f32[648,384]{1,0:T(8,128)S(1)}, u32[]{:S(2)}) copy-start(f32[648,384]{1,0:T(8,128)S(1)} %dynamic-slice_add_fusion.1) | copy-start | bytes 2985988
  84.3 13.4 %collective-permute-start.7 = (f32[324,384]{1,0:T(8,128)}, f32[324,384]{1,0:T(8,128)}, u32[]{:S(2)}, u32[]{:S(2)}) collective-permute-start(f32[324,384]{1,0:T(8,128)} %constant_dynamic-slice_fusion.4), channel_id=1, source_target_pairs={{0,8},{8,0},{16,24},{24,16},{1,9},{9,1},{17,25},{25,17},{2,10},{10... | collective-permute-start | bytes 1493000 | tf_op jit(solution)/shard_map/ppermute | solution.py:117
  88.5 5.3 %copy-start.6 = (f32[648,384]{1,0:T(8,128)S(1)}, f32[648,384]{1,0:T(8,128)}, u32[]{:S(2)}) copy-start(f32[648,384]{1,0:T(8,128)} %copy-done.5) | copy-start | bytes 2985988
  88.5 9.2 %copy-start.4 = (f32[648,384]{1,0:T(8,128)S(1)}, f32[648,384]{1,0:T(8,128)}, u32[]{:S(2)}) copy-start(f32[648,384]{1,0:T(8,128)} %copy-done.3) | copy-start | bytes 2985988
  95.1 7.8 %collective-permute-start.14 = (f32[162,384]{1,0:T(8,128)S(1)}, f32[162,384]{1,0:T(8,128)S(1)}, u32[]{:S(2)}, u32[]{:S(2)}) collective-permute-start(f32[162,384]{1,0:T(8,128)S(1)} %constant_dynamic-slice_fusion), channel_id=1, source_target_pairs={{0,8},{8,0},{16,24},{24,16},{1,9},{9,1},{17,25},{25,17},{2,10},{10... | collective-permute-start | bytes 746504 | tf_op jit(solution)/shard_map/ppermute | solution.py:117
  98.8 6.8 %collective-permute-start.8 = (f32[162,384]{1,0:T(8,128)S(1)}, f32[162,384]{1,0:T(8,128)S(1)}, u32[]{:S(2)}, u32[]{:S(2)}) collective-permute-start(f32[162,384]{1,0:T(8,128)S(1)} %constant_dynamic-slice_fusion.3), channel_id=1, source_target_pairs={{0,16},{8,24},{16,0},{24,8},{1,17},{9,25},{17,1},{25,9},{2,18},{10... | collective-permute-start | bytes 746504 | tf_op jit(solution)/shard_map/ppermute | solution.py:117
  103.0 6.4 %collective-permute-start.15 = (f32[162,384]{1,0:T(8,128)S(1)}, f32[162,384]{1,0:T(8,128)S(1)}, u32[]{:S(2)}, u32[]{:S(2)}) collective-permute-start(f32[162,384]{1,0:T(8,128)S(1)} %dynamic-slice_add_fusion.4), channel_id=1, source_target_pairs={{0,8},{8,0},{16,24},{24,16},{1,9},{9,1},{17,25},{25,17},{2,10},{10... | collective-permute-start | bytes 746504 | tf_op jit(solution)/shard_map/ppermute | solution.py:117
  105.7 6.0 %collective-permute-start.9 = (f32[162,384]{1,0:T(8,128)S(1)}, f32[162,384]{1,0:T(8,128)S(1)}, u32[]{:S(2)}, u32[]{:S(2)}) collective-permute-start(f32[162,384]{1,0:T(8,128)S(1)} %dynamic-slice_add_fusion.5), channel_id=1, source_target_pairs={{0,16},{8,24},{16,0},{24,8},{1,17},{9,25},{17,1},{25,9},{2,18},{10... | collective-permute-start | bytes 746504 | tf_op jit(solution)/shard_map/ppermute | solution.py:117
  109.5 13.7 %collective-permute-start.16 = (f32[324,384]{1,0:T(8,128)S(1)}, f32[324,384]{1,0:T(8,128)S(1)}, u32[]{:S(2)}, u32[]{:S(2)}) collective-permute-start(f32[324,384]{1,0:T(8,128)S(1)} %maximum_select_fusion.5), channel_id=1, source_target_pairs={{0,16},{8,24},{16,0},{24,8},{1,17},{9,25},{17,1},{25,9},{2,18},{10... | collective-permute-start | bytes 1493000 | tf_op jit(solution)/shard_map/ppermute | solution.py:117
  111.8 13.6 %collective-permute-start.10 = (f32[324,384]{1,0:T(8,128)S(1)}, f32[324,384]{1,0:T(8,128)S(1)}, u32[]{:S(2)}, u32[]{:S(2)}) collective-permute-start(f32[324,384]{1,0:T(8,128)S(1)} %maximum_select_fusion.4), channel_id=1, source_target_pairs={{0,8},{8,0},{16,24},{24,16},{1,9},{9,1},{17,25},{25,17},{2,10},{10... | collective-permute-start | bytes 1493000 | tf_op jit(solution)/shard_map/ppermute | solution.py:117
  123.4 4.3 %collective-permute-start.17 = (f32[648,384]{1,0:T(8,128)S(1)}, f32[648,384]{1,0:T(8,128)S(1)}, u32[]{:S(2)}, u32[]{:S(2)}) collective-permute-start(f32[648,384]{1,0:T(8,128)S(1)} %maximum_select_fusion.3), channel_id=1, source_target_pairs={{0,4},{4,0},{1,5},{5,1},{2,6},{6,2},{3,7},{7,3},{8,12},{12,8},{9,1... | collective-permute-start | bytes 2985992 | tf_op jit(solution)/shard_map/ppermute | solution.py:117
  125.6 3.6 %collective-permute-start.11 = (f32[648,384]{1,0:T(8,128)S(1)}, f32[648,384]{1,0:T(8,128)}, u32[]{:S(2)}, u32[]{:S(2)}) collective-permute-start(f32[648,384]{1,0:T(8,128)S(1)} %maximum_select_fusion.2), channel_id=1, source_target_pairs={{0,4},{4,0},{1,5},{5,1},{2,6},{6,2},{3,7},{7,3},{8,12},{12,8},{9,1... | collective-permute-start | bytes 2985992 | tf_op jit(solution)/shard_map/ppermute | solution.py:117
  131.0 9.4 %copy-start.9 = (bf16[96,2,4,160]{0,3,2,1:T(8,128)(2,1)S(1)}, bf16[96,2,4,160]{0,3,2,1:T(8,128)(2,1)}, u32[]{:S(2)}) copy-start(bf16[96,2,4,160]{0,3,2,1:T(8,128)(2,1)} %param.5) | copy-start | bytes 737284
  131.0 9.4 %copy-start.10 = (bf16[96,2,4,160]{0,3,2,1:T(8,128)(2,1)S(1)}, bf16[96,2,4,160]{0,3,2,1:T(8,128)(2,1)}, u32[]{:S(2)}) copy-start(bf16[96,2,4,160]{0,3,2,1:T(8,128)(2,1)} %param.6) | copy-start | bytes 737284
  (2 other events, 2.2 us)
Sparse Core Ops, SparseCore 0:
  88.7 50.2 reduce-scatter.1

commit v10 on v6

--- a/solution.py
+++ b/solution.py
@@ -114,12 +114,13 @@
         keep = lax.dynamic_slice_in_dim(x, bit * m, m, 0)
         send = lax.dynamic_slice_in_dim(x, (1 - bit) * m, m, 0)
         x = keep + exchange(send, axis, level)
-    for axis, level, bit in reversed(steps):
+    for axis, level, bit in reversed(steps[1:]):
         got = exchange(x, axis, level)
         x = lax.select_n(
             bit, jnp.concatenate([x, got], axis=0), jnp.concatenate([got, x], axis=0)
         )
-    return x
+    axis, level, bit = steps[0]
+    return x, exchange(x, axis, level), bit
 
 
 def group_sum(x, near, far):
@@ -129,9 +130,14 @@
     padded_rows = -(-rows // unit) * unit
     x = jnp.pad(x, ((0, padded_rows - rows), (0, 0)))
     half = padded_rows // 2
-    first = halving_sum(x[:half], near_steps + far_steps)
-    second = halving_sum(x[half:], near_steps + far_steps[::-1])
-    return jnp.concatenate([first, second], axis=0)[:rows]
+    mine1, got1, bit = halving_sum(x[:half], near_steps + far_steps)
+    mine2, got2, _ = halving_sum(x[half:], near_steps + far_steps[::-1])
+    both = lax.select_n(
+        bit,
+        jnp.concatenate([mine1, got1, mine2, got2], axis=0),
+        jnp.concatenate([got1, mine1, got2, mine2], axis=0),
+    )
+    return both[:rows]
 
 
 def on_device(features, cotangent, conv_weight, norm_gain, norm_bias):

time: 148 us -> 148 us (level)
  starting transfers between devices: 20.7 us -> 24.1 us
  waiting for transfers between devices: 53.2 us -> 50.1 us
    select_n x6 -> x4, other arithmetic: 3.94 us -> 0.43 us  [halving_sum(): lax.select_n(bit, jnp.concatenate([x, got], axis=0), jnp.concatenate([got...]
    ppermute x12, starting transfers between devices: 10.6 us -> 13.9 us  [exchange(): return lax.ppermute(block, axis, [(i, i ^ level) for i in range(size)])]
    div x1, other arithmetic: 2.28 us -> 5.21 us  [on_device(): summed / math.sqrt(positions)]
    ppermute x12, waiting for transfers between devices: 31.8 us -> 29.3 us  [exchange(): return lax.ppermute(block, axis, [(i, i ^ level) for i in range(size)])]
    unnamed x25 -> x27, local copies, waits for them, and re-layouts: 4.75 us -> 5.49 us
  transfers between devices with their start and end apart: 19 -> 19, of which waited for: 11 -> 8; matrix products, arithmetic and copies ran while one was open for 20% -> 20% of each run, Pallas kernels for 0% -> 0%
where the time goes in v10:
time: 148 us; the launch traced here: 147 us
  waiting for transfers between devices  50.1 us (34%)
  starting transfers between devices  24.1 us (16%)
  other arithmetic  23.9 us (16%)
  Pallas kernels  17.7 us (12%)
  local copies, waits for them, and re-layouts  17 us (11%)
  between operations  14.4 us (10%)
    ppermute x12, waiting for transfers between devices, exchange(): return lax.ppermute(block, axis, [(i, i ^ level) for i in range(size)])  29.3 us
    ppermute x3, waiting for transfers between devices, gather_blocks(): lax.ppermute(block, axis, [(j, (j + d) % size) for j in range(size)])  20.7 us
    pallas_call x1, Pallas kernels, tap_kernel(): pl.pallas_call(body, out_shape=(jax.ShapeDtypeStruct((27, outs, ins), jnp...  17.7 us
    ppermute x12, starting transfers between devices, exchange(): return lax.ppermute(block, axis, [(i, i ^ level) for i in range(size)])  13.9 us
    unnamed x27, local copies, waits for them, and re-layouts  5.49 us
    div x1, other arithmetic, on_device(): summed / math.sqrt(positions)  5.21 us
    add x6, other arithmetic, halving_sum(): x = keep + exchange(send, axis, level)  4.32 us
    ppermute x3, starting transfers between devices, gather_blocks(): lax.ppermute(block, axis, [(j, (j + d) % size) for j in range(size)])  3.83 us
  transfers between devices with their start and end apart: 19, of which 8 were waited for; matrix products, arithmetic and copies ran while one was open for 20% of the time, Pallas kernels for 0%

profile of v10, /device:TPU:9, one launch (start us, length us, event | category | flops | bytes accessed | tf_op | source)
XLA Modules:
  0.0 147.1 jit_solution(15258265295079440210)
XLA Ops:
  7.2 1.3 collective-permute-start
  9.6 1.4 collective-permute-start.2
  12.4 4.3 %copy.14 = bf16[96,27,384]{0,2,1:T(8,128)(2,1)} copy(bf16[96,27,384]{2,0,1:T(8,128)(2,1)} %param.7) | data formatting | bytes 3981312 | tf_op args[2]
  17.7 18.6 %collective-permute-done.1 = bf16[96,2,4,160]{0,3,2,1:T(8,128)(2,1)S(1)} collective-permute-done((bf16[96,2,4,160]{0,3,2,1:T(8,128)(2,1)}, bf16[96,2,4,160]{0,3,2,1:T(8,128)(2,1)S(1)}, u32[]{:S(2)}, u32[]{:S(2)}) %collective-permute-start.1) | collective-permute-done | bytes 245792 | tf_op jit(solution)/shard_map/ppermute | solution.py:34
  37.0 2.1 %collective-permute-done.2 = bf16[96,2,4,160]{0,3,2,1:T(8,128)(2,1)} collective-permute-done((bf16[96,2,4,160]{0,3,2,1:T(8,128)(2,1)}, bf16[96,2,4,160]{0,3,2,1:T(8,128)(2,1)}, u32[]{:S(2)}, u32[]{:S(2)}) %collective-permute-start.2) | collective-permute-done | bytes 245792 | tf_op jit(solution)/shard_map/ppermute | solution.py:34
  39.2 2.1 %select_select_fusion.3 = (bf16[96,2,4,160]{0,3,2,1:T(8,128)(2,1)S(1)}, bf16[96,2,4,160]{0,3,2,1:T(8,128)(2,1)S(1)}, bf16[96,2,4,160]{0,3,2,1:T(8,128)(2,1)S(1)}...) fusion(bf16[96,2,4,160]{0,3,2,1:T(8,128)(2,1)} %copy-done.10, bf16[96,2,4,160]{0,3,2,1:T(8,128)(2,1)} %collective-permute-done.2, ...), kind=kLoop, calls=%fused_computation.41 | loop fusion | flops 1597440 | bytes 2457612 | tf_op jit(solution)/shard_map/select_n | solution.py:38
  42.5 1.8 %maximum_convert_fusion = f32[384,2,4,160]{0,3,2,1:T(8,128)} fusion(bf16[96,2,4,160]{0,3,2,1:T(8,128)(2,1)S(1)} %get-tuple-element.14, bf16[96,2,4,160]{0,3,2,1:T(8,128)(2,1)S(1)} %get-tuple-element.15, bf16[96,2,4,160]{0,3,2,1:T(8,128)(2,1)S(1)} %get-tuple-element.16, bf16[96,2,4,160]{0,3,2,1:T(8,128)(2,1)S(1)} %get-tuple-element.13), kind=kLoop, calls=%fused_computation.24 | loop fusion | flops 3932160 | bytes 2949120 | tf_op jit(solution)/shard_map/convert_element_type | solution.py:149
  44.3 1.9 %copy.13 = f32[384,1280]{1,0:T(8,128)S(1)} copy(f32[384,1280]{0,1:T(8,128)} %bitcast.35) | data formatting | bytes 3932160 | tf_op jit(solution)/shard_map/convert_element_type | solution.py:149
  46.3 1.3 collective-permute-start.4
  47.6 3.7 %collective-permute-start.5 = (bf16[96,4,1,160]{0,3,2,1:T(8,128)(2,1)S(1)}, bf16[96,4,1,160]{0,3,2,1:T(8,128)(2,1)}, u32[]{:S(2)}, u32[]{:S(2)}) collective-permute-start(bf16[96,4,1,160]{0,3,2,1:T(8,128)(2,1)S(1)} %get-tuple-element.21), channel_id=1, source_target_pairs={{4,0},{5,1},{6,2},{7,3},{12,8},{13,9},{14,10},{15,11},{20,16},{21,... | collective-permute-start | bytes 368648 | tf_op jit(solution)/shard_map/ppermute | solution.py:25
  51.4 3.0 %multiply_multiply_fusion = (f32[384,1280]{1,0:T(8,128)}, bf16[1280,384]{0,1:T(8,128)(2,1)S(1)}, f32[384,1280]{1,0:T(8,128)}) fusion(f32[384,1280]{1,0:T(8,128)S(1)} %copy.13, f32[384]{0:T(512)S(1)} %copy-done.11, f32[384]{0:T(512)S(1)} %copy-done.12, f32[1280]{0:T(1024)S(1)} %rsqrt.15), kind=kLoop, calls=%fused_computation.6 | loop fusion | flops 6881280 | bytes 6889472 | tf_op jit(solution)/shard_map/mul | solution.py:166
  54.3 1.3 copy.16.act_ref
  57.6 2.3 %pad_maximum_fusion.cot_ref = bf16[3,4,6,160,96]{4,3,2,1,0:T(8,128)(2,1)} fusion(bf16[1,4,6,160,96]{4,3,2,1,0:T(8,128)(2,1)S(1)} %get-tuple-element.18, bf16[1,4,6,160,96]{4,3,2,1,0:T(8,128)(2,1)S(1)} %get-tuple-element.19, bf16[1,4,6,160,96]{4,3,2,1,0:T(8,128)(2,1)S(1)} %get-tuple-element.17), kind=kLoop, calls=%fused_computation.4 | loop fusion | flops 2211840 | bytes 4423680 | tf_op jit(solution)/shard_map/stack | solution.py:161
  59.9 17.7 %shard_map.68 = (f32[27,96,384]{2,1,0:T(8,128)}, f32[4,97,1280]{2,1,0:T(8,128)}) custom-call(bf16[3,4,6,160,96]{4,3,2,1,0:T(8,128)(2,1)} %pad_maximum_fusion.cot_ref, bf16[1280,384]{1,0:T(8,128)(2,1)} %copy.16.act_ref, bf16[27,384,96]{2,1,0:T(8,128)(2,1)} %bitcast.38, f32[384,1280]{1,0:T(8,128)} %get-tuple-element.12.sx_ref), custom_call_target="tpu_custom_call" | custom-call | flops 5096079360 | bytes 13119488 | tf_op jit(solution)/shard_map/pallas_call | solution.py:73
  77.6 2.4 %fusion.15 = (f32[1296,384]{1,0:T(8,128)S(1)}, f32[1296,384]{1,0:T(8,128)S(1)}) fusion(f32[2592,384]{1,0:T(8,128)} %bitcast.37), kind=kLoop, calls=%fused_computation.56 | loop fusion | bytes 7962624 | tf_op jit(solution)/shard_map/slice | solution.py:133
  81.8 2.2 %collective-permute-done.12 = f32[648,384]{1,0:T(8,128)} collective-permute-done((f32[648,384]{1,0:T(8,128)}, f32[648,384]{1,0:T(8,128)}, u32[]{:S(2)}, u32[]{:S(2)}) %collective-permute-start.12) | collective-permute-done | bytes 995360 | tf_op jit(solution)/shard_map/ppermute | solution.py:108
  84.0 1.6 %dynamic-slice_add_fusion = f32[648,384]{1,0:T(8,128)S(1)} fusion(f32[648,384]{1,0:T(8,128)} %collective-permute-done.12, f32[1296,384]{1,0:T(8,128)} %copy-done, s32[]{:T(128)S(6)} %select_n.274), kind=kLoop, calls=%fused_computation.19 | loop fusion | flops 248832 | bytes 2985988 | tf_op jit(solution)/shard_map/add | solution.py:116
  85.7 1.3 collective-permute-start.13
  87.0 1.3 dynamic-slice_add_fusion.1
  88.4 1.3 collective-permute-start.7
  89.7 9.1 %collective-permute-done.13 = f32[324,384]{1,0:T(8,128)} collective-permute-done((f32[324,384]{1,0:T(8,128)S(1)}, f32[324,384]{1,0:T(8,128)}, u32[]{:S(2)}, u32[]{:S(2)}) %collective-permute-start.13) | collective-permute-done | bytes 497696 | tf_op jit(solution)/shard_map/ppermute | solution.py:108
  100.1 1.3 collective-permute-start.14
  102.8 4.2 %collective-permute-done.14 = f32[162,384]{1,0:T(8,128)S(1)} collective-permute-done((f32[162,384]{1,0:T(8,128)S(1)}, f32[162,384]{1,0:T(8,128)S(1)}, u32[]{:S(2)}, u32[]{:S(2)}) %collective-permute-start.14) | collective-permute-done | bytes 248864 | tf_op jit(solution)/shard_map/ppermute | solution.py:108
  107.1 1.3 collective-permute-start.15
  108.4 1.3 collective-permute-start.9
  109.7 3.5 %collective-permute-done.15 = f32[162,384]{1,0:T(8,128)S(1)} collective-permute-done((f32[162,384]{1,0:T(8,128)S(1)}, f32[162,384]{1,0:T(8,128)S(1)}, u32[]{:S(2)}, u32[]{:S(2)}) %collective-permute-start.15) | collective-permute-done | bytes 248864 | tf_op jit(solution)/shard_map/ppermute | solution.py:108
  113.3 1.3 collective-permute-start.16
  114.7 1.3 collective-permute-start.10
  116.0 9.2 %collective-permute-done.16 = f32[324,384]{1,0:T(8,128)S(1)} collective-permute-done((f32[324,384]{1,0:T(8,128)S(1)}, f32[324,384]{1,0:T(8,128)S(1)}, u32[]{:S(2)}, u32[]{:S(2)}) %collective-permute-start.16) | collective-permute-done | bytes 497696 | tf_op jit(solution)/shard_map/ppermute | solution.py:108
  125.3 2.9 %collective-permute-start.17 = (f32[648,384]{1,0:T(8,128)S(1)}, f32[648,384]{1,0:T(8,128)}, u32[]{:S(2)}, u32[]{:S(2)}) collective-permute-start(f32[648,384]{1,0:T(8,128)S(1)} %maximum_select_fusion.2), channel_id=1, source_target_pairs={{0,4},{4,0},{1,5},{5,1},{2,6},{6,2},{3,7},{7,3},{8,12},{12,8},{9,1... | collective-permute-start | bytes 2985992 | tf_op jit(solution)/shard_map/ppermute | solution.py:108
  131.9 5.2 %fusion = f32[2592,384]{1,0:T(8,128)} fusion(f32[648,384]{1,0:T(8,128)} %collective-permute-done.17, f32[648,384]{1,0:T(8,128)S(1)} %maximum_select_fusion.2, f32[648,384]{1,0:T(8,128)} %collective-permute-done.11, f32[648,384]{1,0:T(8,128)S(1)} %maximum_select_fusion.1, pred[]{:T(512)S(6)} %select_n.265), kind=kLoop, calls=%fused_computation.1 | loop fusion | flops 7962624 | bytes 7962625 | tf_op jit(solution)/shard_map/div | solution.py:173
  138.0 1.4 fusion.13
  (73 shorter events, 17.7 us)
Async XLA Ops:
  7.2 130.0 %reduce-scatter.2.cloned.1.call-start = ((), (), s32[]{:S(2)}) async-start(), calls=%async_computation.1 | async-start | bytes 2662400 | tf_op jit(solution)/shard_map/reduce_scatter | solution.py:176
  7.2 10.5 %collective-permute-start = (bf16[96,2,4,160]{0,3,2,1:T(8,128)(2,1)}, bf16[96,2,4,160]{0,3,2,1:T(8,128)(2,1)S(1)}, u32[]{:S(2)}, u32[]{:S(2)}) collective-permute-start(bf16[96,2,4,160]{0,3,2,1:T(8,128)(2,1)} %param.5), channel_id=1, source_target_pairs={{0,1},{1,2},{2,3},{3,0},{4,5},{5,6},{6,7},{7,4},{8,9},{9,10},{10,1... | collective-permute-start | bytes 737288 | tf_op jit(solution)/shard_map/ppermute | solution.py:34
  8.6 27.8 %collective-permute-start.1 = (bf16[96,2,4,160]{0,3,2,1:T(8,128)(2,1)}, bf16[96,2,4,160]{0,3,2,1:T(8,128)(2,1)S(1)}, u32[]{:S(2)}, u32[]{:S(2)}) collective-permute-start(bf16[96,2,4,160]{0,3,2,1:T(8,128)(2,1)} %param.5), channel_id=1, source_target_pairs={{0,2},{1,3},{2,0},{3,1},{4,6},{5,7},{6,4},{7,5},{8,10},{9,11},{10,... | collective-permute-start | bytes 737288 | tf_op jit(solution)/shard_map/ppermute | solution.py:34
  9.6 29.5 %collective-permute-start.2 = (bf16[96,2,4,160]{0,3,2,1:T(8,128)(2,1)}, bf16[96,2,4,160]{0,3,2,1:T(8,128)(2,1)}, u32[]{:S(2)}, u32[]{:S(2)}) collective-permute-start(bf16[96,2,4,160]{0,3,2,1:T(8,128)(2,1)} %param.5), channel_id=1, source_target_pairs={{0,3},{1,0},{2,1},{3,2},{4,7},{5,4},{6,5},{7,6},{8,11},{9,8},{10,9... | collective-permute-start | bytes 737288 | tf_op jit(solution)/shard_map/ppermute | solution.py:34
  11.0 35.2 %collective-permute-start.3 = (bf16[96,2,4,160]{0,3,2,1:T(8,128)(2,1)}, bf16[96,2,4,160]{0,3,2,1:T(8,128)(2,1)S(1)}, u32[]{:S(2)}, u32[]{:S(2)}) collective-permute-start(bf16[96,2,4,160]{0,3,2,1:T(8,128)(2,1)} %param.6), channel_id=1, source_target_pairs={{8,0},{16,8},{24,16},{9,1},{17,9},{25,17},{10,2},{18,10},{26,18},{... | collective-permute-start | bytes 737288 | tf_op jit(solution)/shard_map/ppermute | solution.py:14
  12.4 4.3 %copy-start.8 = (bf16[96,2,4,160]{0,3,2,1:T(8,128)(2,1)S(1)}, bf16[96,2,4,160]{0,3,2,1:T(8,128)(2,1)}, u32[]{:S(2)}) copy-start(bf16[96,2,4,160]{0,3,2,1:T(8,128)(2,1)} %param.6) | copy-start | bytes 737284
  12.4 26.7 %copy-start.9 = (bf16[96,2,4,160]{0,3,2,1:T(8,128)(2,1)S(1)}, bf16[96,2,4,160]{0,3,2,1:T(8,128)(2,1)}, u32[]{:S(2)}) copy-start(bf16[96,2,4,160]{0,3,2,1:T(8,128)(2,1)} %param.5) | copy-start | bytes 737284
  36.3 0.7 copy-start.10
  44.3 7.1 %copy-start.11 = (f32[384]{0:T(512)S(1)}, f32[384]{0:T(512)}, u32[]{:S(2)}) copy-start(f32[384]{0:T(512)} %param.9) | copy-start | bytes 4612
  44.3 7.1 %copy-start.12 = (f32[384]{0:T(512)S(1)}, f32[384]{0:T(512)}, u32[]{:S(2)}) copy-start(f32[384]{0:T(512)} %param.8) | copy-start | bytes 4612
  46.3 1.3 copy-start.3
  46.3 9.3 %collective-permute-start.4 = (bf16[96,4,1,160]{0,3,2,1:T(8,128)(2,1)S(1)}, bf16[96,4,1,160]{0,3,2,1:T(8,128)(2,1)S(1)}, u32[]{:S(2)}, u32[]{:S(2)}) collective-permute-start(bf16[96,4,1,160]{0,3,2,1:T(8,128)(2,1)S(1)} %get-tuple-element.20), channel_id=1, source_target_pairs={{0,4},{1,5},{2,6},{3,7},{8,12},{9,13},{10,14},{11,15},{16,20},{17,... | collective-permute-start | bytes 368648 | tf_op jit(solution)/shard_map/ppermute | solution.py:24
  47.6 8.0 %collective-permute-start.5 = (bf16[96,4,1,160]{0,3,2,1:T(8,128)(2,1)S(1)}, bf16[96,4,1,160]{0,3,2,1:T(8,128)(2,1)}, u32[]{:S(2)}, u32[]{:S(2)}) collective-permute-start(bf16[96,4,1,160]{0,3,2,1:T(8,128)(2,1)S(1)} %get-tuple-element.21), channel_id=1, source_target_pairs={{4,0},{5,1},{6,2},{7,3},{12,8},{13,9},{14,10},{15,11},{20,16},{21,... | collective-permute-start | bytes 368648 | tf_op jit(solution)/shard_map/ppermute | solution.py:25
  54.3 1.3 copy-start.4
  80.0 1.6 %copy-start = (f32[1296,384]{1,0:T(8,128)}, f32[1296,384]{1,0:T(8,128)S(1)}, u32[]{:S(2)}) copy-start(f32[1296,384]{1,0:T(8,128)S(1)} %get-tuple-element.9) | copy-start | bytes 5971972
  81.1 2.9 %collective-permute-start.12 = (f32[648,384]{1,0:T(8,128)}, f32[648,384]{1,0:T(8,128)}, u32[]{:S(2)}, u32[]{:S(2)}) collective-permute-start(f32[648,384]{1,0:T(8,128)} %constant_dynamic-slice_fusion.2), channel_id=1, source_target_pairs={{0,4},{4,0},{1,5},{5,1},{2,6},{6,2},{3,7},{7,3},{8,12},{12,8},{9,1... | collective-permute-start | bytes 2985992 | tf_op jit(solution)/shard_map/ppermute | solution.py:108
  81.6 5.4 %collective-permute-start.6 = (f32[648,384]{1,0:T(8,128)S(1)}, f32[648,384]{1,0:T(8,128)}, u32[]{:S(2)}, u32[]{:S(2)}) collective-permute-start(f32[648,384]{1,0:T(8,128)S(1)} %constant_dynamic-slice_fusion.5), channel_id=1, source_target_pairs={{0,4},{4,0},{1,5},{5,1},{2,6},{6,2},{3,7},{7,3},{8,12},{12,8},{9,1... | collective-permute-start | bytes 2985992 | tf_op jit(solution)/shard_map/ppermute | solution.py:108
  85.6 2.7 %copy-start.1 = (f32[648,384]{1,0:T(8,128)}, f32[648,384]{1,0:T(8,128)S(1)}, u32[]{:S(2)}) copy-start(f32[648,384]{1,0:T(8,128)S(1)} %dynamic-slice_add_fusion) | copy-start | bytes 2985988
  85.7 13.1 %collective-permute-start.13 = (f32[324,384]{1,0:T(8,128)S(1)}, f32[324,384]{1,0:T(8,128)}, u32[]{:S(2)}, u32[]{:S(2)}) collective-permute-start(f32[324,384]{1,0:T(8,128)S(1)} %constant_dynamic-slice_fusion.1), channel_id=1, source_target_pairs={{0,16},{8,24},{16,0},{24,8},{1,17},{9,25},{17,1},{25,9},{2,18},{10... | collective-permute-start | bytes 1493000 | tf_op jit(solution)/shard_map/ppermute | solution.py:108
  88.4 13.0 %collective-permute-start.7 = (f32[324,384]{1,0:T(8,128)S(1)}, f32[324,384]{1,0:T(8,128)S(1)}, u32[]{:S(2)}, u32[]{:S(2)}) collective-permute-start(f32[324,384]{1,0:T(8,128)S(1)} %constant_dynamic-slice_fusion.4), channel_id=1, source_target_pairs={{0,8},{8,0},{16,24},{24,16},{1,9},{9,1},{17,25},{25,17},{2,10},{10... | collective-permute-start | bytes 1493000 | tf_op jit(solution)/shard_map/ppermute | solution.py:108
  100.1 6.9 %collective-permute-start.14 = (f32[162,384]{1,0:T(8,128)S(1)}, f32[162,384]{1,0:T(8,128)S(1)}, u32[]{:S(2)}, u32[]{:S(2)}) collective-permute-start(f32[162,384]{1,0:T(8,128)S(1)} %constant_dynamic-slice_fusion), channel_id=1, source_target_pairs={{0,8},{8,0},{16,24},{24,16},{1,9},{9,1},{17,25},{25,17},{2,10},{10... | collective-permute-start | bytes 746504 | tf_op jit(solution)/shard_map/ppermute | solution.py:108
  101.5 6.9 %collective-permute-start.8 = (f32[162,384]{1,0:T(8,128)S(1)}, f32[162,384]{1,0:T(8,128)S(1)}, u32[]{:S(2)}, u32[]{:S(2)}) collective-permute-start(f32[162,384]{1,0:T(8,128)S(1)} %constant_dynamic-slice_fusion.3), channel_id=1, source_target_pairs={{0,16},{8,24},{16,0},{24,8},{1,17},{9,25},{17,1},{25,9},{2,18},{10... | collective-permute-start | bytes 746504 | tf_op jit(solution)/shard_map/ppermute | solution.py:108
  107.1 6.1 %collective-permute-start.15 = (f32[162,384]{1,0:T(8,128)S(1)}, f32[162,384]{1,0:T(8,128)S(1)}, u32[]{:S(2)}, u32[]{:S(2)}) collective-permute-start(f32[162,384]{1,0:T(8,128)S(1)} %dynamic-slice_add_fusion.4), channel_id=1, source_target_pairs={{0,8},{8,0},{16,24},{24,16},{1,9},{9,1},{17,25},{25,17},{2,10},{10... | collective-permute-start | bytes 746504 | tf_op jit(solution)/shard_map/ppermute | solution.py:108
  108.4 6.1 %collective-permute-start.9 = (f32[162,384]{1,0:T(8,128)S(1)}, f32[162,384]{1,0:T(8,128)S(1)}, u32[]{:S(2)}, u32[]{:S(2)}) collective-permute-start(f32[162,384]{1,0:T(8,128)S(1)} %dynamic-slice_add_fusion.5), channel_id=1, source_target_pairs={{0,16},{8,24},{16,0},{24,8},{1,17},{9,25},{17,1},{25,9},{2,18},{10... | collective-permute-start | bytes 746504 | tf_op jit(solution)/shard_map/ppermute | solution.py:108
  113.3 11.8 %collective-permute-start.16 = (f32[324,384]{1,0:T(8,128)S(1)}, f32[324,384]{1,0:T(8,128)S(1)}, u32[]{:S(2)}, u32[]{:S(2)}) collective-permute-start(f32[324,384]{1,0:T(8,128)S(1)} %maximum_select_fusion.4), channel_id=1, source_target_pairs={{0,16},{8,24},{16,0},{24,8},{1,17},{9,25},{17,1},{25,9},{2,18},{10... | collective-permute-start | bytes 1493000 | tf_op jit(solution)/shard_map/ppermute | solution.py:108
  114.7 14.2 %copy-start.2 = (f32[96,1280]{0,1:T(8,128)S(1)}, f32[96,1280]{0,1:T(8,128)}, u32[]{:S(2)}) copy-start(f32[96,1280]{0,1:T(8,128)} %get-tuple-element.24) | copy-start | bytes 1474564
  114.7 13.5 %collective-permute-start.10 = (f32[324,384]{1,0:T(8,128)S(1)}, f32[324,384]{1,0:T(8,128)S(1)}, u32[]{:S(2)}, u32[]{:S(2)}) collective-permute-start(f32[324,384]{1,0:T(8,128)S(1)} %maximum_select_fusion.3), channel_id=1, source_target_pairs={{0,8},{8,0},{16,24},{24,16},{1,9},{9,1},{17,25},{25,17},{2,10},{10... | collective-permute-start | bytes 1493000 | tf_op jit(solution)/shard_map/ppermute | solution.py:108
  125.3 4.6 %copy-start.5 = (f32[96,1280]{0,1:T(8,128)S(1)}, f32[96,1280]{0,1:T(8,128)}, u32[]{:S(2)}) copy-start(f32[96,1280]{0,1:T(8,128)} %get-tuple-element.22) | copy-start | bytes 1474564
  125.3 5.6 %collective-permute-start.17 = (f32[648,384]{1,0:T(8,128)S(1)}, f32[648,384]{1,0:T(8,128)}, u32[]{:S(2)}, u32[]{:S(2)}) collective-permute-start(f32[648,384]{1,0:T(8,128)S(1)} %maximum_select_fusion.2), channel_id=1, source_target_pairs={{0,4},{4,0},{1,5},{5,1},{2,6},{6,2},{3,7},{7,3},{8,12},{12,8},{9,1... | collective-permute-start | bytes 2985992 | tf_op jit(solution)/shard_map/ppermute | solution.py:108
  128.3 3.6 %collective-permute-start.11 = (f32[648,384]{1,0:T(8,128)S(1)}, f32[648,384]{1,0:T(8,128)}, u32[]{:S(2)}, u32[]{:S(2)}) collective-permute-start(f32[648,384]{1,0:T(8,128)S(1)} %maximum_select_fusion.1), channel_id=1, source_target_pairs={{0,4},{4,0},{1,5},{5,1},{2,6},{6,2},{3,7},{7,3},{8,12},{12,8},{9,1... | collective-permute-start | bytes 2985992 | tf_op jit(solution)/shard_map/ppermute | solution.py:108
  130.9 7.1 %copy-start.6 = (f32[96,1280]{1,0:T(8,128)S(1)}, f32[96,1280]{1,0:T(8,128)}, u32[]{:S(2)}) copy-start(f32[96,1280]{1,0:T(8,128)} %copy.18) | copy-start | bytes 1474564
  130.9 7.1 %copy-start.7 = (f32[96,1280]{1,0:T(8,128)S(1)}, f32[96,1280]{1,0:T(8,128)}, u32[]{:S(2)}) copy-start(f32[96,1280]{1,0:T(8,128)} %copy.17) | copy-start | bytes 1474564
Sparse Core Ops, SparseCore 0:
  81.9 41.7 reduce-scatter.1

commit v11 on v10

--- a/solution.py
+++ b/solution.py
@@ -17,12 +17,19 @@
 def with_halo(array, sides, width):
     for axis, dim in sides:
         size, length = (lax.axis_size(axis), array.shape[dim])
-        up = [(i, (i + 1) % size) for i in range(size - 1)]
-        down = [(j, i) for i, j in up]
         last = lax.slice_in_dim(array, length - width, length, axis=dim)
         first = lax.slice_in_dim(array, 0, width, axis=dim)
-        before = lax.ppermute(last, axis, up)
-        after = lax.ppermute(first, axis, down)
+        if size == 2:
+            me = lax.axis_index(axis)
+            got = lax.ppermute(lax.select_n(me, last, first), axis, [(0, 1), (1, 0)])
+            zero = jnp.zeros_like(got)
+            before = lax.select_n(me, zero, got)
+            after = lax.select_n(me, got, zero)
+        else:
+            up = [(i, (i + 1) % size) for i in range(size - 1)]
+            down = [(j, i) for i, j in up]
+            before = lax.ppermute(last, axis, up)
+            after = lax.ppermute(first, axis, down)
         array = jnp.concatenate([before, array, after], axis=dim)
     return array
 

time: 148 us -> 143 us (0.966)
  starting transfers between devices: 24.1 us -> 19.5 us
    ppermute x2 -> x1, starting transfers between devices: 5.01 us -> 0.49 us  [with_halo(): got = lax.ppermute(lax.select_n(me, last, first), axis, [(0, 1), (1, 0)])]
  transfers between devices with their start and end apart: 19 -> 18, of which waited for: 8 -> 8; matrix products, arithmetic and copies ran while one was open for 20% -> 20% of each run, Pallas kernels for 0% -> 0%
where the time goes in v11:
time: 143 us; the launch traced here: 142 us
  waiting for transfers between devices  50.1 us (35%)
  other arithmetic  22.9 us (16%)
  starting transfers between devices  19.5 us (14%)
  local copies, waits for them, and re-layouts  17.7 us (12%)
  Pallas kernels  17.7 us (12%)
  between operations  14.4 us (10%)
    ppermute x12, waiting for transfers between devices, exchange(): return lax.ppermute(block, axis, [(i, i ^ level) for i in range(size)])  29.4 us
    ppermute x3, waiting for transfers between devices, gather_blocks(): lax.ppermute(block, axis, [(j, (j + d) % size) for j in range(size)])  20.7 us
    pallas_call x1, Pallas kernels, tap_kernel(): pl.pallas_call(body, out_shape=(jax.ShapeDtypeStruct((27, outs, ins), jnp...  17.7 us
    ppermute x12, starting transfers between devices, exchange(): return lax.ppermute(block, axis, [(i, i ^ level) for i in range(size)])  13.9 us
    unnamed x27, local copies, waits for them, and re-layouts  6.26 us
    div x1, other arithmetic, on_device(): summed / math.sqrt(positions)  5.18 us
    add x6, other arithmetic, halving_sum(): x = keep + exchange(send, axis, level)  4.3 us
    ppermute x3, starting transfers between devices, gather_blocks(): lax.ppermute(block, axis, [(j, (j + d) % size) for j in range(size)])  3.83 us
  transfers between devices with their start and end apart: 18, of which 8 were waited for; matrix products, arithmetic and copies ran while one was open for 20% of the time, Pallas kernels for 0%

profile of v11, /device:TPU:9, one launch (start us, length us, event | category | flops | bytes accessed | tf_op | source)
XLA Modules:
  0.0 142.4 jit_solution(13428225904707277896)
XLA Ops:
  7.2 1.3 collective-permute-start
  9.6 1.4 collective-permute-start.2
  11.0 1.3 collective-permute-start.3
  12.5 4.3 %copy.14 = bf16[96,27,384]{0,2,1:T(8,128)(2,1)} copy(bf16[96,27,384]{2,0,1:T(8,128)(2,1)} %param.7) | data formatting | bytes 3981312 | tf_op args[2]
  17.7 18.6 %collective-permute-done.1 = bf16[96,2,4,160]{0,3,2,1:T(8,128)(2,1)S(1)} collective-permute-done((bf16[96,2,4,160]{0,3,2,1:T(8,128)(2,1)}, bf16[96,2,4,160]{0,3,2,1:T(8,128)(2,1)S(1)}, u32[]{:S(2)}, u32[]{:S(2)}) %collective-permute-start.1) | collective-permute-done | bytes 245792 | tf_op jit(solution)/shard_map/ppermute | solution.py:41
  37.0 2.1 %collective-permute-done.2 = bf16[96,2,4,160]{0,3,2,1:T(8,128)(2,1)} collective-permute-done((bf16[96,2,4,160]{0,3,2,1:T(8,128)(2,1)}, bf16[96,2,4,160]{0,3,2,1:T(8,128)(2,1)}, u32[]{:S(2)}, u32[]{:S(2)}) %collective-permute-start.2) | collective-permute-done | bytes 245792 | tf_op jit(solution)/shard_map/ppermute | solution.py:41
  39.2 2.1 %select_select_fusion.3 = (bf16[96,2,4,160]{0,3,2,1:T(8,128)(2,1)S(1)}, bf16[96,2,4,160]{0,3,2,1:T(8,128)(2,1)S(1)}, bf16[96,2,4,160]{0,3,2,1:T(8,128)(2,1)S(1)}...) fusion(bf16[96,2,4,160]{0,3,2,1:T(8,128)(2,1)} %copy-done.10, bf16[96,2,4,160]{0,3,2,1:T(8,128)(2,1)} %collective-permute-done.2, ...), kind=kLoop, calls=%fused_computation.41 | loop fusion | flops 1597440 | bytes 2457612 | tf_op jit(solution)/shard_map/select_n | solution.py:45
  42.4 1.8 %maximum_convert_fusion = f32[384,2,4,160]{0,3,2,1:T(8,128)} fusion(bf16[96,2,4,160]{0,3,2,1:T(8,128)(2,1)S(1)} %get-tuple-element.14, bf16[96,2,4,160]{0,3,2,1:T(8,128)(2,1)S(1)} %get-tuple-element.15, bf16[96,2,4,160]{0,3,2,1:T(8,128)(2,1)S(1)} %get-tuple-element.16, bf16[96,2,4,160]{0,3,2,1:T(8,128)(2,1)S(1)} %get-tuple-element.13), kind=kLoop, calls=%fused_computation.24 | loop fusion | flops 3932160 | bytes 2949120 | tf_op jit(solution)/shard_map/convert_element_type | solution.py:156
  44.3 1.9 %copy.13 = f32[384,1280]{1,0:T(8,128)S(1)} copy(f32[384,1280]{0,1:T(8,128)} %bitcast.35) | data formatting | bytes 3932160 | tf_op jit(solution)/shard_map/convert_element_type | solution.py:156
  47.6 3.0 %multiply_multiply_fusion = (f32[384,1280]{1,0:T(8,128)}, bf16[1280,384]{0,1:T(8,128)(2,1)S(1)}, f32[384,1280]{1,0:T(8,128)}) fusion(f32[384,1280]{1,0:T(8,128)S(1)} %copy.13, f32[384]{0:T(512)S(1)} %copy-done.11, f32[384]{0:T(512)S(1)} %copy-done.12, f32[1280]{0:T(1024)S(1)} %rsqrt.15), kind=kLoop, calls=%fused_computation.6 | loop fusion | flops 6881280 | bytes 6889472 | tf_op jit(solution)/shard_map/mul | solution.py:173
  50.6 1.3 copy.16.act_ref
  53.0 2.3 %pad_maximum_fusion.cot_ref = bf16[3,4,6,160,96]{4,3,2,1,0:T(8,128)(2,1)} fusion(bf16[1,4,6,160,96]{4,3,2,1,0:T(8,128)(2,1)S(1)} %get-tuple-element.18, bf16[1,4,6,160,96]{4,3,2,1,0:T(8,128)(2,1)S(1)} %get-tuple-element.19, bf16[1,4,6,160,96]{4,3,2,1,0:T(8,128)(2,1)S(1)} %get-tuple-element.17), kind=kLoop, calls=%fused_computation.4 | loop fusion | flops 2211840 | bytes 4423680 | tf_op jit(solution)/shard_map/stack | solution.py:168
  55.3 17.7 %shard_map.68 = (f32[27,96,384]{2,1,0:T(8,128)}, f32[4,97,1280]{2,1,0:T(8,128)}) custom-call(bf16[3,4,6,160,96]{4,3,2,1,0:T(8,128)(2,1)} %pad_maximum_fusion.cot_ref, bf16[1280,384]{1,0:T(8,128)(2,1)} %copy.16.act_ref, bf16[27,384,96]{2,1,0:T(8,128)(2,1)} %bitcast.38, f32[384,1280]{1,0:T(8,128)} %get-tuple-element.12.sx_ref), custom_call_target="tpu_custom_call" | custom-call | flops 5096079360 | bytes 13119488 | tf_op jit(solution)/shard_map/pallas_call | solution.py:80
  72.9 2.4 %fusion.15 = (f32[1296,384]{1,0:T(8,128)S(1)}, f32[1296,384]{1,0:T(8,128)S(1)}) fusion(f32[2592,384]{1,0:T(8,128)} %bitcast.37), kind=kLoop, calls=%fused_computation.59 | loop fusion | bytes 7962624 | tf_op jit(solution)/shard_map/slice | solution.py:140
  77.2 2.2 %collective-permute-done.11 = f32[648,384]{1,0:T(8,128)} collective-permute-done((f32[648,384]{1,0:T(8,128)}, f32[648,384]{1,0:T(8,128)}, u32[]{:S(2)}, u32[]{:S(2)}) %collective-permute-start.11) | collective-permute-done | bytes 995360 | tf_op jit(solution)/shard_map/ppermute | solution.py:115
  79.4 1.6 %dynamic-slice_add_fusion = f32[648,384]{1,0:T(8,128)S(1)} fusion(f32[648,384]{1,0:T(8,128)} %collective-permute-done.11, f32[1296,384]{1,0:T(8,128)} %copy-done, s32[]{:T(128)S(6)} %select_n.298), kind=kLoop, calls=%fused_computation.19 | loop fusion | flops 248832 | bytes 2985988 | tf_op jit(solution)/shard_map/add | solution.py:123
  81.1 1.3 collective-permute-start.12
  82.4 1.3 dynamic-slice_add_fusion.1
  83.8 1.3 collective-permute-start.6
  85.0 9.2 %collective-permute-done.12 = f32[324,384]{1,0:T(8,128)} collective-permute-done((f32[324,384]{1,0:T(8,128)S(1)}, f32[324,384]{1,0:T(8,128)}, u32[]{:S(2)}, u32[]{:S(2)}) %collective-permute-start.12) | collective-permute-done | bytes 497696 | tf_op jit(solution)/shard_map/ppermute | solution.py:115
  95.5 1.3 collective-permute-start.13
  96.9 1.3 collective-permute-start.7
  98.2 4.3 %collective-permute-done.13 = f32[162,384]{1,0:T(8,128)S(1)} collective-permute-done((f32[162,384]{1,0:T(8,128)S(1)}, f32[162,384]{1,0:T(8,128)S(1)}, u32[]{:S(2)}, u32[]{:S(2)}) %collective-permute-start.13) | collective-permute-done | bytes 248864 | tf_op jit(solution)/shard_map/ppermute | solution.py:115
  102.5 1.3 collective-permute-start.14
  103.8 1.3 collective-permute-start.8
  105.1 3.5 %collective-permute-done.14 = f32[162,384]{1,0:T(8,128)S(1)} collective-permute-done((f32[162,384]{1,0:T(8,128)S(1)}, f32[162,384]{1,0:T(8,128)S(1)}, u32[]{:S(2)}, u32[]{:S(2)}) %collective-permute-start.14) | collective-permute-done | bytes 248864 | tf_op jit(solution)/shard_map/ppermute | solution.py:115
  108.7 1.3 collective-permute-start.15
  110.0 1.3 collective-permute-start.9
  111.3 9.1 %collective-permute-done.15 = f32[324,384]{1,0:T(8,128)S(1)} collective-permute-done((f32[324,384]{1,0:T(8,128)S(1)}, f32[324,384]{1,0:T(8,128)S(1)}, u32[]{:S(2)}, u32[]{:S(2)}) %collective-permute-start.15) | collective-permute-done | bytes 497696 | tf_op jit(solution)/shard_map/ppermute | solution.py:115
  120.6 2.9 %collective-permute-start.16 = (f32[648,384]{1,0:T(8,128)S(1)}, f32[648,384]{1,0:T(8,128)}, u32[]{:S(2)}, u32[]{:S(2)}) collective-permute-start(f32[648,384]{1,0:T(8,128)S(1)} %maximum_select_fusion.2), channel_id=1, source_target_pairs={{0,4},{4,0},{1,5},{5,1},{2,6},{6,2},{3,7},{7,3},{8,12},{12,8},{9,1... | collective-permute-start | bytes 2985992 | tf_op jit(solution)/shard_map/ppermute | solution.py:115
  127.3 5.2 %fusion = f32[2592,384]{1,0:T(8,128)} fusion(f32[648,384]{1,0:T(8,128)} %collective-permute-done.16, f32[648,384]{1,0:T(8,128)S(1)} %maximum_select_fusion.2, f32[648,384]{1,0:T(8,128)} %collective-permute-done.10, f32[648,384]{1,0:T(8,128)S(1)} %maximum_select_fusion.1, pred[]{:T(512)S(6)} %select_n.289), kind=kLoop, calls=%fused_computation.1 | loop fusion | flops 7962624 | bytes 7962625 | tf_op jit(solution)/shard_map/div | solution.py:180
  133.3 1.4 fusion.13
  (72 shorter events, 15.5 us)
Async XLA Ops:
  7.2 125.3 %reduce-scatter.2.cloned.1.call-start = ((), (), s32[]{:S(2)}) async-start(), calls=%async_computation.1 | async-start | bytes 2662400 | tf_op jit(solution)/shard_map/reduce_scatter | solution.py:183
  7.2 10.5 %collective-permute-start = (bf16[96,2,4,160]{0,3,2,1:T(8,128)(2,1)}, bf16[96,2,4,160]{0,3,2,1:T(8,128)(2,1)S(1)}, u32[]{:S(2)}, u32[]{:S(2)}) collective-permute-start(bf16[96,2,4,160]{0,3,2,1:T(8,128)(2,1)} %param.5), channel_id=1, source_target_pairs={{0,1},{1,2},{2,3},{3,0},{4,5},{5,6},{6,7},{7,4},{8,9},{9,10},{10,1... | collective-permute-start | bytes 737288 | tf_op jit(solution)/shard_map/ppermute | solution.py:41
  8.6 27.8 %collective-permute-start.1 = (bf16[96,2,4,160]{0,3,2,1:T(8,128)(2,1)}, bf16[96,2,4,160]{0,3,2,1:T(8,128)(2,1)S(1)}, u32[]{:S(2)}, u32[]{:S(2)}) collective-permute-start(bf16[96,2,4,160]{0,3,2,1:T(8,128)(2,1)} %param.5), channel_id=1, source_target_pairs={{0,2},{1,3},{2,0},{3,1},{4,6},{5,7},{6,4},{7,5},{8,10},{9,11},{10,... | collective-permute-start | bytes 737288 | tf_op jit(solution)/shard_map/ppermute | solution.py:41
  9.6 29.5 %collective-permute-start.2 = (bf16[96,2,4,160]{0,3,2,1:T(8,128)(2,1)}, bf16[96,2,4,160]{0,3,2,1:T(8,128)(2,1)}, u32[]{:S(2)}, u32[]{:S(2)}) collective-permute-start(bf16[96,2,4,160]{0,3,2,1:T(8,128)(2,1)} %param.5), channel_id=1, source_target_pairs={{0,3},{1,0},{2,1},{3,2},{4,7},{5,4},{6,5},{7,6},{8,11},{9,8},{10,9... | collective-permute-start | bytes 737288 | tf_op jit(solution)/shard_map/ppermute | solution.py:41
  11.0 35.2 %collective-permute-start.3 = (bf16[96,2,4,160]{0,3,2,1:T(8,128)(2,1)}, bf16[96,2,4,160]{0,3,2,1:T(8,128)(2,1)S(1)}, u32[]{:S(2)}, u32[]{:S(2)}) collective-permute-start(bf16[96,2,4,160]{0,3,2,1:T(8,128)(2,1)} %param.6), channel_id=1, source_target_pairs={{8,0},{16,8},{24,16},{9,1},{17,9},{25,17},{10,2},{18,10},{26,18},{... | collective-permute-start | bytes 737288 | tf_op jit(solution)/shard_map/ppermute | solution.py:14
  12.4 4.3 %copy-start.8 = (bf16[96,2,4,160]{0,3,2,1:T(8,128)(2,1)S(1)}, bf16[96,2,4,160]{0,3,2,1:T(8,128)(2,1)}, u32[]{:S(2)}) copy-start(bf16[96,2,4,160]{0,3,2,1:T(8,128)(2,1)} %param.6) | copy-start | bytes 737284
  12.4 26.7 %copy-start.9 = (bf16[96,2,4,160]{0,3,2,1:T(8,128)(2,1)S(1)}, bf16[96,2,4,160]{0,3,2,1:T(8,128)(2,1)}, u32[]{:S(2)}) copy-start(bf16[96,2,4,160]{0,3,2,1:T(8,128)(2,1)} %param.5) | copy-start | bytes 737284
  36.3 0.7 copy-start.10
  44.3 3.3 %copy-start.11 = (f32[384]{0:T(512)S(1)}, f32[384]{0:T(512)}, u32[]{:S(2)}) copy-start(f32[384]{0:T(512)} %param.9) | copy-start | bytes 4612
  44.3 3.3 %copy-start.12 = (f32[384]{0:T(512)S(1)}, f32[384]{0:T(512)}, u32[]{:S(2)}) copy-start(f32[384]{0:T(512)} %param.8) | copy-start | bytes 4612
  46.3 0.8 copy-start.3
  47.1 4.8 %collective-permute-start.4 = (bf16[96,4,1,160]{0,3,2,1:T(8,128)(2,1)S(1)}, bf16[96,4,1,160]{0,3,2,1:T(8,128)(2,1)S(1)}, u32[]{:S(2)}, u32[]{:S(2)}) collective-permute-start(bf16[96,4,1,160]{0,3,2,1:T(8,128)(2,1)S(1)} %slice_select_fusion), channel_id=1, source_target_pairs={{0,4},{4,0},{1,5},{5,1},{2,6},{6,2},{3,7},{7,3},{8,12},{12,8},{9,1... | collective-permute-start | bytes 368648 | tf_op jit(solution)/shard_map/ppermute | solution.py:24
  50.6 1.4 copy-start.4
  75.4 1.6 %copy-start = (f32[1296,384]{1,0:T(8,128)}, f32[1296,384]{1,0:T(8,128)S(1)}, u32[]{:S(2)}) copy-start(f32[1296,384]{1,0:T(8,128)S(1)} %get-tuple-element.9) | copy-start | bytes 5971972
  76.5 2.9 %collective-permute-start.11 = (f32[648,384]{1,0:T(8,128)}, f32[648,384]{1,0:T(8,128)}, u32[]{:S(2)}, u32[]{:S(2)}) collective-permute-start(f32[648,384]{1,0:T(8,128)} %constant_dynamic-slice_fusion.2), channel_id=1, source_target_pairs={{0,4},{4,0},{1,5},{5,1},{2,6},{6,2},{3,7},{7,3},{8,12},{12,8},{9,1... | collective-permute-start | bytes 2985992 | tf_op jit(solution)/shard_map/ppermute | solution.py:115
  77.0 5.4 %collective-permute-start.5 = (f32[648,384]{1,0:T(8,128)S(1)}, f32[648,384]{1,0:T(8,128)}, u32[]{:S(2)}, u32[]{:S(2)}) collective-permute-start(f32[648,384]{1,0:T(8,128)S(1)} %constant_dynamic-slice_fusion.5), channel_id=1, source_target_pairs={{0,4},{4,0},{1,5},{5,1},{2,6},{6,2},{3,7},{7,3},{8,12},{12,8},{9,1... | collective-permute-start | bytes 2985992 | tf_op jit(solution)/shard_map/ppermute | solution.py:115
  81.0 2.7 %copy-start.1 = (f32[648,384]{1,0:T(8,128)}, f32[648,384]{1,0:T(8,128)S(1)}, u32[]{:S(2)}) copy-start(f32[648,384]{1,0:T(8,128)S(1)} %dynamic-slice_add_fusion) | copy-start | bytes 2985988
  81.1 13.1 %collective-permute-start.12 = (f32[324,384]{1,0:T(8,128)S(1)}, f32[324,384]{1,0:T(8,128)}, u32[]{:S(2)}, u32[]{:S(2)}) collective-permute-start(f32[324,384]{1,0:T(8,128)S(1)} %constant_dynamic-slice_fusion.1), channel_id=1, source_target_pairs={{0,16},{8,24},{16,0},{24,8},{1,17},{9,25},{17,1},{25,9},{2,18},{10... | collective-permute-start | bytes 1493000 | tf_op jit(solution)/shard_map/ppermute | solution.py:115
  83.8 13.0 %collective-permute-start.6 = (f32[324,384]{1,0:T(8,128)S(1)}, f32[324,384]{1,0:T(8,128)S(1)}, u32[]{:S(2)}, u32[]{:S(2)}) collective-permute-start(f32[324,384]{1,0:T(8,128)S(1)} %constant_dynamic-slice_fusion.4), channel_id=1, source_target_pairs={{0,8},{8,0},{16,24},{24,16},{1,9},{9,1},{17,25},{25,17},{2,10},{10... | collective-permute-start | bytes 1493000 | tf_op jit(solution)/shard_map/ppermute | solution.py:115
  95.5 6.9 %collective-permute-start.13 = (f32[162,384]{1,0:T(8,128)S(1)}, f32[162,384]{1,0:T(8,128)S(1)}, u32[]{:S(2)}, u32[]{:S(2)}) collective-permute-start(f32[162,384]{1,0:T(8,128)S(1)} %constant_dynamic-slice_fusion), channel_id=1, source_target_pairs={{0,8},{8,0},{16,24},{24,16},{1,9},{9,1},{17,25},{25,17},{2,10},{10... | collective-permute-start | bytes 746504 | tf_op jit(solution)/shard_map/ppermute | solution.py:115
  96.9 6.9 %collective-permute-start.7 = (f32[162,384]{1,0:T(8,128)S(1)}, f32[162,384]{1,0:T(8,128)S(1)}, u32[]{:S(2)}, u32[]{:S(2)}) collective-permute-start(f32[162,384]{1,0:T(8,128)S(1)} %constant_dynamic-slice_fusion.3), channel_id=1, source_target_pairs={{0,16},{8,24},{16,0},{24,8},{1,17},{9,25},{17,1},{25,9},{2,18},{10... | collective-permute-start | bytes 746504 | tf_op jit(solution)/shard_map/ppermute | solution.py:115
  102.5 6.1 %collective-permute-start.14 = (f32[162,384]{1,0:T(8,128)S(1)}, f32[162,384]{1,0:T(8,128)S(1)}, u32[]{:S(2)}, u32[]{:S(2)}) collective-permute-start(f32[162,384]{1,0:T(8,128)S(1)} %dynamic-slice_add_fusion.4), channel_id=1, source_target_pairs={{0,8},{8,0},{16,24},{24,16},{1,9},{9,1},{17,25},{25,17},{2,10},{10... | collective-permute-start | bytes 746504 | tf_op jit(solution)/shard_map/ppermute | solution.py:115
  103.8 6.2 %collective-permute-start.8 = (f32[162,384]{1,0:T(8,128)S(1)}, f32[162,384]{1,0:T(8,128)S(1)}, u32[]{:S(2)}, u32[]{:S(2)}) collective-permute-start(f32[162,384]{1,0:T(8,128)S(1)} %dynamic-slice_add_fusion.5), channel_id=1, source_target_pairs={{0,16},{8,24},{16,0},{24,8},{1,17},{9,25},{17,1},{25,9},{2,18},{10... | collective-permute-start | bytes 746504 | tf_op jit(solution)/shard_map/ppermute | solution.py:115
  108.7 11.7 %collective-permute-start.15 = (f32[324,384]{1,0:T(8,128)S(1)}, f32[324,384]{1,0:T(8,128)S(1)}, u32[]{:S(2)}, u32[]{:S(2)}) collective-permute-start(f32[324,384]{1,0:T(8,128)S(1)} %maximum_select_fusion.4), channel_id=1, source_target_pairs={{0,16},{8,24},{16,0},{24,8},{1,17},{9,25},{17,1},{25,9},{2,18},{10... | collective-permute-start | bytes 1493000 | tf_op jit(solution)/shard_map/ppermute | solution.py:115
  110.0 14.2 %copy-start.2 = (f32[96,1280]{0,1:T(8,128)S(1)}, f32[96,1280]{0,1:T(8,128)}, u32[]{:S(2)}) copy-start(f32[96,1280]{0,1:T(8,128)} %get-tuple-element.22) | copy-start | bytes 1474564
  110.0 13.5 %collective-permute-start.9 = (f32[324,384]{1,0:T(8,128)S(1)}, f32[324,384]{1,0:T(8,128)S(1)}, u32[]{:S(2)}, u32[]{:S(2)}) collective-permute-start(f32[324,384]{1,0:T(8,128)S(1)} %maximum_select_fusion.3), channel_id=1, source_target_pairs={{0,8},{8,0},{16,24},{24,16},{1,9},{9,1},{17,25},{25,17},{2,10},{10... | collective-permute-start | bytes 1493000 | tf_op jit(solution)/shard_map/ppermute | solution.py:115
  120.6 4.6 %copy-start.5 = (f32[96,1280]{0,1:T(8,128)S(1)}, f32[96,1280]{0,1:T(8,128)}, u32[]{:S(2)}) copy-start(f32[96,1280]{0,1:T(8,128)} %get-tuple-element.20) | copy-start | bytes 1474564
  120.6 5.7 %collective-permute-start.16 = (f32[648,384]{1,0:T(8,128)S(1)}, f32[648,384]{1,0:T(8,128)}, u32[]{:S(2)}, u32[]{:S(2)}) collective-permute-start(f32[648,384]{1,0:T(8,128)S(1)} %maximum_select_fusion.2), channel_id=1, source_target_pairs={{0,4},{4,0},{1,5},{5,1},{2,6},{6,2},{3,7},{7,3},{8,12},{12,8},{9,1... | collective-permute-start | bytes 2985992 | tf_op jit(solution)/shard_map/ppermute | solution.py:115
  123.7 3.6 %collective-permute-start.10 = (f32[648,384]{1,0:T(8,128)S(1)}, f32[648,384]{1,0:T(8,128)}, u32[]{:S(2)}, u32[]{:S(2)}) collective-permute-start(f32[648,384]{1,0:T(8,128)S(1)} %maximum_select_fusion.1), channel_id=1, source_target_pairs={{0,4},{4,0},{1,5},{5,1},{2,6},{6,2},{3,7},{7,3},{8,12},{12,8},{9,1... | collective-permute-start | bytes 2985992 | tf_op jit(solution)/shard_map/ppermute | solution.py:115
  126.2 7.0 %copy-start.6 = (f32[96,1280]{1,0:T(8,128)S(1)}, f32[96,1280]{1,0:T(8,128)}, u32[]{:S(2)}) copy-start(f32[96,1280]{1,0:T(8,128)} %copy.18) | copy-start | bytes 1474564
  126.3 7.0 %copy-start.7 = (f32[96,1280]{1,0:T(8,128)S(1)}, f32[96,1280]{1,0:T(8,128)}, u32[]{:S(2)}) copy-start(f32[96,1280]{1,0:T(8,128)} %copy.17) | copy-start | bytes 1474564
Sparse Core Ops, SparseCore 0:
  77.3 42.3 reduce-scatter.1

commit v12 on v11

--- a/solution.py
+++ b/solution.py
@@ -121,13 +121,12 @@
         keep = lax.dynamic_slice_in_dim(x, bit * m, m, 0)
         send = lax.dynamic_slice_in_dim(x, (1 - bit) * m, m, 0)
         x = keep + exchange(send, axis, level)
-    for axis, level, bit in reversed(steps[1:]):
+    for axis, level, bit in reversed(steps):
         got = exchange(x, axis, level)
         x = lax.select_n(
             bit, jnp.concatenate([x, got], axis=0), jnp.concatenate([got, x], axis=0)
         )
-    axis, level, bit = steps[0]
-    return x, exchange(x, axis, level), bit
+    return x
 
 
 def group_sum(x, near, far):
@@ -136,15 +135,21 @@
     rows = x.shape[0]
     padded_rows = -(-rows // unit) * unit
     x = jnp.pad(x, ((0, padded_rows - rows), (0, 0)))
-    half = padded_rows // 2
-    mine1, got1, bit = halving_sum(x[:half], near_steps + far_steps)
-    mine2, got2, _ = halving_sum(x[half:], near_steps + far_steps[::-1])
-    both = lax.select_n(
-        bit,
-        jnp.concatenate([mine1, got1, mine2, got2], axis=0),
-        jnp.concatenate([got1, mine1, got2, mine2], axis=0),
-    )
-    return both[:rows]
+    for axis, level, bit in near_steps:
+        m = x.shape[0] // 2
+        keep = lax.dynamic_slice_in_dim(x, bit * m, m, 0)
+        send = lax.dynamic_slice_in_dim(x, (1 - bit) * m, m, 0)
+        x = keep + exchange(send, axis, level)
+    half = x.shape[0] // 2
+    x = jnp.concatenate(
+        [halving_sum(x[:half], far_steps), halving_sum(x[half:], far_steps[::-1])], axis=0
+    )
+    for axis, level, bit in reversed(near_steps):
+        got = exchange(x, axis, level)
+        x = lax.select_n(
+            bit, jnp.concatenate([x, got], axis=0), jnp.concatenate([got, x], axis=0)
+        )
+    return x[:rows]
 
 
 def on_device(features, cotangent, conv_weight, norm_gain, norm_bias):

time: 143 us -> 145 us (1.014); the launches traced: 142 us -> 142 us
  waiting for transfers between devices: 50.1 us -> 53.5 us
  starting transfers between devices: 19.5 us -> 17.8 us
  local copies, waits for them, and re-layouts: 17.7 us -> 16.1 us
    ppermute x12 -> x10, waiting for transfers between devices: 29.4 us -> 32.7 us  [exchange(): return lax.ppermute(block, axis, [(i, i ^ level) for i in range(size)])]
    add x6 -> x4, other arithmetic: 4.3 us -> 1.25 us  [halving_sum(): x = keep + exchange(send, axis, level)]
    dynamic_slice x0 -> x1, local copies, waits for them, and re-layouts: none -> 2.98 us  [group_sum(): send = lax.dynamic_slice_in_dim(x, (1 - bit) * m, m, 0)]
    slice x1, local copies, waits for them, and re-layouts: 2.41 us -> 0.13 us  [group_sum(): x[:half]]
    add x0 -> x1, other arithmetic: none -> 1.75 us  [group_sum(): x = keep + exchange(send, axis, level)]
    ppermute x12 -> x10, starting transfers between devices: 13.9 us -> 12.2 us  [exchange(): return lax.ppermute(block, axis, [(i, i ^ level) for i in range(size)])]
    unnamed x27 -> x19, local copies, waits for them, and re-layouts: 6.26 us -> 5.84 us
  transfers between devices with their start and end apart: 18 -> 16, of which waited for: 8 -> 9; matrix products, arithmetic and copies ran while one was open for 20% -> 17% of each run, Pallas kernels for 0% -> 0%
where the time goes in v12:
time: 145 us; the launch traced here: 142 us
  waiting for transfers between devices  53.5 us (37%)
  other arithmetic  22.5 us (16%)
  starting transfers between devices  17.8 us (12%)
  Pallas kernels  17.6 us (12%)
  local copies, waits for them, and re-layouts  16.1 us (11%)
  between operations  14.4 us (10%)
    ppermute x10, waiting for transfers between devices, exchange(): return lax.ppermute(block, axis, [(i, i ^ level) for i in range(size)])  32.7 us
    ppermute x3, waiting for transfers between devices, gather_blocks(): lax.ppermute(block, axis, [(j, (j + d) % size) for j in range(size)])  20.7 us
    pallas_call x1, Pallas kernels, tap_kernel(): pl.pallas_call(body, out_shape=(jax.ShapeDtypeStruct((27, outs, ins), jnp...  17.6 us
    ppermute x10, starting transfers between devices, exchange(): return lax.ppermute(block, axis, [(i, i ^ level) for i in range(size)])  12.2 us
    unnamed x19, local copies, waits for them, and re-layouts  5.84 us
    div x1, other arithmetic, on_device(): summed / math.sqrt(positions)  4.53 us
    ppermute x3, starting transfers between devices, gather_blocks(): lax.ppermute(block, axis, [(j, (j + d) % size) for j in range(size)])  3.83 us
    mul x1, other arithmetic, on_device(): slope = sig * (1.0 + normed * (1.0 - sig)) * norm_gain[:, None]  2.99 us
  transfers between devices with their start and end apart: 16, of which 9 were waited for; matrix products, arithmetic and copies ran while one was open for 17% of the time, Pallas kernels for 0%

profile of v12, /device:TPU:9, one launch (start us, length us, event | category | flops | bytes accessed | tf_op | source)
XLA Modules:
  0.0 142.0 jit_solution(783844378274905044)
XLA Ops:
  7.2 1.3 collective-permute-start
  9.6 1.4 collective-permute-start.2
  11.0 1.3 collective-permute-start.3
  12.5 4.3 %copy.14 = bf16[96,27,384]{0,2,1:T(8,128)(2,1)} copy(bf16[96,27,384]{2,0,1:T(8,128)(2,1)} %param.7) | data formatting | bytes 3981312 | tf_op args[2]
  17.7 18.6 %collective-permute-done.1 = bf16[96,2,4,160]{0,3,2,1:T(8,128)(2,1)S(1)} collective-permute-done((bf16[96,2,4,160]{0,3,2,1:T(8,128)(2,1)}, bf16[96,2,4,160]{0,3,2,1:T(8,128)(2,1)S(1)}, u32[]{:S(2)}, u32[]{:S(2)}) %collective-permute-start.1) | collective-permute-done | bytes 245792 | tf_op jit(solution)/shard_map/ppermute | solution.py:41
  37.0 2.1 %collective-permute-done.2 = bf16[96,2,4,160]{0,3,2,1:T(8,128)(2,1)} collective-permute-done((bf16[96,2,4,160]{0,3,2,1:T(8,128)(2,1)}, bf16[96,2,4,160]{0,3,2,1:T(8,128)(2,1)}, u32[]{:S(2)}, u32[]{:S(2)}) %collective-permute-start.2) | collective-permute-done | bytes 245792 | tf_op jit(solution)/shard_map/ppermute | solution.py:41
  39.2 2.1 %select_select_fusion.3 = (bf16[96,2,4,160]{0,3,2,1:T(8,128)(2,1)S(1)}, bf16[96,2,4,160]{0,3,2,1:T(8,128)(2,1)S(1)}, bf16[96,2,4,160]{0,3,2,1:T(8,128)(2,1)S(1)}...) fusion(bf16[96,2,4,160]{0,3,2,1:T(8,128)(2,1)} %copy-done.6, bf16[96,2,4,160]{0,3,2,1:T(8,128)(2,1)} %collective-permute-done.2, ...), kind=kLoop, calls=%fused_computation.41 | loop fusion | flops 1597440 | bytes 2457612 | tf_op jit(solution)/shard_map/select_n | solution.py:45
  42.4 1.8 %maximum_convert_fusion = f32[384,2,4,160]{0,3,2,1:T(8,128)} fusion(bf16[96,2,4,160]{0,3,2,1:T(8,128)(2,1)S(1)} %get-tuple-element.14, bf16[96,2,4,160]{0,3,2,1:T(8,128)(2,1)S(1)} %get-tuple-element.15, bf16[96,2,4,160]{0,3,2,1:T(8,128)(2,1)S(1)} %get-tuple-element.16, bf16[96,2,4,160]{0,3,2,1:T(8,128)(2,1)S(1)} %get-tuple-element.13), kind=kLoop, calls=%fused_computation.24 | loop fusion | flops 3932160 | bytes 2949120 | tf_op jit(solution)/shard_map/convert_element_type | solution.py:161
  44.3 1.9 %copy.13 = f32[384,1280]{1,0:T(8,128)S(1)} copy(f32[384,1280]{0,1:T(8,128)} %bitcast.35) | data formatting | bytes 3932160 | tf_op jit(solution)/shard_map/convert_element_type | solution.py:161
  47.6 3.0 %multiply_multiply_fusion = (f32[384,1280]{1,0:T(8,128)}, bf16[1280,384]{0,1:T(8,128)(2,1)S(1)}, f32[384,1280]{1,0:T(8,128)}) fusion(f32[384,1280]{1,0:T(8,128)S(1)} %copy.13, f32[384]{0:T(512)S(1)} %copy-done.7, f32[384]{0:T(512)S(1)} %copy-done.8, f32[1280]{0:T(1024)S(1)} %rsqrt.15), kind=kLoop, calls=%fused_computation.8 | loop fusion | flops 6881280 | bytes 6889472 | tf_op jit(solution)/shard_map/mul | solution.py:178
  50.6 1.3 copy.16.act_ref
  53.0 2.3 %pad_maximum_fusion.cot_ref = bf16[3,4,6,160,96]{4,3,2,1,0:T(8,128)(2,1)} fusion(bf16[1,4,6,160,96]{4,3,2,1,0:T(8,128)(2,1)S(1)} %get-tuple-element.18, bf16[1,4,6,160,96]{4,3,2,1,0:T(8,128)(2,1)S(1)} %get-tuple-element.19, bf16[1,4,6,160,96]{4,3,2,1,0:T(8,128)(2,1)S(1)} %get-tuple-element.17), kind=kLoop, calls=%fused_computation.4 | loop fusion | flops 2211840 | bytes 4423680 | tf_op jit(solution)/shard_map/stack | solution.py:173
  55.3 17.6 %shard_map.68 = (f32[27,96,384]{2,1,0:T(8,128)}, f32[4,97,1280]{2,1,0:T(8,128)}) custom-call(bf16[3,4,6,160,96]{4,3,2,1,0:T(8,128)(2,1)} %pad_maximum_fusion.cot_ref, bf16[1280,384]{1,0:T(8,128)(2,1)} %copy.16.act_ref, bf16[27,384,96]{2,1,0:T(8,128)(2,1)} %bitcast.39, f32[384,1280]{1,0:T(8,128)} %get-tuple-element.12.sx_ref), custom_call_target="tpu_custom_call" | custom-call | flops 5096079360 | bytes 13119488 | tf_op jit(solution)/shard_map/pallas_call | solution.py:80
  72.9 3.0 %constant_dynamic-slice_fusion.4 = f32[1296,384]{1,0:T(8,128)} fusion(f32[2592,384]{1,0:T(8,128)} %bitcast.36, s32[]{:T(128)S(6)} %select_n.297), kind=kLoop, calls=%fused_computation.56 | loop fusion | bytes 3981316 | tf_op jit(solution)/shard_map/dynamic_slice | solution.py:141
  75.9 4.2 %collective-permute-done.5 = f32[1296,384]{1,0:T(8,128)S(1)} collective-permute-done((f32[1296,384]{1,0:T(8,128)}, f32[1296,384]{1,0:T(8,128)S(1)}, u32[]{:S(2)}, u32[]{:S(2)}) %collective-permute-start.5) | collective-permute-done | bytes 1990688 | tf_op jit(solution)/shard_map/ppermute | solution.py:115
  80.1 1.8 %dynamic-slice_add_fusion = f32[1296,384]{1,0:T(8,128)S(1)} fusion(f32[1296,384]{1,0:T(8,128)S(1)} %collective-permute-done.5, f32[2592,384]{1,0:T(8,128)} %bitcast.37, s32[]{:T(128)S(6)} %select_n.296), kind=kLoop, calls=%fused_computation.7 | loop fusion | flops 497664 | bytes 5971972 | tf_op jit(solution)/shard_map/add | solution.py:142
  82.1 1.3 collective-permute-start.10
  83.4 1.3 collective-permute-start.6
  84.8 10.4 %collective-permute-done.10 = f32[324,384]{1,0:T(8,128)S(1)} collective-permute-done((f32[324,384]{1,0:T(8,128)S(1)}, f32[324,384]{1,0:T(8,128)S(1)}, u32[]{:S(2)}, u32[]{:S(2)}) %collective-permute-start.10) | collective-permute-done | bytes 497696 | tf_op jit(solution)/shard_map/ppermute | solution.py:115
  95.3 1.3 collective-permute-start.11
  96.6 1.1 dynamic-slice_add_fusion.2
  97.7 1.3 collective-permute-start.7
  99.0 3.3 %collective-permute-done.11 = f32[162,384]{1,0:T(8,128)S(1)} collective-permute-done((f32[162,384]{1,0:T(8,128)S(1)}, f32[162,384]{1,0:T(8,128)S(1)}, u32[]{:S(2)}, u32[]{:S(2)}) %collective-permute-start.11) | collective-permute-done | bytes 248864 | tf_op jit(solution)/shard_map/ppermute | solution.py:115
  102.4 1.3 collective-permute-start.12
  104.5 1.3 collective-permute-start.8
  105.8 2.8 %collective-permute-done.12 = f32[162,384]{1,0:T(8,128)S(1)} collective-permute-done((f32[162,384]{1,0:T(8,128)S(1)}, f32[162,384]{1,0:T(8,128)S(1)}, u32[]{:S(2)}, u32[]{:S(2)}) %collective-permute-start.12) | collective-permute-done | bytes 248864 | tf_op jit(solution)/shard_map/ppermute | solution.py:115
  108.7 1.3 collective-permute-start.13
  111.4 10.7 %collective-permute-done.13 = f32[324,384]{1,0:T(8,128)S(1)} collective-permute-done((f32[324,384]{1,0:T(8,128)S(1)}, f32[324,384]{1,0:T(8,128)S(1)}, u32[]{:S(2)}, u32[]{:S(2)}) %collective-permute-start.13) | collective-permute-done | bytes 497696 | tf_op jit(solution)/shard_map/ppermute | solution.py:115
  122.4 1.4 pad_maximum_fusion.1
  123.8 2.3 %collective-permute-start.14 = (f32[1296,384]{1,0:T(8,128)}, f32[1296,384]{1,0:T(8,128)}, u32[]{:S(2)}, u32[]{:S(2)}) collective-permute-start(f32[1296,384]{1,0:T(8,128)} %pad_maximum_fusion.1), channel_id=1, source_target_pairs={{0,4},{4,0},{1,5},{5,1},{2,6},{6,2},{3,7},{7,3},{8,12},{12,8},{9,1... | collective-permute-start | bytes 5971976 | tf_op jit(solution)/shard_map/ppermute | solution.py:115
  128.2 1.5 %fusion.13 = bf16[96,1280]{1,0:T(8,128)(2,1)S(1)} fusion(f32[96,1280]{1,0:T(8,128)} %copy.18, f32[1,97,1280]{2,1,0:T(8,128)} %reduce-scatter.2.cloned.1.call-done, f32[96,1280]{1,0:T(8,128)S(1)} %copy.17, f32[384,1280]{1,0:T(8,128)} %get-tuple-element.10, s32[]{:T(128)S(6)} %select_n.285, f32[1280]{0:T(1024)S(1)} %slice_reduce_fusion, ...), kind=kLoop, calls=%fused_computation.35 | loop fusion | flops 983040 | bytes 2227204 | tf_op jit(solution)/shard_map/convert_element_type | solution.py:198
  130.6 4.5 %fusion = f32[2592,384]{1,0:T(8,128)} fusion(f32[1296,384]{1,0:T(8,128)} %collective-permute-done.14, f32[648,384]{1,0:T(8,128)S(1)} %maximum_select_fusion.2, f32[648,384]{1,0:T(8,128)S(1)} %maximum_select_fusion.1, pred[]{:T(512)S(6)} %select_n.287), kind=kLoop, calls=%fused_computation.1 | loop fusion | flops 5971968 | bytes 7962625 | tf_op jit(solution)/shard_map/div | solution.py:185
  (59 shorter events, 12.4 us)
Async XLA Ops:
  7.2 120.2 %reduce-scatter.2.cloned.1.call-start = ((), (), s32[]{:S(2)}) async-start(), calls=%async_computation.1 | async-start | bytes 2662400 | tf_op jit(solution)/shard_map/reduce_scatter | solution.py:188
  7.2 10.5 %collective-permute-start = (bf16[96,2,4,160]{0,3,2,1:T(8,128)(2,1)}, bf16[96,2,4,160]{0,3,2,1:T(8,128)(2,1)S(1)}, u32[]{:S(2)}, u32[]{:S(2)}) collective-permute-start(bf16[96,2,4,160]{0,3,2,1:T(8,128)(2,1)} %param.5), channel_id=1, source_target_pairs={{0,1},{1,2},{2,3},{3,0},{4,5},{5,6},{6,7},{7,4},{8,9},{9,10},{10,1... | collective-permute-start | bytes 737288 | tf_op jit(solution)/shard_map/ppermute | solution.py:41
  8.6 27.8 %collective-permute-start.1 = (bf16[96,2,4,160]{0,3,2,1:T(8,128)(2,1)}, bf16[96,2,4,160]{0,3,2,1:T(8,128)(2,1)S(1)}, u32[]{:S(2)}, u32[]{:S(2)}) collective-permute-start(bf16[96,2,4,160]{0,3,2,1:T(8,128)(2,1)} %param.5), channel_id=1, source_target_pairs={{0,2},{1,3},{2,0},{3,1},{4,6},{5,7},{6,4},{7,5},{8,10},{9,11},{10,... | collective-permute-start | bytes 737288 | tf_op jit(solution)/shard_map/ppermute | solution.py:41
  9.6 29.5 %collective-permute-start.2 = (bf16[96,2,4,160]{0,3,2,1:T(8,128)(2,1)}, bf16[96,2,4,160]{0,3,2,1:T(8,128)(2,1)}, u32[]{:S(2)}, u32[]{:S(2)}) collective-permute-start(bf16[96,2,4,160]{0,3,2,1:T(8,128)(2,1)} %param.5), channel_id=1, source_target_pairs={{0,3},{1,0},{2,1},{3,2},{4,7},{5,4},{6,5},{7,6},{8,11},{9,8},{10,9... | collective-permute-start | bytes 737288 | tf_op jit(solution)/shard_map/ppermute | solution.py:41
  11.0 35.2 %collective-permute-start.3 = (bf16[96,2,4,160]{0,3,2,1:T(8,128)(2,1)}, bf16[96,2,4,160]{0,3,2,1:T(8,128)(2,1)S(1)}, u32[]{:S(2)}, u32[]{:S(2)}) collective-permute-start(bf16[96,2,4,160]{0,3,2,1:T(8,128)(2,1)} %param.6), channel_id=1, source_target_pairs={{8,0},{16,8},{24,16},{9,1},{17,9},{25,17},{10,2},{18,10},{26,18},{... | collective-permute-start | bytes 737288 | tf_op jit(solution)/shard_map/ppermute | solution.py:14
  12.4 4.3 %copy-start.4 = (bf16[96,2,4,160]{0,3,2,1:T(8,128)(2,1)S(1)}, bf16[96,2,4,160]{0,3,2,1:T(8,128)(2,1)}, u32[]{:S(2)}) copy-start(bf16[96,2,4,160]{0,3,2,1:T(8,128)(2,1)} %param.6) | copy-start | bytes 737284
  12.4 26.7 %copy-start.5 = (bf16[96,2,4,160]{0,3,2,1:T(8,128)(2,1)S(1)}, bf16[96,2,4,160]{0,3,2,1:T(8,128)(2,1)}, u32[]{:S(2)}) copy-start(bf16[96,2,4,160]{0,3,2,1:T(8,128)(2,1)} %param.5) | copy-start | bytes 737284
  36.3 0.7 copy-start.6
  44.3 3.3 %copy-start.7 = (f32[384]{0:T(512)S(1)}, f32[384]{0:T(512)}, u32[]{:S(2)}) copy-start(f32[384]{0:T(512)} %param.9) | copy-start | bytes 4612
  44.3 3.3 %copy-start.8 = (f32[384]{0:T(512)S(1)}, f32[384]{0:T(512)}, u32[]{:S(2)}) copy-start(f32[384]{0:T(512)} %param.8) | copy-start | bytes 4612
  46.3 0.8 copy-start.1
  47.1 4.8 %collective-permute-start.4 = (bf16[96,4,1,160]{0,3,2,1:T(8,128)(2,1)S(1)}, bf16[96,4,1,160]{0,3,2,1:T(8,128)(2,1)S(1)}, u32[]{:S(2)}, u32[]{:S(2)}) collective-permute-start(bf16[96,4,1,160]{0,3,2,1:T(8,128)(2,1)S(1)} %slice_select_fusion), channel_id=1, source_target_pairs={{0,4},{4,0},{1,5},{5,1},{2,6},{6,2},{3,7},{7,3},{8,12},{12,8},{9,1... | collective-permute-start | bytes 368648 | tf_op jit(solution)/shard_map/ppermute | solution.py:24
  50.6 1.4 copy-start.2
  75.9 4.2 %collective-permute-start.5 = (f32[1296,384]{1,0:T(8,128)}, f32[1296,384]{1,0:T(8,128)S(1)}, u32[]{:S(2)}, u32[]{:S(2)}) collective-permute-start(f32[1296,384]{1,0:T(8,128)} %constant_dynamic-slice_fusion.4), channel_id=1, source_target_pairs={{0,4},{4,0},{1,5},{5,1},{2,6},{6,2},{3,7},{7,3},{8,12},{12,8},{9,1... | collective-permute-start | bytes 5971976 | tf_op jit(solution)/shard_map/ppermute | solution.py:115
  82.1 13.1 %collective-permute-start.10 = (f32[324,384]{1,0:T(8,128)S(1)}, f32[324,384]{1,0:T(8,128)S(1)}, u32[]{:S(2)}, u32[]{:S(2)}) collective-permute-start(f32[324,384]{1,0:T(8,128)S(1)} %constant_dynamic-slice_fusion.1), channel_id=1, source_target_pairs={{0,16},{8,24},{16,0},{24,8},{1,17},{9,25},{17,1},{25,9},{2,18},{10... | collective-permute-start | bytes 1493000 | tf_op jit(solution)/shard_map/ppermute | solution.py:115
  83.4 13.2 %collective-permute-start.6 = (f32[324,384]{1,0:T(8,128)S(1)}, f32[324,384]{1,0:T(8,128)}, u32[]{:S(2)}, u32[]{:S(2)}) collective-permute-start(f32[324,384]{1,0:T(8,128)S(1)} %constant_dynamic-slice_fusion.3), channel_id=1, source_target_pairs={{0,8},{8,0},{16,24},{24,16},{1,9},{9,1},{17,25},{25,17},{2,10},{10... | collective-permute-start | bytes 1493000 | tf_op jit(solution)/shard_map/ppermute | solution.py:115
  95.3 7.1 %collective-permute-start.11 = (f32[162,384]{1,0:T(8,128)S(1)}, f32[162,384]{1,0:T(8,128)S(1)}, u32[]{:S(2)}, u32[]{:S(2)}) collective-permute-start(f32[162,384]{1,0:T(8,128)S(1)} %constant_dynamic-slice_fusion), channel_id=1, source_target_pairs={{0,8},{8,0},{16,24},{24,16},{1,9},{9,1},{17,25},{25,17},{2,10},{10... | collective-permute-start | bytes 746504 | tf_op jit(solution)/shard_map/ppermute | solution.py:115
  97.7 6.8 %collective-permute-start.7 = (f32[162,384]{1,0:T(8,128)S(1)}, f32[162,384]{1,0:T(8,128)S(1)}, u32[]{:S(2)}, u32[]{:S(2)}) collective-permute-start(f32[162,384]{1,0:T(8,128)S(1)} %constant_dynamic-slice_fusion.2), channel_id=1, source_target_pairs={{0,16},{8,24},{16,0},{24,8},{1,17},{9,25},{17,1},{25,9},{2,18},{10... | collective-permute-start | bytes 746504 | tf_op jit(solution)/shard_map/ppermute | solution.py:115
  102.4 6.2 %collective-permute-start.12 = (f32[162,384]{1,0:T(8,128)S(1)}, f32[162,384]{1,0:T(8,128)S(1)}, u32[]{:S(2)}, u32[]{:S(2)}) collective-permute-start(f32[162,384]{1,0:T(8,128)S(1)} %dynamic-slice_add_fusion.3), channel_id=1, source_target_pairs={{0,8},{8,0},{16,24},{24,16},{1,9},{9,1},{17,25},{25,17},{2,10},{10... | collective-permute-start | bytes 746504 | tf_op jit(solution)/shard_map/ppermute | solution.py:115
  104.5 5.9 %collective-permute-start.8 = (f32[162,384]{1,0:T(8,128)S(1)}, f32[162,384]{1,0:T(8,128)S(1)}, u32[]{:S(2)}, u32[]{:S(2)}) collective-permute-start(f32[162,384]{1,0:T(8,128)S(1)} %dynamic-slice_add_fusion.4), channel_id=1, source_target_pairs={{0,16},{8,24},{16,0},{24,8},{1,17},{9,25},{17,1},{25,9},{2,18},{10... | collective-permute-start | bytes 746504 | tf_op jit(solution)/shard_map/ppermute | solution.py:115
  108.7 13.3 %collective-permute-start.13 = (f32[324,384]{1,0:T(8,128)S(1)}, f32[324,384]{1,0:T(8,128)S(1)}, u32[]{:S(2)}, u32[]{:S(2)}) collective-permute-start(f32[324,384]{1,0:T(8,128)S(1)} %maximum_select_fusion.4), channel_id=1, source_target_pairs={{0,16},{8,24},{16,0},{24,8},{1,17},{9,25},{17,1},{25,9},{2,18},{10... | collective-permute-start | bytes 1493000 | tf_op jit(solution)/shard_map/ppermute | solution.py:115
  110.5 11.7 %collective-permute-start.9 = (f32[324,384]{1,0:T(8,128)S(1)}, f32[324,384]{1,0:T(8,128)S(1)}, u32[]{:S(2)}, u32[]{:S(2)}) collective-permute-start(f32[324,384]{1,0:T(8,128)S(1)} %maximum_select_fusion.3), channel_id=1, source_target_pairs={{0,8},{8,0},{16,24},{24,16},{1,9},{9,1},{17,25},{25,17},{2,10},{10... | collective-permute-start | bytes 1493000 | tf_op jit(solution)/shard_map/ppermute | solution.py:115
  122.4 3.7 %copy-start = (f32[96,1280]{0,1:T(8,128)S(1)}, f32[96,1280]{0,1:T(8,128)}, u32[]{:S(2)}) copy-start(f32[96,1280]{0,1:T(8,128)} %get-tuple-element.22) | copy-start | bytes 1474564
  122.4 4.7 %copy-start.3 = (f32[96,1280]{0,1:T(8,128)S(1)}, f32[96,1280]{0,1:T(8,128)}, u32[]{:S(2)}) copy-start(f32[96,1280]{0,1:T(8,128)} %get-tuple-element.20) | copy-start | bytes 1474564
  123.8 6.8 %collective-permute-start.14 = (f32[1296,384]{1,0:T(8,128)}, f32[1296,384]{1,0:T(8,128)}, u32[]{:S(2)}, u32[]{:S(2)}) collective-permute-start(f32[1296,384]{1,0:T(8,128)} %pad_maximum_fusion.1), channel_id=1, source_target_pairs={{0,4},{4,0},{1,5},{5,1},{2,6},{6,2},{3,7},{7,3},{8,12},{12,8},{9,1... | collective-permute-start | bytes 5971976 | tf_op jit(solution)/shard_map/ppermute | solution.py:115
Sparse Core Ops, SparseCore 0:
  84.9 40.8 reduce-scatter.1
